TPU v7x, 32 devices: a whole 2x2x4 slice. The times are simulated.
32 devices in a mesh: tm: 8 (over y, x, core), row: 4 (over z).
Axes of the slice: x: 2, y: 2, z: 4, core: 2. Of those that a mesh axis runs over, the one named last changes fastest.
Arguments:
- section_maps: float32 [8, 1024, 1024], P('tm', 'row'), may hold values from -0.04375 to 1.09375, as said below
- terminal_cost: float32 [512, 512], P('row'), may hold values from -0.075 to 1.075, as said below
- terminal_states: float32 [512, 2048], replicated, may hold values from -6 to 6
Outputs:
- trajectories: float32 [8, 1024, 2048], P('tm', 'row')
- section_cost: float32 [8, 2048], P('tm', 'row')
Inputs may be any that keep to these rules, and one draw needn't show every extreme that they name: `section_maps`: each section map is its diagonal plus small entries off the diagonal. `terminal_cost`: symmetric.
All inputs are finite; a program needn't handle non-finite values.
Results may differ from a plain program's by a relative error of at most 0.0003.
Values sent between devices are 32-bit elements; how exact they have to be, the bound alone decides.
No kernel may reach another device: no remote copies, remote signals or barrier semaphores. Data moves between devices by JAX's collectives and lax.ppermute only.
A program may use at most 64 MiB of HBM per device.

v0:
```python
import jax
import jax.numpy as jnp
from jax import lax
from jax.sharding import PartitionSpec as P


def shifted(block, axis, distance):
    devices = range(lax.axis_size(axis))
    route = [(i - distance, i) for i in devices if i - distance in devices]
    return lax.ppermute(block, axis, route)


def product(left, right):
    return jnp.dot(left, right, precision=lax.Precision.HIGHEST, preferred_element_type=jnp.float32)


def body(section_maps, terminal_cost, terminal_states):
    running = section_maps[0]
    state_dim = running.shape[1] // 2
    tm_count = lax.axis_size("tm")
    tm_place = lax.axis_index("tm")
    for level_index in range((tm_count - 1).bit_length()):
        stride = 1 << level_index
        gathered = lax.all_gather(running, "row", axis=0, tiled=True)
        further = shifted(gathered, "tm", -stride)
        combined = product(running, further)
        running = jnp.where(tm_place + stride < tm_count, combined, running)
    portion = lax.all_gather(terminal_cost, "row", axis=0, tiled=True)
    columns = lax.dynamic_slice_in_dim(running, state_dim, portion.shape[0], 1)
    value_rows = running[:, :state_dim] + product(columns, portion)
    rows_traj = product(value_rows, terminal_states)
    regrouped = lax.all_to_all(rows_traj, "row", split_axis=1, concat_axis=0, tiled=True)
    section_cost = jnp.sum(regrouped[:state_dim] * regrouped[state_dim:], axis=0) / state_dim
    return (rows_traj[None], section_cost[None])


def solution(mesh):
    in_specs = (P("tm", "row", None), P("row", None), P())
    out_specs = (P("tm", "row", None), P("tm", "row"))
    return jax.shard_map(body, mesh=mesh, in_specs=in_specs, out_specs=out_specs, check_vma=False)
```

profile of v0, /device:TPU:0, one launch (start us, length us, event | category | flops | bytes accessed | tf_op | source)
XLA Modules:
  0.0 577.2 jit_solution(18376967483935607676)
XLA Ops:
  7.2 0.0 all-gather.12.cloned.1.call-start
  7.2 0.7 all-gather.12.cloned.1.call-update
  7.9 0.0 all-gather.6.cloned.1.call-start
  7.9 85.1 %all-gather.12.cloned.1.call-done = f32[1,1024,1024]{2,1,0:T(8,128)} async-done(((f32[1,256,1024]{2,1,0:T(8,128)}), f32[1,1024,1024]{2,1,0:T(8,128)}) %all-gather.12.cloned.1.call-update) | async-done | bytes 4194320 | tf_op jit(solution)/shard_map/all_gather | solution.py:24
  93.0 1.3 collective-permute-start
  94.3 8.1 %collective-permute-done = f32[1024,1024]{1,0:T(8,128)} collective-permute-done((f32[1024,1024]{1,0:T(8,128)}, f32[1024,1024]{1,0:T(8,128)}, u32[]{:S(2)}, u32[]{:S(2)}) %collective-permute-start) | collective-permute-done | bytes 4194336 | tf_op jit(solution)/shard_map/ppermute | solution.py:10
  102.4 7.4 %convolution_select_fusion.2 = f32[256,1024]{1,0:T(8,128)} fusion(f32[1024,1024]{1,0:T(8,128)} %collective-permute-done, f32[1,256,1024]{2,1,0:T(8,128)} %param.3, pred[]{:T(512)S(6)} %lt.11), kind=kOutput, calls=%fused_computation.3 | convolution fusion | flops 3221487616 | bytes 6291457 | tf_op jit(solution)/shard_map/dot_general | solution.py:14
  109.9 0.0 all-gather.8.cloned.1.call-start
  109.9 119.6 %all-gather.6.cloned.1.call-done = f32[1024,1024]{1,0:T(8,128)} async-done(((f32[256,1024]{1,0:T(8,128)}), f32[1024,1024]{1,0:T(8,128)}) %all-gather.6.cloned.1.call-update) | async-done | bytes 4194320 | tf_op jit(solution)/shard_map/all_gather | solution.py:24
  229.5 1.3 collective-permute-start.1
  230.8 93.1 %collective-permute-done.1 = f32[1024,1024]{1,0:T(8,128)} collective-permute-done((f32[1024,1024]{1,0:T(8,128)}, f32[1024,1024]{1,0:T(8,128)}, u32[]{:S(2)}, u32[]{:S(2)}) %collective-permute-start.1) | collective-permute-done | bytes 4194336 | tf_op jit(solution)/shard_map/ppermute | solution.py:10
  323.9 7.5 %convolution_select_fusion.1 = f32[256,1024]{1,0:T(8,128)} fusion(f32[256,1024]{1,0:T(8,128)} %convolution_select_fusion.2, f32[1024,1024]{1,0:T(8,128)} %collective-permute-done.1, pred[]{:T(512)S(6)} %lt.10), kind=kOutput, calls=%fused_computation.2 | convolution fusion | flops 3221487616 | bytes 6291457 | tf_op jit(solution)/shard_map/dot_general | solution.py:14
  331.5 0.0 all-gather.10.cloned.1.call-start
  331.5 79.5 %all-gather.8.cloned.1.call-done = f32[1024,1024]{1,0:T(8,128)} async-done(((f32[256,1024]{1,0:T(8,128)}), f32[1024,1024]{1,0:T(8,128)}) %all-gather.8.cloned.1.call-update) | async-done | bytes 4194320 | tf_op jit(solution)/shard_map/all_gather | solution.py:24
  411.0 1.5 collective-permute-start.2
  412.5 92.9 %collective-permute-done.2 = f32[1024,1024]{1,0:T(8,128)} collective-permute-done((f32[1024,1024]{1,0:T(8,128)}, f32[1024,1024]{1,0:T(8,128)}, u32[]{:S(2)}, u32[]{:S(2)}) %collective-permute-start.2) | collective-permute-done | bytes 4194336 | tf_op jit(solution)/shard_map/ppermute | solution.py:10
  505.4 6.6 %convolution_select_fusion = f32[256,1024]{1,0:T(8,128)S(1)} fusion(f32[256,1024]{1,0:T(8,128)} %convolution_select_fusion.1, f32[1024,1024]{1,0:T(8,128)} %collective-permute-done.2, pred[]{:T(512)S(6)} %lt.9), kind=kOutput, calls=%fused_computation.1 | convolution fusion | flops 3221487616 | bytes 6291457 | tf_op jit(solution)/shard_map/dot_general | solution.py:14
  512.0 0.0 all-gather.10.cloned.1.call-done
  512.0 2.3 fusion.2
  514.3 5.5 fusion.4
  519.8 0.2 copy.8
  520.0 50.0 %all_to_all.16 = f32[256,4,512]{2,0,1:T(8,128)S(1)} all-to-all(f32[256,4,512]{2,0,1:T(8,128)S(1)} %bitcast.21), channel_id=1, replica_groups=mesh['tm'=8,'row'=4] {'row'}, dimensions={1} | all-to-all | bytes 4194304 | tf_op jit(solution)/shard_map/all_to_all | solution.py:32
  570.0 0.1 fusion
  570.1 0.6 broadcast_multiply_fusion
  (5 shorter events, 0.1 us)
Async XLA Ops:
  7.2 85.9 %all-gather.12.cloned.1.call-start = ((), (), s32[]{:S(2)}) async-start(), calls=%async_computation.4 | async-start | bytes 5242880 | tf_op jit(solution)/shard_map/all_gather | solution.py:24
  7.9 221.6 %all-gather.6.cloned.1.call-start = ((), (), s32[]{:S(2)}) async-start(), calls=%async_computation.1 | async-start | bytes 5242880 | tf_op jit(solution)/shard_map/all_gather | solution.py:24
  93.0 9.4 %collective-permute-start = (f32[1024,1024]{1,0:T(8,128)}, f32[1024,1024]{1,0:T(8,128)}, u32[]{:S(2)}, u32[]{:S(2)}) collective-permute-start(f32[1024,1024]{1,0:T(8,128)} %bitcast.23), channel_id=1, source_target_pairs={{4,0},{8,4},{12,8},{16,12},{20,16},{24,20},{28,24},{5,1},{9,5},{13... | collective-permute-start | bytes 12582920 | tf_op jit(solution)/shard_map/ppermute | solution.py:10
  109.9 301.2 %all-gather.8.cloned.1.call-start = ((), (), s32[]{:S(2)}) async-start(), calls=%async_computation.2 | async-start | bytes 5242880 | tf_op jit(solution)/shard_map/all_gather | solution.py:24
  229.5 94.4 %collective-permute-start.1 = (f32[1024,1024]{1,0:T(8,128)}, f32[1024,1024]{1,0:T(8,128)}, u32[]{:S(2)}, u32[]{:S(2)}) collective-permute-start(f32[1024,1024]{1,0:T(8,128)} %all-gather.6.cloned.1.call-done), channel_id=1, source_target_pairs={{8,0},{12,4},{16,8},{20,12},{24,16},{28,20},{9,1},{13,5},{17,9},{2... | collective-permute-start | bytes 12582920 | tf_op jit(solution)/shard_map/ppermute | solution.py:10
  331.5 180.6 %all-gather.10.cloned.1.call-start = ((), (), s32[]{:S(2)}) async-start(), calls=%async_computation.3 | async-start | bytes 1310720 | tf_op jit(solution)/shard_map/all_gather | solution.py:28
  411.0 94.4 %collective-permute-start.2 = (f32[1024,1024]{1,0:T(8,128)}, f32[1024,1024]{1,0:T(8,128)}, u32[]{:S(2)}, u32[]{:S(2)}) collective-permute-start(f32[1024,1024]{1,0:T(8,128)} %all-gather.8.cloned.1.call-done), channel_id=1, source_target_pairs={{16,0},{20,4},{24,8},{28,12},{17,1},{21,5},{25,9},{29,13},{18,2},{... | collective-permute-start | bytes 12582920 | tf_op jit(solution)/shard_map/ppermute | solution.py:10
  519.8 50.2 %copy-start = (f32[256,2048]{1,0:T(8,128)}, f32[256,2048]{1,0:T(8,128)S(1)}, u32[]{:S(2)}) copy-start(f32[256,2048]{1,0:T(8,128)S(1)} %fusion.4) | copy-start | bytes 6291460
Sparse Core Ops, SparseCore 0:
  9.5 83.4 all-gather.11
  110.0 119.4 all-gather.5
  331.6 79.3 all-gather.7
  412.7 29.3 all-gather.9
where the time goes:
time: 577 us
  waiting for transfers between devices  479 us (83%)
  blocking collectives  50 us (9%)
  matrix products  29.3 us (5%)
  between operations  13.9 us (2%)
    all_gather x3, waiting for transfers between devices, body(): gathered = lax.all_gather(running, 'row', axis=0, tiled=True)  284 us
    ppermute x3, waiting for transfers between devices, shifted(): return lax.ppermute(block, axis, route)  194 us
    all_to_all x1, blocking collectives, body(): lax.all_to_all(rows_traj, 'row', split_axis=1, concat_axis=0, tiled=True)  50 us
    dot_general x5, matrix products, product(): jnp.dot(left, right, precision=lax.Precision.HIGHEST, preferred_element_t...  29.3 us
  transfers between devices with their start and end apart: 7, of which 6 were waited for; matrix products, arithmetic and copies ran while one was open for 1% of the time, Pallas kernels for 0%

commit v1 on v0

v1 whole, which is shorter than its diff:
```python
import jax
import jax.numpy as jnp
from jax import lax
from jax.sharding import PartitionSpec as P

CHUNKS = 4
AXES = ("tm", "row")


def product(left, right):
    return jnp.dot(left, right, precision=lax.Precision.HIGHEST, preferred_element_type=jnp.float32)


def assemble(pieces, place, count):
    ordered = []
    for q in range(count):
        picked = pieces[0]
        for d in range(1, count):
            picked = jnp.where((place - d) % count == q, pieces[d], picked)
        ordered.append(picked)
    return jnp.concatenate(ordered, axis=0)


def spread(block, source, target, count, with_self):
    pieces = [block] if with_self else []
    for d in range(0 if not with_self else 1, count):
        pairs = [(source * count + q, target * count + (q + d) % count) for q in range(count)]
        pieces.append(lax.ppermute(block, AXES, pairs))
    return pieces


def body(section_maps, terminal_cost, terminal_states):
    groups = lax.axis_size("tm")
    count = lax.axis_size("row")
    group = lax.axis_index("tm")
    place = lax.axis_index("row")
    local = section_maps[0]
    state_dim = local.shape[1] // 2
    width = state_dim // CHUNKS

    cost_rows = assemble(spread(terminal_cost, groups - 1, groups - 1, count, True), place, count)
    identity = jnp.eye(state_dim, dtype=jnp.float32)
    terminal_map = jnp.concatenate([identity, cost_rows], axis=0)
    incoming = [terminal_map[:, j * width:(j + 1) * width] for j in range(CHUNKS)]
    own = [None] * CHUNKS
    whole_first = [None] * CHUNKS
    for k in range(groups - 1, -1, -1):
        for j in range(CHUNKS):
            fresh = product(local, incoming[j])
            own[j] = fresh if own[j] is None else jnp.where(group == k, fresh, own[j])
            if k > 0:
                got = assemble(spread(fresh, k, k - 1, count, False), place, count)
                incoming[j] = jnp.where(group == k - 1, got, incoming[j])
            else:
                whole_first[j] = assemble(spread(fresh, 0, 0, count, True), place, count)
    own_rows = jnp.concatenate(own, axis=1)
    rows_traj = product(own_rows, terminal_states)

    cols = terminal_states.shape[1] // count
    my_cols = lax.dynamic_slice_in_dim(terminal_states, place * cols, cols, 1)

    def cost_of(whole):
        traj_cols = product(whole, my_cols)
        return jnp.sum(traj_cols[:state_dim] * traj_cols[state_dim:], axis=0) / state_dim

    next_whole = jnp.concatenate(incoming, axis=1)
    next_cost = cost_of(next_whole)
    back = lax.ppermute(next_cost, "tm", [(g, g + 1) for g in range(groups - 1)])
    first_cost = cost_of(jnp.concatenate(whole_first, axis=1))
    section_cost = jnp.where(group == 0, first_cost, back)
    return (rows_traj[None], section_cost[None])


def solution(mesh):
    in_specs = (P("tm", "row", None), P("row", None), P())
    out_specs = (P("tm", "row", None), P("tm", "row"))
    return jax.shard_map(body, mesh=mesh, in_specs=in_specs, out_specs=out_specs, check_vma=False)
```

time: 577 us -> 579 us (level); the launches traced: 577 us -> 569 us
  starting transfers between devices: 4.18 us -> 474 us
  waiting for transfers between devices: 479 us -> 34.1 us
  blocking collectives: 50 us -> 0 us
  matrix products: 29.3 us -> 49.9 us
  between operations: 13.9 us -> 3.56 us
    ppermute x3 -> x128, starting transfers between devices: 4.02 us -> 474 us  [the longest x127 469 us: spread(): pieces.append(lax.ppermute(block, AXES, pairs))]
    all_gather x4 -> x0, waiting for transfers between devices: 284 us -> none  [the longest x3 284 us: body(): gathered = lax.all_gather(running, 'row', axis=0, tiled=True)]
    ppermute x3 -> x128, waiting for transfers between devices: 194 us -> 34.1 us  [the longest x127 34.1 us: spread(): pieces.append(lax.ppermute(block, AXES, pairs))]
    all_to_all x1 -> x0, blocking collectives: 50 us -> none  [body(): lax.all_to_all(rows_traj, 'row', split_axis=1, concat_axis=0, tiled=True)]
    dot_general x5 -> x35, matrix products: 29.3 us -> 49.9 us  [product(): jnp.dot(left, right, precision=lax.Precision.HIGHEST, preferred_element_t...]
  transfers between devices with their start and end apart: 7 -> 128, of which waited for: 6 -> 5; matrix products, arithmetic and copies ran while one was open for 1% -> 9% of each run, Pallas kernels for 0% -> 0%
where the time goes in v1:
time: 579 us; the launch traced here: 569 us
  starting transfers between devices  474 us (82%)
  matrix products  49.9 us (9%)
  waiting for transfers between devices  34.1 us (6%)
    ppermute x127, starting transfers between devices, spread(): pieces.append(lax.ppermute(block, AXES, pairs))  469 us
    dot_general x35, matrix products, product(): jnp.dot(left, right, precision=lax.Precision.HIGHEST, preferred_element_t...  49.9 us
    ppermute x127, waiting for transfers between devices, spread(): pieces.append(lax.ppermute(block, AXES, pairs))  34.1 us
  transfers between devices with their start and end apart: 128, of which 5 were waited for; matrix products, arithmetic and copies ran while one was open for 9% of the time, Pallas kernels for 0%

profile of v1, /device:TPU:0, one launch (start us, length us, event | category | flops | bytes accessed | tf_op | source)
XLA Modules:
  0.0 568.7 jit_solution(16307977139727474224)
XLA Ops:
  1.8 7.8 %collective-permute-start = (f32[128,512]{0,1:T(8,128)S(1)}, f32[128,512]{0,1:T(8,128)S(1)}, u32[]{:S(2)}, u32[]{:S(2)}) collective-permute-start(f32[128,512]{0,1:T(8,128)S(1)} %copy.5), channel_id=1, source_target_pairs={{28,31},{29,28},{30,29},{31,30}} | collective-permute-start | bytes 786440 | tf_op jit(solution)/shard_map/ppermute | solution.py:28
  24.7 10.5 %collective-permute-start.87 = (f32[256,128]{0,1:T(8,128)S(1)}, f32[256,128]{0,1:T(8,128)S(1)}, u32[]{:S(2)}, u32[]{:S(2)}) collective-permute-start(f32[256,128]{0,1:T(8,128)S(1)} %convolution_bitcast_fusion.8), channel_id=1, source_target_pairs={{28,27},{29,24},{30,25},{31,26}} | collective-permute-start | bytes 393224 | tf_op jit(solution)/shard_map/ppermute | solution.py:28
  35.3 6.7 %collective-permute-start.88 = (f32[256,128]{0,1:T(8,128)S(1)}, f32[256,128]{0,1:T(8,128)S(1)}, u32[]{:S(2)}, u32[]{:S(2)}) collective-permute-start(f32[256,128]{0,1:T(8,128)S(1)} %convolution_bitcast_fusion.8), channel_id=1, source_target_pairs={{28,26},{29,27},{30,24},{31,25}} | collective-permute-start | bytes 393224 | tf_op jit(solution)/shard_map/ppermute | solution.py:28
  42.0 6.7 %collective-permute-start.89 = (f32[256,128]{0,1:T(8,128)S(1)}, f32[256,128]{0,1:T(8,128)S(1)}, u32[]{:S(2)}, u32[]{:S(2)}) collective-permute-start(f32[256,128]{0,1:T(8,128)S(1)} %convolution_bitcast_fusion.8), channel_id=1, source_target_pairs={{28,25},{29,26},{30,27},{31,24}} | collective-permute-start | bytes 393224 | tf_op jit(solution)/shard_map/ppermute | solution.py:28
  148.4 7.0 %collective-permute-start.92 = (f32[256,128]{0,1:T(8,128)S(1)}, f32[256,128]{0,1:T(8,128)S(1)}, u32[]{:S(2)}, u32[]{:S(2)}) collective-permute-start(f32[256,128]{0,1:T(8,128)S(1)} %convolution_bitcast_fusion.7), channel_id=1, source_target_pairs={{24,22},{25,23},{26,20},{27,21}} | collective-permute-start | bytes 393224 | tf_op jit(solution)/shard_map/ppermute | solution.py:28
  155.5 7.0 %collective-permute-start.93 = (f32[256,128]{0,1:T(8,128)S(1)}, f32[256,128]{0,1:T(8,128)S(1)}, u32[]{:S(2)}, u32[]{:S(2)}) collective-permute-start(f32[256,128]{0,1:T(8,128)S(1)} %convolution_bitcast_fusion.7), channel_id=1, source_target_pairs={{24,21},{25,22},{26,23},{27,20}} | collective-permute-start | bytes 393224 | tf_op jit(solution)/shard_map/ppermute | solution.py:28
  162.5 7.0 %collective-permute-start.94 = (f32[256,128]{0,1:T(8,128)S(1)}, f32[256,128]{0,1:T(8,128)S(1)}, u32[]{:S(2)}, u32[]{:S(2)}) collective-permute-start(f32[256,128]{0,1:T(8,128)S(1)} %convolution_bitcast_fusion.7), channel_id=1, source_target_pairs={{24,20},{25,21},{26,22},{27,23}} | collective-permute-start | bytes 393224 | tf_op jit(solution)/shard_map/ppermute | solution.py:28
  171.1 7.0 %collective-permute-start.63 = (f32[256,128]{0,1:T(8,128)S(1)}, f32[256,128]{0,1:T(8,128)S(1)}, u32[]{:S(2)}, u32[]{:S(2)}) collective-permute-start(f32[256,128]{0,1:T(8,128)S(1)} %convolution_bitcast_fusion.15), channel_id=1, source_target_pairs={{24,23},{25,20},{26,21},{27,22}} | collective-permute-start | bytes 393224 | tf_op jit(solution)/shard_map/ppermute | solution.py:28
  180.5 7.0 %collective-permute-start.64 = (f32[256,128]{0,1:T(8,128)S(1)}, f32[256,128]{0,1:T(8,128)S(1)}, u32[]{:S(2)}, u32[]{:S(2)}) collective-permute-start(f32[256,128]{0,1:T(8,128)S(1)} %convolution_bitcast_fusion.15), channel_id=1, source_target_pairs={{24,22},{25,23},{26,20},{27,21}} | collective-permute-start | bytes 393224 | tf_op jit(solution)/shard_map/ppermute | solution.py:28
  187.5 7.0 %collective-permute-start.65 = (f32[256,128]{0,1:T(8,128)S(1)}, f32[256,128]{0,1:T(8,128)S(1)}, u32[]{:S(2)}, u32[]{:S(2)}) collective-permute-start(f32[256,128]{0,1:T(8,128)S(1)} %convolution_bitcast_fusion.15), channel_id=1, source_target_pairs={{24,21},{25,22},{26,23},{27,20}} | collective-permute-start | bytes 393224 | tf_op jit(solution)/shard_map/ppermute | solution.py:28
  194.5 7.0 %collective-permute-start.66 = (f32[256,128]{0,1:T(8,128)S(1)}, f32[256,128]{0,1:T(8,128)S(1)}, u32[]{:S(2)}, u32[]{:S(2)}) collective-permute-start(f32[256,128]{0,1:T(8,128)S(1)} %convolution_bitcast_fusion.15), channel_id=1, source_target_pairs={{24,20},{25,21},{26,22},{27,23}} | collective-permute-start | bytes 393224 | tf_op jit(solution)/shard_map/ppermute | solution.py:28
  201.6 7.0 %collective-permute-start.35 = (f32[256,128]{0,1:T(8,128)S(1)}, f32[256,128]{0,1:T(8,128)S(1)}, u32[]{:S(2)}, u32[]{:S(2)}) collective-permute-start(f32[256,128]{0,1:T(8,128)S(1)} %convolution_bitcast_fusion.23), channel_id=1, source_target_pairs={{24,23},{25,20},{26,21},{27,22}} | collective-permute-start | bytes 393224 | tf_op jit(solution)/shard_map/ppermute | solution.py:28
  209.9 7.0 %collective-permute-start.36 = (f32[256,128]{0,1:T(8,128)S(1)}, f32[256,128]{0,1:T(8,128)S(1)}, u32[]{:S(2)}, u32[]{:S(2)}) collective-permute-start(f32[256,128]{0,1:T(8,128)S(1)} %convolution_bitcast_fusion.23), channel_id=1, source_target_pairs={{24,22},{25,23},{26,20},{27,21}} | collective-permute-start | bytes 393224 | tf_op jit(solution)/shard_map/ppermute | solution.py:28
  216.9 7.0 %collective-permute-start.37 = (f32[256,128]{0,1:T(8,128)S(1)}, f32[256,128]{0,1:T(8,128)S(1)}, u32[]{:S(2)}, u32[]{:S(2)}) collective-permute-start(f32[256,128]{0,1:T(8,128)S(1)} %convolution_bitcast_fusion.23), channel_id=1, source_target_pairs={{24,21},{25,22},{26,23},{27,20}} | collective-permute-start | bytes 393224 | tf_op jit(solution)/shard_map/ppermute | solution.py:28
  223.9 7.0 %collective-permute-start.38 = (f32[256,128]{0,1:T(8,128)S(1)}, f32[256,128]{0,1:T(8,128)S(1)}, u32[]{:S(2)}, u32[]{:S(2)}) collective-permute-start(f32[256,128]{0,1:T(8,128)S(1)} %convolution_bitcast_fusion.23), channel_id=1, source_target_pairs={{24,20},{25,21},{26,22},{27,23}} | collective-permute-start | bytes 393224 | tf_op jit(solution)/shard_map/ppermute | solution.py:28
  231.0 7.2 %collective-permute-start.7 = (f32[256,128]{0,1:T(8,128)S(1)}, f32[256,128]{0,1:T(8,128)S(1)}, u32[]{:S(2)}, u32[]{:S(2)}) collective-permute-start(f32[256,128]{0,1:T(8,128)S(1)} %convolution_bitcast_fusion.31), channel_id=1, source_target_pairs={{24,23},{25,20},{26,21},{27,22}} | collective-permute-start | bytes 393224 | tf_op jit(solution)/shard_map/ppermute | solution.py:28
  239.4 7.0 %collective-permute-start.8 = (f32[256,128]{0,1:T(8,128)S(1)}, f32[256,128]{0,1:T(8,128)S(1)}, u32[]{:S(2)}, u32[]{:S(2)}) collective-permute-start(f32[256,128]{0,1:T(8,128)S(1)} %convolution_bitcast_fusion.31), channel_id=1, source_target_pairs={{24,22},{25,23},{26,20},{27,21}} | collective-permute-start | bytes 393224 | tf_op jit(solution)/shard_map/ppermute | solution.py:28
  246.5 7.0 %collective-permute-start.9 = (f32[256,128]{0,1:T(8,128)S(1)}, f32[256,128]{0,1:T(8,128)S(1)}, u32[]{:S(2)}, u32[]{:S(2)}) collective-permute-start(f32[256,128]{0,1:T(8,128)S(1)} %convolution_bitcast_fusion.31), channel_id=1, source_target_pairs={{24,21},{25,22},{26,23},{27,20}} | collective-permute-start | bytes 393224 | tf_op jit(solution)/shard_map/ppermute | solution.py:28
  253.5 7.0 %collective-permute-start.10 = (f32[256,128]{0,1:T(8,128)S(1)}, f32[256,128]{0,1:T(8,128)S(1)}, u32[]{:S(2)}, u32[]{:S(2)}) collective-permute-start(f32[256,128]{0,1:T(8,128)S(1)} %convolution_bitcast_fusion.31), channel_id=1, source_target_pairs={{24,20},{25,21},{26,22},{27,23}} | collective-permute-start | bytes 393224 | tf_op jit(solution)/shard_map/ppermute | solution.py:28
  260.5 7.0 %collective-permute-start.95 = (f32[256,128]{0,1:T(8,128)S(1)}, f32[256,128]{0,1:T(8,128)S(1)}, u32[]{:S(2)}, u32[]{:S(2)}) collective-permute-start(f32[256,128]{0,1:T(8,128)S(1)} %convolution_bitcast_fusion.6), channel_id=1, source_target_pairs={{20,19},{21,16},{22,17},{23,18}} | collective-permute-start | bytes 393224 | tf_op jit(solution)/shard_map/ppermute | solution.py:28
  378.6 9.1 %collective-permute-start.71 = (f32[256,128]{0,1:T(8,128)S(1)}, f32[256,128]{0,1:T(8,128)S(1)}, u32[]{:S(2)}, u32[]{:S(2)}) collective-permute-start(f32[256,128]{0,1:T(8,128)S(1)} %convolution_bitcast_fusion.13), channel_id=1, source_target_pairs={{16,15},{17,12},{18,13},{19,14}} | collective-permute-start | bytes 393224 | tf_op jit(solution)/shard_map/ppermute | solution.py:28
  391.2 9.1 %collective-permute-start.43 = (f32[256,128]{0,1:T(8,128)S(1)}, f32[256,128]{0,1:T(8,128)S(1)}, u32[]{:S(2)}, u32[]{:S(2)}) collective-permute-start(f32[256,128]{0,1:T(8,128)S(1)} %convolution_bitcast_fusion.21), channel_id=1, source_target_pairs={{16,15},{17,12},{18,13},{19,14}} | collective-permute-start | bytes 393224 | tf_op jit(solution)/shard_map/ppermute | solution.py:28
  403.7 9.1 %collective-permute-start.15 = (f32[256,128]{0,1:T(8,128)S(1)}, f32[256,128]{0,1:T(8,128)S(1)}, u32[]{:S(2)}, u32[]{:S(2)}) collective-permute-start(f32[256,128]{0,1:T(8,128)S(1)} %convolution_bitcast_fusion.29), channel_id=1, source_target_pairs={{16,15},{17,12},{18,13},{19,14}} | collective-permute-start | bytes 393224 | tf_op jit(solution)/shard_map/ppermute | solution.py:28
  458.2 26.5 %collective-permute-done.111 = f32[256,128]{0,1:T(8,128)S(1)} collective-permute-done((f32[256,128]{0,1:T(8,128)S(1)}, f32[256,128]{0,1:T(8,128)S(1)}, u32[]{:S(2)}, u32[]{:S(2)}) %collective-permute-start.111) | collective-permute-done | bytes 131104 | tf_op jit(solution)/shard_map/ppermute | solution.py:28
  (327 shorter events, 367.2 us)
Async XLA Ops:
  24.7 41.1 %collective-permute-start.87 = (f32[256,128]{0,1:T(8,128)S(1)}, f32[256,128]{0,1:T(8,128)S(1)}, u32[]{:S(2)}, u32[]{:S(2)}) collective-permute-start(f32[256,128]{0,1:T(8,128)S(1)} %convolution_bitcast_fusion.8), channel_id=1, source_target_pairs={{28,27},{29,24},{30,25},{31,26}} | collective-permute-start | bytes 393224 | tf_op jit(solution)/shard_map/ppermute | solution.py:28
  35.3 37.3 %collective-permute-start.88 = (f32[256,128]{0,1:T(8,128)S(1)}, f32[256,128]{0,1:T(8,128)S(1)}, u32[]{:S(2)}, u32[]{:S(2)}) collective-permute-start(f32[256,128]{0,1:T(8,128)S(1)} %convolution_bitcast_fusion.8), channel_id=1, source_target_pairs={{28,26},{29,27},{30,24},{31,25}} | collective-permute-start | bytes 393224 | tf_op jit(solution)/shard_map/ppermute | solution.py:28
  42.0 37.3 %collective-permute-start.89 = (f32[256,128]{0,1:T(8,128)S(1)}, f32[256,128]{0,1:T(8,128)S(1)}, u32[]{:S(2)}, u32[]{:S(2)}) collective-permute-start(f32[256,128]{0,1:T(8,128)S(1)} %convolution_bitcast_fusion.8), channel_id=1, source_target_pairs={{28,25},{29,26},{30,27},{31,24}} | collective-permute-start | bytes 393224 | tf_op jit(solution)/shard_map/ppermute | solution.py:28
  48.8 37.3 %collective-permute-start.90 = (f32[256,128]{0,1:T(8,128)S(1)}, f32[256,128]{0,1:T(8,128)S(1)}, u32[]{:S(2)}, u32[]{:S(2)}) collective-permute-start(f32[256,128]{0,1:T(8,128)S(1)} %convolution_bitcast_fusion.8), channel_id=1, source_target_pairs={{28,24},{29,25},{30,26},{31,27}} | collective-permute-start | bytes 393224 | tf_op jit(solution)/shard_map/ppermute | solution.py:28
  86.1 35.2 %collective-permute-start.31 = (f32[256,128]{0,1:T(8,128)S(1)}, f32[256,128]{0,1:T(8,128)S(1)}, u32[]{:S(2)}, u32[]{:S(2)}) collective-permute-start(f32[256,128]{0,1:T(8,128)S(1)} %convolution_bitcast_fusion.24), channel_id=1, source_target_pairs={{28,27},{29,24},{30,25},{31,26}} | collective-permute-start | bytes 393224 | tf_op jit(solution)/shard_map/ppermute | solution.py:28
  141.6 38.9 %collective-permute-start.91 = (f32[256,128]{0,1:T(8,128)S(1)}, f32[256,128]{0,1:T(8,128)S(1)}, u32[]{:S(2)}, u32[]{:S(2)}) collective-permute-start(f32[256,128]{0,1:T(8,128)S(1)} %convolution_bitcast_fusion.7), channel_id=1, source_target_pairs={{24,23},{25,20},{26,21},{27,22}} | collective-permute-start | bytes 393224 | tf_op jit(solution)/shard_map/ppermute | solution.py:28
  148.4 39.1 %collective-permute-start.92 = (f32[256,128]{0,1:T(8,128)S(1)}, f32[256,128]{0,1:T(8,128)S(1)}, u32[]{:S(2)}, u32[]{:S(2)}) collective-permute-start(f32[256,128]{0,1:T(8,128)S(1)} %convolution_bitcast_fusion.7), channel_id=1, source_target_pairs={{24,22},{25,23},{26,20},{27,21}} | collective-permute-start | bytes 393224 | tf_op jit(solution)/shard_map/ppermute | solution.py:28
  155.5 39.1 %collective-permute-start.93 = (f32[256,128]{0,1:T(8,128)S(1)}, f32[256,128]{0,1:T(8,128)S(1)}, u32[]{:S(2)}, u32[]{:S(2)}) collective-permute-start(f32[256,128]{0,1:T(8,128)S(1)} %convolution_bitcast_fusion.7), channel_id=1, source_target_pairs={{24,21},{25,22},{26,23},{27,20}} | collective-permute-start | bytes 393224 | tf_op jit(solution)/shard_map/ppermute | solution.py:28
  162.5 39.1 %collective-permute-start.94 = (f32[256,128]{0,1:T(8,128)S(1)}, f32[256,128]{0,1:T(8,128)S(1)}, u32[]{:S(2)}, u32[]{:S(2)}) collective-permute-start(f32[256,128]{0,1:T(8,128)S(1)} %convolution_bitcast_fusion.7), channel_id=1, source_target_pairs={{24,20},{25,21},{26,22},{27,23}} | collective-permute-start | bytes 393224 | tf_op jit(solution)/shard_map/ppermute | solution.py:28
  171.1 38.8 %collective-permute-start.63 = (f32[256,128]{0,1:T(8,128)S(1)}, f32[256,128]{0,1:T(8,128)S(1)}, u32[]{:S(2)}, u32[]{:S(2)}) collective-permute-start(f32[256,128]{0,1:T(8,128)S(1)} %convolution_bitcast_fusion.15), channel_id=1, source_target_pairs={{24,23},{25,20},{26,21},{27,22}} | collective-permute-start | bytes 393224 | tf_op jit(solution)/shard_map/ppermute | solution.py:28
  180.5 36.4 %collective-permute-start.64 = (f32[256,128]{0,1:T(8,128)S(1)}, f32[256,128]{0,1:T(8,128)S(1)}, u32[]{:S(2)}, u32[]{:S(2)}) collective-permute-start(f32[256,128]{0,1:T(8,128)S(1)} %convolution_bitcast_fusion.15), channel_id=1, source_target_pairs={{24,22},{25,23},{26,20},{27,21}} | collective-permute-start | bytes 393224 | tf_op jit(solution)/shard_map/ppermute | solution.py:28
  187.5 36.4 %collective-permute-start.65 = (f32[256,128]{0,1:T(8,128)S(1)}, f32[256,128]{0,1:T(8,128)S(1)}, u32[]{:S(2)}, u32[]{:S(2)}) collective-permute-start(f32[256,128]{0,1:T(8,128)S(1)} %convolution_bitcast_fusion.15), channel_id=1, source_target_pairs={{24,21},{25,22},{26,23},{27,20}} | collective-permute-start | bytes 393224 | tf_op jit(solution)/shard_map/ppermute | solution.py:28
  194.5 36.4 %collective-permute-start.66 = (f32[256,128]{0,1:T(8,128)S(1)}, f32[256,128]{0,1:T(8,128)S(1)}, u32[]{:S(2)}, u32[]{:S(2)}) collective-permute-start(f32[256,128]{0,1:T(8,128)S(1)} %convolution_bitcast_fusion.15), channel_id=1, source_target_pairs={{24,20},{25,21},{26,22},{27,23}} | collective-permute-start | bytes 393224 | tf_op jit(solution)/shard_map/ppermute | solution.py:28
  201.6 37.9 %collective-permute-start.35 = (f32[256,128]{0,1:T(8,128)S(1)}, f32[256,128]{0,1:T(8,128)S(1)}, u32[]{:S(2)}, u32[]{:S(2)}) collective-permute-start(f32[256,128]{0,1:T(8,128)S(1)} %convolution_bitcast_fusion.23), channel_id=1, source_target_pairs={{24,23},{25,20},{26,21},{27,22}} | collective-permute-start | bytes 393224 | tf_op jit(solution)/shard_map/ppermute | solution.py:28
  209.9 36.6 %collective-permute-start.36 = (f32[256,128]{0,1:T(8,128)S(1)}, f32[256,128]{0,1:T(8,128)S(1)}, u32[]{:S(2)}, u32[]{:S(2)}) collective-permute-start(f32[256,128]{0,1:T(8,128)S(1)} %convolution_bitcast_fusion.23), channel_id=1, source_target_pairs={{24,22},{25,23},{26,20},{27,21}} | collective-permute-start | bytes 393224 | tf_op jit(solution)/shard_map/ppermute | solution.py:28
  216.9 36.6 %collective-permute-start.37 = (f32[256,128]{0,1:T(8,128)S(1)}, f32[256,128]{0,1:T(8,128)S(1)}, u32[]{:S(2)}, u32[]{:S(2)}) collective-permute-start(f32[256,128]{0,1:T(8,128)S(1)} %convolution_bitcast_fusion.23), channel_id=1, source_target_pairs={{24,21},{25,22},{26,23},{27,20}} | collective-permute-start | bytes 393224 | tf_op jit(solution)/shard_map/ppermute | solution.py:28
  223.9 36.6 %collective-permute-start.38 = (f32[256,128]{0,1:T(8,128)S(1)}, f32[256,128]{0,1:T(8,128)S(1)}, u32[]{:S(2)}, u32[]{:S(2)}) collective-permute-start(f32[256,128]{0,1:T(8,128)S(1)} %convolution_bitcast_fusion.23), channel_id=1, source_target_pairs={{24,20},{25,21},{26,22},{27,23}} | collective-permute-start | bytes 393224 | tf_op jit(solution)/shard_map/ppermute | solution.py:28
  231.0 37.9 %collective-permute-start.7 = (f32[256,128]{0,1:T(8,128)S(1)}, f32[256,128]{0,1:T(8,128)S(1)}, u32[]{:S(2)}, u32[]{:S(2)}) collective-permute-start(f32[256,128]{0,1:T(8,128)S(1)} %convolution_bitcast_fusion.31), channel_id=1, source_target_pairs={{24,23},{25,20},{26,21},{27,22}} | collective-permute-start | bytes 393224 | tf_op jit(solution)/shard_map/ppermute | solution.py:28
  239.4 35.8 %collective-permute-start.8 = (f32[256,128]{0,1:T(8,128)S(1)}, f32[256,128]{0,1:T(8,128)S(1)}, u32[]{:S(2)}, u32[]{:S(2)}) collective-permute-start(f32[256,128]{0,1:T(8,128)S(1)} %convolution_bitcast_fusion.31), channel_id=1, source_target_pairs={{24,22},{25,23},{26,20},{27,21}} | collective-permute-start | bytes 393224 | tf_op jit(solution)/shard_map/ppermute | solution.py:28
  449.0 35.7 %collective-permute-start.111 = (f32[256,128]{0,1:T(8,128)S(1)}, f32[256,128]{0,1:T(8,128)S(1)}, u32[]{:S(2)}, u32[]{:S(2)}) collective-permute-start(f32[256,128]{0,1:T(8,128)S(1)} %convolution_bitcast_fusion.2), channel_id=1, source_target_pairs={{4,3},{5,0},{6,1},{7,2}} | collective-permute-start | bytes 393224 | tf_op jit(solution)/shard_map/ppermute | solution.py:28
  451.6 38.4 %collective-permute-start.112 = (f32[256,128]{0,1:T(8,128)S(1)}, f32[256,128]{0,1:T(8,128)S(1)}, u32[]{:S(2)}, u32[]{:S(2)}) collective-permute-start(f32[256,128]{0,1:T(8,128)S(1)} %convolution_bitcast_fusion.2), channel_id=1, source_target_pairs={{4,2},{5,3},{6,0},{7,1}} | collective-permute-start | bytes 393224 | tf_op jit(solution)/shard_map/ppermute | solution.py:28
  452.9 38.4 %collective-permute-start.113 = (f32[256,128]{0,1:T(8,128)S(1)}, f32[256,128]{0,1:T(8,128)S(1)}, u32[]{:S(2)}, u32[]{:S(2)}) collective-permute-start(f32[256,128]{0,1:T(8,128)S(1)} %convolution_bitcast_fusion.2), channel_id=1, source_target_pairs={{4,1},{5,2},{6,3},{7,0}} | collective-permute-start | bytes 393224 | tf_op jit(solution)/shard_map/ppermute | solution.py:28
  454.2 38.4 %collective-permute-start.114 = (f32[256,128]{0,1:T(8,128)S(1)}, f32[256,128]{0,1:T(8,128)S(1)}, u32[]{:S(2)}, u32[]{:S(2)}) collective-permute-start(f32[256,128]{0,1:T(8,128)S(1)} %convolution_bitcast_fusion.2), channel_id=1, source_target_pairs={{4,0},{5,1},{6,2},{7,3}} | collective-permute-start | bytes 393224 | tf_op jit(solution)/shard_map/ppermute | solution.py:28
  455.5 39.7 %collective-permute-start.83 = (f32[256,128]{0,1:T(8,128)S(1)}, f32[256,128]{0,1:T(8,128)S(1)}, u32[]{:S(2)}, u32[]{:S(2)}) collective-permute-start(f32[256,128]{0,1:T(8,128)S(1)} %convolution_bitcast_fusion.10), channel_id=1, source_target_pairs={{4,3},{5,0},{6,1},{7,2}} | collective-permute-start | bytes 393224 | tf_op jit(solution)/shard_map/ppermute | solution.py:28
  (106 other events, 1770.4 us)

commit v2 on v0

v2 whole, which is shorter than its diff:
```python
import jax
import jax.numpy as jnp
from jax import lax
from jax.sharding import PartitionSpec as P


def product(left, right):
    return jnp.dot(left, right, precision=lax.Precision.HIGHEST, preferred_element_type=jnp.float32)


def body(section_maps, terminal_cost, terminal_states):
    groups = lax.axis_size("tm")
    count = lax.axis_size("row")
    group = lax.axis_index("tm")
    place = lax.axis_index("row")
    state_dim = terminal_cost.shape[1]
    width = state_dim // count

    whole_map = lax.all_gather(section_maps[0], "row", axis=0, tiled=True)
    rows_id = lax.broadcasted_iota(jnp.int32, (state_dim, width), 0)
    cols_id = lax.broadcasted_iota(jnp.int32, (state_dim, width), 1) + place * width
    identity_cols = (rows_id == cols_id).astype(jnp.float32)
    incoming = jnp.concatenate([identity_cols, terminal_cost.T], axis=0)

    own = None
    for k in range(groups - 1, -1, -1):
        fresh = product(whole_map, incoming)
        own = fresh if own is None else jnp.where(group == k, fresh, own)
        if k > 0:
            got = lax.ppermute(fresh, "tm", [(k, k - 1)])
            incoming = jnp.where(group == k - 1, got, incoming)

    value_map = lax.all_gather(own, "row", axis=1, tiled=True)
    rows = value_map.shape[0] // count
    my_rows = lax.dynamic_slice_in_dim(value_map, place * rows, rows, 0)
    rows_traj = product(my_rows, terminal_states)

    cols = terminal_states.shape[1] // count
    my_cols = lax.dynamic_slice_in_dim(terminal_states, place * cols, cols, 1)
    traj_cols = product(value_map, my_cols)
    section_cost = jnp.sum(traj_cols[:state_dim] * traj_cols[state_dim:], axis=0) / state_dim
    return (rows_traj[None], section_cost[None])


def solution(mesh):
    in_specs = (P("tm", "row", None), P("row", None), P())
    out_specs = (P("tm", "row", None), P("tm", "row"))
    return jax.shard_map(body, mesh=mesh, in_specs=in_specs, out_specs=out_specs, check_vma=False)
```

time: 577 us -> 255 us (0.44)
  waiting for transfers between devices: 479 us -> 164 us
  blocking collectives: 50 us -> 0 us
  matrix products: 29.3 us -> 66.5 us
    ppermute x3 -> x7, waiting for transfers between devices: 194 us -> 35.6 us  [body(): got = lax.ppermute(fresh, 'tm', [(k, k - 1)])]
    all_gather x4 -> x2, waiting for transfers between devices: 284 us -> 127 us  [the longest x1 85 us: body(): whole_map = lax.all_gather(section_maps[0], 'row', axis=0, tiled=True)]
    all_to_all x1 -> x0, blocking collectives: 50 us -> none  [body(): lax.all_to_all(rows_traj, 'row', split_axis=1, concat_axis=0, tiled=True)]
    dot_general x5 -> x10, matrix products: 29.3 us -> 66.5 us  [product(): jnp.dot(left, right, precision=lax.Precision.HIGHEST, preferred_element_t...]
  transfers between devices with their start and end apart: 7 -> 9, of which waited for: 6 -> 3; matrix products, arithmetic and copies ran while one was open for 1% -> 0% of each run, Pallas kernels for 0% -> 0%
where the time goes in v2:
time: 255 us; the launch traced here: 254 us
  waiting for transfers between devices  164 us (64%)
  matrix products  66.5 us (26%)
  between operations  14.2 us (6%)
  starting transfers between devices  8.99 us (4%)
    all_gather x1, waiting for transfers between devices, body(): whole_map = lax.all_gather(section_maps[0], 'row', axis=0, tiled=True)  85 us
    dot_general x10, matrix products, product(): jnp.dot(left, right, precision=lax.Precision.HIGHEST, preferred_element_t...  66.5 us
    all_gather x1, waiting for transfers between devices, body(): value_map = lax.all_gather(own, 'row', axis=1, tiled=True)  42.5 us
    ppermute x7, waiting for transfers between devices, body(): got = lax.ppermute(fresh, 'tm', [(k, k - 1)])  35.6 us
    ppermute x7, starting transfers between devices, body(): got = lax.ppermute(fresh, 'tm', [(k, k - 1)])  8.92 us
  transfers between devices with their start and end apart: 9, of which 3 were waited for; matrix products, arithmetic and copies ran while one was open for 0% of the time, Pallas kernels for 0%

profile of v2, /device:TPU:0, one launch (start us, length us, event | category | flops | bytes accessed | tf_op | source)
XLA Modules:
  0.0 254.5 jit_solution(3124104674899493065)
XLA Ops:
  7.2 0.7 all-gather.6.cloned.1.call-update
  8.1 85.0 %all-gather.6.cloned.1.call-done = f32[1,1024,1024]{2,1,0:T(8,128)} async-done(((f32[1,256,1024]{2,1,0:T(8,128)}), f32[1,1024,1024]{2,1,0:T(8,128)}) %all-gather.6.cloned.1.call-update) | async-done | bytes 4194320 | tf_op jit(solution)/shard_map/all_gather | solution.py:19
  93.0 6.7 %fusion.16 = f32[1024,128]{0,1:T(8,128)S(1)} fusion(f32[1,1024,1024]{2,1,0:T(8,128)} %all-gather.6.cloned.1.call-done, f32[512,128]{0,1:T(8,128)} %bitcast.62, f32[512,128]{0,1:T(8,128)S(1)} %fusion.49), kind=kOutput, calls=%fused_computation.17 | convolution fusion | flops 1610743808 | bytes 5242880 | tf_op jit(solution)/shard_map/dot_general | solution.py:8
  99.7 0.7 collective-permute-start
  100.5 6.5 %fusion.19 = f32[1024,128]{0,1:T(8,128)S(1)} fusion(f32[1024,128]{0,1:T(8,128)S(1)} %fusion.48, f32[1,1024,1024]{2,1,0:T(8,128)} %all-gather.6.cloned.1.call-done), kind=kOutput, calls=%fused_computation.18 | convolution fusion | flops 1610612736 | bytes 5242880 | tf_op jit(solution)/shard_map/dot_general | solution.py:8
  107.1 0.7 collective-permute-start.1
  107.8 6.5 %fusion.22 = f32[1024,128]{0,1:T(8,128)S(1)} fusion(f32[1,1024,1024]{2,1,0:T(8,128)} %all-gather.6.cloned.1.call-done, f32[1024,128]{0,1:T(8,128)S(1)} %collective-permute-done.1, f32[1024,128]{0,1:T(8,128)S(1)} %fusion.48, pred[]{:T(512)S(6)} %eq.36), kind=kOutput, calls=%fused_computation.19 | convolution fusion | flops 1610743808 | bytes 5767169 | tf_op jit(solution)/shard_map/dot_general | solution.py:8
  114.3 1.5 collective-permute-start.2
  115.9 6.5 %fusion.25 = f32[1024,128]{0,1:T(8,128)S(1)} fusion(f32[1024,128]{0,1:T(8,128)S(1)} %broadcast_select_fusion.1, f32[1,1024,1024]{2,1,0:T(8,128)} %all-gather.6.cloned.1.call-done), kind=kOutput, calls=%fused_computation.20 | convolution fusion | flops 1610612736 | bytes 5242880 | tf_op jit(solution)/shard_map/dot_general | solution.py:8
  122.5 1.5 collective-permute-start.3
  123.9 6.5 %fusion.28 = f32[1024,128]{0,1:T(8,128)S(1)} fusion(f32[1,1024,1024]{2,1,0:T(8,128)} %all-gather.6.cloned.1.call-done, f32[1024,128]{0,1:T(8,128)} %collective-permute-done.3, f32[1024,128]{0,1:T(8,128)S(1)} %broadcast_select_fusion.1, pred[]{:T(512)S(6)} %eq.34), kind=kOutput, calls=%fused_computation.21 | convolution fusion | flops 1610743808 | bytes 5767169 | tf_op jit(solution)/shard_map/dot_general | solution.py:8
  130.5 1.5 collective-permute-start.4
  132.0 0.1 broadcast_select_fusion.3
  132.1 7.3 %fusion.31 = f32[1024,128]{0,1:T(8,128)} fusion(f32[1024,128]{0,1:T(8,128)S(1)} %broadcast_select_fusion.3, f32[1,1024,1024]{2,1,0:T(8,128)} %all-gather.6.cloned.1.call-done), kind=kOutput, calls=%fused_computation.22 | convolution fusion | flops 1610612736 | bytes 5242880 | tf_op jit(solution)/shard_map/dot_general | solution.py:8
  139.4 1.6 collective-permute-start.5
  141.0 7.4 %fusion.34 = f32[1024,128]{0,1:T(8,128)} fusion(f32[1,1024,1024]{2,1,0:T(8,128)} %all-gather.6.cloned.1.call-done, f32[1024,128]{0,1:T(8,128)} %collective-permute-done.5, f32[1024,128]{0,1:T(8,128)S(1)} %broadcast_select_fusion.3, pred[]{:T(512)S(6)} %eq.32), kind=kOutput, calls=%fused_computation.23 | convolution fusion | flops 1610743808 | bytes 5767169 | tf_op jit(solution)/shard_map/dot_general | solution.py:8
  148.3 1.5 collective-permute-start.6
  149.9 35.5 %collective-permute-done.6 = f32[1024,128]{0,1:T(8,128)} collective-permute-done((f32[1024,128]{0,1:T(8,128)}, f32[1024,128]{0,1:T(8,128)}, u32[]{:S(2)}, u32[]{:S(2)}) %collective-permute-start.6) | collective-permute-done | bytes 524320 | tf_op jit(solution)/shard_map/ppermute | solution.py:30
  185.4 7.4 %fusion.40 = f32[1024,128]{0,1:T(8,128)} fusion(f32[1,1024,1024]{2,1,0:T(8,128)} %all-gather.6.cloned.1.call-done, f32[1024,128]{0,1:T(8,128)} %fusion.34, f32[1024,128]{0,1:T(8,128)} %fusion.31, f32[1024,128]{0,1:T(8,128)S(1)} %copy-done.2, f32[1024,128]{0,1:T(8,128)S(1)} %fusion.25, f32[1024,128]{0,1:T(8,128)S(1)} %fusion.22, ...), kind=kOutput, calls=%fused_computation.25 | convolution fusion | flops 1611792384 | bytes 9961479 | tf_op jit(solution)/shard_map/dot_general | solution.py:8
  192.9 42.5 %all-gather.4.cloned.1.call-done = f32[1024,512]{0,1:T(8,128)} async-done(((f32[1024,128]{0,1:T(8,128)}), f32[1024,512]{0,1:T(8,128)}) %all-gather.4.cloned.1.call-update) | async-done | bytes 2097168 | tf_op jit(solution)/shard_map/all_gather | solution.py:33
  235.4 5.5 %fusion.44 = f32[1024,512]{1,0:T(8,128)S(1)} fusion(f32[1024,512]{0,1:T(8,128)} %all-gather.4.cloned.1.call-done, f32[512,2048]{1,0:T(8,128)} %param.5, s32[]{:T(128)S(6)} %select_n.100), kind=kOutput, calls=%fused_computation.28 | convolution fusion | flops 3221225472 | bytes 5242884 | tf_op jit(solution)/shard_map/dot_general | solution.py:8
  240.8 0.1 fusion.43
  241.0 0.6 broadcast_multiply_fusion
  241.6 6.1 %convolution_bitcast_fusion = f32[1,256,2048]{2,1,0:T(8,128)} fusion(f32[512,2048]{1,0:T(8,128)S(1)} %copy-done, f32[1024,512]{0,1:T(8,128)} %all-gather.4.cloned.1.call-done, s32[]{:T(128)S(6)} %select_n.99), kind=kOutput, calls=%fused_computation.16 | convolution fusion | flops 3221225472 | bytes 6815748 | tf_op jit(solution)/shard_map/dot_general | solution.py:8
  (21 shorter events, 0.4 us)
Async XLA Ops:
  7.2 93.3 %copy-start.3 = (f32[128,512]{1,0:T(8,128)S(1)}, f32[128,512]{1,0:T(8,128)}, u32[]{:S(2)}) copy-start(f32[128,512]{1,0:T(8,128)} %param.4) | copy-start | bytes 786436
  7.2 85.9 %all-gather.6.cloned.1.call-start = ((), (), s32[]{:S(2)}) async-start(), calls=%async_computation.1 | async-start | bytes 5242880 | tf_op jit(solution)/shard_map/all_gather | solution.py:19
  7.9 227.4 %all-gather.4.cloned.1.call-start = ((), (), s32[]{:S(2)}) async-start(), calls=%async_computation | async-start | bytes 2621440 | tf_op jit(solution)/shard_map/all_gather | solution.py:33
  99.7 0.7 collective-permute-start
  107.1 0.7 collective-permute-start.1
  114.3 1.5 collective-permute-start.2
  122.5 1.5 collective-permute-start.3
  130.5 1.5 copy-start.1
  130.5 1.5 collective-permute-start.4
  139.4 46.0 %copy-start.2 = (f32[1024,128]{0,1:T(8,128)S(1)}, f32[1024,128]{0,1:T(8,128)}, u32[]{:S(2)}) copy-start(f32[1024,128]{0,1:T(8,128)} %copy-done.1) | copy-start | bytes 1572868
  139.4 1.6 collective-permute-start.5
  148.3 37.1 %collective-permute-start.6 = (f32[1024,128]{0,1:T(8,128)}, f32[1024,128]{0,1:T(8,128)}, u32[]{:S(2)}, u32[]{:S(2)}) collective-permute-start(f32[1024,128]{0,1:T(8,128)} %fusion.34), channel_id=1, source_target_pairs={{4,0},{5,1},{6,2},{7,3}} | collective-permute-start | bytes 1572872 | tf_op jit(solution)/shard_map/ppermute | solution.py:30
  235.3 6.2 %copy-start = (f32[512,2048]{1,0:T(8,128)S(1)}, f32[512,2048]{1,0:T(8,128)}, u32[]{:S(2)}) copy-start(f32[512,2048]{1,0:T(8,128)} %param.5) | copy-start | bytes 12582916
Sparse Core Ops, SparseCore 0:
  9.6 83.4 all-gather.5
  193.0 42.3 all-gather.3

commit v3 on v2

--- a/solution.py
+++ b/solution.py
@@ -5,7 +5,7 @@
 
 
 def product(left, right):
-    return jnp.dot(left, right, precision=lax.Precision.HIGHEST, preferred_element_type=jnp.float32)
+    return jnp.dot(left, right, precision=lax.Precision.HIGH, preferred_element_type=jnp.float32)
 
 
 def body(section_maps, terminal_cost, terminal_states):

time: 255 us -> 235 us (0.922)
  matrix products: 66.5 us -> 46.3 us
    dot_general x10, matrix products: 66.5 us -> 46.3 us  [product(): jnp.dot(left, right, precision=lax.Precision.HIGH, preferred_element_type...]
where the time goes in v3:
time: 235 us; the launch traced here: 234 us
  waiting for transfers between devices  164 us (70%)
  matrix products  46.3 us (20%)
  between operations  14.2 us (6%)
  starting transfers between devices  8.77 us (4%)
    all_gather x1, waiting for transfers between devices, body(): whole_map = lax.all_gather(section_maps[0], 'row', axis=0, tiled=True)  85 us
    dot_general x10, matrix products, product(): jnp.dot(left, right, precision=lax.Precision.HIGH, preferred_element_type...  46.3 us
    all_gather x1, waiting for transfers between devices, body(): value_map = lax.all_gather(own, 'row', axis=1, tiled=True)  42.5 us
    ppermute x7, waiting for transfers between devices, body(): got = lax.ppermute(fresh, 'tm', [(k, k - 1)])  35.8 us
    ppermute x7, starting transfers between devices, body(): got = lax.ppermute(fresh, 'tm', [(k, k - 1)])  8.7 us
  transfers between devices with their start and end apart: 9, of which 3 were waited for; matrix products, arithmetic and copies ran while one was open for 0% of the time, Pallas kernels for 0%

profile of v3, /device:TPU:0, one launch (start us, length us, event | category | flops | bytes accessed | tf_op | source)
XLA Modules:
  0.0 234.3 jit_solution(12991811942382830728)
XLA Ops:
  7.2 0.7 all-gather.6.cloned.1.call-update
  8.1 85.0 %all-gather.6.cloned.1.call-done = f32[1,1024,1024]{2,1,0:T(8,128)} async-done(((f32[1,256,1024]{2,1,0:T(8,128)}), f32[1,1024,1024]{2,1,0:T(8,128)}) %all-gather.6.cloned.1.call-update) | async-done | bytes 4194320 | tf_op jit(solution)/shard_map/all_gather | solution.py:19
  93.0 4.5 %fusion.16 = f32[1024,128]{0,1:T(8,128)S(1)} fusion(f32[1,1024,1024]{2,1,0:T(8,128)} %all-gather.6.cloned.1.call-done, f32[512,128]{0,1:T(8,128)} %bitcast.62, f32[512,128]{0,1:T(8,128)S(1)} %fusion.49), kind=kOutput, calls=%fused_computation.17 | convolution fusion | flops 805437440 | bytes 5242880 | tf_op jit(solution)/shard_map/dot_general | solution.py:8
  97.5 0.7 collective-permute-start
  98.3 4.4 %fusion.19 = f32[1024,128]{0,1:T(8,128)S(1)} fusion(f32[1024,128]{0,1:T(8,128)S(1)} %fusion.48, f32[1,1024,1024]{2,1,0:T(8,128)} %all-gather.6.cloned.1.call-done), kind=kOutput, calls=%fused_computation.18 | convolution fusion | flops 805306368 | bytes 5242880 | tf_op jit(solution)/shard_map/dot_general | solution.py:8
  102.7 0.7 collective-permute-start.1
  103.4 4.4 %fusion.22 = f32[1024,128]{0,1:T(8,128)S(1)} fusion(f32[1,1024,1024]{2,1,0:T(8,128)} %all-gather.6.cloned.1.call-done, f32[1024,128]{0,1:T(8,128)S(1)} %collective-permute-done.1, f32[1024,128]{0,1:T(8,128)S(1)} %fusion.48, pred[]{:T(512)S(6)} %eq.36), kind=kOutput, calls=%fused_computation.19 | convolution fusion | flops 805437440 | bytes 5767169 | tf_op jit(solution)/shard_map/dot_general | solution.py:8
  107.9 1.5 collective-permute-start.2
  109.4 4.4 %fusion.25 = f32[1024,128]{0,1:T(8,128)S(1)} fusion(f32[1024,128]{0,1:T(8,128)S(1)} %broadcast_select_fusion.1, f32[1,1024,1024]{2,1,0:T(8,128)} %all-gather.6.cloned.1.call-done), kind=kOutput, calls=%fused_computation.20 | convolution fusion | flops 805306368 | bytes 5242880 | tf_op jit(solution)/shard_map/dot_general | solution.py:8
  113.8 1.5 collective-permute-start.3
  115.3 4.4 %fusion.28 = f32[1024,128]{0,1:T(8,128)S(1)} fusion(f32[1,1024,1024]{2,1,0:T(8,128)} %all-gather.6.cloned.1.call-done, f32[1024,128]{0,1:T(8,128)} %collective-permute-done.3, f32[1024,128]{0,1:T(8,128)S(1)} %broadcast_select_fusion.1, pred[]{:T(512)S(6)} %eq.34), kind=kOutput, calls=%fused_computation.21 | convolution fusion | flops 805437440 | bytes 5767169 | tf_op jit(solution)/shard_map/dot_general | solution.py:8
  119.7 1.5 collective-permute-start.4
  121.2 0.1 broadcast_select_fusion.3
  121.3 5.2 %fusion.31 = f32[1024,128]{0,1:T(8,128)} fusion(f32[1024,128]{0,1:T(8,128)S(1)} %broadcast_select_fusion.3, f32[1,1024,1024]{2,1,0:T(8,128)} %all-gather.6.cloned.1.call-done), kind=kOutput, calls=%fused_computation.22 | convolution fusion | flops 805306368 | bytes 5242880 | tf_op jit(solution)/shard_map/dot_general | solution.py:8
  126.5 1.6 collective-permute-start.5
  128.1 5.2 %fusion.34 = f32[1024,128]{0,1:T(8,128)} fusion(f32[1,1024,1024]{2,1,0:T(8,128)} %all-gather.6.cloned.1.call-done, f32[1024,128]{0,1:T(8,128)} %collective-permute-done.5, f32[1024,128]{0,1:T(8,128)S(1)} %broadcast_select_fusion.3, pred[]{:T(512)S(6)} %eq.32), kind=kOutput, calls=%fused_computation.23 | convolution fusion | flops 805437440 | bytes 5767169 | tf_op jit(solution)/shard_map/dot_general | solution.py:8
  133.3 1.3 collective-permute-start.6
  134.6 35.8 %collective-permute-done.6 = f32[1024,128]{0,1:T(8,128)} collective-permute-done((f32[1024,128]{0,1:T(8,128)}, f32[1024,128]{0,1:T(8,128)}, u32[]{:S(2)}, u32[]{:S(2)}) %collective-permute-start.6) | collective-permute-done | bytes 524320 | tf_op jit(solution)/shard_map/ppermute | solution.py:30
  170.4 5.4 %fusion.40 = f32[1024,128]{0,1:T(8,128)} fusion(f32[1,1024,1024]{2,1,0:T(8,128)} %all-gather.6.cloned.1.call-done, f32[1024,128]{0,1:T(8,128)} %fusion.34, f32[1024,128]{0,1:T(8,128)} %fusion.31, f32[1024,128]{0,1:T(8,128)S(1)} %copy-done.2, f32[1024,128]{0,1:T(8,128)S(1)} %fusion.25, f32[1024,128]{0,1:T(8,128)S(1)} %fusion.22, ...), kind=kOutput, calls=%fused_computation.25 | convolution fusion | flops 806486016 | bytes 9961479 | tf_op jit(solution)/shard_map/dot_general | solution.py:8
  175.8 42.5 %all-gather.4.cloned.1.call-done = f32[1024,512]{0,1:T(8,128)} async-done(((f32[1024,128]{0,1:T(8,128)}), f32[1024,512]{0,1:T(8,128)}) %all-gather.4.cloned.1.call-update) | async-done | bytes 2097168 | tf_op jit(solution)/shard_map/all_gather | solution.py:33
  218.3 3.8 %fusion.44 = f32[1024,512]{1,0:T(8,128)S(1)} fusion(f32[1024,512]{0,1:T(8,128)} %all-gather.4.cloned.1.call-done, f32[512,2048]{1,0:T(8,128)} %param.5, s32[]{:T(128)S(6)} %select_n.100), kind=kOutput, calls=%fused_computation.28 | convolution fusion | flops 1610612736 | bytes 5242884 | tf_op jit(solution)/shard_map/dot_general | solution.py:8
  222.2 0.1 fusion.43
  222.3 0.6 broadcast_multiply_fusion
  222.9 4.6 %convolution_bitcast_fusion = f32[1,256,2048]{2,1,0:T(8,128)} fusion(f32[512,2048]{1,0:T(8,128)S(1)} %copy-done, f32[1024,512]{0,1:T(8,128)} %all-gather.4.cloned.1.call-done, s32[]{:T(128)S(6)} %select_n.99), kind=kOutput, calls=%fused_computation.16 | convolution fusion | flops 1610612736 | bytes 6815748 | tf_op jit(solution)/shard_map/dot_general | solution.py:8
  (21 shorter events, 0.4 us)
Async XLA Ops:
  7.2 91.1 %copy-start.3 = (f32[128,512]{1,0:T(8,128)S(1)}, f32[128,512]{1,0:T(8,128)}, u32[]{:S(2)}) copy-start(f32[128,512]{1,0:T(8,128)} %param.4) | copy-start | bytes 786436
  7.2 85.9 %all-gather.6.cloned.1.call-start = ((), (), s32[]{:S(2)}) async-start(), calls=%async_computation.1 | async-start | bytes 5242880 | tf_op jit(solution)/shard_map/all_gather | solution.py:19
  7.9 210.4 %all-gather.4.cloned.1.call-start = ((), (), s32[]{:S(2)}) async-start(), calls=%async_computation | async-start | bytes 2621440 | tf_op jit(solution)/shard_map/all_gather | solution.py:33
  97.5 0.7 collective-permute-start
  102.7 0.7 collective-permute-start.1
  107.9 1.5 collective-permute-start.2
  113.8 1.5 collective-permute-start.3
  119.7 1.5 copy-start.1
  119.7 1.5 collective-permute-start.4
  126.5 43.9 %copy-start.2 = (f32[1024,128]{0,1:T(8,128)S(1)}, f32[1024,128]{0,1:T(8,128)}, u32[]{:S(2)}) copy-start(f32[1024,128]{0,1:T(8,128)} %copy-done.1) | copy-start | bytes 1572868
  126.5 1.6 collective-permute-start.5
  133.3 37.1 %collective-permute-start.6 = (f32[1024,128]{0,1:T(8,128)}, f32[1024,128]{0,1:T(8,128)}, u32[]{:S(2)}, u32[]{:S(2)}) collective-permute-start(f32[1024,128]{0,1:T(8,128)} %fusion.34), channel_id=1, source_target_pairs={{4,0},{5,1},{6,2},{7,3}} | collective-permute-start | bytes 1572872 | tf_op jit(solution)/shard_map/ppermute | solution.py:30
  218.3 4.6 %copy-start = (f32[512,2048]{1,0:T(8,128)S(1)}, f32[512,2048]{1,0:T(8,128)}, u32[]{:S(2)}) copy-start(f32[512,2048]{1,0:T(8,128)} %param.5) | copy-start | bytes 12582916
Sparse Core Ops, SparseCore 0:
  9.6 83.4 all-gather.5
  176.0 42.3 all-gather.3

commit v4 on v3

--- a/solution.py
+++ b/solution.py
@@ -2,6 +2,8 @@
 import jax.numpy as jnp
 from jax import lax
 from jax.sharding import PartitionSpec as P
+
+CHUNKS = 2
 
 
 def product(left, right):
@@ -22,15 +24,18 @@
     identity_cols = (rows_id == cols_id).astype(jnp.float32)
     incoming = jnp.concatenate([identity_cols, terminal_cost.T], axis=0)
 
-    own = None
+    step = width // CHUNKS
+    incoming = [incoming[:, j * step:(j + 1) * step] for j in range(CHUNKS)]
+    own = [None] * CHUNKS
     for k in range(groups - 1, -1, -1):
-        fresh = product(whole_map, incoming)
-        own = fresh if own is None else jnp.where(group == k, fresh, own)
-        if k > 0:
-            got = lax.ppermute(fresh, "tm", [(k, k - 1)])
-            incoming = jnp.where(group == k - 1, got, incoming)
+        for j in range(CHUNKS):
+            fresh = product(whole_map, incoming[j])
+            own[j] = fresh if own[j] is None else jnp.where(group == k, fresh, own[j])
+            if k > 0:
+                got = lax.ppermute(fresh, "tm", [(k, k - 1)])
+                incoming[j] = jnp.where(group == k - 1, got, incoming[j])
 
-    value_map = lax.all_gather(own, "row", axis=1, tiled=True)
+    value_map = lax.all_gather(jnp.concatenate(own, axis=1), "row", axis=1, tiled=True)
     rows = value_map.shape[0] // count
     my_rows = lax.dynamic_slice_in_dim(value_map, place * rows, rows, 0)
     rows_traj = product(my_rows, terminal_states)

time: 235 us -> 214 us (0.911)
  waiting for transfers between devices: 164 us -> 138 us
    ppermute x7 -> x14, waiting for transfers between devices: 35.8 us -> 9.41 us  [body(): got = lax.ppermute(fresh, 'tm', [(k, k - 1)])]
    ppermute x7 -> x14, starting transfers between devices: 8.7 us -> 11.1 us  [body(): got = lax.ppermute(fresh, 'tm', [(k, k - 1)])]
    dot_general x10 -> x18, matrix products: 46.3 us -> 47.3 us  [product(): jnp.dot(left, right, precision=lax.Precision.HIGH, preferred_element_type...]
  transfers between devices with their start and end apart: 9 -> 16, of which waited for: 3 -> 4; matrix products, arithmetic and copies ran while one was open for 0% -> 13% of each run, Pallas kernels for 0% -> 0%
where the time goes in v4:
time: 214 us; the launch traced here: 213 us
  waiting for transfers between devices  138 us (64%)
  matrix products  47.3 us (22%)
  between operations  14.4 us (7%)
  starting transfers between devices  11.1 us (5%)
    all_gather x1, waiting for transfers between devices, body(): whole_map = lax.all_gather(section_maps[0], 'row', axis=0, tiled=True)  85 us
    dot_general x18, matrix products, product(): jnp.dot(left, right, precision=lax.Precision.HIGH, preferred_element_type...  47.3 us
    all_gather x1, waiting for transfers between devices, body(): lax.all_gather(jnp.concatenate(own, axis=1), 'row', axis=1, tiled=True)  43.3 us
    ppermute x14, starting transfers between devices, body(): got = lax.ppermute(fresh, 'tm', [(k, k - 1)])  11.1 us
    ppermute x14, waiting for transfers between devices, body(): got = lax.ppermute(fresh, 'tm', [(k, k - 1)])  9.41 us
  transfers between devices with their start and end apart: 16, of which 4 were waited for; matrix products, arithmetic and copies ran while one was open for 13% of the time, Pallas kernels for 0%

profile of v4, /device:TPU:0, one launch (start us, length us, event | category | flops | bytes accessed | tf_op | source)
XLA Modules:
  0.0 213.2 jit_solution(14733782890660387137)
XLA Ops:
  8.1 85.0 %all-gather.6.cloned.1.call-done = f32[1,1024,1024]{2,1,0:T(8,128)} async-done(((f32[1,256,1024]{2,1,0:T(8,128)}), f32[1,1024,1024]{2,1,0:T(8,128)}) %all-gather.6.cloned.1.call-update) | async-done | bytes 4194320 | tf_op jit(solution)/shard_map/all_gather | solution.py:21
  93.0 4.4 %fusion.32 = f32[1024,64]{0,1:T(8,128)S(1)} fusion(f32[1,1024,1024]{2,1,0:T(8,128)} %all-gather.6.cloned.1.call-done, f32[512,128]{0,1:T(8,128)S(1)} %fusion.93, f32[512,128]{0,1:T(8,128)} %bitcast.117), kind=kOutput, calls=%fused_computation.33 | convolution fusion | flops 402718720 | bytes 4980736 | tf_op jit(solution)/shard_map/dot_general | solution.py:10
  98.2 2.2 %fusion.59 = f32[1024,64]{0,1:T(8,128)S(1)} fusion(f32[1,1024,1024]{2,1,0:T(8,128)S(1)} %copy-done, f32[512,128]{0,1:T(8,128)S(1)} %bitcast.118, f32[512,128]{0,1:T(8,128)S(1)} %fusion.93), kind=kOutput, calls=%fused_computation.42 | convolution fusion | flops 402718720 | bytes 4980736 | tf_op jit(solution)/shard_map/dot_general | solution.py:10
  101.1 4.4 %fusion.35 = f32[1024,64]{0,1:T(8,128)S(1)} fusion(f32[1024,64]{0,1:T(8,128)S(1)} %get-tuple-element.2, f32[1,1024,1024]{2,1,0:T(8,128)} %all-gather.6.cloned.1.call-done), kind=kOutput, calls=%fused_computation.34 | convolution fusion | flops 402653184 | bytes 4718592 | tf_op jit(solution)/shard_map/dot_general | solution.py:10
  106.2 2.2 %fusion.62 = f32[1024,64]{0,1:T(8,128)S(1)} fusion(f32[1024,64]{0,1:T(8,128)S(1)} %get-tuple-element.3, f32[1,1024,1024]{2,1,0:T(8,128)S(1)} %copy-done.1), kind=kOutput, calls=%fused_computation.43 | convolution fusion | flops 402653184 | bytes 4718592 | tf_op jit(solution)/shard_map/dot_general | solution.py:10
  109.0 2.1 %fusion.38 = f32[1024,64]{0,1:T(8,128)S(1)} fusion(f32[1,1024,1024]{2,1,0:T(8,128)S(1)} %copy-done.1, f32[1024,64]{0,1:T(8,128)S(1)} %collective-permute-done.1, f32[1024,64]{0,1:T(8,128)S(1)} %get-tuple-element.2, pred[]{:T(512)S(6)} %eq.21), kind=kOutput, calls=%fused_computation.35 | convolution fusion | flops 402718720 | bytes 4980737 | tf_op jit(solution)/shard_map/dot_general | solution.py:10
  111.9 2.1 %fusion.65 = f32[1024,64]{0,1:T(8,128)S(1)} fusion(f32[1,1024,1024]{2,1,0:T(8,128)S(1)} %copy-done.1, f32[1024,64]{0,1:T(8,128)S(1)} %collective-permute-done.8, f32[1024,64]{0,1:T(8,128)S(1)} %get-tuple-element.3, pred[]{:T(512)S(6)} %eq.21), kind=kOutput, calls=%fused_computation.44 | convolution fusion | flops 402718720 | bytes 4980737 | tf_op jit(solution)/shard_map/dot_general | solution.py:10
  115.0 2.2 %fusion.41 = f32[1024,64]{0,1:T(8,128)S(1)} fusion(f32[1024,64]{0,1:T(8,128)S(1)} %broadcast_select_fusion.5, f32[1,1024,1024]{2,1,0:T(8,128)S(1)} %copy-done.1), kind=kOutput, calls=%fused_computation.36 | convolution fusion | flops 402653184 | bytes 4718592 | tf_op jit(solution)/shard_map/dot_general | solution.py:10
  117.9 2.2 %fusion.68 = f32[1024,64]{0,1:T(8,128)S(1)} fusion(f32[1024,64]{0,1:T(8,128)S(1)} %broadcast_select_fusion.4, f32[1,1024,1024]{2,1,0:T(8,128)S(1)} %copy-done.1), kind=kOutput, calls=%fused_computation.45 | convolution fusion | flops 402653184 | bytes 4718592 | tf_op jit(solution)/shard_map/dot_general | solution.py:10
  120.7 2.1 %fusion.44 = f32[1024,64]{0,1:T(8,128)S(1)} fusion(f32[1,1024,1024]{2,1,0:T(8,128)S(1)} %copy-done.1, f32[1024,64]{0,1:T(8,128)S(1)} %collective-permute-done.3, f32[1024,64]{0,1:T(8,128)S(1)} %broadcast_select_fusion.5, pred[]{:T(512)S(6)} %eq.19), kind=kOutput, calls=%fused_computation.37 | convolution fusion | flops 402718720 | bytes 4980737 | tf_op jit(solution)/shard_map/dot_general | solution.py:10
  123.5 2.1 %fusion.71 = f32[1024,64]{0,1:T(8,128)S(1)} fusion(f32[1,1024,1024]{2,1,0:T(8,128)S(1)} %copy-done.1, f32[1024,64]{0,1:T(8,128)S(1)} %collective-permute-done.10, f32[1024,64]{0,1:T(8,128)S(1)} %broadcast_select_fusion.4, pred[]{:T(512)S(6)} %eq.19), kind=kOutput, calls=%fused_computation.46 | convolution fusion | flops 402718720 | bytes 4980737 | tf_op jit(solution)/shard_map/dot_general | solution.py:10
  126.4 2.2 %fusion.47 = f32[1024,64]{0,1:T(8,128)S(1)} fusion(f32[1024,64]{0,1:T(8,128)S(1)} %broadcast_select_fusion.9, f32[1,1024,1024]{2,1,0:T(8,128)S(1)} %copy-done.1), kind=kOutput, calls=%fused_computation.38 | convolution fusion | flops 402653184 | bytes 4718592 | tf_op jit(solution)/shard_map/dot_general | solution.py:10
  129.3 2.2 %fusion.74 = f32[1024,64]{0,1:T(8,128)S(1)} fusion(f32[1024,64]{0,1:T(8,128)S(1)} %broadcast_select_fusion.8, f32[1,1024,1024]{2,1,0:T(8,128)S(1)} %copy-done.1), kind=kOutput, calls=%fused_computation.47 | convolution fusion | flops 402653184 | bytes 4718592 | tf_op jit(solution)/shard_map/dot_general | solution.py:10
  132.2 2.1 %fusion.50 = f32[1024,64]{0,1:T(8,128)S(1)} fusion(f32[1,1024,1024]{2,1,0:T(8,128)S(1)} %copy-done.1, f32[1024,64]{0,1:T(8,128)S(1)} %collective-permute-done.5, f32[1024,64]{0,1:T(8,128)S(1)} %broadcast_select_fusion.9, pred[]{:T(512)S(6)} %eq.17), kind=kOutput, calls=%fused_computation.39 | convolution fusion | flops 402718720 | bytes 4980737 | tf_op jit(solution)/shard_map/dot_general | solution.py:10
  134.3 1.5 collective-permute-start.6
  135.8 2.1 %fusion.77 = f32[1024,64]{0,1:T(8,128)S(1)} fusion(f32[1,1024,1024]{2,1,0:T(8,128)S(1)} %copy-done.1, f32[1024,64]{0,1:T(8,128)S(1)} %collective-permute-done.12, f32[1024,64]{0,1:T(8,128)S(1)} %broadcast_select_fusion.8, pred[]{:T(512)S(6)} %eq.17), kind=kOutput, calls=%fused_computation.48 | convolution fusion | flops 402718720 | bytes 4980737 | tf_op jit(solution)/shard_map/dot_general | solution.py:10
  138.0 1.3 collective-permute-start.13
  139.3 7.9 %collective-permute-done.6 = f32[1024,64]{0,1:T(8,128)S(1)} collective-permute-done((f32[1024,64]{0,1:T(8,128)S(1)}, f32[1024,64]{0,1:T(8,128)S(1)}, u32[]{:S(2)}, u32[]{:S(2)}) %collective-permute-start.6) | collective-permute-done | bytes 262176 | tf_op jit(solution)/shard_map/ppermute | solution.py:35
  147.2 2.2 %fusion.56 = f32[1024,64]{0,1:T(8,128)S(1)} fusion(f32[1,1024,1024]{2,1,0:T(8,128)S(1)} %copy-done.1, f32[1024,64]{0,1:T(8,128)S(1)} %fusion.50, f32[1024,64]{0,1:T(8,128)S(1)} %fusion.47, f32[1024,64]{0,1:T(8,128)S(1)} %fusion.44, f32[1024,64]{0,1:T(8,128)S(1)} %fusion.41, f32[1024,64]{0,1:T(8,128)S(1)} %fusion.38, f32[1024,64]{0,1:T(8,128)S(1)} %fusion.35, ...), kind=kOutput, calls=%fused_computation.41 | convolution fusion | flops 403243008 | bytes 7077895 | tf_op jit(solution)/shard_map/dot_general | solution.py:10
  149.3 1.5 collective-permute-done.13
  150.8 2.2 %fusion.83 = f32[1024,64]{0,1:T(8,128)S(1)} fusion(f32[1,1024,1024]{2,1,0:T(8,128)S(1)} %copy-done.1, f32[1024,64]{0,1:T(8,128)S(1)} %fusion.77, f32[1024,64]{0,1:T(8,128)S(1)} %fusion.74, f32[1024,64]{0,1:T(8,128)S(1)} %fusion.71, f32[1024,64]{0,1:T(8,128)S(1)} %fusion.68, f32[1024,64]{0,1:T(8,128)S(1)} %fusion.65, f32[1024,64]{0,1:T(8,128)S(1)} %fusion.62, ...), kind=kOutput, calls=%fused_computation.50 | convolution fusion | flops 403243008 | bytes 7077895 | tf_op jit(solution)/shard_map/dot_general | solution.py:10
  153.9 43.3 %all-gather.4.cloned.1.call-done = f32[1024,512]{0,1:T(8,128)} async-done(((f32[1024,128]{0,1:T(8,128)}), f32[1024,512]{0,1:T(8,128)}) %all-gather.4.cloned.1.call-update) | async-done | bytes 2097168 | tf_op jit(solution)/shard_map/all_gather | solution.py:38
  197.2 3.8 %fusion.87 = f32[1024,512]{1,0:T(8,128)S(1)} fusion(f32[1024,512]{0,1:T(8,128)} %all-gather.4.cloned.1.call-done, f32[512,2048]{1,0:T(8,128)} %param.5, s32[]{:T(128)S(6)} %select_n.170), kind=kOutput, calls=%fused_computation.53 | convolution fusion | flops 1610612736 | bytes 5242884 | tf_op jit(solution)/shard_map/dot_general | solution.py:10
  201.8 4.6 %convolution_bitcast_fusion = f32[1,256,2048]{2,1,0:T(8,128)} fusion(f32[512,2048]{1,0:T(8,128)S(1)} %copy-done.2, f32[1024,512]{0,1:T(8,128)} %all-gather.4.cloned.1.call-done, s32[]{:T(128)S(6)} %select_n.169), kind=kOutput, calls=%fused_computation.32 | convolution fusion | flops 1610612736 | bytes 6815748 | tf_op jit(solution)/shard_map/dot_general | solution.py:10
  (46 shorter events, 11.0 us)
Async XLA Ops:
  7.2 91.0 %copy-start.3 = (f32[128,512]{1,0:T(8,128)S(1)}, f32[128,512]{1,0:T(8,128)}, u32[]{:S(2)}) copy-start(f32[128,512]{1,0:T(8,128)} %param.4) | copy-start | bytes 786436
  7.2 85.9 %all-gather.6.cloned.1.call-start = ((), (), s32[]{:S(2)}) async-start(), calls=%async_computation.1 | async-start | bytes 5242880 | tf_op jit(solution)/shard_map/all_gather | solution.py:21
  7.9 189.3 %all-gather.4.cloned.1.call-start = ((), (), s32[]{:S(2)}) async-start(), calls=%async_computation | async-start | bytes 2621440 | tf_op jit(solution)/shard_map/all_gather | solution.py:38
  93.0 5.1 %copy-start = (f32[1,1024,1024]{2,1,0:T(8,128)S(1)}, f32[1,1024,1024]{2,1,0:T(8,128)}, u32[]{:S(2)}) copy-start(f32[1,1024,1024]{2,1,0:T(8,128)} %all-gather.6.cloned.1.call-done) | copy-start | bytes 12582916
  97.5 3.6 %collective-permute-start = (f32[1024,64]{0,1:T(8,128)S(1)}, f32[1024,64]{0,1:T(8,128)S(1)}, u32[]{:S(2)}, u32[]{:S(2)}) collective-permute-start(f32[1024,64]{0,1:T(8,128)S(1)} %fusion.32), channel_id=1, source_target_pairs={{28,24},{29,25},{30,26},{31,27}} | collective-permute-start | bytes 786440 | tf_op jit(solution)/shard_map/ppermute | solution.py:35
  100.3 0.7 collective-permute-start.7
  101.0 5.2 %copy-start.1 = (f32[1,1024,1024]{2,1,0:T(8,128)S(1)}, f32[1,1024,1024]{2,1,0:T(8,128)}, u32[]{:S(2)}) copy-start(f32[1,1024,1024]{2,1,0:T(8,128)} %all-gather.6.cloned.1.call-done) | copy-start | bytes 12582916
  105.5 3.5 %collective-permute-start.1 = (f32[1024,64]{0,1:T(8,128)S(1)}, f32[1024,64]{0,1:T(8,128)S(1)}, u32[]{:S(2)}, u32[]{:S(2)}) collective-permute-start(f32[1024,64]{0,1:T(8,128)S(1)} %fusion.35), channel_id=1, source_target_pairs={{24,20},{25,21},{26,22},{27,23}} | collective-permute-start | bytes 786440 | tf_op jit(solution)/shard_map/ppermute | solution.py:35
  108.4 3.5 %collective-permute-start.8 = (f32[1024,64]{0,1:T(8,128)S(1)}, f32[1024,64]{0,1:T(8,128)S(1)}, u32[]{:S(2)}, u32[]{:S(2)}) collective-permute-start(f32[1024,64]{0,1:T(8,128)S(1)} %fusion.62), channel_id=1, source_target_pairs={{24,20},{25,21},{26,22},{27,23}} | collective-permute-start | bytes 786440 | tf_op jit(solution)/shard_map/ppermute | solution.py:35
  111.2 3.7 %collective-permute-start.2 = (f32[1024,64]{0,1:T(8,128)S(1)}, f32[1024,64]{0,1:T(8,128)S(1)}, u32[]{:S(2)}, u32[]{:S(2)}) collective-permute-start(f32[1024,64]{0,1:T(8,128)S(1)} %fusion.38), channel_id=1, source_target_pairs={{20,16},{21,17},{22,18},{23,19}} | collective-permute-start | bytes 786440 | tf_op jit(solution)/shard_map/ppermute | solution.py:35
  114.0 3.8 %collective-permute-start.9 = (f32[1024,64]{0,1:T(8,128)S(1)}, f32[1024,64]{0,1:T(8,128)S(1)}, u32[]{:S(2)}, u32[]{:S(2)}) collective-permute-start(f32[1024,64]{0,1:T(8,128)S(1)} %fusion.65), channel_id=1, source_target_pairs={{20,16},{21,17},{22,18},{23,19}} | collective-permute-start | bytes 786440 | tf_op jit(solution)/shard_map/ppermute | solution.py:35
  117.1 3.6 %collective-permute-start.3 = (f32[1024,64]{0,1:T(8,128)S(1)}, f32[1024,64]{0,1:T(8,128)S(1)}, u32[]{:S(2)}, u32[]{:S(2)}) collective-permute-start(f32[1024,64]{0,1:T(8,128)S(1)} %fusion.41), channel_id=1, source_target_pairs={{16,12},{17,13},{18,14},{19,15}} | collective-permute-start | bytes 786440 | tf_op jit(solution)/shard_map/ppermute | solution.py:35
  120.0 3.5 %collective-permute-start.10 = (f32[1024,64]{0,1:T(8,128)S(1)}, f32[1024,64]{0,1:T(8,128)S(1)}, u32[]{:S(2)}, u32[]{:S(2)}) collective-permute-start(f32[1024,64]{0,1:T(8,128)S(1)} %fusion.68), channel_id=1, source_target_pairs={{16,12},{17,13},{18,14},{19,15}} | collective-permute-start | bytes 786440 | tf_op jit(solution)/shard_map/ppermute | solution.py:35
  122.8 3.5 %collective-permute-start.4 = (f32[1024,64]{0,1:T(8,128)S(1)}, f32[1024,64]{0,1:T(8,128)S(1)}, u32[]{:S(2)}, u32[]{:S(2)}) collective-permute-start(f32[1024,64]{0,1:T(8,128)S(1)} %fusion.44), channel_id=1, source_target_pairs={{12,8},{13,9},{14,10},{15,11}} | collective-permute-start | bytes 786440 | tf_op jit(solution)/shard_map/ppermute | solution.py:35
  125.7 3.6 %collective-permute-start.11 = (f32[1024,64]{0,1:T(8,128)S(1)}, f32[1024,64]{0,1:T(8,128)S(1)}, u32[]{:S(2)}, u32[]{:S(2)}) collective-permute-start(f32[1024,64]{0,1:T(8,128)S(1)} %fusion.71), channel_id=1, source_target_pairs={{12,8},{13,9},{14,10},{15,11}} | collective-permute-start | bytes 786440 | tf_op jit(solution)/shard_map/ppermute | solution.py:35
  128.6 3.6 %collective-permute-start.5 = (f32[1024,64]{0,1:T(8,128)S(1)}, f32[1024,64]{0,1:T(8,128)S(1)}, u32[]{:S(2)}, u32[]{:S(2)}) collective-permute-start(f32[1024,64]{0,1:T(8,128)S(1)} %fusion.47), channel_id=1, source_target_pairs={{8,4},{9,5},{10,6},{11,7}} | collective-permute-start | bytes 786440 | tf_op jit(solution)/shard_map/ppermute | solution.py:35
  131.5 4.4 %collective-permute-start.12 = (f32[1024,64]{0,1:T(8,128)S(1)}, f32[1024,64]{0,1:T(8,128)S(1)}, u32[]{:S(2)}, u32[]{:S(2)}) collective-permute-start(f32[1024,64]{0,1:T(8,128)S(1)} %fusion.74), channel_id=1, source_target_pairs={{8,4},{9,5},{10,6},{11,7}} | collective-permute-start | bytes 786440 | tf_op jit(solution)/shard_map/ppermute | solution.py:35
  134.3 12.8 %collective-permute-start.6 = (f32[1024,64]{0,1:T(8,128)S(1)}, f32[1024,64]{0,1:T(8,128)S(1)}, u32[]{:S(2)}, u32[]{:S(2)}) collective-permute-start(f32[1024,64]{0,1:T(8,128)S(1)} %fusion.50), channel_id=1, source_target_pairs={{4,0},{5,1},{6,2},{7,3}} | collective-permute-start | bytes 786440 | tf_op jit(solution)/shard_map/ppermute | solution.py:35
  138.0 12.8 %collective-permute-start.13 = (f32[1024,64]{0,1:T(8,128)S(1)}, f32[1024,64]{0,1:T(8,128)S(1)}, u32[]{:S(2)}, u32[]{:S(2)}) collective-permute-start(f32[1024,64]{0,1:T(8,128)S(1)} %fusion.77), channel_id=1, source_target_pairs={{4,0},{5,1},{6,2},{7,3}} | collective-permute-start | bytes 786440 | tf_op jit(solution)/shard_map/ppermute | solution.py:35
  197.2 4.6 %copy-start.2 = (f32[512,2048]{1,0:T(8,128)S(1)}, f32[512,2048]{1,0:T(8,128)}, u32[]{:S(2)}) copy-start(f32[512,2048]{1,0:T(8,128)} %param.5) | copy-start | bytes 12582916
Sparse Core Ops, SparseCore 0:
  9.6 83.4 all-gather.5
  154.0 43.1 all-gather.3

commit v5 on v4

--- a/solution.py
+++ b/solution.py
@@ -29,7 +29,8 @@
     own = [None] * CHUNKS
     for k in range(groups - 1, -1, -1):
         for j in range(CHUNKS):
-            fresh = product(whole_map, incoming[j])
+            fresh = lax.cond(group == k, product, lambda a, b: jnp.zeros((a.shape[0], b.shape[1]), jnp.float32),
+                             whole_map, incoming[j])
             own[j] = fresh if own[j] is None else jnp.where(group == k, fresh, own[j])
             if k > 0:
                 got = lax.ppermute(fresh, "tm", [(k, k - 1)])

time: 214 us -> 228 us (1.065)
  waiting for transfers between devices: 138 us -> 174 us
  matrix products: 47.3 us -> 17.3 us
  local copies, waits for them, and re-layouts: 0.02 us -> 3.42 us
  other arithmetic: 1.92 us -> 5.09 us
    ppermute x14, waiting for transfers between devices: 9.41 us -> 46.3 us  [body(): got = lax.ppermute(fresh, 'tm', [(k, k - 1)])]
    dot_general x18 -> x4, matrix products: 47.3 us -> 17.3 us  [product(): jnp.dot(left, right, precision=lax.Precision.HIGH, preferred_element_type...]
  transfers between devices with their start and end apart: 16 -> 16, of which waited for: 4 -> 4; matrix products, arithmetic and copies ran while one was open for 13% -> 5% of each run, Pallas kernels for 0% -> 0%
where the time goes in v5:
time: 228 us
  waiting for transfers between devices  174 us (76%)
  matrix products  17.3 us (8%)
  between operations  14.6 us (6%)
  starting transfers between devices  13.1 us (6%)
  other arithmetic  5.09 us (2%)
  local copies, waits for them, and re-layouts  3.42 us (2%)
    all_gather x1, waiting for transfers between devices, body(): whole_map = lax.all_gather(section_maps[0], 'row', axis=0, tiled=True)  84 us
    ppermute x14, waiting for transfers between devices, body(): got = lax.ppermute(fresh, 'tm', [(k, k - 1)])  46.3 us
    all_gather x1, waiting for transfers between devices, body(): lax.all_gather(jnp.concatenate(own, axis=1), 'row', axis=1, tiled=True)  42.7 us
    dot_general x4, matrix products, product(): jnp.dot(left, right, precision=lax.Precision.HIGH, preferred_element_type...  17.3 us
    ppermute x14, starting transfers between devices, body(): got = lax.ppermute(fresh, 'tm', [(k, k - 1)])  13 us
  transfers between devices with their start and end apart: 16, of which 4 were waited for; matrix products, arithmetic and copies ran while one was open for 5% of the time, Pallas kernels for 0%

profile of v5, /device:TPU:0, one launch (start us, length us, event | category | flops | bytes accessed | tf_op | source)
XLA Modules:
  0.0 227.6 jit_solution(2070906354707801984)
XLA Ops:
  7.2 0.7 all-gather.6.cloned.1.call-update
  8.1 1.0 fusion.8
  9.1 84.0 %all-gather.6.cloned.1.call-done = f32[1,1024,1024]{2,1,0:T(8,128)} async-done(((f32[1,256,1024]{2,1,0:T(8,128)}), f32[1,1024,1024]{2,1,0:T(8,128)}) %all-gather.6.cloned.1.call-update) | async-done | bytes 4194320 | tf_op jit(solution)/shard_map/all_gather | solution.py:21
  93.1 0.7 collective-permute-start
  93.8 0.7 collective-permute-start.7
  98.7 1.4 collective-permute-start.10
  101.0 1.4 collective-permute-start.11
  103.3 1.4 collective-permute-start.12
  104.8 1.0 copy.12
  105.8 1.3 collective-permute-start.6
  107.2 1.0 copy.21
  108.2 1.5 collective-permute-start.13
  109.7 44.7 %collective-permute-done.6 = f32[1024,64]{1,0:T(8,128)} collective-permute-done((f32[1024,64]{1,0:T(8,128)}, f32[1024,64]{1,0:T(8,128)}, u32[]{:S(2)}, u32[]{:S(2)}) %collective-permute-start.6) | collective-permute-done | bytes 262176 | tf_op jit(solution)/shard_map/ppermute | solution.py:36
  154.4 4.7 %conditional.23 = (f32[1024,64]{0,1:T(8,128)S(1)}) conditional(s32[]{:T(128)} %convert_element_type.35, () %tuple.104, (pred[]{:T(512)}, f32[1024,64]{1,0:T(8,128)}, f32[1024,64]{0,1:T(8,128)S(1)}, f32[1024,1024]{1,0:T(8,128)}) %tuple.204), branch_computations={%region_14.15_spmd, %region_15.16_spmd} | conditional | flops 402718720 | bytes 5505033 | solution.py:32
  154.6 4.5 %convolution_bitcast_fusion = f32[1024,64]{0,1:T(8,128)S(1)} fusion(f32[1024,1024]{1,0:T(8,128)} %get-tuple-element.141, f32[1024,64]{1,0:T(8,128)} %get-tuple-element.139, f32[1024,64]{1,0:T(8,128)S(1)} %copy.13, pred[]{:T(512)} %get-tuple-element.138), kind=kOutput, calls=%fused_computation | convolution fusion | flops 402718720 | bytes 4980737 | tf_op jit(solution)/shard_map/cond/branch_1_fun/dot_general | solution.py:10
  159.1 0.7 copy-done.9
  159.8 1.9 select_select_fusion.1
  161.7 1.5 collective-permute-done.13
  163.2 4.7 %conditional.31 = (f32[1024,64]{0,1:T(8,128)S(1)}) conditional(s32[]{:T(128)} %convert_element_type.35, () %tuple.120, (pred[]{:T(512)}, f32[1024,64]{1,0:T(8,128)}, f32[1024,64]{0,1:T(8,128)S(1)}, f32[1024,1024]{1,0:T(8,128)}) %tuple.205), branch_computations={%region_30.31_spmd, %region_31.32_spmd} | conditional | flops 402718720 | bytes 5505033 | solution.py:32
  163.4 4.5 %convolution_bitcast_fusion.1 = f32[1024,64]{0,1:T(8,128)S(1)} fusion(f32[1024,1024]{1,0:T(8,128)} %get-tuple-element.159, f32[1024,64]{1,0:T(8,128)} %get-tuple-element.157, f32[1024,64]{1,0:T(8,128)S(1)} %copy.22, pred[]{:T(512)} %get-tuple-element.156), kind=kOutput, calls=%fused_computation.3 | convolution fusion | flops 402718720 | bytes 4980737 | tf_op jit(solution)/shard_map/cond/branch_1_fun/dot_general | solution.py:10
  168.1 0.8 pad_maximum_fusion
  169.0 42.7 %all-gather.4.cloned.1.call-done = f32[1024,512]{0,1:T(8,128)} async-done(((f32[1024,128]{0,1:T(8,128)}), f32[1024,512]{0,1:T(8,128)}) %all-gather.4.cloned.1.call-update) | async-done | bytes 2097168 | tf_op jit(solution)/shard_map/all_gather | solution.py:39
  211.6 3.8 %fusion.5 = f32[1024,512]{1,0:T(8,128)S(1)} fusion(f32[1024,512]{0,1:T(8,128)} %all-gather.4.cloned.1.call-done, f32[512,2048]{1,0:T(8,128)} %param.37, s32[]{:T(128)S(6)} %select_n.176), kind=kOutput, calls=%fused_computation.9 | convolution fusion | flops 1610612736 | bytes 5242884 | tf_op jit(solution)/shard_map/dot_general | solution.py:10
  216.2 4.6 %convolution_bitcast_fusion.2 = f32[1,256,2048]{2,1,0:T(8,128)} fusion(f32[512,2048]{1,0:T(8,128)S(1)} %copy-done, f32[1024,512]{0,1:T(8,128)} %all-gather.4.cloned.1.call-done, s32[]{:T(128)S(6)} %select_n.175), kind=kOutput, calls=%fused_computation.6 | convolution fusion | flops 1610612736 | bytes 6815748 | tf_op jit(solution)/shard_map/dot_general | solution.py:10
  (90 shorter events, 7.7 us)
Async XLA Ops:
  7.2 85.9 %all-gather.6.cloned.1.call-start = ((), (), s32[]{:S(2)}) async-start(), calls=%async_computation.1 | async-start | bytes 5242880 | tf_op jit(solution)/shard_map/all_gather | solution.py:21
  7.9 203.7 %all-gather.4.cloned.1.call-start = ((), (), s32[]{:S(2)}) async-start(), calls=%async_computation | async-start | bytes 2621440 | tf_op jit(solution)/shard_map/all_gather | solution.py:39
  93.1 1.4 collective-permute-start
  93.8 1.5 collective-permute-start.7
  94.6 1.5 collective-permute-start.1
  95.4 1.5 collective-permute-start.8
  96.2 1.5 collective-permute-start.2
  97.0 1.7 collective-permute-start.9
  97.9 2.2 collective-permute-start.3
  98.7 2.2 collective-permute-start.10
  100.2 2.2 copy-start.3
  100.2 2.2 collective-permute-start.4
  101.0 2.2 collective-permute-start.11
  102.5 2.2 copy-start.6
  102.5 2.2 collective-permute-start.5
  103.3 3.8 %copy-start.7 = (f32[1024,64]{0,1:T(8,128)}, f32[1024,64]{0,1:T(8,128)S(1)}, u32[]{:S(2)}) copy-start(f32[1024,64]{0,1:T(8,128)S(1)} %get-tuple-element.213) | copy-start | bytes 786436
  103.3 3.8 %collective-permute-start.12 = (f32[1024,64]{0,1:T(8,128)S(1)}, f32[1024,64]{0,1:T(8,128)}, u32[]{:S(2)}, u32[]{:S(2)}) collective-permute-start(f32[1024,64]{0,1:T(8,128)S(1)} %get-tuple-element.213), channel_id=1, source_target_pairs={{8,4},{9,5},{10,6},{11,7}} | collective-permute-start | bytes 786440 | tf_op jit(solution)/shard_map/ppermute | solution.py:36
  105.8 48.7 %collective-permute-start.6 = (f32[1024,64]{1,0:T(8,128)}, f32[1024,64]{1,0:T(8,128)}, u32[]{:S(2)}, u32[]{:S(2)}) collective-permute-start(f32[1024,64]{1,0:T(8,128)} %copy.12), channel_id=1, source_target_pairs={{4,0},{5,1},{6,2},{7,3}} | collective-permute-start | bytes 786440 | tf_op jit(solution)/shard_map/ppermute | solution.py:36
  108.2 55.0 %collective-permute-start.13 = (f32[1024,64]{1,0:T(8,128)}, f32[1024,64]{1,0:T(8,128)}, u32[]{:S(2)}, u32[]{:S(2)}) collective-permute-start(f32[1024,64]{1,0:T(8,128)} %copy.21), channel_id=1, source_target_pairs={{4,0},{5,1},{6,2},{7,3}} | collective-permute-start | bytes 786440 | tf_op jit(solution)/shard_map/ppermute | solution.py:36
  159.8 8.1 %copy-start.2 = (f32[1024,64]{0,1:T(8,128)S(1)}, f32[1024,64]{0,1:T(8,128)}, u32[]{:S(2)}) copy-start(f32[1024,64]{0,1:T(8,128)} %copy-done.1) | copy-start | bytes 786436
  161.7 6.2 %copy-start.5 = (f32[1024,64]{0,1:T(8,128)S(1)}, f32[1024,64]{0,1:T(8,128)}, u32[]{:S(2)}) copy-start(f32[1024,64]{0,1:T(8,128)} %copy-done.4) | copy-start | bytes 786436
  161.7 6.2 %copy-start.8 = (f32[1024,64]{0,1:T(8,128)S(1)}, f32[1024,64]{0,1:T(8,128)}, u32[]{:S(2)}) copy-start(f32[1024,64]{0,1:T(8,128)} %copy-done.7) | copy-start | bytes 786436
  163.2 4.9 %copy-start.10 = (f32[1024,64]{0,1:T(8,128)S(1)}, f32[1024,64]{0,1:T(8,128)}, u32[]{:S(2)}) copy-start(f32[1024,64]{0,1:T(8,128)} %select_select_fusion.1) | copy-start | bytes 786436
  211.6 4.6 %copy-start = (f32[512,2048]{1,0:T(8,128)S(1)}, f32[512,2048]{1,0:T(8,128)}, u32[]{:S(2)}) copy-start(f32[512,2048]{1,0:T(8,128)} %param.37) | copy-start | bytes 12582916
  (3 other events, 5.1 us)
Sparse Core Ops, SparseCore 0:
  9.5 83.4 all-gather.5
  169.1 42.5 all-gather.3

commit v6 on v4

--- a/solution.py
+++ b/solution.py
@@ -35,15 +35,38 @@
                 got = lax.ppermute(fresh, "tm", [(k, k - 1)])
                 incoming[j] = jnp.where(group == k - 1, got, incoming[j])
 
-    value_map = lax.all_gather(jnp.concatenate(own, axis=1), "row", axis=1, tiled=True)
-    rows = value_map.shape[0] // count
-    my_rows = lax.dynamic_slice_in_dim(value_map, place * rows, rows, 0)
-    rows_traj = product(my_rows, terminal_states)
+    own_cols = jnp.concatenate(own, axis=1)
+    rows = own_cols.shape[0] // count
+    half = count // 2
+    blocks = own_cols.reshape(count, rows, width)
+    main_pieces = [blocks[place]]
+    pair_pieces = [blocks[(place + half) % count]]
+    for d in range(1, count):
+        target = (place + d) % count
+        payload = jnp.concatenate([blocks[target], blocks[(target + half) % count]], axis=0)
+        got = lax.ppermute(payload, "row", [(z, (z + d) % count) for z in range(count)])
+        main_pieces.append(got[:rows])
+        pair_pieces.append(got[rows:])
 
+    def in_order(pieces):
+        ordered = []
+        for q in range(count):
+            picked = pieces[0]
+            for d in range(1, count):
+                picked = jnp.where((place - d) % count == q, pieces[d], picked)
+            ordered.append(picked)
+        return jnp.concatenate(ordered, axis=1)
+
+    rows_traj = product(in_order(main_pieces), terminal_states)
+    pair_traj = product(in_order(pair_pieces), terminal_states)
+    partial = jnp.sum(rows_traj * pair_traj, axis=0)
     cols = terminal_states.shape[1] // count
-    my_cols = lax.dynamic_slice_in_dim(terminal_states, place * cols, cols, 1)
-    traj_cols = product(value_map, my_cols)
-    section_cost = jnp.sum(traj_cols[:state_dim] * traj_cols[state_dim:], axis=0) / state_dim
+    total = lax.dynamic_slice_in_dim(partial, place * cols, cols, 0)
+    for e in range(1, half):
+        target = (place + e) % count
+        sent = lax.dynamic_slice_in_dim(partial, target * cols, cols, 0)
+        total = total + lax.ppermute(sent, "row", [(z, (z + e) % count) for z in range(count)])
+    section_cost = total / state_dim
     return (rows_traj[None], section_cost[None])
 
 

time: 214 us -> 199 us (0.930)
  waiting for transfers between devices: 138 us -> 120 us
  starting transfers between devices: 11.1 us -> 15.6 us
    all_gather x1 -> x0, waiting for transfers between devices: 43.3 us -> none  [body(): lax.all_gather(jnp.concatenate(own, axis=1), 'row', axis=1, tiled=True)]
    ppermute x0 -> x4, waiting for transfers between devices: none -> 25.2 us  [the longest x3 21.3 us: body(): lax.ppermute(payload, 'row', [(z, (z + d) % count) for z in range(count)])]
    ppermute x0 -> x4, starting transfers between devices: none -> 4.55 us  [the longest x3 3.11 us: body(): lax.ppermute(payload, 'row', [(z, (z + d) % count) for z in range(count)])]
  transfers between devices with their start and end apart: 16 -> 19, of which waited for: 4 -> 6; matrix products, arithmetic and copies ran while one was open for 13% -> 14% of each run, Pallas kernels for 0% -> 0%
where the time goes in v6:
time: 199 us; the launch traced here: 198 us
  waiting for transfers between devices  120 us (60%)
  matrix products  45.5 us (23%)
  starting transfers between devices  15.6 us (8%)
  between operations  14.6 us (7%)
    all_gather x1, waiting for transfers between devices, body(): whole_map = lax.all_gather(section_maps[0], 'row', axis=0, tiled=True)  85 us
    dot_general x18, matrix products, product(): jnp.dot(left, right, precision=lax.Precision.HIGH, preferred_element_type...  45.5 us
    ppermute x3, waiting for transfers between devices, body(): lax.ppermute(payload, 'row', [(z, (z + d) % count) for z in range(count)])  21.3 us
    ppermute x14, starting transfers between devices, body(): got = lax.ppermute(fresh, 'tm', [(k, k - 1)])  11.1 us
    ppermute x14, waiting for transfers between devices, body(): got = lax.ppermute(fresh, 'tm', [(k, k - 1)])  9.3 us
  transfers between devices with their start and end apart: 19, of which 6 were waited for; matrix products, arithmetic and copies ran while one was open for 14% of the time, Pallas kernels for 0%

profile of v6, /device:TPU:0, one launch (start us, length us, event | category | flops | bytes accessed | tf_op | source)
XLA Modules:
  0.0 198.4 jit_solution(9217134673732809590)
XLA Ops:
  8.0 85.0 %all-gather.3.cloned.1.call-done = f32[1,1024,1024]{2,1,0:T(8,128)} async-done(((f32[1,256,1024]{2,1,0:T(8,128)}), f32[1,1024,1024]{2,1,0:T(8,128)}) %all-gather.3.cloned.1.call-update) | async-done | bytes 4194320 | tf_op jit(solution)/shard_map/all_gather | solution.py:21
  93.0 4.4 %fusion.33 = f32[1024,64]{0,1:T(8,128)S(1)} fusion(f32[1,1024,1024]{2,1,0:T(8,128)} %all-gather.3.cloned.1.call-done, f32[512,128]{0,1:T(8,128)S(1)} %fusion.105, f32[512,128]{0,1:T(8,128)} %bitcast.160), kind=kOutput, calls=%fused_computation.34 | convolution fusion | flops 402718720 | bytes 4980736 | tf_op jit(solution)/shard_map/dot_general | solution.py:10
  98.2 2.2 %fusion.60 = f32[1024,64]{0,1:T(8,128)S(1)} fusion(f32[1,1024,1024]{2,1,0:T(8,128)S(1)} %copy-done, f32[512,128]{0,1:T(8,128)S(1)} %bitcast.161, f32[512,128]{0,1:T(8,128)S(1)} %fusion.105), kind=kOutput, calls=%fused_computation.43 | convolution fusion | flops 402718720 | bytes 4980736 | tf_op jit(solution)/shard_map/dot_general | solution.py:10
  101.2 4.4 %fusion.36 = f32[1024,64]{0,1:T(8,128)S(1)} fusion(f32[1024,64]{0,1:T(8,128)S(1)} %get-tuple-element.17, f32[1,1024,1024]{2,1,0:T(8,128)} %all-gather.3.cloned.1.call-done), kind=kOutput, calls=%fused_computation.35 | convolution fusion | flops 402653184 | bytes 4718592 | tf_op jit(solution)/shard_map/dot_general | solution.py:10
  106.3 2.2 %fusion.63 = f32[1024,64]{0,1:T(8,128)S(1)} fusion(f32[1024,64]{0,1:T(8,128)S(1)} %get-tuple-element.18, f32[1,1024,1024]{2,1,0:T(8,128)S(1)} %copy-done.1), kind=kOutput, calls=%fused_computation.44 | convolution fusion | flops 402653184 | bytes 4718592 | tf_op jit(solution)/shard_map/dot_general | solution.py:10
  109.2 2.1 %fusion.39 = f32[1024,64]{0,1:T(8,128)S(1)} fusion(f32[1,1024,1024]{2,1,0:T(8,128)S(1)} %copy-done.1, f32[1024,64]{0,1:T(8,128)S(1)} %collective-permute-done.1, f32[1024,64]{0,1:T(8,128)S(1)} %get-tuple-element.17, pred[]{:T(512)S(6)} %eq.132), kind=kOutput, calls=%fused_computation.36 | convolution fusion | flops 402718720 | bytes 4980737 | tf_op jit(solution)/shard_map/dot_general | solution.py:10
  112.0 2.1 %fusion.66 = f32[1024,64]{0,1:T(8,128)S(1)} fusion(f32[1,1024,1024]{2,1,0:T(8,128)S(1)} %copy-done.1, f32[1024,64]{0,1:T(8,128)S(1)} %collective-permute-done.8, f32[1024,64]{0,1:T(8,128)S(1)} %get-tuple-element.18, pred[]{:T(512)S(6)} %eq.132), kind=kOutput, calls=%fused_computation.45 | convolution fusion | flops 402718720 | bytes 4980737 | tf_op jit(solution)/shard_map/dot_general | solution.py:10
  115.1 2.2 %fusion.42 = f32[1024,64]{0,1:T(8,128)S(1)} fusion(f32[1024,64]{0,1:T(8,128)S(1)} %broadcast_select_fusion.5, f32[1,1024,1024]{2,1,0:T(8,128)S(1)} %copy-done.1), kind=kOutput, calls=%fused_computation.37 | convolution fusion | flops 402653184 | bytes 4718592 | tf_op jit(solution)/shard_map/dot_general | solution.py:10
  118.0 2.2 %fusion.69 = f32[1024,64]{0,1:T(8,128)S(1)} fusion(f32[1024,64]{0,1:T(8,128)S(1)} %broadcast_select_fusion.4, f32[1,1024,1024]{2,1,0:T(8,128)S(1)} %copy-done.1), kind=kOutput, calls=%fused_computation.46 | convolution fusion | flops 402653184 | bytes 4718592 | tf_op jit(solution)/shard_map/dot_general | solution.py:10
  120.8 2.1 %fusion.45 = f32[1024,64]{0,1:T(8,128)S(1)} fusion(f32[1,1024,1024]{2,1,0:T(8,128)S(1)} %copy-done.1, f32[1024,64]{0,1:T(8,128)S(1)} %collective-permute-done.3, f32[1024,64]{0,1:T(8,128)S(1)} %broadcast_select_fusion.5, pred[]{:T(512)S(6)} %eq.130), kind=kOutput, calls=%fused_computation.38 | convolution fusion | flops 402718720 | bytes 4980737 | tf_op jit(solution)/shard_map/dot_general | solution.py:10
  123.6 2.1 %fusion.72 = f32[1024,64]{0,1:T(8,128)S(1)} fusion(f32[1,1024,1024]{2,1,0:T(8,128)S(1)} %copy-done.1, f32[1024,64]{0,1:T(8,128)S(1)} %collective-permute-done.10, f32[1024,64]{0,1:T(8,128)S(1)} %broadcast_select_fusion.4, pred[]{:T(512)S(6)} %eq.130), kind=kOutput, calls=%fused_computation.47 | convolution fusion | flops 402718720 | bytes 4980737 | tf_op jit(solution)/shard_map/dot_general | solution.py:10
  126.5 2.2 %fusion.48 = f32[1024,64]{0,1:T(8,128)S(1)} fusion(f32[1024,64]{0,1:T(8,128)S(1)} %broadcast_select_fusion.9, f32[1,1024,1024]{2,1,0:T(8,128)S(1)} %copy-done.1), kind=kOutput, calls=%fused_computation.39 | convolution fusion | flops 402653184 | bytes 4718592 | tf_op jit(solution)/shard_map/dot_general | solution.py:10
  129.4 2.2 %fusion.75 = f32[1024,64]{0,1:T(8,128)S(1)} fusion(f32[1024,64]{0,1:T(8,128)S(1)} %broadcast_select_fusion.8, f32[1,1024,1024]{2,1,0:T(8,128)S(1)} %copy-done.1), kind=kOutput, calls=%fused_computation.48 | convolution fusion | flops 402653184 | bytes 4718592 | tf_op jit(solution)/shard_map/dot_general | solution.py:10
  132.3 2.1 %fusion.51 = f32[1024,64]{0,1:T(8,128)S(1)} fusion(f32[1,1024,1024]{2,1,0:T(8,128)S(1)} %copy-done.1, f32[1024,64]{0,1:T(8,128)S(1)} %collective-permute-done.5, f32[1024,64]{0,1:T(8,128)S(1)} %broadcast_select_fusion.9, pred[]{:T(512)S(6)} %eq.128), kind=kOutput, calls=%fused_computation.40 | convolution fusion | flops 402718720 | bytes 4980737 | tf_op jit(solution)/shard_map/dot_general | solution.py:10
  135.9 2.1 %fusion.78 = f32[1024,64]{0,1:T(8,128)S(1)} fusion(f32[1,1024,1024]{2,1,0:T(8,128)S(1)} %copy-done.1, f32[1024,64]{0,1:T(8,128)S(1)} %collective-permute-done.12, f32[1024,64]{0,1:T(8,128)S(1)} %broadcast_select_fusion.8, pred[]{:T(512)S(6)} %eq.128), kind=kOutput, calls=%fused_computation.49 | convolution fusion | flops 402718720 | bytes 4980737 | tf_op jit(solution)/shard_map/dot_general | solution.py:10
  139.4 7.8 %collective-permute-done.6 = f32[1024,64]{0,1:T(8,128)S(1)} collective-permute-done((f32[1024,64]{0,1:T(8,128)S(1)}, f32[1024,64]{0,1:T(8,128)S(1)}, u32[]{:S(2)}, u32[]{:S(2)}) %collective-permute-start.6) | collective-permute-done | bytes 262176 | tf_op jit(solution)/shard_map/ppermute | solution.py:35
  147.1 2.2 %fusion.57 = f32[1024,64]{0,1:T(8,128)S(1)} fusion(f32[1,1024,1024]{2,1,0:T(8,128)S(1)} %copy-done.1, f32[1024,64]{0,1:T(8,128)S(1)} %fusion.51, f32[1024,64]{0,1:T(8,128)S(1)} %fusion.48, f32[1024,64]{0,1:T(8,128)S(1)} %fusion.45, f32[1024,64]{0,1:T(8,128)S(1)} %fusion.42, f32[1024,64]{0,1:T(8,128)S(1)} %fusion.39, f32[1024,64]{0,1:T(8,128)S(1)} %fusion.36, ...), kind=kOutput, calls=%fused_computation.42 | convolution fusion | flops 403243008 | bytes 7077895 | tf_op jit(solution)/shard_map/dot_general | solution.py:10
  150.8 2.2 %fusion.84 = f32[1024,64]{0,1:T(8,128)S(1)} fusion(f32[1,1024,1024]{2,1,0:T(8,128)S(1)} %copy-done.1, f32[1024,64]{0,1:T(8,128)S(1)} %fusion.78, f32[1024,64]{0,1:T(8,128)S(1)} %fusion.75, f32[1024,64]{0,1:T(8,128)S(1)} %fusion.72, f32[1024,64]{0,1:T(8,128)S(1)} %fusion.69, f32[1024,64]{0,1:T(8,128)S(1)} %fusion.66, f32[1024,64]{0,1:T(8,128)S(1)} %fusion.63, ...), kind=kOutput, calls=%fused_computation.51 | convolution fusion | flops 403243008 | bytes 7077895 | tf_op jit(solution)/shard_map/dot_general | solution.py:10
  155.3 2.1 %collective-permute-start.16 = (f32[512,128]{0,1:T(8,128)S(1)}, f32[512,128]{0,1:T(8,128)S(1)}, u32[]{:S(2)}, u32[]{:S(2)}) collective-permute-start(f32[512,128]{0,1:T(8,128)S(1)} %pad_maximum_fusion.4), channel_id=1, source_target_pairs={{0,1},{1,2},{2,3},{3,0},{4,5},{5,6},{6,7},{7,4},{8,9},{9,10},{10,1... | collective-permute-start | bytes 786440 | tf_op jit(solution)/shard_map/ppermute | solution.py:47
  157.4 7.3 %collective-permute-done.14 = f32[512,128]{0,1:T(8,128)S(1)} collective-permute-done((f32[512,128]{0,1:T(8,128)S(1)}, f32[512,128]{0,1:T(8,128)S(1)}, u32[]{:S(2)}, u32[]{:S(2)}) %collective-permute-start.14) | collective-permute-done | bytes 262176 | tf_op jit(solution)/shard_map/ppermute | solution.py:47
  164.7 13.9 %collective-permute-done.15 = f32[512,128]{0,1:T(8,128)S(1)} collective-permute-done((f32[512,128]{0,1:T(8,128)S(1)}, f32[512,128]{0,1:T(8,128)S(1)}, u32[]{:S(2)}, u32[]{:S(2)}) %collective-permute-start.15) | collective-permute-done | bytes 262176 | tf_op jit(solution)/shard_map/ppermute | solution.py:47
  178.8 4.3 %fusion.87 = f32[256,2048]{1,0:T(8,128)S(1)} fusion(f32[512,2048]{1,0:T(8,128)} %param.5, f32[256,128]{0,1:T(8,128)S(1)} %get-tuple-element.9, f32[256,128]{0,1:T(8,128)S(1)} %get-tuple-element.7, f32[256,128]{0,1:T(8,128)S(1)} %get-tuple-element.6, f32[256,128]{0,1:T(8,128)S(1)} %get-tuple-element.5), kind=kOutput, calls=%fused_computation.55 | convolution fusion | flops 1611005952 | bytes 6815744 | tf_op jit(solution)/shard_map/dot_general | solution.py:10
  183.2 2.2 %fusion.32 = f32[2048]{0:T(1024)S(1)} fusion(f32[256,2048]{1,0:T(8,128)S(1)} %fusion.87, f32[512,2048]{1,0:T(8,128)S(1)} %copy-done.2, f32[256,128]{0,1:T(8,128)S(1)} %get-tuple-element.8, f32[256,128]{0,1:T(8,128)S(1)} %get-tuple-element.4, f32[256,128]{0,1:T(8,128)S(1)} %get-tuple-element.3, f32[256,128]{0,1:T(8,128)S(1)} %get-tuple-element.2), kind=kOutput, calls=%fused_computation.33 | convolution fusion | flops 1612052480 | bytes 6823936 | tf_op jit(solution)/shard_map/dot_general | solution.py:10
  187.0 3.9 %collective-permute-done.17 = f32[512]{0:T(512)S(1)} collective-permute-done((f32[512]{0:T(512)S(1)}, f32[512]{0:T(512)S(1)}, u32[]{:S(2)}, u32[]{:S(2)}) %collective-permute-start.17) | collective-permute-done | bytes 2080 | tf_op jit(solution)/shard_map/ppermute | solution.py:68
  (64 shorter events, 18.3 us)
Async XLA Ops:
  7.2 91.0 %copy-start.4 = (f32[128,512]{1,0:T(8,128)S(1)}, f32[128,512]{1,0:T(8,128)}, u32[]{:S(2)}) copy-start(f32[128,512]{1,0:T(8,128)} %param.4) | copy-start | bytes 786436
  7.2 85.9 %all-gather.3.cloned.1.call-start = ((), (), s32[]{:S(2)}) async-start(), calls=%async_computation | async-start | bytes 5242880 | tf_op jit(solution)/shard_map/all_gather | solution.py:21
  93.0 5.1 %copy-start = (f32[1,1024,1024]{2,1,0:T(8,128)S(1)}, f32[1,1024,1024]{2,1,0:T(8,128)}, u32[]{:S(2)}) copy-start(f32[1,1024,1024]{2,1,0:T(8,128)} %all-gather.3.cloned.1.call-done) | copy-start | bytes 12582916
  97.5 3.7 %collective-permute-start = (f32[1024,64]{0,1:T(8,128)S(1)}, f32[1024,64]{0,1:T(8,128)S(1)}, u32[]{:S(2)}, u32[]{:S(2)}) collective-permute-start(f32[1024,64]{0,1:T(8,128)S(1)} %fusion.33), channel_id=1, source_target_pairs={{28,24},{29,25},{30,26},{31,27}} | collective-permute-start | bytes 786440 | tf_op jit(solution)/shard_map/ppermute | solution.py:35
  100.3 0.8 collective-permute-start.7
  101.1 5.2 %copy-start.1 = (f32[1,1024,1024]{2,1,0:T(8,128)S(1)}, f32[1,1024,1024]{2,1,0:T(8,128)}, u32[]{:S(2)}) copy-start(f32[1,1024,1024]{2,1,0:T(8,128)} %all-gather.3.cloned.1.call-done) | copy-start | bytes 12582916
  105.6 3.5 %collective-permute-start.1 = (f32[1024,64]{0,1:T(8,128)S(1)}, f32[1024,64]{0,1:T(8,128)S(1)}, u32[]{:S(2)}, u32[]{:S(2)}) collective-permute-start(f32[1024,64]{0,1:T(8,128)S(1)} %fusion.36), channel_id=1, source_target_pairs={{24,20},{25,21},{26,22},{27,23}} | collective-permute-start | bytes 786440 | tf_op jit(solution)/shard_map/ppermute | solution.py:35
  108.5 3.5 %collective-permute-start.8 = (f32[1024,64]{0,1:T(8,128)S(1)}, f32[1024,64]{0,1:T(8,128)S(1)}, u32[]{:S(2)}, u32[]{:S(2)}) collective-permute-start(f32[1024,64]{0,1:T(8,128)S(1)} %fusion.63), channel_id=1, source_target_pairs={{24,20},{25,21},{26,22},{27,23}} | collective-permute-start | bytes 786440 | tf_op jit(solution)/shard_map/ppermute | solution.py:35
  111.3 3.7 %collective-permute-start.2 = (f32[1024,64]{0,1:T(8,128)S(1)}, f32[1024,64]{0,1:T(8,128)S(1)}, u32[]{:S(2)}, u32[]{:S(2)}) collective-permute-start(f32[1024,64]{0,1:T(8,128)S(1)} %fusion.39), channel_id=1, source_target_pairs={{20,16},{21,17},{22,18},{23,19}} | collective-permute-start | bytes 786440 | tf_op jit(solution)/shard_map/ppermute | solution.py:35
  114.1 3.8 %collective-permute-start.9 = (f32[1024,64]{0,1:T(8,128)S(1)}, f32[1024,64]{0,1:T(8,128)S(1)}, u32[]{:S(2)}, u32[]{:S(2)}) collective-permute-start(f32[1024,64]{0,1:T(8,128)S(1)} %fusion.66), channel_id=1, source_target_pairs={{20,16},{21,17},{22,18},{23,19}} | collective-permute-start | bytes 786440 | tf_op jit(solution)/shard_map/ppermute | solution.py:35
  117.2 3.6 %collective-permute-start.3 = (f32[1024,64]{0,1:T(8,128)S(1)}, f32[1024,64]{0,1:T(8,128)S(1)}, u32[]{:S(2)}, u32[]{:S(2)}) collective-permute-start(f32[1024,64]{0,1:T(8,128)S(1)} %fusion.42), channel_id=1, source_target_pairs={{16,12},{17,13},{18,14},{19,15}} | collective-permute-start | bytes 786440 | tf_op jit(solution)/shard_map/ppermute | solution.py:35
  120.1 3.5 %collective-permute-start.10 = (f32[1024,64]{0,1:T(8,128)S(1)}, f32[1024,64]{0,1:T(8,128)S(1)}, u32[]{:S(2)}, u32[]{:S(2)}) collective-permute-start(f32[1024,64]{0,1:T(8,128)S(1)} %fusion.69), channel_id=1, source_target_pairs={{16,12},{17,13},{18,14},{19,15}} | collective-permute-start | bytes 786440 | tf_op jit(solution)/shard_map/ppermute | solution.py:35
  123.0 3.5 %collective-permute-start.4 = (f32[1024,64]{0,1:T(8,128)S(1)}, f32[1024,64]{0,1:T(8,128)S(1)}, u32[]{:S(2)}, u32[]{:S(2)}) collective-permute-start(f32[1024,64]{0,1:T(8,128)S(1)} %fusion.45), channel_id=1, source_target_pairs={{12,8},{13,9},{14,10},{15,11}} | collective-permute-start | bytes 786440 | tf_op jit(solution)/shard_map/ppermute | solution.py:35
  125.8 3.6 %collective-permute-start.11 = (f32[1024,64]{0,1:T(8,128)S(1)}, f32[1024,64]{0,1:T(8,128)S(1)}, u32[]{:S(2)}, u32[]{:S(2)}) collective-permute-start(f32[1024,64]{0,1:T(8,128)S(1)} %fusion.72), channel_id=1, source_target_pairs={{12,8},{13,9},{14,10},{15,11}} | collective-permute-start | bytes 786440 | tf_op jit(solution)/shard_map/ppermute | solution.py:35
  128.7 3.6 %collective-permute-start.5 = (f32[1024,64]{0,1:T(8,128)S(1)}, f32[1024,64]{0,1:T(8,128)S(1)}, u32[]{:S(2)}, u32[]{:S(2)}) collective-permute-start(f32[1024,64]{0,1:T(8,128)S(1)} %fusion.48), channel_id=1, source_target_pairs={{8,4},{9,5},{10,6},{11,7}} | collective-permute-start | bytes 786440 | tf_op jit(solution)/shard_map/ppermute | solution.py:35
  131.6 4.4 %collective-permute-start.12 = (f32[1024,64]{0,1:T(8,128)S(1)}, f32[1024,64]{0,1:T(8,128)S(1)}, u32[]{:S(2)}, u32[]{:S(2)}) collective-permute-start(f32[1024,64]{0,1:T(8,128)S(1)} %fusion.75), channel_id=1, source_target_pairs={{8,4},{9,5},{10,6},{11,7}} | collective-permute-start | bytes 786440 | tf_op jit(solution)/shard_map/ppermute | solution.py:35
  134.4 12.7 %collective-permute-start.6 = (f32[1024,64]{0,1:T(8,128)S(1)}, f32[1024,64]{0,1:T(8,128)S(1)}, u32[]{:S(2)}, u32[]{:S(2)}) collective-permute-start(f32[1024,64]{0,1:T(8,128)S(1)} %fusion.51), channel_id=1, source_target_pairs={{4,0},{5,1},{6,2},{7,3}} | collective-permute-start | bytes 786440 | tf_op jit(solution)/shard_map/ppermute | solution.py:35
  138.1 12.7 %collective-permute-start.13 = (f32[1024,64]{0,1:T(8,128)S(1)}, f32[1024,64]{0,1:T(8,128)S(1)}, u32[]{:S(2)}, u32[]{:S(2)}) collective-permute-start(f32[1024,64]{0,1:T(8,128)S(1)} %fusion.78), channel_id=1, source_target_pairs={{4,0},{5,1},{6,2},{7,3}} | collective-permute-start | bytes 786440 | tf_op jit(solution)/shard_map/ppermute | solution.py:35
  154.2 10.6 %collective-permute-start.14 = (f32[512,128]{0,1:T(8,128)S(1)}, f32[512,128]{0,1:T(8,128)S(1)}, u32[]{:S(2)}, u32[]{:S(2)}) collective-permute-start(f32[512,128]{0,1:T(8,128)S(1)} %pad_maximum_fusion.2), channel_id=1, source_target_pairs={{0,3},{1,0},{2,1},{3,2},{4,7},{5,4},{6,5},{7,6},{8,11},{9,8},{10,9... | collective-permute-start | bytes 786440 | tf_op jit(solution)/shard_map/ppermute | solution.py:47
  155.0 23.6 %collective-permute-start.15 = (f32[512,128]{0,1:T(8,128)S(1)}, f32[512,128]{0,1:T(8,128)S(1)}, u32[]{:S(2)}, u32[]{:S(2)}) collective-permute-start(f32[512,128]{0,1:T(8,128)S(1)} %pad_maximum_fusion.3), channel_id=1, source_target_pairs={{0,2},{1,3},{2,0},{3,1},{4,6},{5,7},{6,4},{7,5},{8,10},{9,11},{10,... | collective-permute-start | bytes 786440 | tf_op jit(solution)/shard_map/ppermute | solution.py:47
  155.3 23.3 %collective-permute-start.16 = (f32[512,128]{0,1:T(8,128)S(1)}, f32[512,128]{0,1:T(8,128)S(1)}, u32[]{:S(2)}, u32[]{:S(2)}) collective-permute-start(f32[512,128]{0,1:T(8,128)S(1)} %pad_maximum_fusion.4), channel_id=1, source_target_pairs={{0,1},{1,2},{2,3},{3,0},{4,5},{5,6},{6,7},{7,4},{8,9},{9,10},{10,1... | collective-permute-start | bytes 786440 | tf_op jit(solution)/shard_map/ppermute | solution.py:47
  178.7 4.5 %copy-start.2 = (f32[512,2048]{1,0:T(8,128)S(1)}, f32[512,2048]{1,0:T(8,128)}, u32[]{:S(2)}) copy-start(f32[512,2048]{1,0:T(8,128)} %param.5) | copy-start | bytes 12582916
  183.1 8.5 %copy-start.3 = (f32[256,2048]{1,0:T(8,128)}, f32[256,2048]{1,0:T(8,128)S(1)}, u32[]{:S(2)}) copy-start(f32[256,2048]{1,0:T(8,128)S(1)} %fusion.87) | copy-start | bytes 6291460
  185.5 5.4 %collective-permute-start.17 = (f32[512]{0:T(512)S(1)}, f32[512]{0:T(512)S(1)}, u32[]{:S(2)}, u32[]{:S(2)}) collective-permute-start(f32[512]{0:T(512)S(1)} %dynamic_slice.36), channel_id=1, source_target_pairs={{0,1},{1,2},{2,3},{3,0},{4,5},{5,6},{6,7},{7,4},{8,9},{9,10},{10,1... | collective-permute-start | bytes 6152 | tf_op jit(solution)/shard_map/ppermute | solution.py:68
Sparse Core Ops, SparseCore 0:
  9.6 83.4 all-gather.2

commit v7 on v6

--- a/solution.py
+++ b/solution.py
@@ -10,6 +10,21 @@
     return jnp.dot(left, right, precision=lax.Precision.HIGH, preferred_element_type=jnp.float32)
 
 
+def line_gather(block, place, count):
+    rightward = block
+    leftward = block
+    from_left = []
+    from_right = []
+    for t in range(1, count):
+        rightward = lax.ppermute(rightward, "row", [(z, z + 1) for z in range(t - 1, count - 1)])
+        leftward = lax.ppermute(leftward, "row", [(z, z - 1) for z in range(1, count - t + 1)])
+        from_left.append(rightward)
+        from_right.append(leftward)
+    by_offset = jnp.concatenate(from_left[::-1] + [block] + from_right, axis=0)
+    rows = block.shape[0]
+    return lax.dynamic_slice_in_dim(by_offset, (count - 1 - place) * rows, count * rows, 0)
+
+
 def body(section_maps, terminal_cost, terminal_states):
     groups = lax.axis_size("tm")
     count = lax.axis_size("row")
@@ -18,7 +33,7 @@
     state_dim = terminal_cost.shape[1]
     width = state_dim // count
 
-    whole_map = lax.all_gather(section_maps[0], "row", axis=0, tiled=True)
+    whole_map = line_gather(section_maps[0], place, count)
     rows_id = lax.broadcasted_iota(jnp.int32, (state_dim, width), 0)
     cols_id = lax.broadcasted_iota(jnp.int32, (state_dim, width), 1) + place * width
     identity_cols = (rows_id == cols_id).astype(jnp.float32)

time: 199 us -> 207 us (1.040); the launches traced: 198 us -> 204 us
  waiting for transfers between devices: 120 us -> 84.6 us
  starting transfers between devices: 15.6 us -> 39.2 us
  matrix products: 45.5 us -> 67 us
  between operations: 14.6 us -> 1.46 us
  local copies, waits for them, and re-layouts: 1.21 us -> 8.84 us
    all_gather x1 -> x0, waiting for transfers between devices: 85 us -> none  [body(): whole_map = lax.all_gather(section_maps[0], 'row', axis=0, tiled=True)]
    ppermute x0 -> x6, waiting for transfers between devices: none -> 66.2 us  [the longest x3 44.8 us: line_gather(): lax.ppermute(leftward, 'row', [(z, z - 1) for z in range(1, count - t + 1)])]
    dot_general x18, matrix products: 45.5 us -> 67 us  [product(): jnp.dot(left, right, precision=lax.Precision.HIGH, preferred_element_type...]
    ppermute x0 -> x6, starting transfers between devices: none -> 12.2 us  [the longest x3 8.35 us: line_gather(): lax.ppermute(rightward, 'row', [(z, z + 1) for z in range(t - 1, count -...]
    ppermute x14, waiting for transfers between devices: 9.3 us -> 0.04 us  [body(): got = lax.ppermute(fresh, 'tm', [(k, k - 1)])]
    unnamed x13 -> x61, local copies, waits for them, and re-layouts: 0.08 us -> 6.42 us
    ppermute x1, starting transfers between devices: 1.43 us -> 6.17 us  [body(): lax.ppermute(sent, 'row', [(z, (z + e) % count) for z in range(count)])]
    ppermute x3, waiting for transfers between devices: 21.3 us -> 17.1 us  [body(): lax.ppermute(payload, 'row', [(z, (z + d) % count) for z in range(count)])]
  transfers between devices with their start and end apart: 19 -> 24, of which waited for: 6 -> 7; matrix products, arithmetic and copies ran while one was open for 14% -> 28% of each run, Pallas kernels for 0% -> 0%
where the time goes in v7:
time: 207 us; the launch traced here: 204 us
  waiting for transfers between devices  84.6 us (41%)
  matrix products  67 us (32%)
  starting transfers between devices  39.2 us (19%)
  local copies, waits for them, and re-layouts  8.84 us (4%)
  other arithmetic  3.22 us (2%)
    dot_general x18, matrix products, product(): jnp.dot(left, right, precision=lax.Precision.HIGH, preferred_element_type...  67 us
    ppermute x3, waiting for transfers between devices, line_gather(): lax.ppermute(leftward, 'row', [(z, z - 1) for z in range(1, count - t + 1)])  44.8 us
    ppermute x3, waiting for transfers between devices, line_gather(): lax.ppermute(rightward, 'row', [(z, z + 1) for z in range(t - 1, count -...  21.4 us
    ppermute x3, waiting for transfers between devices, body(): lax.ppermute(payload, 'row', [(z, (z + d) % count) for z in range(count)])  17.1 us
    ppermute x14, starting transfers between devices, body(): got = lax.ppermute(fresh, 'tm', [(k, k - 1)])  14.7 us
    ppermute x3, starting transfers between devices, line_gather(): lax.ppermute(rightward, 'row', [(z, z + 1) for z in range(t - 1, count -...  8.35 us
    unnamed x61, local copies, waits for them, and re-layouts  6.42 us
    ppermute x1, starting transfers between devices, body(): lax.ppermute(sent, 'row', [(z, (z + e) % count) for z in range(count)])  6.17 us
  transfers between devices with their start and end apart: 24, of which 7 were waited for; matrix products, arithmetic and copies ran while one was open for 28% of the time, Pallas kernels for 0%

profile of v7, /device:TPU:0, one launch (start us, length us, event | category | flops | bytes accessed | tf_op | source)
XLA Modules:
  0.0 204.3 jit_solution(15546694145351748079)
XLA Ops:
  0.6 5.0 %collective-permute-start = (f32[256,1024]{1,0:T(8,128)}, f32[256,1024]{1,0:T(8,128)S(1)}, u32[]{:S(2)}, u32[]{:S(2)}) collective-permute-start(f32[256,1024]{1,0:T(8,128)} %bitcast.66), channel_id=1, source_target_pairs={{0,1},{1,2},{2,3},{4,5},{5,6},{6,7},{8,9},{9,10},{10,11},{12,13},{... | collective-permute-start | bytes 3145736 | tf_op jit(solution)/shard_map/ppermute | solution.py:19
  7.0 21.3 %collective-permute-done = f32[256,1024]{1,0:T(8,128)S(1)} collective-permute-done((f32[256,1024]{1,0:T(8,128)}, f32[256,1024]{1,0:T(8,128)S(1)}, u32[]{:S(2)}, u32[]{:S(2)}) %collective-permute-start) | collective-permute-done | bytes 1048608 | tf_op jit(solution)/shard_map/ppermute | solution.py:19
  30.0 2.4 %collective-permute-done.3 = f32[256,1024]{1,0:T(8,128)S(1)} collective-permute-done((f32[256,1024]{1,0:T(8,128)}, f32[256,1024]{1,0:T(8,128)S(1)}, u32[]{:S(2)}, u32[]{:S(2)}) %collective-permute-start.3) | collective-permute-done | bytes 1048608 | tf_op jit(solution)/shard_map/ppermute | solution.py:20
  35.3 23.9 %collective-permute-done.4 = f32[256,1024]{1,0:T(8,128)} collective-permute-done((f32[256,1024]{1,0:T(8,128)S(1)}, f32[256,1024]{1,0:T(8,128)}, u32[]{:S(2)}, u32[]{:S(2)}) %collective-permute-start.4) | collective-permute-done | bytes 1048608 | tf_op jit(solution)/shard_map/ppermute | solution.py:20
  66.1 18.5 %collective-permute-done.5 = f32[256,1024]{1,0:T(8,128)} collective-permute-done((f32[256,1024]{1,0:T(8,128)}, f32[256,1024]{1,0:T(8,128)}, u32[]{:S(2)}, u32[]{:S(2)}) %collective-permute-start.5) | collective-permute-done | bytes 1048608 | tf_op jit(solution)/shard_map/ppermute | solution.py:20
  92.3 5.1 %fusion.27 = f32[1024,64]{0,1:T(8,128)} fusion(f32[1024,64]{0,1:T(8,128)S(1)} %get-tuple-element.18, f32[1792,1024]{1,0:T(8,128)} %copy-done, s32[]{:T(128)S(6)} %select_n.369), kind=kOutput, calls=%fused_computation.33 | convolution fusion | flops 402653184 | bytes 4718596 | tf_op jit(solution)/shard_map/dot_general | solution.py:10
  98.8 4.9 %fusion.42 = f32[1024,64]{0,1:T(8,128)} fusion(f32[1024,64]{0,1:T(8,128)S(1)} %get-tuple-element.17, f32[1792,1024]{1,0:T(8,128)} %copy-done, s32[]{:T(128)S(6)} %select_n.369), kind=kOutput, calls=%fused_computation.48 | convolution fusion | flops 402653184 | bytes 4718596 | tf_op jit(solution)/shard_map/dot_general | solution.py:10
  105.3 5.0 %fusion.25 = f32[1024,64]{0,1:T(8,128)} fusion(f32[1792,1024]{1,0:T(8,128)} %copy-done, s32[]{:T(128)S(6)} %select_n.369, f32[1024,64]{0,1:T(8,128)} %collective-permute-done.14, f32[1024,64]{0,1:T(8,128)} %copy-done.7, pred[]{:T(512)S(6)} %eq.132), kind=kOutput, calls=%fused_computation.31 | convolution fusion | flops 402718720 | bytes 4980741 | tf_op jit(solution)/shard_map/dot_general | solution.py:10
  111.6 4.4 %fusion.40 = f32[1024,64]{0,1:T(8,128)S(1)} fusion(f32[1792,1024]{1,0:T(8,128)} %copy-done, s32[]{:T(128)S(6)} %select_n.369, f32[1024,64]{0,1:T(8,128)} %collective-permute-done.7, f32[1024,64]{0,1:T(8,128)S(1)} %get-tuple-element.17, pred[]{:T(512)S(6)} %eq.132), kind=kOutput, calls=%fused_computation.46 | convolution fusion | flops 402718720 | bytes 4980741 | tf_op jit(solution)/shard_map/dot_general | solution.py:10
  117.9 4.2 %fusion.23 = f32[1024,64]{0,1:T(8,128)S(1)} fusion(f32[1024,64]{0,1:T(8,128)S(1)} %broadcast_select_fusion.4, f32[1792,1024]{1,0:T(8,128)} %copy-done, s32[]{:T(128)S(6)} %select_n.369), kind=kOutput, calls=%fused_computation.29 | convolution fusion | flops 402653184 | bytes 4718596 | tf_op jit(solution)/shard_map/dot_general | solution.py:10
  123.9 2.8 %fusion.38 = f32[1024,64]{0,1:T(8,128)} fusion(f32[1024,64]{0,1:T(8,128)S(1)} %broadcast_select_fusion.5, f32[1792,1024]{1,0:T(8,128)S(1)} %bitcast.57, s32[]{:T(128)S(6)} %select_n.369), kind=kOutput, calls=%fused_computation.44 | convolution fusion | flops 402653184 | bytes 4718596 | tf_op jit(solution)/shard_map/dot_general | solution.py:10
  128.0 2.7 %fusion.21 = f32[1024,64]{0,1:T(8,128)} fusion(f32[1792,1024]{1,0:T(8,128)S(1)} %bitcast.57, s32[]{:T(128)S(6)} %select_n.369, f32[1024,64]{0,1:T(8,128)S(1)} %collective-permute-done.16, f32[1024,64]{0,1:T(8,128)S(1)} %broadcast_select_fusion.4, pred[]{:T(512)S(6)} %eq.130), kind=kOutput, calls=%fused_computation.27 | convolution fusion | flops 402718720 | bytes 4980741 | tf_op jit(solution)/shard_map/dot_general | solution.py:10
  131.5 4.4 %fusion.36 = f32[1024,64]{0,1:T(8,128)S(1)} fusion(f32[1792,1024]{1,0:T(8,128)} %copy-done, s32[]{:T(128)S(6)} %select_n.369, f32[1024,64]{0,1:T(8,128)} %collective-permute-done.9, f32[1024,64]{0,1:T(8,128)} %copy-done.4, pred[]{:T(512)S(6)} %eq.130), kind=kOutput, calls=%fused_computation.42 | convolution fusion | flops 402718720 | bytes 4980741 | tf_op jit(solution)/shard_map/dot_general | solution.py:10
  136.7 4.4 %fusion.19 = f32[1024,64]{0,1:T(8,128)S(1)} fusion(f32[1024,64]{0,1:T(8,128)S(1)} %broadcast_select_fusion.8, f32[1792,1024]{1,0:T(8,128)} %copy-done, s32[]{:T(128)S(6)} %select_n.369), kind=kOutput, calls=%fused_computation.25 | convolution fusion | flops 402653184 | bytes 4718596 | tf_op jit(solution)/shard_map/dot_general | solution.py:10
  141.8 4.9 %fusion.34 = f32[1024,64]{0,1:T(8,128)} fusion(f32[1024,64]{0,1:T(8,128)S(1)} %broadcast_select_fusion.9, f32[1792,1024]{1,0:T(8,128)} %copy-done, s32[]{:T(128)S(6)} %select_n.369), kind=kOutput, calls=%fused_computation.40 | convolution fusion | flops 402653184 | bytes 4718596 | tf_op jit(solution)/shard_map/dot_general | solution.py:10
  148.2 2.7 %fusion.17 = f32[1024,64]{0,1:T(8,128)} fusion(f32[1792,1024]{1,0:T(8,128)S(1)} %bitcast.59, s32[]{:T(128)S(6)} %select_n.369, f32[1024,64]{0,1:T(8,128)S(1)} %collective-permute-done.18, f32[1024,64]{0,1:T(8,128)S(1)} %broadcast_select_fusion.8, pred[]{:T(512)S(6)} %eq.128), kind=kOutput, calls=%fused_computation.23 | convolution fusion | flops 402718720 | bytes 4980741 | tf_op jit(solution)/shard_map/dot_general | solution.py:10
  152.6 4.4 %fusion.32 = f32[1024,64]{0,1:T(8,128)S(1)} fusion(f32[1792,1024]{1,0:T(8,128)} %copy-done, s32[]{:T(128)S(6)} %select_n.369, f32[1024,64]{0,1:T(8,128)} %collective-permute-done.11, f32[1024,64]{0,1:T(8,128)S(1)} %broadcast_select_fusion.9, pred[]{:T(512)S(6)} %eq.128), kind=kOutput, calls=%fused_computation.38 | convolution fusion | flops 402718720 | bytes 4980741 | tf_op jit(solution)/shard_map/dot_general | solution.py:10
  158.3 4.4 %convolution_select_fusion = f32[1024,64]{0,1:T(8,128)S(1)} fusion(f32[1792,1024]{1,0:T(8,128)} %copy-done, s32[]{:T(128)S(6)} %select_n.369, f32[1024,64]{0,1:T(8,128)} %fusion.17, f32[1024,64]{0,1:T(8,128)} %copy-done.13, f32[1024,64]{0,1:T(8,128)} %fusion.21, f32[1024,64]{0,1:T(8,128)} %copy-done.12, f32[1024,64]{0,1:T(8,128)} %fusion.25, ...), kind=kOutput, calls=%fused_computation.2 | convolution fusion | flops 403243008 | bytes 7083008 | tf_op jit(solution)/shard_map/dot_general | solution.py:10
  166.1 5.6 %collective-permute-start.21 = (f32[512,128]{0,1:T(8,128)S(1)}, f32[512,128]{0,1:T(8,128)S(1)}, u32[]{:S(2)}, u32[]{:S(2)}) collective-permute-start(f32[512,128]{0,1:T(8,128)S(1)} %pad_maximum_fusion.3), channel_id=1, source_target_pairs={{0,2},{1,3},{2,0},{3,1},{4,6},{5,7},{6,4},{7,5},{8,10},{9,11},{10,... | collective-permute-start | bytes 786440 | tf_op jit(solution)/shard_map/ppermute | solution.py:62
  172.3 3.2 %collective-permute-done.22 = f32[512,128]{0,1:T(8,128)S(1)} collective-permute-done((f32[512,128]{0,1:T(8,128)S(1)}, f32[512,128]{0,1:T(8,128)S(1)}, u32[]{:S(2)}, u32[]{:S(2)}) %collective-permute-start.22) | collective-permute-done | bytes 262176 | tf_op jit(solution)/shard_map/ppermute | solution.py:62
  175.5 13.9 %collective-permute-done.21 = f32[512,128]{0,1:T(8,128)S(1)} collective-permute-done((f32[512,128]{0,1:T(8,128)S(1)}, f32[512,128]{0,1:T(8,128)S(1)}, u32[]{:S(2)}, u32[]{:S(2)}) %collective-permute-start.21) | collective-permute-done | bytes 262176 | tf_op jit(solution)/shard_map/ppermute | solution.py:62
  189.5 4.2 %fusion.1 = f32[256,2048]{1,0:T(8,128)S(1)} fusion(f32[512,2048]{1,0:T(8,128)} %param.5, f32[256,128]{0,1:T(8,128)S(1)} %get-tuple-element.9, f32[256,128]{0,1:T(8,128)S(1)} %get-tuple-element.7, f32[256,128]{0,1:T(8,128)S(1)} %get-tuple-element.6, f32[256,128]{0,1:T(8,128)S(1)} %get-tuple-element.5), kind=kOutput, calls=%fused_computation.7 | convolution fusion | flops 1611005952 | bytes 6815744 | tf_op jit(solution)/shard_map/dot_general | solution.py:10
  193.8 2.2 %fusion = f32[2048]{0:T(1024)S(1)} fusion(f32[256,2048]{1,0:T(8,128)S(1)} %fusion.1, f32[512,2048]{1,0:T(8,128)S(1)} %copy-done.1, f32[256,128]{0,1:T(8,128)S(1)} %get-tuple-element.8, f32[256,128]{0,1:T(8,128)S(1)} %get-tuple-element.4, f32[256,128]{0,1:T(8,128)S(1)} %get-tuple-element.3, f32[256,128]{0,1:T(8,128)S(1)} %get-tuple-element.2), kind=kOutput, calls=%fused_computation.1 | convolution fusion | flops 1612052480 | bytes 6823936 | tf_op jit(solution)/shard_map/dot_general | solution.py:10
  196.1 6.2 %collective-permute-start.23 = (f32[512]{0:T(512)S(1)}, f32[512]{0:T(512)S(1)}, u32[]{:S(2)}, u32[]{:S(2)}) collective-permute-start(f32[512]{0:T(512)S(1)} %dynamic_slice.40), channel_id=1, source_target_pairs={{0,1},{1,2},{2,3},{3,0},{4,5},{5,6},{6,7},{7,4},{8,9},{9,10},{10,1... | collective-permute-start | bytes 6152 | tf_op jit(solution)/shard_map/ppermute | solution.py:83
  (125 shorter events, 42.0 us)
Async XLA Ops:
  0.6 27.7 %collective-permute-start = (f32[256,1024]{1,0:T(8,128)}, f32[256,1024]{1,0:T(8,128)S(1)}, u32[]{:S(2)}, u32[]{:S(2)}) collective-permute-start(f32[256,1024]{1,0:T(8,128)} %bitcast.66), channel_id=1, source_target_pairs={{0,1},{1,2},{2,3},{4,5},{5,6},{6,7},{8,9},{9,10},{10,11},{12,13},{... | collective-permute-start | bytes 3145736 | tf_op jit(solution)/shard_map/ppermute | solution.py:19
  5.7 26.7 %collective-permute-start.3 = (f32[256,1024]{1,0:T(8,128)}, f32[256,1024]{1,0:T(8,128)S(1)}, u32[]{:S(2)}, u32[]{:S(2)}) collective-permute-start(f32[256,1024]{1,0:T(8,128)} %bitcast.67), channel_id=1, source_target_pairs={{1,0},{2,1},{3,2},{5,4},{6,5},{7,6},{9,8},{10,9},{11,10},{13,12},{... | collective-permute-start | bytes 3145736 | tf_op jit(solution)/shard_map/ppermute | solution.py:20
  28.3 5.4 %collective-permute-start.1 = (f32[256,1024]{1,0:T(8,128)S(1)}, f32[256,1024]{1,0:T(8,128)}, u32[]{:S(2)}, u32[]{:S(2)}) collective-permute-start(f32[256,1024]{1,0:T(8,128)S(1)} %collective-permute-done), channel_id=1, source_target_pairs={{1,2},{2,3},{5,6},{6,7},{9,10},{10,11},{13,14},{14,15},{17,18},{18... | collective-permute-start | bytes 3145736 | tf_op jit(solution)/shard_map/ppermute | solution.py:19
  32.4 26.8 %collective-permute-start.4 = (f32[256,1024]{1,0:T(8,128)S(1)}, f32[256,1024]{1,0:T(8,128)}, u32[]{:S(2)}, u32[]{:S(2)}) collective-permute-start(f32[256,1024]{1,0:T(8,128)S(1)} %collective-permute-done.3), channel_id=1, source_target_pairs={{1,0},{2,1},{5,4},{6,5},{9,8},{10,9},{13,12},{14,13},{17,16},{18,1... | collective-permute-start | bytes 3145736 | tf_op jit(solution)/shard_map/ppermute | solution.py:20
  33.7 26.9 %collective-permute-start.2 = (f32[256,1024]{1,0:T(8,128)}, f32[256,1024]{1,0:T(8,128)}, u32[]{:S(2)}, u32[]{:S(2)}) collective-permute-start(f32[256,1024]{1,0:T(8,128)} %collective-permute-done.1), channel_id=1, source_target_pairs={{2,3},{6,7},{10,11},{14,15},{18,19},{22,23},{26,27},{30,31}} | collective-permute-start | bytes 3145736 | tf_op jit(solution)/shard_map/ppermute | solution.py:19
  59.2 25.4 %collective-permute-start.5 = (f32[256,1024]{1,0:T(8,128)}, f32[256,1024]{1,0:T(8,128)}, u32[]{:S(2)}, u32[]{:S(2)}) collective-permute-start(f32[256,1024]{1,0:T(8,128)} %collective-permute-done.4), channel_id=1, source_target_pairs={{1,0},{5,4},{9,8},{13,12},{17,16},{21,20},{25,24},{29,28}} | collective-permute-start | bytes 3145736 | tf_op jit(solution)/shard_map/ppermute | solution.py:20
  90.8 1.4 collective-permute-start.6
  91.5 0.7 collective-permute-start.13
  97.4 7.8 %collective-permute-start.14 = (f32[1024,64]{0,1:T(8,128)}, f32[1024,64]{0,1:T(8,128)}, u32[]{:S(2)}, u32[]{:S(2)}) collective-permute-start(f32[1024,64]{0,1:T(8,128)} %fusion.27), channel_id=1, source_target_pairs={{24,20},{25,21},{26,22},{27,23}} | collective-permute-start | bytes 786440 | tf_op jit(solution)/shard_map/ppermute | solution.py:50
  103.8 7.8 %collective-permute-start.7 = (f32[1024,64]{0,1:T(8,128)}, f32[1024,64]{0,1:T(8,128)}, u32[]{:S(2)}, u32[]{:S(2)}) collective-permute-start(f32[1024,64]{0,1:T(8,128)} %fusion.42), channel_id=1, source_target_pairs={{24,20},{25,21},{26,22},{27,23}} | collective-permute-start | bytes 786440 | tf_op jit(solution)/shard_map/ppermute | solution.py:50
  110.2 6.6 %collective-permute-start.15 = (f32[1024,64]{0,1:T(8,128)}, f32[1024,64]{0,1:T(8,128)}, u32[]{:S(2)}, u32[]{:S(2)}) collective-permute-start(f32[1024,64]{0,1:T(8,128)} %fusion.25), channel_id=1, source_target_pairs={{20,16},{21,17},{22,18},{23,19}} | collective-permute-start | bytes 786440 | tf_op jit(solution)/shard_map/ppermute | solution.py:50
  116.0 6.8 %collective-permute-start.8 = (f32[1024,64]{0,1:T(8,128)S(1)}, f32[1024,64]{0,1:T(8,128)S(1)}, u32[]{:S(2)}, u32[]{:S(2)}) collective-permute-start(f32[1024,64]{0,1:T(8,128)S(1)} %fusion.40), channel_id=1, source_target_pairs={{20,16},{21,17},{22,18},{23,19}} | collective-permute-start | bytes 786440 | tf_op jit(solution)/shard_map/ppermute | solution.py:50
  122.1 5.9 %collective-permute-start.16 = (f32[1024,64]{0,1:T(8,128)S(1)}, f32[1024,64]{0,1:T(8,128)S(1)}, u32[]{:S(2)}, u32[]{:S(2)}) collective-permute-start(f32[1024,64]{0,1:T(8,128)S(1)} %fusion.23), channel_id=1, source_target_pairs={{16,12},{17,13},{18,14},{19,15}} | collective-permute-start | bytes 786440 | tf_op jit(solution)/shard_map/ppermute | solution.py:50
  126.6 4.8 %collective-permute-start.9 = (f32[1024,64]{0,1:T(8,128)}, f32[1024,64]{0,1:T(8,128)}, u32[]{:S(2)}, u32[]{:S(2)}) collective-permute-start(f32[1024,64]{0,1:T(8,128)} %fusion.38), channel_id=1, source_target_pairs={{16,12},{17,13},{18,14},{19,15}} | collective-permute-start | bytes 786440 | tf_op jit(solution)/shard_map/ppermute | solution.py:50
  130.8 5.8 %collective-permute-start.17 = (f32[1024,64]{0,1:T(8,128)}, f32[1024,64]{0,1:T(8,128)S(1)}, u32[]{:S(2)}, u32[]{:S(2)}) collective-permute-start(f32[1024,64]{0,1:T(8,128)} %fusion.21), channel_id=1, source_target_pairs={{12,8},{13,9},{14,10},{15,11}} | collective-permute-start | bytes 786440 | tf_op jit(solution)/shard_map/ppermute | solution.py:50
  135.9 5.9 %collective-permute-start.10 = (f32[1024,64]{0,1:T(8,128)S(1)}, f32[1024,64]{0,1:T(8,128)S(1)}, u32[]{:S(2)}, u32[]{:S(2)}) collective-permute-start(f32[1024,64]{0,1:T(8,128)S(1)} %fusion.36), channel_id=1, source_target_pairs={{12,8},{13,9},{14,10},{15,11}} | collective-permute-start | bytes 786440 | tf_op jit(solution)/shard_map/ppermute | solution.py:50
  141.0 7.1 %collective-permute-start.18 = (f32[1024,64]{0,1:T(8,128)S(1)}, f32[1024,64]{0,1:T(8,128)S(1)}, u32[]{:S(2)}, u32[]{:S(2)}) collective-permute-start(f32[1024,64]{0,1:T(8,128)S(1)} %fusion.19), channel_id=1, source_target_pairs={{8,4},{9,5},{10,6},{11,7}} | collective-permute-start | bytes 786440 | tf_op jit(solution)/shard_map/ppermute | solution.py:50
  146.7 5.8 %collective-permute-start.11 = (f32[1024,64]{0,1:T(8,128)}, f32[1024,64]{0,1:T(8,128)}, u32[]{:S(2)}, u32[]{:S(2)}) collective-permute-start(f32[1024,64]{0,1:T(8,128)} %fusion.34), channel_id=1, source_target_pairs={{8,4},{9,5},{10,6},{11,7}} | collective-permute-start | bytes 786440 | tf_op jit(solution)/shard_map/ppermute | solution.py:50
  150.9 7.3 %collective-permute-start.19 = (f32[1024,64]{0,1:T(8,128)}, f32[1024,64]{0,1:T(8,128)}, u32[]{:S(2)}, u32[]{:S(2)}) collective-permute-start(f32[1024,64]{0,1:T(8,128)} %fusion.17), channel_id=1, source_target_pairs={{4,0},{5,1},{6,2},{7,3}} | collective-permute-start | bytes 786440 | tf_op jit(solution)/shard_map/ppermute | solution.py:50
  156.9 5.7 %collective-permute-start.12 = (f32[1024,64]{0,1:T(8,128)S(1)}, f32[1024,64]{0,1:T(8,128)S(1)}, u32[]{:S(2)}, u32[]{:S(2)}) collective-permute-start(f32[1024,64]{0,1:T(8,128)S(1)} %fusion.32), channel_id=1, source_target_pairs={{4,0},{5,1},{6,2},{7,3}} | collective-permute-start | bytes 786440 | tf_op jit(solution)/shard_map/ppermute | solution.py:50
  166.0 9.5 %collective-permute-start.22 = (f32[512,128]{0,1:T(8,128)S(1)}, f32[512,128]{0,1:T(8,128)S(1)}, u32[]{:S(2)}, u32[]{:S(2)}) collective-permute-start(f32[512,128]{0,1:T(8,128)S(1)} %pad_maximum_fusion.4), channel_id=1, source_target_pairs={{0,1},{1,2},{2,3},{3,0},{4,5},{5,6},{6,7},{7,4},{8,9},{9,10},{10,1... | collective-permute-start | bytes 786440 | tf_op jit(solution)/shard_map/ppermute | solution.py:62
  166.1 23.2 %collective-permute-start.21 = (f32[512,128]{0,1:T(8,128)S(1)}, f32[512,128]{0,1:T(8,128)S(1)}, u32[]{:S(2)}, u32[]{:S(2)}) collective-permute-start(f32[512,128]{0,1:T(8,128)S(1)} %pad_maximum_fusion.3), channel_id=1, source_target_pairs={{0,2},{1,3},{2,0},{3,1},{4,6},{5,7},{6,4},{7,5},{8,10},{9,11},{10,... | collective-permute-start | bytes 786440 | tf_op jit(solution)/shard_map/ppermute | solution.py:62
  171.8 17.6 %collective-permute-start.20 = (f32[512,128]{0,1:T(8,128)S(1)}, f32[512,128]{0,1:T(8,128)S(1)}, u32[]{:S(2)}, u32[]{:S(2)}) collective-permute-start(f32[512,128]{0,1:T(8,128)S(1)} %pad_maximum_fusion.2), channel_id=1, source_target_pairs={{0,3},{1,0},{2,1},{3,2},{4,7},{5,4},{6,5},{7,6},{8,11},{9,8},{10,9... | collective-permute-start | bytes 786440 | tf_op jit(solution)/shard_map/ppermute | solution.py:62
  196.1 7.5 %collective-permute-start.23 = (f32[512]{0:T(512)S(1)}, f32[512]{0:T(512)S(1)}, u32[]{:S(2)}, u32[]{:S(2)}) collective-permute-start(f32[512]{0:T(512)S(1)} %dynamic_slice.40), channel_id=1, source_target_pairs={{0,1},{1,2},{2,3},{3,0},{4,5},{5,6},{6,7},{7,4},{8,9},{9,10},{10,1... | collective-permute-start | bytes 6152 | tf_op jit(solution)/shard_map/ppermute | solution.py:83
  (26 other events, 289.4 us)

commit v8 on v7

--- a/solution.py
+++ b/solution.py
@@ -33,7 +33,7 @@
     state_dim = terminal_cost.shape[1]
     width = state_dim // count
 
-    whole_map = line_gather(section_maps[0], place, count)
+    whole_map = lax.optimization_barrier(line_gather(section_maps[0], place, count))
     rows_id = lax.broadcasted_iota(jnp.int32, (state_dim, width), 0)
     cols_id = lax.broadcasted_iota(jnp.int32, (state_dim, width), 1) + place * width
     identity_cols = (rows_id == cols_id).astype(jnp.float32)

time: 207 us -> 183 us (0.88); the launches traced: 204 us -> 183 us
  matrix products: 67 us -> 41.5 us
  waiting for transfers between devices: 84.6 us -> 96.5 us
  starting transfers between devices: 39.2 us -> 34.5 us
    dot_general x18, matrix products: 67 us -> 41.5 us  [product(): jnp.dot(left, right, precision=lax.Precision.HIGH, preferred_element_type...]
    ppermute x14, waiting for transfers between devices: 0.04 us -> 10.1 us  [body(): got = lax.ppermute(fresh, 'tm', [(k, k - 1)])]
    ppermute x14, starting transfers between devices: 14.7 us -> 11.1 us  [body(): got = lax.ppermute(fresh, 'tm', [(k, k - 1)])]
    unnamed x61 -> x21, local copies, waits for them, and re-layouts: 6.42 us -> 4.63 us
  transfers between devices with their start and end apart: 24 -> 24, of which waited for: 7 -> 9; matrix products, arithmetic and copies ran while one was open for 28% -> 16% of each run, Pallas kernels for 0% -> 0%
where the time goes in v8:
time: 183 us
  waiting for transfers between devices  96.5 us (53%)
  matrix products  41.5 us (23%)
  starting transfers between devices  34.5 us (19%)
  local copies, waits for them, and re-layouts  7.63 us (4%)
    ppermute x3, waiting for transfers between devices, line_gather(): lax.ppermute(leftward, 'row', [(z, z - 1) for z in range(1, count - t + 1)])  46 us
    dot_general x18, matrix products, product(): jnp.dot(left, right, precision=lax.Precision.HIGH, preferred_element_type...  41.5 us
    ppermute x3, waiting for transfers between devices, line_gather(): lax.ppermute(rightward, 'row', [(z, z + 1) for z in range(t - 1, count -...  21.4 us
    ppermute x3, waiting for transfers between devices, body(): lax.ppermute(payload, 'row', [(z, (z + d) % count) for z in range(count)])  17.2 us
    ppermute x14, starting transfers between devices, body(): got = lax.ppermute(fresh, 'tm', [(k, k - 1)])  11.1 us
    ppermute x14, waiting for transfers between devices, body(): got = lax.ppermute(fresh, 'tm', [(k, k - 1)])  10.1 us
    ppermute x3, starting transfers between devices, line_gather(): lax.ppermute(rightward, 'row', [(z, z + 1) for z in range(t - 1, count -...  8.44 us
    ppermute x1, starting transfers between devices, body(): lax.ppermute(sent, 'row', [(z, (z + e) % count) for z in range(count)])  6.19 us
  transfers between devices with their start and end apart: 24, of which 9 were waited for; matrix products, arithmetic and copies ran while one was open for 16% of the time, Pallas kernels for 0%

profile of v8, /device:TPU:0, one launch (start us, length us, event | category | flops | bytes accessed | tf_op | source)
XLA Modules:
  0.0 182.7 jit_solution(12266905240245148117)
XLA Ops:
  0.6 5.2 %collective-permute-start = (f32[256,1024]{1,0:T(8,128)}, f32[256,1024]{1,0:T(8,128)S(1)}, u32[]{:S(2)}, u32[]{:S(2)}) collective-permute-start(f32[256,1024]{1,0:T(8,128)} %bitcast.76), channel_id=1, source_target_pairs={{0,1},{1,2},{2,3},{4,5},{5,6},{6,7},{8,9},{9,10},{10,11},{12,13},{... | collective-permute-start | bytes 3145736 | tf_op jit(solution)/shard_map/ppermute | solution.py:19
  7.1 21.3 %collective-permute-done = f32[256,1024]{1,0:T(8,128)S(1)} collective-permute-done((f32[256,1024]{1,0:T(8,128)}, f32[256,1024]{1,0:T(8,128)S(1)}, u32[]{:S(2)}, u32[]{:S(2)}) %collective-permute-start) | collective-permute-done | bytes 1048608 | tf_op jit(solution)/shard_map/ppermute | solution.py:19
  30.1 2.4 %collective-permute-done.3 = f32[256,1024]{1,0:T(8,128)S(1)} collective-permute-done((f32[256,1024]{1,0:T(8,128)}, f32[256,1024]{1,0:T(8,128)S(1)}, u32[]{:S(2)}, u32[]{:S(2)}) %collective-permute-start.3) | collective-permute-done | bytes 1048608 | tf_op jit(solution)/shard_map/ppermute | solution.py:20
  35.5 23.8 %collective-permute-done.4 = f32[256,1024]{1,0:T(8,128)} collective-permute-done((f32[256,1024]{1,0:T(8,128)S(1)}, f32[256,1024]{1,0:T(8,128)}, u32[]{:S(2)}, u32[]{:S(2)}) %collective-permute-start.4) | collective-permute-done | bytes 1048608 | tf_op jit(solution)/shard_map/ppermute | solution.py:20
  65.0 19.7 %collective-permute-done.5 = f32[256,1024]{1,0:T(8,128)} collective-permute-done((f32[256,1024]{1,0:T(8,128)}, f32[256,1024]{1,0:T(8,128)}, u32[]{:S(2)}, u32[]{:S(2)}) %collective-permute-start.5) | collective-permute-done | bytes 1048608 | tf_op jit(solution)/shard_map/ppermute | solution.py:20
  92.6 4.4 %fusion.46 = f32[1024,64]{0,1:T(8,128)S(1)} fusion(f32[1024,1024]{1,0:T(8,128)} %copy-done, f32[1024,64]{0,1:T(8,128)S(1)} %get-tuple-element.18), kind=kOutput, calls=%fused_computation.99 | convolution fusion | flops 402653184 | bytes 4718592 | tf_op jit(solution)/shard_map/dot_general | solution.py:10
  97.7 2.0 %fusion.43 = f32[1024,64]{0,1:T(8,128)S(1)} fusion(f32[1024,1024]{1,0:T(8,128)S(1)} %copy-done.1, f32[1024,64]{0,1:T(8,128)S(1)} %get-tuple-element.17), kind=kOutput, calls=%fused_computation.96 | convolution fusion | flops 402653184 | bytes 4718592 | tf_op jit(solution)/shard_map/dot_general | solution.py:10
  100.4 2.0 %fusion.35 = f32[1024,64]{0,1:T(8,128)S(1)} fusion(f32[1024,1024]{1,0:T(8,128)S(1)} %copy-done.1, f32[1024,64]{0,1:T(8,128)S(1)} %collective-permute-done.14, f32[1024,64]{0,1:T(8,128)S(1)} %get-tuple-element.18, pred[]{:T(512)S(6)} %eq.132), kind=kOutput, calls=%fused_computation.72 | convolution fusion | flops 402718720 | bytes 4980737 | tf_op jit(solution)/shard_map/dot_general | solution.py:10
  106.1 2.0 %fusion.47 = f32[1024,64]{0,1:T(8,128)S(1)} fusion(f32[1024,1024]{1,0:T(8,128)S(1)} %copy-done.1, f32[1024,64]{0,1:T(8,128)S(1)} %broadcast_select_fusion.4), kind=kOutput, calls=%fused_computation.100 | convolution fusion | flops 402653184 | bytes 4718592 | tf_op jit(solution)/shard_map/dot_general | solution.py:10
  108.9 2.0 %fusion.44 = f32[1024,64]{0,1:T(8,128)S(1)} fusion(f32[1024,1024]{1,0:T(8,128)S(1)} %copy-done.1, f32[1024,64]{0,1:T(8,128)S(1)} %broadcast_select_fusion.5), kind=kOutput, calls=%fused_computation.97 | convolution fusion | flops 402653184 | bytes 4718592 | tf_op jit(solution)/shard_map/dot_general | solution.py:10
  111.6 2.0 %fusion.33 = f32[1024,64]{0,1:T(8,128)S(1)} fusion(f32[1024,1024]{1,0:T(8,128)S(1)} %copy-done.1, f32[1024,64]{0,1:T(8,128)S(1)} %collective-permute-done.16, f32[1024,64]{0,1:T(8,128)S(1)} %broadcast_select_fusion.4, pred[]{:T(512)S(6)} %eq.130), kind=kOutput, calls=%fused_computation.70 | convolution fusion | flops 402718720 | bytes 4980737 | tf_op jit(solution)/shard_map/dot_general | solution.py:10
  114.3 2.0 %fusion.32 = f32[1024,64]{0,1:T(8,128)S(1)} fusion(f32[1024,1024]{1,0:T(8,128)S(1)} %copy-done.1, f32[1024,64]{0,1:T(8,128)S(1)} %collective-permute-done.9, f32[1024,64]{0,1:T(8,128)S(1)} %broadcast_select_fusion.5, pred[]{:T(512)S(6)} %eq.130), kind=kOutput, calls=%fused_computation.69 | convolution fusion | flops 402718720 | bytes 4980737 | tf_op jit(solution)/shard_map/dot_general | solution.py:10
  117.1 2.0 %fusion.48 = f32[1024,64]{0,1:T(8,128)S(1)} fusion(f32[1024,1024]{1,0:T(8,128)S(1)} %copy-done.1, f32[1024,64]{0,1:T(8,128)S(1)} %broadcast_select_fusion.8), kind=kOutput, calls=%fused_computation.101 | convolution fusion | flops 402653184 | bytes 4718592 | tf_op jit(solution)/shard_map/dot_general | solution.py:10
  119.9 2.0 %fusion.45 = f32[1024,64]{0,1:T(8,128)S(1)} fusion(f32[1024,1024]{1,0:T(8,128)S(1)} %copy-done.1, f32[1024,64]{0,1:T(8,128)S(1)} %broadcast_select_fusion.9), kind=kOutput, calls=%fused_computation.98 | convolution fusion | flops 402653184 | bytes 4718592 | tf_op jit(solution)/shard_map/dot_general | solution.py:10
  126.2 2.0 %fusion.30 = f32[1024,64]{0,1:T(8,128)S(1)} fusion(f32[1024,1024]{1,0:T(8,128)S(1)} %copy-done.1, f32[1024,64]{0,1:T(8,128)S(1)} %collective-permute-done.11, f32[1024,64]{0,1:T(8,128)S(1)} %broadcast_select_fusion.9, pred[]{:T(512)S(6)} %eq.128), kind=kOutput, calls=%fused_computation.67 | convolution fusion | flops 402718720 | bytes 4980737 | tf_op jit(solution)/shard_map/dot_general | solution.py:10
  129.5 8.5 %collective-permute-done.19 = f32[1024,64]{0,1:T(8,128)S(1)} collective-permute-done((f32[1024,64]{0,1:T(8,128)S(1)}, f32[1024,64]{0,1:T(8,128)S(1)}, u32[]{:S(2)}, u32[]{:S(2)}) %collective-permute-start.19) | collective-permute-done | bytes 262176 | tf_op jit(solution)/shard_map/ppermute | solution.py:50
  138.0 2.0 %convolution_select_fusion = f32[1024,64]{0,1:T(8,128)S(1)} fusion(f32[1024,1024]{1,0:T(8,128)S(1)} %copy-done.1, f32[1024,64]{0,1:T(8,128)S(1)} %fusion.31, f32[1024,64]{0,1:T(8,128)S(1)} %fusion.48, f32[1024,64]{0,1:T(8,128)S(1)} %fusion.33, f32[1024,64]{0,1:T(8,128)S(1)} %fusion.47, f32[1024,64]{0,1:T(8,128)S(1)} %fusion.35, f32[1024,64]{0,1:T(8,128)S(1)} %fusion.46, ...), kind=kOutput, calls=%fused_computation.2 | convolution fusion | flops 403243008 | bytes 7077895 | tf_op jit(solution)/shard_map/dot_general | solution.py:10
  141.6 2.0 %convolution_select_fusion.1 = f32[1024,64]{0,1:T(8,128)S(1)} fusion(f32[1024,1024]{1,0:T(8,128)S(1)} %copy-done.1, f32[1024,64]{0,1:T(8,128)S(1)} %fusion.30, f32[1024,64]{0,1:T(8,128)S(1)} %fusion.45, f32[1024,64]{0,1:T(8,128)S(1)} %fusion.32, f32[1024,64]{0,1:T(8,128)S(1)} %fusion.44, f32[1024,64]{0,1:T(8,128)S(1)} %fusion.34, ...), kind=kOutput, calls=%fused_computation.3 | convolution fusion | flops 403243008 | bytes 7077895 | tf_op jit(solution)/shard_map/dot_general | solution.py:10
  144.9 4.4 %collective-permute-start.21 = (f32[512,128]{0,1:T(8,128)S(1)}, f32[512,128]{0,1:T(8,128)S(1)}, u32[]{:S(2)}, u32[]{:S(2)}) collective-permute-start(f32[512,128]{0,1:T(8,128)S(1)} %pad_maximum_fusion.3), channel_id=1, source_target_pairs={{0,2},{1,3},{2,0},{3,1},{4,6},{5,7},{6,4},{7,5},{8,10},{9,11},{10,... | collective-permute-start | bytes 786440 | tf_op jit(solution)/shard_map/ppermute | solution.py:62
  149.9 5.7 %collective-permute-done.22 = f32[512,128]{0,1:T(8,128)S(1)} collective-permute-done((f32[512,128]{0,1:T(8,128)S(1)}, f32[512,128]{0,1:T(8,128)S(1)}, u32[]{:S(2)}, u32[]{:S(2)}) %collective-permute-start.22) | collective-permute-done | bytes 262176 | tf_op jit(solution)/shard_map/ppermute | solution.py:62
  155.6 11.5 %collective-permute-done.21 = f32[512,128]{0,1:T(8,128)S(1)} collective-permute-done((f32[512,128]{0,1:T(8,128)S(1)}, f32[512,128]{0,1:T(8,128)S(1)}, u32[]{:S(2)}, u32[]{:S(2)}) %collective-permute-start.21) | collective-permute-done | bytes 262176 | tf_op jit(solution)/shard_map/ppermute | solution.py:62
  167.3 4.3 %fusion.1 = f32[256,2048]{1,0:T(8,128)S(1)} fusion(f32[512,2048]{1,0:T(8,128)} %param.5, f32[256,128]{0,1:T(8,128)S(1)} %get-tuple-element.9, f32[256,128]{0,1:T(8,128)S(1)} %get-tuple-element.7, f32[256,128]{0,1:T(8,128)S(1)} %get-tuple-element.6, f32[256,128]{0,1:T(8,128)S(1)} %get-tuple-element.5), kind=kOutput, calls=%fused_computation.7 | convolution fusion | flops 1611005952 | bytes 6815744 | tf_op jit(solution)/shard_map/dot_general | solution.py:10
  171.7 2.3 %fusion = f32[2048]{0:T(1024)S(1)} fusion(f32[256,2048]{1,0:T(8,128)S(1)} %fusion.1, f32[512,2048]{1,0:T(8,128)S(1)} %copy-done.2, f32[256,128]{0,1:T(8,128)S(1)} %get-tuple-element.8, f32[256,128]{0,1:T(8,128)S(1)} %get-tuple-element.4, f32[256,128]{0,1:T(8,128)S(1)} %get-tuple-element.3, f32[256,128]{0,1:T(8,128)S(1)} %get-tuple-element.2), kind=kOutput, calls=%fused_computation.1 | convolution fusion | flops 1612052480 | bytes 6823936 | tf_op jit(solution)/shard_map/dot_general | solution.py:10
  174.0 6.2 %collective-permute-start.23 = (f32[512]{0:T(512)S(1)}, f32[512]{0:T(512)S(1)}, u32[]{:S(2)}, u32[]{:S(2)}) collective-permute-start(f32[512]{0:T(512)S(1)} %dynamic_slice.40), channel_id=1, source_target_pairs={{0,1},{1,2},{2,3},{3,0},{4,5},{5,6},{6,7},{7,4},{8,9},{9,10},{10,1... | collective-permute-start | bytes 6152 | tf_op jit(solution)/shard_map/ppermute | solution.py:83
  (83 shorter events, 39.2 us)
Async XLA Ops:
  0.6 27.8 %collective-permute-start = (f32[256,1024]{1,0:T(8,128)}, f32[256,1024]{1,0:T(8,128)S(1)}, u32[]{:S(2)}, u32[]{:S(2)}) collective-permute-start(f32[256,1024]{1,0:T(8,128)} %bitcast.76), channel_id=1, source_target_pairs={{0,1},{1,2},{2,3},{4,5},{5,6},{6,7},{8,9},{9,10},{10,11},{12,13},{... | collective-permute-start | bytes 3145736 | tf_op jit(solution)/shard_map/ppermute | solution.py:19
  5.8 26.7 %collective-permute-start.3 = (f32[256,1024]{1,0:T(8,128)}, f32[256,1024]{1,0:T(8,128)S(1)}, u32[]{:S(2)}, u32[]{:S(2)}) collective-permute-start(f32[256,1024]{1,0:T(8,128)} %bitcast.77), channel_id=1, source_target_pairs={{1,0},{2,1},{3,2},{5,4},{6,5},{7,6},{9,8},{10,9},{11,10},{13,12},{... | collective-permute-start | bytes 3145736 | tf_op jit(solution)/shard_map/ppermute | solution.py:20
  28.4 5.4 %collective-permute-start.1 = (f32[256,1024]{1,0:T(8,128)S(1)}, f32[256,1024]{1,0:T(8,128)}, u32[]{:S(2)}, u32[]{:S(2)}) collective-permute-start(f32[256,1024]{1,0:T(8,128)S(1)} %collective-permute-done), channel_id=1, source_target_pairs={{1,2},{2,3},{5,6},{6,7},{9,10},{10,11},{13,14},{14,15},{17,18},{18... | collective-permute-start | bytes 3145736 | tf_op jit(solution)/shard_map/ppermute | solution.py:19
  32.5 26.8 %collective-permute-start.4 = (f32[256,1024]{1,0:T(8,128)S(1)}, f32[256,1024]{1,0:T(8,128)}, u32[]{:S(2)}, u32[]{:S(2)}) collective-permute-start(f32[256,1024]{1,0:T(8,128)S(1)} %collective-permute-done.3), channel_id=1, source_target_pairs={{1,0},{2,1},{5,4},{6,5},{9,8},{10,9},{13,12},{14,13},{17,16},{18,1... | collective-permute-start | bytes 3145736 | tf_op jit(solution)/shard_map/ppermute | solution.py:20
  33.8 26.9 %collective-permute-start.2 = (f32[256,1024]{1,0:T(8,128)}, f32[256,1024]{1,0:T(8,128)}, u32[]{:S(2)}, u32[]{:S(2)}) collective-permute-start(f32[256,1024]{1,0:T(8,128)} %collective-permute-done.1), channel_id=1, source_target_pairs={{2,3},{6,7},{10,11},{14,15},{18,19},{22,23},{26,27},{30,31}} | collective-permute-start | bytes 3145736 | tf_op jit(solution)/shard_map/ppermute | solution.py:19
  59.3 25.4 %collective-permute-start.5 = (f32[256,1024]{1,0:T(8,128)}, f32[256,1024]{1,0:T(8,128)}, u32[]{:S(2)}, u32[]{:S(2)}) collective-permute-start(f32[256,1024]{1,0:T(8,128)} %collective-permute-done.4), channel_id=1, source_target_pairs={{1,0},{5,4},{9,8},{13,12},{17,16},{21,20},{25,24},{29,28}} | collective-permute-start | bytes 3145736 | tf_op jit(solution)/shard_map/ppermute | solution.py:20
  91.0 1.5 collective-permute-start.6
  91.7 0.8 collective-permute-start.13
  97.0 3.4 %collective-permute-start.14 = (f32[1024,64]{0,1:T(8,128)S(1)}, f32[1024,64]{0,1:T(8,128)S(1)}, u32[]{:S(2)}, u32[]{:S(2)}) collective-permute-start(f32[1024,64]{0,1:T(8,128)S(1)} %fusion.46), channel_id=1, source_target_pairs={{24,20},{25,21},{26,22},{27,23}} | collective-permute-start | bytes 786440 | tf_op jit(solution)/shard_map/ppermute | solution.py:50
  99.7 3.4 %collective-permute-start.7 = (f32[1024,64]{0,1:T(8,128)S(1)}, f32[1024,64]{0,1:T(8,128)S(1)}, u32[]{:S(2)}, u32[]{:S(2)}) collective-permute-start(f32[1024,64]{0,1:T(8,128)S(1)} %fusion.43), channel_id=1, source_target_pairs={{24,20},{25,21},{26,22},{27,23}} | collective-permute-start | bytes 786440 | tf_op jit(solution)/shard_map/ppermute | solution.py:50
  102.4 3.6 %collective-permute-start.15 = (f32[1024,64]{0,1:T(8,128)S(1)}, f32[1024,64]{0,1:T(8,128)S(1)}, u32[]{:S(2)}, u32[]{:S(2)}) collective-permute-start(f32[1024,64]{0,1:T(8,128)S(1)} %fusion.35), channel_id=1, source_target_pairs={{20,16},{21,17},{22,18},{23,19}} | collective-permute-start | bytes 786440 | tf_op jit(solution)/shard_map/ppermute | solution.py:50
  105.2 3.6 %collective-permute-start.8 = (f32[1024,64]{0,1:T(8,128)S(1)}, f32[1024,64]{0,1:T(8,128)S(1)}, u32[]{:S(2)}, u32[]{:S(2)}) collective-permute-start(f32[1024,64]{0,1:T(8,128)S(1)} %fusion.34), channel_id=1, source_target_pairs={{20,16},{21,17},{22,18},{23,19}} | collective-permute-start | bytes 786440 | tf_op jit(solution)/shard_map/ppermute | solution.py:50
  108.1 3.5 %collective-permute-start.16 = (f32[1024,64]{0,1:T(8,128)S(1)}, f32[1024,64]{0,1:T(8,128)S(1)}, u32[]{:S(2)}, u32[]{:S(2)}) collective-permute-start(f32[1024,64]{0,1:T(8,128)S(1)} %fusion.47), channel_id=1, source_target_pairs={{16,12},{17,13},{18,14},{19,15}} | collective-permute-start | bytes 786440 | tf_op jit(solution)/shard_map/ppermute | solution.py:50
  110.9 3.4 %collective-permute-start.9 = (f32[1024,64]{0,1:T(8,128)S(1)}, f32[1024,64]{0,1:T(8,128)S(1)}, u32[]{:S(2)}, u32[]{:S(2)}) collective-permute-start(f32[1024,64]{0,1:T(8,128)S(1)} %fusion.44), channel_id=1, source_target_pairs={{16,12},{17,13},{18,14},{19,15}} | collective-permute-start | bytes 786440 | tf_op jit(solution)/shard_map/ppermute | solution.py:50
  113.6 3.4 %collective-permute-start.17 = (f32[1024,64]{0,1:T(8,128)S(1)}, f32[1024,64]{0,1:T(8,128)S(1)}, u32[]{:S(2)}, u32[]{:S(2)}) collective-permute-start(f32[1024,64]{0,1:T(8,128)S(1)} %fusion.33), channel_id=1, source_target_pairs={{12,8},{13,9},{14,10},{15,11}} | collective-permute-start | bytes 786440 | tf_op jit(solution)/shard_map/ppermute | solution.py:50
  116.3 3.5 %collective-permute-start.10 = (f32[1024,64]{0,1:T(8,128)S(1)}, f32[1024,64]{0,1:T(8,128)S(1)}, u32[]{:S(2)}, u32[]{:S(2)}) collective-permute-start(f32[1024,64]{0,1:T(8,128)S(1)} %fusion.32), channel_id=1, source_target_pairs={{12,8},{13,9},{14,10},{15,11}} | collective-permute-start | bytes 786440 | tf_op jit(solution)/shard_map/ppermute | solution.py:50
  119.1 3.5 %collective-permute-start.18 = (f32[1024,64]{0,1:T(8,128)S(1)}, f32[1024,64]{0,1:T(8,128)S(1)}, u32[]{:S(2)}, u32[]{:S(2)}) collective-permute-start(f32[1024,64]{0,1:T(8,128)S(1)} %fusion.48), channel_id=1, source_target_pairs={{8,4},{9,5},{10,6},{11,7}} | collective-permute-start | bytes 786440 | tf_op jit(solution)/shard_map/ppermute | solution.py:50
  121.9 4.2 %collective-permute-start.11 = (f32[1024,64]{0,1:T(8,128)S(1)}, f32[1024,64]{0,1:T(8,128)S(1)}, u32[]{:S(2)}, u32[]{:S(2)}) collective-permute-start(f32[1024,64]{0,1:T(8,128)S(1)} %fusion.45), channel_id=1, source_target_pairs={{8,4},{9,5},{10,6},{11,7}} | collective-permute-start | bytes 786440 | tf_op jit(solution)/shard_map/ppermute | solution.py:50
  124.6 13.4 %collective-permute-start.19 = (f32[1024,64]{0,1:T(8,128)S(1)}, f32[1024,64]{0,1:T(8,128)S(1)}, u32[]{:S(2)}, u32[]{:S(2)}) collective-permute-start(f32[1024,64]{0,1:T(8,128)S(1)} %fusion.31), channel_id=1, source_target_pairs={{4,0},{5,1},{6,2},{7,3}} | collective-permute-start | bytes 786440 | tf_op jit(solution)/shard_map/ppermute | solution.py:50
  128.2 13.4 %collective-permute-start.12 = (f32[1024,64]{0,1:T(8,128)S(1)}, f32[1024,64]{0,1:T(8,128)S(1)}, u32[]{:S(2)}, u32[]{:S(2)}) collective-permute-start(f32[1024,64]{0,1:T(8,128)S(1)} %fusion.30), channel_id=1, source_target_pairs={{4,0},{5,1},{6,2},{7,3}} | collective-permute-start | bytes 786440 | tf_op jit(solution)/shard_map/ppermute | solution.py:50
  144.8 10.8 %collective-permute-start.22 = (f32[512,128]{0,1:T(8,128)S(1)}, f32[512,128]{0,1:T(8,128)S(1)}, u32[]{:S(2)}, u32[]{:S(2)}) collective-permute-start(f32[512,128]{0,1:T(8,128)S(1)} %pad_maximum_fusion.4), channel_id=1, source_target_pairs={{0,1},{1,2},{2,3},{3,0},{4,5},{5,6},{6,7},{7,4},{8,9},{9,10},{10,1... | collective-permute-start | bytes 786440 | tf_op jit(solution)/shard_map/ppermute | solution.py:62
  144.9 22.2 %collective-permute-start.21 = (f32[512,128]{0,1:T(8,128)S(1)}, f32[512,128]{0,1:T(8,128)S(1)}, u32[]{:S(2)}, u32[]{:S(2)}) collective-permute-start(f32[512,128]{0,1:T(8,128)S(1)} %pad_maximum_fusion.3), channel_id=1, source_target_pairs={{0,2},{1,3},{2,0},{3,1},{4,6},{5,7},{6,4},{7,5},{8,10},{9,11},{10,... | collective-permute-start | bytes 786440 | tf_op jit(solution)/shard_map/ppermute | solution.py:62
  149.4 17.7 %collective-permute-start.20 = (f32[512,128]{0,1:T(8,128)S(1)}, f32[512,128]{0,1:T(8,128)S(1)}, u32[]{:S(2)}, u32[]{:S(2)}) collective-permute-start(f32[512,128]{0,1:T(8,128)S(1)} %pad_maximum_fusion.2), channel_id=1, source_target_pairs={{0,3},{1,0},{2,1},{3,2},{4,7},{5,4},{6,5},{7,6},{8,11},{9,8},{10,9... | collective-permute-start | bytes 786440 | tf_op jit(solution)/shard_map/ppermute | solution.py:62
  174.0 8.0 %collective-permute-start.23 = (f32[512]{0:T(512)S(1)}, f32[512]{0:T(512)S(1)}, u32[]{:S(2)}, u32[]{:S(2)}) collective-permute-start(f32[512]{0:T(512)S(1)} %dynamic_slice.40), channel_id=1, source_target_pairs={{0,1},{1,2},{2,3},{3,0},{4,5},{5,6},{6,7},{7,4},{8,9},{9,10},{10,1... | collective-permute-start | bytes 6152 | tf_op jit(solution)/shard_map/ppermute | solution.py:83
  (6 other events, 88.9 us)

commit v9 on v8

--- a/solution.py
+++ b/solution.py
@@ -33,7 +33,12 @@
     state_dim = terminal_cost.shape[1]
     width = state_dim // count
 
-    whole_map = lax.optimization_barrier(line_gather(section_maps[0], place, count))
+    local = section_maps[0]
+    cut = local.shape[0] // 2
+    upper = line_gather(local[:cut], place, count).reshape(count, cut, local.shape[1])
+    lower = line_gather(local[cut:], place, count).reshape(count, cut, local.shape[1])
+    whole_map = jnp.concatenate([upper, lower], axis=1).reshape(count * local.shape[0], local.shape[1])
+    whole_map = lax.optimization_barrier(whole_map)
     rows_id = lax.broadcasted_iota(jnp.int32, (state_dim, width), 0)
     cols_id = lax.broadcasted_iota(jnp.int32, (state_dim, width), 1) + place * width
     identity_cols = (rows_id == cols_id).astype(jnp.float32)
@@ -77,10 +82,15 @@
     partial = jnp.sum(rows_traj * pair_traj, axis=0)
     cols = terminal_states.shape[1] // count
     total = lax.dynamic_slice_in_dim(partial, place * cols, cols, 0)
-    for e in range(1, half):
-        target = (place + e) % count
-        sent = lax.dynamic_slice_in_dim(partial, target * cols, cols, 0)
-        total = total + lax.ppermute(sent, "row", [(z, (z + e) % count) for z in range(count)])
+    if half == 2:
+        partner = [(z, z ^ 1) for z in range(count)]
+        sent = lax.dynamic_slice_in_dim(partial, (place ^ 1) * cols, cols, 0)
+        total = total + lax.ppermute(sent, "row", partner)
+    else:
+        for e in range(1, half):
+            target = (place + e) % count
+            sent = lax.dynamic_slice_in_dim(partial, target * cols, cols, 0)
+            total = total + lax.ppermute(sent, "row", [(z, (z + e) % count) for z in range(count)])
     section_cost = total / state_dim
     return (rows_traj[None], section_cost[None])
 

time: 183 us -> 179 us (0.978)
  waiting for transfers between devices: 96.5 us -> 81.8 us
  starting transfers between devices: 34.5 us -> 42.8 us
    ppermute x3 -> x6, waiting for transfers between devices: 46 us -> 38.3 us  [line_gather(): lax.ppermute(leftward, 'row', [(z, z - 1) for z in range(1, count - t + 1)])]
    ppermute x3 -> x6, waiting for transfers between devices: 21.4 us -> 14.8 us  [line_gather(): lax.ppermute(rightward, 'row', [(z, z + 1) for z in range(t - 1, count -...]
    ppermute x3 -> x6, starting transfers between devices: 8.44 us -> 13.5 us  [line_gather(): lax.ppermute(rightward, 'row', [(z, z + 1) for z in range(t - 1, count -...]
    ppermute x3 -> x6, starting transfers between devices: 3.85 us -> 7.71 us  [line_gather(): lax.ppermute(leftward, 'row', [(z, z - 1) for z in range(1, count - t + 1)])]
    unnamed x21 -> x26, local copies, waits for them, and re-layouts: 4.63 us -> 6.11 us
  transfers between devices with their start and end apart: 24 -> 30, of which waited for: 9 -> 12; matrix products, arithmetic and copies ran while one was open for 16% -> 17% of each run, Pallas kernels for 0% -> 0%
where the time goes in v9:
time: 179 us; the launch traced here: 178 us
  waiting for transfers between devices  81.8 us (46%)
  starting transfers between devices  42.8 us (24%)
  matrix products  41.5 us (23%)
  local copies, waits for them, and re-layouts  8.99 us (5%)
  other arithmetic  1.85 us (1%)
    dot_general x18, matrix products, product(): jnp.dot(left, right, precision=lax.Precision.HIGH, preferred_element_type...  41.5 us
    ppermute x6, waiting for transfers between devices, line_gather(): lax.ppermute(leftward, 'row', [(z, z - 1) for z in range(1, count - t + 1)])  38.3 us
    ppermute x3, waiting for transfers between devices, body(): lax.ppermute(payload, 'row', [(z, (z + d) % count) for z in range(count)])  17 us
    ppermute x6, waiting for transfers between devices, line_gather(): lax.ppermute(rightward, 'row', [(z, z + 1) for z in range(t - 1, count -...  14.8 us
    ppermute x6, starting transfers between devices, line_gather(): lax.ppermute(rightward, 'row', [(z, z + 1) for z in range(t - 1, count -...  13.5 us
    ppermute x14, starting transfers between devices, body(): got = lax.ppermute(fresh, 'tm', [(k, k - 1)])  11.1 us
    ppermute x14, waiting for transfers between devices, body(): got = lax.ppermute(fresh, 'tm', [(k, k - 1)])  10 us
    ppermute x6, starting transfers between devices, line_gather(): lax.ppermute(leftward, 'row', [(z, z - 1) for z in range(1, count - t + 1)])  7.71 us
  transfers between devices with their start and end apart: 30, of which 12 were waited for; matrix products, arithmetic and copies ran while one was open for 17% of the time, Pallas kernels for 0%

profile of v9, /device:TPU:0, one launch (start us, length us, event | category | flops | bytes accessed | tf_op | source)
XLA Modules:
  0.0 178.3 jit_solution(8773243251849733108)
XLA Ops:
  2.0 5.0 %collective-permute-start = (f32[128,1024]{1,0:T(8,128)S(1)}, f32[128,1024]{1,0:T(8,128)S(1)}, u32[]{:S(2)}, u32[]{:S(2)}) collective-permute-start(f32[128,1024]{1,0:T(8,128)S(1)} %get-tuple-element.4), channel_id=1, source_target_pairs={{0,1},{1,2},{2,3},{4,5},{5,6},{6,7},{8,9},{9,10},{10,11},{12,13},{... | collective-permute-start | bytes 1572872 | tf_op jit(solution)/shard_map/ppermute | solution.py:19
  7.0 3.5 %collective-permute-start.6 = (f32[128,1024]{1,0:T(8,128)S(1)}, f32[128,1024]{1,0:T(8,128)S(1)}, u32[]{:S(2)}, u32[]{:S(2)}) collective-permute-start(f32[128,1024]{1,0:T(8,128)S(1)} %get-tuple-element.5), channel_id=1, source_target_pairs={{0,1},{1,2},{2,3},{4,5},{5,6},{6,7},{8,9},{9,10},{10,11},{12,13},{... | collective-permute-start | bytes 1572872 | tf_op jit(solution)/shard_map/ppermute | solution.py:19
  13.1 6.2 %collective-permute-done = f32[128,1024]{1,0:T(8,128)S(1)} collective-permute-done((f32[128,1024]{1,0:T(8,128)S(1)}, f32[128,1024]{1,0:T(8,128)S(1)}, u32[]{:S(2)}, u32[]{:S(2)}) %collective-permute-start) | collective-permute-done | bytes 524320 | tf_op jit(solution)/shard_map/ppermute | solution.py:19
  20.7 8.7 %collective-permute-done.6 = f32[128,1024]{1,0:T(8,128)S(1)} collective-permute-done((f32[128,1024]{1,0:T(8,128)S(1)}, f32[128,1024]{1,0:T(8,128)S(1)}, u32[]{:S(2)}, u32[]{:S(2)}) %collective-permute-start.6) | collective-permute-done | bytes 524320 | tf_op jit(solution)/shard_map/ppermute | solution.py:19
  32.2 4.6 %collective-permute-done.3 = f32[128,1024]{1,0:T(8,128)S(1)} collective-permute-done((f32[128,1024]{1,0:T(8,128)S(1)}, f32[128,1024]{1,0:T(8,128)S(1)}, u32[]{:S(2)}, u32[]{:S(2)}) %collective-permute-start.3) | collective-permute-done | bytes 524320 | tf_op jit(solution)/shard_map/ppermute | solution.py:20
  40.3 11.8 %collective-permute-done.10 = f32[128,1024]{1,0:T(8,128)} collective-permute-done((f32[128,1024]{1,0:T(8,128)S(1)}, f32[128,1024]{1,0:T(8,128)}, u32[]{:S(2)}, u32[]{:S(2)}) %collective-permute-start.10) | collective-permute-done | bytes 524320 | tf_op jit(solution)/shard_map/ppermute | solution.py:20
  53.4 9.9 %collective-permute-done.4 = f32[128,1024]{1,0:T(8,128)} collective-permute-done((f32[128,1024]{1,0:T(8,128)S(1)}, f32[128,1024]{1,0:T(8,128)}, u32[]{:S(2)}, u32[]{:S(2)}) %collective-permute-start.4) | collective-permute-done | bytes 524320 | tf_op jit(solution)/shard_map/ppermute | solution.py:20
  70.4 4.1 %collective-permute-done.11 = f32[128,1024]{1,0:T(8,128)S(1)} collective-permute-done((f32[128,1024]{1,0:T(8,128)}, f32[128,1024]{1,0:T(8,128)S(1)}, u32[]{:S(2)}, u32[]{:S(2)}) %collective-permute-start.11) | collective-permute-done | bytes 524320 | tf_op jit(solution)/shard_map/ppermute | solution.py:20
  74.6 7.9 %collective-permute-done.5 = f32[128,1024]{1,0:T(8,128)S(1)} collective-permute-done((f32[128,1024]{1,0:T(8,128)}, f32[128,1024]{1,0:T(8,128)S(1)}, u32[]{:S(2)}, u32[]{:S(2)}) %collective-permute-start.5) | collective-permute-done | bytes 524320 | tf_op jit(solution)/shard_map/ppermute | solution.py:20
  89.4 4.4 %fusion.46 = f32[1024,64]{0,1:T(8,128)S(1)} fusion(f32[1024,1024]{1,0:T(8,128)} %bitcast.83, f32[1024,64]{0,1:T(8,128)S(1)} %get-tuple-element.22), kind=kOutput, calls=%fused_computation.110 | convolution fusion | flops 402653184 | bytes 4718592 | tf_op jit(solution)/shard_map/dot_general | solution.py:10
  94.4 2.0 %fusion.43 = f32[1024,64]{0,1:T(8,128)S(1)} fusion(f32[1024,1024]{1,0:T(8,128)S(1)} %bitcast.84, f32[1024,64]{0,1:T(8,128)S(1)} %get-tuple-element.21), kind=kOutput, calls=%fused_computation.107 | convolution fusion | flops 402653184 | bytes 4718592 | tf_op jit(solution)/shard_map/dot_general | solution.py:10
  97.2 2.0 %fusion.35 = f32[1024,64]{0,1:T(8,128)S(1)} fusion(f32[1024,1024]{1,0:T(8,128)S(1)} %bitcast.85, f32[1024,64]{0,1:T(8,128)S(1)} %collective-permute-done.20, f32[1024,64]{0,1:T(8,128)S(1)} %get-tuple-element.22, pred[]{:T(512)S(6)} %eq.131), kind=kOutput, calls=%fused_computation.75 | convolution fusion | flops 402718720 | bytes 4980737 | tf_op jit(solution)/shard_map/dot_general | solution.py:10
  105.6 2.0 %fusion.44 = f32[1024,64]{0,1:T(8,128)S(1)} fusion(f32[1024,1024]{1,0:T(8,128)S(1)} %bitcast.88, f32[1024,64]{0,1:T(8,128)S(1)} %broadcast_select_fusion.5), kind=kOutput, calls=%fused_computation.108 | convolution fusion | flops 402653184 | bytes 4718592 | tf_op jit(solution)/shard_map/dot_general | solution.py:10
  108.4 2.0 %fusion.33 = f32[1024,64]{0,1:T(8,128)S(1)} fusion(f32[1024,1024]{1,0:T(8,128)S(1)} %bitcast.89, f32[1024,64]{0,1:T(8,128)S(1)} %collective-permute-done.22, f32[1024,64]{0,1:T(8,128)S(1)} %broadcast_select_fusion.4, pred[]{:T(512)S(6)} %eq.129), kind=kOutput, calls=%fused_computation.73 | convolution fusion | flops 402718720 | bytes 4980737 | tf_op jit(solution)/shard_map/dot_general | solution.py:10
  111.1 2.0 %fusion.32 = f32[1024,64]{0,1:T(8,128)S(1)} fusion(f32[1024,1024]{1,0:T(8,128)S(1)} %bitcast.90, f32[1024,64]{0,1:T(8,128)S(1)} %collective-permute-done.15, f32[1024,64]{0,1:T(8,128)S(1)} %broadcast_select_fusion.5, pred[]{:T(512)S(6)} %eq.129), kind=kOutput, calls=%fused_computation.72 | convolution fusion | flops 402718720 | bytes 4980737 | tf_op jit(solution)/shard_map/dot_general | solution.py:10
  126.3 8.5 %collective-permute-done.25 = f32[1024,64]{0,1:T(8,128)S(1)} collective-permute-done((f32[1024,64]{0,1:T(8,128)S(1)}, f32[1024,64]{0,1:T(8,128)S(1)}, u32[]{:S(2)}, u32[]{:S(2)}) %collective-permute-start.25) | collective-permute-done | bytes 262176 | tf_op jit(solution)/shard_map/ppermute | solution.py:55
  134.8 2.0 %convolution_select_fusion = f32[1024,64]{0,1:T(8,128)S(1)} fusion(f32[1024,1024]{1,0:T(8,128)S(1)} %bitcast.95, f32[1024,64]{0,1:T(8,128)S(1)} %fusion.31, f32[1024,64]{0,1:T(8,128)S(1)} %fusion.48, f32[1024,64]{0,1:T(8,128)S(1)} %fusion.33, f32[1024,64]{0,1:T(8,128)S(1)} %fusion.47, f32[1024,64]{0,1:T(8,128)S(1)} %fusion.35, f32[1024,64]{0,1:T(8,128)S(1)} %fusion.46, ...), kind=kOutput, calls=%fused_computation.3 | convolution fusion | flops 403243008 | bytes 7077895 | tf_op jit(solution)/shard_map/dot_general | solution.py:10
  138.3 2.0 %convolution_select_fusion.1 = f32[1024,64]{0,1:T(8,128)S(1)} fusion(f32[1024,1024]{1,0:T(8,128)S(1)} %bitcast.96, f32[1024,64]{0,1:T(8,128)S(1)} %fusion.30, f32[1024,64]{0,1:T(8,128)S(1)} %fusion.45, f32[1024,64]{0,1:T(8,128)S(1)} %fusion.32, f32[1024,64]{0,1:T(8,128)S(1)} %fusion.44, f32[1024,64]{0,1:T(8,128)S(1)} %fusion.34, f32[1024,64]{0,1:T(8,128)S(1)} %fusion.43, ...), kind=kOutput, calls=%fused_computation.4 | convolution fusion | flops 403243008 | bytes 7077895 | tf_op jit(solution)/shard_map/dot_general | solution.py:10
  142.4 3.5 %collective-permute-start.26 = (f32[512,128]{0,1:T(8,128)S(1)}, f32[512,128]{0,1:T(8,128)S(1)}, u32[]{:S(2)}, u32[]{:S(2)}) collective-permute-start(f32[512,128]{0,1:T(8,128)S(1)} %pad_maximum_fusion.3), channel_id=1, source_target_pairs={{0,3},{1,0},{2,1},{3,2},{4,7},{5,4},{6,5},{7,6},{8,11},{9,8},{10,9... | collective-permute-start | bytes 786440 | tf_op jit(solution)/shard_map/ppermute | solution.py:67
  145.9 6.7 %collective-permute-done.28 = f32[512,128]{0,1:T(8,128)S(1)} collective-permute-done((f32[512,128]{0,1:T(8,128)S(1)}, f32[512,128]{0,1:T(8,128)S(1)}, u32[]{:S(2)}, u32[]{:S(2)}) %collective-permute-start.28) | collective-permute-done | bytes 262176 | tf_op jit(solution)/shard_map/ppermute | solution.py:67
  152.6 10.3 %collective-permute-done.27 = f32[512,128]{0,1:T(8,128)S(1)} collective-permute-done((f32[512,128]{0,1:T(8,128)S(1)}, f32[512,128]{0,1:T(8,128)S(1)}, u32[]{:S(2)}, u32[]{:S(2)}) %collective-permute-start.27) | collective-permute-done | bytes 262176 | tf_op jit(solution)/shard_map/ppermute | solution.py:67
  163.1 4.3 %fusion.1 = f32[256,2048]{1,0:T(8,128)S(1)} fusion(f32[512,2048]{1,0:T(8,128)} %param.5, f32[256,128]{0,1:T(8,128)S(1)} %get-tuple-element.13, f32[256,128]{0,1:T(8,128)S(1)} %get-tuple-element.11, f32[256,128]{0,1:T(8,128)S(1)} %get-tuple-element.10, f32[256,128]{0,1:T(8,128)S(1)} %get-tuple-element.9), kind=kOutput, calls=%fused_computation.8 | convolution fusion | flops 1611005952 | bytes 6815744 | tf_op jit(solution)/shard_map/dot_general | solution.py:10
  167.6 2.2 %fusion = f32[2048]{0:T(1024)S(1)} fusion(f32[256,2048]{1,0:T(8,128)S(1)} %fusion.1, f32[512,2048]{1,0:T(8,128)S(1)} %copy-done.2, f32[256,128]{0,1:T(8,128)S(1)} %get-tuple-element.12, f32[256,128]{0,1:T(8,128)S(1)} %get-tuple-element.8, f32[256,128]{0,1:T(8,128)S(1)} %get-tuple-element.7, f32[256,128]{0,1:T(8,128)S(1)} %get-tuple-element.6), kind=kOutput, calls=%fused_computation.2 | convolution fusion | flops 1612052480 | bytes 6823936 | tf_op jit(solution)/shard_map/dot_general | solution.py:10
  169.9 6.2 %collective-permute-start.29 = (f32[512]{0:T(512)S(1)}, f32[512]{0:T(512)S(1)}, u32[]{:S(2)}, u32[]{:S(2)}) collective-permute-start(f32[512]{0:T(512)S(1)} %dynamic_slice.44), channel_id=1, source_target_pairs={{0,1},{1,0},{2,3},{3,2},{4,5},{5,4},{6,7},{7,6},{8,9},{9,8},{10,11... | collective-permute-start | bytes 6152 | tf_op jit(solution)/shard_map/ppermute | solution.py:88
  (104 shorter events, 54.7 us)
Async XLA Ops:
  2.0 17.3 %collective-permute-start = (f32[128,1024]{1,0:T(8,128)S(1)}, f32[128,1024]{1,0:T(8,128)S(1)}, u32[]{:S(2)}, u32[]{:S(2)}) collective-permute-start(f32[128,1024]{1,0:T(8,128)S(1)} %get-tuple-element.4), channel_id=1, source_target_pairs={{0,1},{1,2},{2,3},{4,5},{5,6},{6,7},{8,9},{9,10},{10,11},{12,13},{... | collective-permute-start | bytes 1572872 | tf_op jit(solution)/shard_map/ppermute | solution.py:19
  7.0 22.4 %collective-permute-start.6 = (f32[128,1024]{1,0:T(8,128)S(1)}, f32[128,1024]{1,0:T(8,128)S(1)}, u32[]{:S(2)}, u32[]{:S(2)}) collective-permute-start(f32[128,1024]{1,0:T(8,128)S(1)} %get-tuple-element.5), channel_id=1, source_target_pairs={{0,1},{1,2},{2,3},{4,5},{5,6},{6,7},{8,9},{9,10},{10,11},{12,13},{... | collective-permute-start | bytes 1572872 | tf_op jit(solution)/shard_map/ppermute | solution.py:19
  10.5 20.4 %collective-permute-start.9 = (f32[128,1024]{1,0:T(8,128)S(1)}, f32[128,1024]{1,0:T(8,128)S(1)}, u32[]{:S(2)}, u32[]{:S(2)}) collective-permute-start(f32[128,1024]{1,0:T(8,128)S(1)} %get-tuple-element.5), channel_id=1, source_target_pairs={{1,0},{2,1},{3,2},{5,4},{6,5},{7,6},{9,8},{10,9},{11,10},{13,12},{... | collective-permute-start | bytes 1572872 | tf_op jit(solution)/shard_map/ppermute | solution.py:20
  11.8 24.9 %collective-permute-start.3 = (f32[128,1024]{1,0:T(8,128)S(1)}, f32[128,1024]{1,0:T(8,128)S(1)}, u32[]{:S(2)}, u32[]{:S(2)}) collective-permute-start(f32[128,1024]{1,0:T(8,128)S(1)} %get-tuple-element.4), channel_id=1, source_target_pairs={{1,0},{2,1},{3,2},{5,4},{6,5},{7,6},{9,8},{10,9},{11,10},{13,12},{... | collective-permute-start | bytes 1572872 | tf_op jit(solution)/shard_map/ppermute | solution.py:20
  19.3 18.8 %collective-permute-start.1 = (f32[128,1024]{1,0:T(8,128)S(1)}, f32[128,1024]{1,0:T(8,128)}, u32[]{:S(2)}, u32[]{:S(2)}) collective-permute-start(f32[128,1024]{1,0:T(8,128)S(1)} %collective-permute-done), channel_id=1, source_target_pairs={{1,2},{2,3},{5,6},{6,7},{9,10},{10,11},{13,14},{14,15},{17,18},{18... | collective-permute-start | bytes 1572872 | tf_op jit(solution)/shard_map/ppermute | solution.py:19
  29.4 10.1 %collective-permute-start.7 = (f32[128,1024]{1,0:T(8,128)S(1)}, f32[128,1024]{1,0:T(8,128)}, u32[]{:S(2)}, u32[]{:S(2)}) collective-permute-start(f32[128,1024]{1,0:T(8,128)S(1)} %collective-permute-done.6), channel_id=1, source_target_pairs={{1,2},{2,3},{5,6},{6,7},{9,10},{10,11},{13,14},{14,15},{17,18},{18... | collective-permute-start | bytes 1572872 | tf_op jit(solution)/shard_map/ppermute | solution.py:19
  30.9 21.2 %collective-permute-start.10 = (f32[128,1024]{1,0:T(8,128)S(1)}, f32[128,1024]{1,0:T(8,128)}, u32[]{:S(2)}, u32[]{:S(2)}) collective-permute-start(f32[128,1024]{1,0:T(8,128)S(1)} %collective-permute-done.9), channel_id=1, source_target_pairs={{1,0},{2,1},{5,4},{6,5},{9,8},{10,9},{13,12},{14,13},{17,16},{18,1... | collective-permute-start | bytes 1572872 | tf_op jit(solution)/shard_map/ppermute | solution.py:20
  36.8 26.6 %collective-permute-start.4 = (f32[128,1024]{1,0:T(8,128)S(1)}, f32[128,1024]{1,0:T(8,128)}, u32[]{:S(2)}, u32[]{:S(2)}) collective-permute-start(f32[128,1024]{1,0:T(8,128)S(1)} %collective-permute-done.3), channel_id=1, source_target_pairs={{1,0},{2,1},{5,4},{6,5},{9,8},{10,9},{13,12},{14,13},{17,16},{18,1... | collective-permute-start | bytes 1572872 | tf_op jit(solution)/shard_map/ppermute | solution.py:20
  38.1 26.5 %collective-permute-start.2 = (f32[128,1024]{1,0:T(8,128)}, f32[128,1024]{1,0:T(8,128)}, u32[]{:S(2)}, u32[]{:S(2)}) collective-permute-start(f32[128,1024]{1,0:T(8,128)} %collective-permute-done.1), channel_id=1, source_target_pairs={{2,3},{6,7},{10,11},{14,15},{18,19},{22,23},{26,27},{30,31}} | collective-permute-start | bytes 1572872 | tf_op jit(solution)/shard_map/ppermute | solution.py:19
  39.5 27.3 %collective-permute-start.8 = (f32[128,1024]{1,0:T(8,128)}, f32[128,1024]{1,0:T(8,128)S(1)}, u32[]{:S(2)}, u32[]{:S(2)}) collective-permute-start(f32[128,1024]{1,0:T(8,128)} %collective-permute-done.7), channel_id=1, source_target_pairs={{2,3},{6,7},{10,11},{14,15},{18,19},{22,23},{26,27},{30,31}} | collective-permute-start | bytes 1572872 | tf_op jit(solution)/shard_map/ppermute | solution.py:19
  52.1 22.4 %collective-permute-start.11 = (f32[128,1024]{1,0:T(8,128)}, f32[128,1024]{1,0:T(8,128)S(1)}, u32[]{:S(2)}, u32[]{:S(2)}) collective-permute-start(f32[128,1024]{1,0:T(8,128)} %collective-permute-done.10), channel_id=1, source_target_pairs={{1,0},{5,4},{9,8},{13,12},{17,16},{21,20},{25,24},{29,28}} | collective-permute-start | bytes 1572872 | tf_op jit(solution)/shard_map/ppermute | solution.py:20
  63.3 19.2 %collective-permute-start.5 = (f32[128,1024]{1,0:T(8,128)}, f32[128,1024]{1,0:T(8,128)S(1)}, u32[]{:S(2)}, u32[]{:S(2)}) collective-permute-start(f32[128,1024]{1,0:T(8,128)} %collective-permute-done.4), channel_id=1, source_target_pairs={{1,0},{5,4},{9,8},{13,12},{17,16},{21,20},{25,24},{29,28}} | collective-permute-start | bytes 1572872 | tf_op jit(solution)/shard_map/ppermute | solution.py:20
  96.5 3.6 %collective-permute-start.13 = (f32[1024,64]{0,1:T(8,128)S(1)}, f32[1024,64]{0,1:T(8,128)S(1)}, u32[]{:S(2)}, u32[]{:S(2)}) collective-permute-start(f32[1024,64]{0,1:T(8,128)S(1)} %fusion.43), channel_id=1, source_target_pairs={{24,20},{25,21},{26,22},{27,23}} | collective-permute-start | bytes 786440 | tf_op jit(solution)/shard_map/ppermute | solution.py:55
  99.2 3.6 %collective-permute-start.21 = (f32[1024,64]{0,1:T(8,128)S(1)}, f32[1024,64]{0,1:T(8,128)S(1)}, u32[]{:S(2)}, u32[]{:S(2)}) collective-permute-start(f32[1024,64]{0,1:T(8,128)S(1)} %fusion.35), channel_id=1, source_target_pairs={{20,16},{21,17},{22,18},{23,19}} | collective-permute-start | bytes 786440 | tf_op jit(solution)/shard_map/ppermute | solution.py:55
  104.9 3.5 %collective-permute-start.22 = (f32[1024,64]{0,1:T(8,128)S(1)}, f32[1024,64]{0,1:T(8,128)S(1)}, u32[]{:S(2)}, u32[]{:S(2)}) collective-permute-start(f32[1024,64]{0,1:T(8,128)S(1)} %fusion.47), channel_id=1, source_target_pairs={{16,12},{17,13},{18,14},{19,15}} | collective-permute-start | bytes 786440 | tf_op jit(solution)/shard_map/ppermute | solution.py:55
  113.1 3.5 %collective-permute-start.16 = (f32[1024,64]{0,1:T(8,128)S(1)}, f32[1024,64]{0,1:T(8,128)S(1)}, u32[]{:S(2)}, u32[]{:S(2)}) collective-permute-start(f32[1024,64]{0,1:T(8,128)S(1)} %fusion.32), channel_id=1, source_target_pairs={{12,8},{13,9},{14,10},{15,11}} | collective-permute-start | bytes 786440 | tf_op jit(solution)/shard_map/ppermute | solution.py:55
  115.9 3.7 %collective-permute-start.24 = (f32[1024,64]{0,1:T(8,128)S(1)}, f32[1024,64]{0,1:T(8,128)S(1)}, u32[]{:S(2)}, u32[]{:S(2)}) collective-permute-start(f32[1024,64]{0,1:T(8,128)S(1)} %fusion.48), channel_id=1, source_target_pairs={{8,4},{9,5},{10,6},{11,7}} | collective-permute-start | bytes 786440 | tf_op jit(solution)/shard_map/ppermute | solution.py:55
  118.7 4.2 %collective-permute-start.17 = (f32[1024,64]{0,1:T(8,128)S(1)}, f32[1024,64]{0,1:T(8,128)S(1)}, u32[]{:S(2)}, u32[]{:S(2)}) collective-permute-start(f32[1024,64]{0,1:T(8,128)S(1)} %fusion.45), channel_id=1, source_target_pairs={{8,4},{9,5},{10,6},{11,7}} | collective-permute-start | bytes 786440 | tf_op jit(solution)/shard_map/ppermute | solution.py:55
  121.6 13.2 %collective-permute-start.25 = (f32[1024,64]{0,1:T(8,128)S(1)}, f32[1024,64]{0,1:T(8,128)S(1)}, u32[]{:S(2)}, u32[]{:S(2)}) collective-permute-start(f32[1024,64]{0,1:T(8,128)S(1)} %fusion.31), channel_id=1, source_target_pairs={{4,0},{5,1},{6,2},{7,3}} | collective-permute-start | bytes 786440 | tf_op jit(solution)/shard_map/ppermute | solution.py:55
  125.0 13.4 %collective-permute-start.18 = (f32[1024,64]{0,1:T(8,128)S(1)}, f32[1024,64]{0,1:T(8,128)S(1)}, u32[]{:S(2)}, u32[]{:S(2)}) collective-permute-start(f32[1024,64]{0,1:T(8,128)S(1)} %fusion.30), channel_id=1, source_target_pairs={{4,0},{5,1},{6,2},{7,3}} | collective-permute-start | bytes 786440 | tf_op jit(solution)/shard_map/ppermute | solution.py:55
  141.5 11.1 %collective-permute-start.28 = (f32[512,128]{0,1:T(8,128)S(1)}, f32[512,128]{0,1:T(8,128)S(1)}, u32[]{:S(2)}, u32[]{:S(2)}) collective-permute-start(f32[512,128]{0,1:T(8,128)S(1)} %pad_maximum_fusion.5), channel_id=1, source_target_pairs={{0,1},{1,2},{2,3},{3,0},{4,5},{5,6},{6,7},{7,4},{8,9},{9,10},{10,1... | collective-permute-start | bytes 786440 | tf_op jit(solution)/shard_map/ppermute | solution.py:67
  141.7 21.3 %collective-permute-start.27 = (f32[512,128]{0,1:T(8,128)S(1)}, f32[512,128]{0,1:T(8,128)S(1)}, u32[]{:S(2)}, u32[]{:S(2)}) collective-permute-start(f32[512,128]{0,1:T(8,128)S(1)} %pad_maximum_fusion.4), channel_id=1, source_target_pairs={{0,2},{1,3},{2,0},{3,1},{4,6},{5,7},{6,4},{7,5},{8,10},{9,11},{10,... | collective-permute-start | bytes 786440 | tf_op jit(solution)/shard_map/ppermute | solution.py:67
  142.4 20.6 %collective-permute-start.26 = (f32[512,128]{0,1:T(8,128)S(1)}, f32[512,128]{0,1:T(8,128)S(1)}, u32[]{:S(2)}, u32[]{:S(2)}) collective-permute-start(f32[512,128]{0,1:T(8,128)S(1)} %pad_maximum_fusion.3), channel_id=1, source_target_pairs={{0,3},{1,0},{2,1},{3,2},{4,7},{5,4},{6,5},{7,6},{8,11},{9,8},{10,9... | collective-permute-start | bytes 786440 | tf_op jit(solution)/shard_map/ppermute | solution.py:67
  169.9 7.8 %collective-permute-start.29 = (f32[512]{0:T(512)S(1)}, f32[512]{0:T(512)S(1)}, u32[]{:S(2)}, u32[]{:S(2)}) collective-permute-start(f32[512]{0:T(512)S(1)} %dynamic_slice.44), channel_id=1, source_target_pairs={{0,1},{1,0},{2,3},{3,2},{4,5},{5,4},{6,7},{7,6},{8,9},{9,8},{10,11... | collective-permute-start | bytes 6152 | tf_op jit(solution)/shard_map/ppermute | solution.py:88
  (12 other events, 109.3 us)

commit v10 on v9

--- a/solution.py
+++ b/solution.py
@@ -77,20 +77,25 @@
             ordered.append(picked)
         return jnp.concatenate(ordered, axis=1)
 
-    rows_traj = product(in_order(main_pieces), terminal_states)
-    pair_traj = product(in_order(pair_pieces), terminal_states)
-    partial = jnp.sum(rows_traj * pair_traj, axis=0)
+    main_rows = in_order(main_pieces)
+    pair_rows = in_order(pair_pieces)
     cols = terminal_states.shape[1] // count
-    total = lax.dynamic_slice_in_dim(partial, place * cols, cols, 0)
+
+    def partial_for(target):
+        states = lax.dynamic_slice_in_dim(terminal_states, target * cols, cols, 1)
+        return jnp.sum(product(main_rows, states) * product(pair_rows, states), axis=0)
+
     if half == 2:
-        partner = [(z, z ^ 1) for z in range(count)]
-        sent = lax.dynamic_slice_in_dim(partial, (place ^ 1) * cols, cols, 0)
-        total = total + lax.ppermute(sent, "row", partner)
+        sent = partial_for(place ^ 1)
+        got = lax.ppermute(sent, "row", [(z, z ^ 1) for z in range(count)])
+        rows_traj = product(main_rows, terminal_states)
+        total = partial_for(place) + got
     else:
+        rows_traj = product(main_rows, terminal_states)
+        total = partial_for(place)
         for e in range(1, half):
             target = (place + e) % count
-            sent = lax.dynamic_slice_in_dim(partial, target * cols, cols, 0)
-            total = total + lax.ppermute(sent, "row", [(z, (z + e) % count) for z in range(count)])
+            total = total + lax.ppermute(partial_for(target), "row", [(z, (z + e) % count) for z in range(count)])
     section_cost = total / state_dim
     return (rows_traj[None], section_cost[None])
 

time: 179 us -> 179 us (level)
    dot_general x18 -> x21, matrix products: 41.5 us -> 42.3 us  [product(): jnp.dot(left, right, precision=lax.Precision.HIGH, preferred_element_type...]
    unnamed x26 -> x24, local copies, waits for them, and re-layouts: 6.11 us -> 6.11 us
  transfers between devices with their start and end apart: 30 -> 30, of which waited for: 12 -> 12; matrix products, arithmetic and copies ran while one was open for 17% -> 18% of each run, Pallas kernels for 0% -> 0%
where the time goes in v10:
time: 179 us; the launch traced here: 178 us
  waiting for transfers between devices  81.1 us (45%)
  starting transfers between devices  42.8 us (24%)
  matrix products  42.3 us (24%)
  local copies, waits for them, and re-layouts  8.91 us (5%)
    dot_general x21, matrix products, product(): jnp.dot(left, right, precision=lax.Precision.HIGH, preferred_element_type...  42.3 us
    ppermute x6, waiting for transfers between devices, line_gather(): lax.ppermute(leftward, 'row', [(z, z - 1) for z in range(1, count - t + 1)])  38.3 us
    ppermute x3, waiting for transfers between devices, body(): lax.ppermute(payload, 'row', [(z, (z + d) % count) for z in range(count)])  17 us
    ppermute x6, waiting for transfers between devices, line_gather(): lax.ppermute(rightward, 'row', [(z, z + 1) for z in range(t - 1, count -...  14.8 us
    ppermute x6, starting transfers between devices, line_gather(): lax.ppermute(rightward, 'row', [(z, z + 1) for z in range(t - 1, count -...  13.6 us
    ppermute x14, starting transfers between devices, body(): got = lax.ppermute(fresh, 'tm', [(k, k - 1)])  11.1 us
    ppermute x14, waiting for transfers between devices, body(): got = lax.ppermute(fresh, 'tm', [(k, k - 1)])  10.1 us
    ppermute x6, starting transfers between devices, line_gather(): lax.ppermute(leftward, 'row', [(z, z - 1) for z in range(1, count - t + 1)])  7.71 us
  transfers between devices with their start and end apart: 30, of which 12 were waited for; matrix products, arithmetic and copies ran while one was open for 18% of the time, Pallas kernels for 0%

profile of v10, /device:TPU:0, one launch (start us, length us, event | category | flops | bytes accessed | tf_op | source)
XLA Modules:
  0.0 178.3 jit_solution(11404224762817996705)
XLA Ops:
  2.0 5.0 %collective-permute-start = (f32[128,1024]{1,0:T(8,128)S(1)}, f32[128,1024]{1,0:T(8,128)S(1)}, u32[]{:S(2)}, u32[]{:S(2)}) collective-permute-start(f32[128,1024]{1,0:T(8,128)S(1)} %get-tuple-element.4), channel_id=1, source_target_pairs={{0,1},{1,2},{2,3},{4,5},{5,6},{6,7},{8,9},{9,10},{10,11},{12,13},{... | collective-permute-start | bytes 1572872 | tf_op jit(solution)/shard_map/ppermute | solution.py:19
  7.0 3.5 %collective-permute-start.6 = (f32[128,1024]{1,0:T(8,128)S(1)}, f32[128,1024]{1,0:T(8,128)S(1)}, u32[]{:S(2)}, u32[]{:S(2)}) collective-permute-start(f32[128,1024]{1,0:T(8,128)S(1)} %get-tuple-element.5), channel_id=1, source_target_pairs={{0,1},{1,2},{2,3},{4,5},{5,6},{6,7},{8,9},{9,10},{10,11},{12,13},{... | collective-permute-start | bytes 1572872 | tf_op jit(solution)/shard_map/ppermute | solution.py:19
  13.1 6.2 %collective-permute-done = f32[128,1024]{1,0:T(8,128)S(1)} collective-permute-done((f32[128,1024]{1,0:T(8,128)S(1)}, f32[128,1024]{1,0:T(8,128)S(1)}, u32[]{:S(2)}, u32[]{:S(2)}) %collective-permute-start) | collective-permute-done | bytes 524320 | tf_op jit(solution)/shard_map/ppermute | solution.py:19
  20.7 8.7 %collective-permute-done.6 = f32[128,1024]{1,0:T(8,128)S(1)} collective-permute-done((f32[128,1024]{1,0:T(8,128)S(1)}, f32[128,1024]{1,0:T(8,128)S(1)}, u32[]{:S(2)}, u32[]{:S(2)}) %collective-permute-start.6) | collective-permute-done | bytes 524320 | tf_op jit(solution)/shard_map/ppermute | solution.py:19
  32.2 4.6 %collective-permute-done.3 = f32[128,1024]{1,0:T(8,128)S(1)} collective-permute-done((f32[128,1024]{1,0:T(8,128)S(1)}, f32[128,1024]{1,0:T(8,128)S(1)}, u32[]{:S(2)}, u32[]{:S(2)}) %collective-permute-start.3) | collective-permute-done | bytes 524320 | tf_op jit(solution)/shard_map/ppermute | solution.py:20
  40.3 11.8 %collective-permute-done.10 = f32[128,1024]{1,0:T(8,128)} collective-permute-done((f32[128,1024]{1,0:T(8,128)S(1)}, f32[128,1024]{1,0:T(8,128)}, u32[]{:S(2)}, u32[]{:S(2)}) %collective-permute-start.10) | collective-permute-done | bytes 524320 | tf_op jit(solution)/shard_map/ppermute | solution.py:20
  53.4 9.9 %collective-permute-done.4 = f32[128,1024]{1,0:T(8,128)} collective-permute-done((f32[128,1024]{1,0:T(8,128)S(1)}, f32[128,1024]{1,0:T(8,128)}, u32[]{:S(2)}, u32[]{:S(2)}) %collective-permute-start.4) | collective-permute-done | bytes 524320 | tf_op jit(solution)/shard_map/ppermute | solution.py:20
  70.4 4.1 %collective-permute-done.11 = f32[128,1024]{1,0:T(8,128)S(1)} collective-permute-done((f32[128,1024]{1,0:T(8,128)}, f32[128,1024]{1,0:T(8,128)S(1)}, u32[]{:S(2)}, u32[]{:S(2)}) %collective-permute-start.11) | collective-permute-done | bytes 524320 | tf_op jit(solution)/shard_map/ppermute | solution.py:20
  74.6 7.9 %collective-permute-done.5 = f32[128,1024]{1,0:T(8,128)S(1)} collective-permute-done((f32[128,1024]{1,0:T(8,128)}, f32[128,1024]{1,0:T(8,128)S(1)}, u32[]{:S(2)}, u32[]{:S(2)}) %collective-permute-start.5) | collective-permute-done | bytes 524320 | tf_op jit(solution)/shard_map/ppermute | solution.py:20
  85.7 2.0 %fusion.28 = f32[1024,64]{0,1:T(8,128)S(1)} fusion(f32[1024,1024]{1,0:T(8,128)S(1)} %bitcast.82, f32[512,128]{0,1:T(8,128)S(1)} %bitcast.100, f32[512,128]{0,1:T(8,128)S(1)} %fusion.11), kind=kOutput, calls=%fused_computation.72 | convolution fusion | flops 402718720 | bytes 4980736 | tf_op jit(solution)/shard_map/dot_general | solution.py:10
  89.4 4.4 %fusion.45 = f32[1024,64]{0,1:T(8,128)S(1)} fusion(f32[1024,1024]{1,0:T(8,128)} %bitcast.83, f32[1024,64]{0,1:T(8,128)S(1)} %get-tuple-element.22), kind=kOutput, calls=%fused_computation.113 | convolution fusion | flops 402653184 | bytes 4718592 | tf_op jit(solution)/shard_map/dot_general | solution.py:10
  94.4 2.0 %fusion.42 = f32[1024,64]{0,1:T(8,128)S(1)} fusion(f32[1024,1024]{1,0:T(8,128)S(1)} %bitcast.84, f32[1024,64]{0,1:T(8,128)S(1)} %get-tuple-element.21), kind=kOutput, calls=%fused_computation.110 | convolution fusion | flops 402653184 | bytes 4718592 | tf_op jit(solution)/shard_map/dot_general | solution.py:10
  97.2 2.0 %fusion.27 = f32[1024,64]{0,1:T(8,128)S(1)} fusion(f32[1024,1024]{1,0:T(8,128)S(1)} %bitcast.85, f32[1024,64]{0,1:T(8,128)S(1)} %collective-permute-done.20, f32[1024,64]{0,1:T(8,128)S(1)} %get-tuple-element.22, pred[]{:T(512)S(6)} %eq.131), kind=kOutput, calls=%fused_computation.71 | convolution fusion | flops 402718720 | bytes 4980737 | tf_op jit(solution)/shard_map/dot_general | solution.py:10
  105.6 2.0 %fusion.43 = f32[1024,64]{0,1:T(8,128)S(1)} fusion(f32[1024,1024]{1,0:T(8,128)S(1)} %bitcast.88, f32[1024,64]{0,1:T(8,128)S(1)} %broadcast_select_fusion.5), kind=kOutput, calls=%fused_computation.111 | convolution fusion | flops 402653184 | bytes 4718592 | tf_op jit(solution)/shard_map/dot_general | solution.py:10
  108.4 2.0 %fusion.25 = f32[1024,64]{0,1:T(8,128)S(1)} fusion(f32[1024,1024]{1,0:T(8,128)S(1)} %bitcast.89, f32[1024,64]{0,1:T(8,128)S(1)} %collective-permute-done.22, f32[1024,64]{0,1:T(8,128)S(1)} %broadcast_select_fusion.4, pred[]{:T(512)S(6)} %eq.129), kind=kOutput, calls=%fused_computation.69 | convolution fusion | flops 402718720 | bytes 4980737 | tf_op jit(solution)/shard_map/dot_general | solution.py:10
  111.1 2.0 %fusion.24 = f32[1024,64]{0,1:T(8,128)S(1)} fusion(f32[1024,1024]{1,0:T(8,128)S(1)} %bitcast.90, f32[1024,64]{0,1:T(8,128)S(1)} %collective-permute-done.15, f32[1024,64]{0,1:T(8,128)S(1)} %broadcast_select_fusion.5, pred[]{:T(512)S(6)} %eq.129), kind=kOutput, calls=%fused_computation.68 | convolution fusion | flops 402718720 | bytes 4980737 | tf_op jit(solution)/shard_map/dot_general | solution.py:10
  126.2 8.5 %collective-permute-done.25 = f32[1024,64]{0,1:T(8,128)S(1)} collective-permute-done((f32[1024,64]{0,1:T(8,128)S(1)}, f32[1024,64]{0,1:T(8,128)S(1)}, u32[]{:S(2)}, u32[]{:S(2)}) %collective-permute-start.25) | collective-permute-done | bytes 262176 | tf_op jit(solution)/shard_map/ppermute | solution.py:55
  134.8 2.0 %convolution_select_fusion = f32[1024,64]{0,1:T(8,128)S(1)} fusion(f32[1024,1024]{1,0:T(8,128)S(1)} %bitcast.95, f32[1024,64]{0,1:T(8,128)S(1)} %fusion.23, f32[1024,64]{0,1:T(8,128)S(1)} %fusion.47, f32[1024,64]{0,1:T(8,128)S(1)} %fusion.25, f32[1024,64]{0,1:T(8,128)S(1)} %fusion.46, f32[1024,64]{0,1:T(8,128)S(1)} %fusion.27, f32[1024,64]{0,1:T(8,128)S(1)} %fusion.45, ...), kind=kOutput, calls=%fused_computation.6 | convolution fusion | flops 403243008 | bytes 7077895 | tf_op jit(solution)/shard_map/dot_general | solution.py:10
  138.3 2.0 %convolution_select_fusion.1 = f32[1024,64]{0,1:T(8,128)S(1)} fusion(f32[1024,1024]{1,0:T(8,128)S(1)} %bitcast.96, f32[1024,64]{0,1:T(8,128)S(1)} %fusion.22, f32[1024,64]{0,1:T(8,128)S(1)} %fusion.44, f32[1024,64]{0,1:T(8,128)S(1)} %fusion.24, f32[1024,64]{0,1:T(8,128)S(1)} %fusion.43, f32[1024,64]{0,1:T(8,128)S(1)} %fusion.26, f32[1024,64]{0,1:T(8,128)S(1)} %fusion.42, ...), kind=kOutput, calls=%fused_computation.7 | convolution fusion | flops 403243008 | bytes 7077895 | tf_op jit(solution)/shard_map/dot_general | solution.py:10
  142.4 3.5 %collective-permute-start.26 = (f32[512,128]{0,1:T(8,128)S(1)}, f32[512,128]{0,1:T(8,128)S(1)}, u32[]{:S(2)}, u32[]{:S(2)}) collective-permute-start(f32[512,128]{0,1:T(8,128)S(1)} %pad_maximum_fusion.7), channel_id=1, source_target_pairs={{0,3},{1,0},{2,1},{3,2},{4,7},{5,4},{6,5},{7,6},{8,11},{9,8},{10,9... | collective-permute-start | bytes 786440 | tf_op jit(solution)/shard_map/ppermute | solution.py:67
  145.9 6.7 %collective-permute-done.28 = f32[512,128]{0,1:T(8,128)S(1)} collective-permute-done((f32[512,128]{0,1:T(8,128)S(1)}, f32[512,128]{0,1:T(8,128)S(1)}, u32[]{:S(2)}, u32[]{:S(2)}) %collective-permute-start.28) | collective-permute-done | bytes 262176 | tf_op jit(solution)/shard_map/ppermute | solution.py:67
  152.6 10.3 %collective-permute-done.27 = f32[512,128]{0,1:T(8,128)S(1)} collective-permute-done((f32[512,128]{0,1:T(8,128)S(1)}, f32[512,128]{0,1:T(8,128)S(1)}, u32[]{:S(2)}, u32[]{:S(2)}) %collective-permute-start.27) | collective-permute-done | bytes 262176 | tf_op jit(solution)/shard_map/ppermute | solution.py:67
  165.7 3.5 %convolution_bitcast_fusion = f32[1,256,2048]{2,1,0:T(8,128)} fusion(f32[512,2048]{1,0:T(8,128)S(1)} %copy-done.2, f32[256,128]{0,1:T(8,128)S(1)} %get-tuple-element.13, f32[256,128]{0,1:T(8,128)S(1)} %get-tuple-element.11, f32[256,128]{0,1:T(8,128)S(1)} %get-tuple-element.10, f32[256,128]{0,1:T(8,128)S(1)} %get-tuple-element.9), kind=kOutput, calls=%fused_computation.1 | convolution fusion | flops 1611005952 | bytes 6815744 | tf_op jit(solution)/shard_map/dot_general | solution.py:10
  169.9 6.2 %collective-permute-start.29 = (f32[512]{0:T(512)S(1)}, f32[512]{0:T(512)S(1)}, u32[]{:S(2)}, u32[]{:S(2)}) collective-permute-start(f32[512]{0:T(512)S(1)} %fusion.1), channel_id=1, source_target_pairs={{0,1},{1,0},{2,3},{3,2},{4,5},{5,4},{6,7},{7,6},{8,9},{9,8},{10,11... | collective-permute-start | bytes 6152 | tf_op jit(solution)/shard_map/ppermute | solution.py:90
  (104 shorter events, 55.8 us)
Async XLA Ops:
  2.0 17.3 %collective-permute-start = (f32[128,1024]{1,0:T(8,128)S(1)}, f32[128,1024]{1,0:T(8,128)S(1)}, u32[]{:S(2)}, u32[]{:S(2)}) collective-permute-start(f32[128,1024]{1,0:T(8,128)S(1)} %get-tuple-element.4), channel_id=1, source_target_pairs={{0,1},{1,2},{2,3},{4,5},{5,6},{6,7},{8,9},{9,10},{10,11},{12,13},{... | collective-permute-start | bytes 1572872 | tf_op jit(solution)/shard_map/ppermute | solution.py:19
  7.0 22.4 %collective-permute-start.6 = (f32[128,1024]{1,0:T(8,128)S(1)}, f32[128,1024]{1,0:T(8,128)S(1)}, u32[]{:S(2)}, u32[]{:S(2)}) collective-permute-start(f32[128,1024]{1,0:T(8,128)S(1)} %get-tuple-element.5), channel_id=1, source_target_pairs={{0,1},{1,2},{2,3},{4,5},{5,6},{6,7},{8,9},{9,10},{10,11},{12,13},{... | collective-permute-start | bytes 1572872 | tf_op jit(solution)/shard_map/ppermute | solution.py:19
  10.5 20.3 %collective-permute-start.9 = (f32[128,1024]{1,0:T(8,128)S(1)}, f32[128,1024]{1,0:T(8,128)S(1)}, u32[]{:S(2)}, u32[]{:S(2)}) collective-permute-start(f32[128,1024]{1,0:T(8,128)S(1)} %get-tuple-element.5), channel_id=1, source_target_pairs={{1,0},{2,1},{3,2},{5,4},{6,5},{7,6},{9,8},{10,9},{11,10},{13,12},{... | collective-permute-start | bytes 1572872 | tf_op jit(solution)/shard_map/ppermute | solution.py:20
  11.8 24.9 %collective-permute-start.3 = (f32[128,1024]{1,0:T(8,128)S(1)}, f32[128,1024]{1,0:T(8,128)S(1)}, u32[]{:S(2)}, u32[]{:S(2)}) collective-permute-start(f32[128,1024]{1,0:T(8,128)S(1)} %get-tuple-element.4), channel_id=1, source_target_pairs={{1,0},{2,1},{3,2},{5,4},{6,5},{7,6},{9,8},{10,9},{11,10},{13,12},{... | collective-permute-start | bytes 1572872 | tf_op jit(solution)/shard_map/ppermute | solution.py:20
  19.3 18.8 %collective-permute-start.1 = (f32[128,1024]{1,0:T(8,128)S(1)}, f32[128,1024]{1,0:T(8,128)}, u32[]{:S(2)}, u32[]{:S(2)}) collective-permute-start(f32[128,1024]{1,0:T(8,128)S(1)} %collective-permute-done), channel_id=1, source_target_pairs={{1,2},{2,3},{5,6},{6,7},{9,10},{10,11},{13,14},{14,15},{17,18},{18... | collective-permute-start | bytes 1572872 | tf_op jit(solution)/shard_map/ppermute | solution.py:19
  29.4 10.1 %collective-permute-start.7 = (f32[128,1024]{1,0:T(8,128)S(1)}, f32[128,1024]{1,0:T(8,128)}, u32[]{:S(2)}, u32[]{:S(2)}) collective-permute-start(f32[128,1024]{1,0:T(8,128)S(1)} %collective-permute-done.6), channel_id=1, source_target_pairs={{1,2},{2,3},{5,6},{6,7},{9,10},{10,11},{13,14},{14,15},{17,18},{18... | collective-permute-start | bytes 1572872 | tf_op jit(solution)/shard_map/ppermute | solution.py:19
  30.9 21.2 %collective-permute-start.10 = (f32[128,1024]{1,0:T(8,128)S(1)}, f32[128,1024]{1,0:T(8,128)}, u32[]{:S(2)}, u32[]{:S(2)}) collective-permute-start(f32[128,1024]{1,0:T(8,128)S(1)} %collective-permute-done.9), channel_id=1, source_target_pairs={{1,0},{2,1},{5,4},{6,5},{9,8},{10,9},{13,12},{14,13},{17,16},{18,1... | collective-permute-start | bytes 1572872 | tf_op jit(solution)/shard_map/ppermute | solution.py:20
  36.8 26.6 %collective-permute-start.4 = (f32[128,1024]{1,0:T(8,128)S(1)}, f32[128,1024]{1,0:T(8,128)}, u32[]{:S(2)}, u32[]{:S(2)}) collective-permute-start(f32[128,1024]{1,0:T(8,128)S(1)} %collective-permute-done.3), channel_id=1, source_target_pairs={{1,0},{2,1},{5,4},{6,5},{9,8},{10,9},{13,12},{14,13},{17,16},{18,1... | collective-permute-start | bytes 1572872 | tf_op jit(solution)/shard_map/ppermute | solution.py:20
  38.1 26.5 %collective-permute-start.2 = (f32[128,1024]{1,0:T(8,128)}, f32[128,1024]{1,0:T(8,128)}, u32[]{:S(2)}, u32[]{:S(2)}) collective-permute-start(f32[128,1024]{1,0:T(8,128)} %collective-permute-done.1), channel_id=1, source_target_pairs={{2,3},{6,7},{10,11},{14,15},{18,19},{22,23},{26,27},{30,31}} | collective-permute-start | bytes 1572872 | tf_op jit(solution)/shard_map/ppermute | solution.py:19
  39.5 27.3 %collective-permute-start.8 = (f32[128,1024]{1,0:T(8,128)}, f32[128,1024]{1,0:T(8,128)S(1)}, u32[]{:S(2)}, u32[]{:S(2)}) collective-permute-start(f32[128,1024]{1,0:T(8,128)} %collective-permute-done.7), channel_id=1, source_target_pairs={{2,3},{6,7},{10,11},{14,15},{18,19},{22,23},{26,27},{30,31}} | collective-permute-start | bytes 1572872 | tf_op jit(solution)/shard_map/ppermute | solution.py:19
  52.1 22.4 %collective-permute-start.11 = (f32[128,1024]{1,0:T(8,128)}, f32[128,1024]{1,0:T(8,128)S(1)}, u32[]{:S(2)}, u32[]{:S(2)}) collective-permute-start(f32[128,1024]{1,0:T(8,128)} %collective-permute-done.10), channel_id=1, source_target_pairs={{1,0},{5,4},{9,8},{13,12},{17,16},{21,20},{25,24},{29,28}} | collective-permute-start | bytes 1572872 | tf_op jit(solution)/shard_map/ppermute | solution.py:20
  63.3 19.2 %collective-permute-start.5 = (f32[128,1024]{1,0:T(8,128)}, f32[128,1024]{1,0:T(8,128)S(1)}, u32[]{:S(2)}, u32[]{:S(2)}) collective-permute-start(f32[128,1024]{1,0:T(8,128)} %collective-permute-done.4), channel_id=1, source_target_pairs={{1,0},{5,4},{9,8},{13,12},{17,16},{21,20},{25,24},{29,28}} | collective-permute-start | bytes 1572872 | tf_op jit(solution)/shard_map/ppermute | solution.py:20
  96.5 3.6 %collective-permute-start.13 = (f32[1024,64]{0,1:T(8,128)S(1)}, f32[1024,64]{0,1:T(8,128)S(1)}, u32[]{:S(2)}, u32[]{:S(2)}) collective-permute-start(f32[1024,64]{0,1:T(8,128)S(1)} %fusion.42), channel_id=1, source_target_pairs={{24,20},{25,21},{26,22},{27,23}} | collective-permute-start | bytes 786440 | tf_op jit(solution)/shard_map/ppermute | solution.py:55
  99.2 3.6 %collective-permute-start.21 = (f32[1024,64]{0,1:T(8,128)S(1)}, f32[1024,64]{0,1:T(8,128)S(1)}, u32[]{:S(2)}, u32[]{:S(2)}) collective-permute-start(f32[1024,64]{0,1:T(8,128)S(1)} %fusion.27), channel_id=1, source_target_pairs={{20,16},{21,17},{22,18},{23,19}} | collective-permute-start | bytes 786440 | tf_op jit(solution)/shard_map/ppermute | solution.py:55
  104.9 3.5 %collective-permute-start.22 = (f32[1024,64]{0,1:T(8,128)S(1)}, f32[1024,64]{0,1:T(8,128)S(1)}, u32[]{:S(2)}, u32[]{:S(2)}) collective-permute-start(f32[1024,64]{0,1:T(8,128)S(1)} %fusion.46), channel_id=1, source_target_pairs={{16,12},{17,13},{18,14},{19,15}} | collective-permute-start | bytes 786440 | tf_op jit(solution)/shard_map/ppermute | solution.py:55
  113.1 3.5 %collective-permute-start.16 = (f32[1024,64]{0,1:T(8,128)S(1)}, f32[1024,64]{0,1:T(8,128)S(1)}, u32[]{:S(2)}, u32[]{:S(2)}) collective-permute-start(f32[1024,64]{0,1:T(8,128)S(1)} %fusion.24), channel_id=1, source_target_pairs={{12,8},{13,9},{14,10},{15,11}} | collective-permute-start | bytes 786440 | tf_op jit(solution)/shard_map/ppermute | solution.py:55
  115.9 3.7 %collective-permute-start.24 = (f32[1024,64]{0,1:T(8,128)S(1)}, f32[1024,64]{0,1:T(8,128)S(1)}, u32[]{:S(2)}, u32[]{:S(2)}) collective-permute-start(f32[1024,64]{0,1:T(8,128)S(1)} %fusion.47), channel_id=1, source_target_pairs={{8,4},{9,5},{10,6},{11,7}} | collective-permute-start | bytes 786440 | tf_op jit(solution)/shard_map/ppermute | solution.py:55
  118.7 4.2 %collective-permute-start.17 = (f32[1024,64]{0,1:T(8,128)S(1)}, f32[1024,64]{0,1:T(8,128)S(1)}, u32[]{:S(2)}, u32[]{:S(2)}) collective-permute-start(f32[1024,64]{0,1:T(8,128)S(1)} %fusion.44), channel_id=1, source_target_pairs={{8,4},{9,5},{10,6},{11,7}} | collective-permute-start | bytes 786440 | tf_op jit(solution)/shard_map/ppermute | solution.py:55
  121.6 13.2 %collective-permute-start.25 = (f32[1024,64]{0,1:T(8,128)S(1)}, f32[1024,64]{0,1:T(8,128)S(1)}, u32[]{:S(2)}, u32[]{:S(2)}) collective-permute-start(f32[1024,64]{0,1:T(8,128)S(1)} %fusion.23), channel_id=1, source_target_pairs={{4,0},{5,1},{6,2},{7,3}} | collective-permute-start | bytes 786440 | tf_op jit(solution)/shard_map/ppermute | solution.py:55
  125.0 13.4 %collective-permute-start.18 = (f32[1024,64]{0,1:T(8,128)S(1)}, f32[1024,64]{0,1:T(8,128)S(1)}, u32[]{:S(2)}, u32[]{:S(2)}) collective-permute-start(f32[1024,64]{0,1:T(8,128)S(1)} %fusion.22), channel_id=1, source_target_pairs={{4,0},{5,1},{6,2},{7,3}} | collective-permute-start | bytes 786440 | tf_op jit(solution)/shard_map/ppermute | solution.py:55
  141.5 11.1 %collective-permute-start.28 = (f32[512,128]{0,1:T(8,128)S(1)}, f32[512,128]{0,1:T(8,128)S(1)}, u32[]{:S(2)}, u32[]{:S(2)}) collective-permute-start(f32[512,128]{0,1:T(8,128)S(1)} %pad_maximum_fusion.9), channel_id=1, source_target_pairs={{0,1},{1,2},{2,3},{3,0},{4,5},{5,6},{6,7},{7,4},{8,9},{9,10},{10,1... | collective-permute-start | bytes 786440 | tf_op jit(solution)/shard_map/ppermute | solution.py:67
  141.7 21.3 %collective-permute-start.27 = (f32[512,128]{0,1:T(8,128)S(1)}, f32[512,128]{0,1:T(8,128)S(1)}, u32[]{:S(2)}, u32[]{:S(2)}) collective-permute-start(f32[512,128]{0,1:T(8,128)S(1)} %pad_maximum_fusion.8), channel_id=1, source_target_pairs={{0,2},{1,3},{2,0},{3,1},{4,6},{5,7},{6,4},{7,5},{8,10},{9,11},{10,... | collective-permute-start | bytes 786440 | tf_op jit(solution)/shard_map/ppermute | solution.py:67
  142.4 20.6 %collective-permute-start.26 = (f32[512,128]{0,1:T(8,128)S(1)}, f32[512,128]{0,1:T(8,128)S(1)}, u32[]{:S(2)}, u32[]{:S(2)}) collective-permute-start(f32[512,128]{0,1:T(8,128)S(1)} %pad_maximum_fusion.7), channel_id=1, source_target_pairs={{0,3},{1,0},{2,1},{3,2},{4,7},{5,4},{6,5},{7,6},{8,11},{9,8},{10,9... | collective-permute-start | bytes 786440 | tf_op jit(solution)/shard_map/ppermute | solution.py:67
  169.9 7.8 %collective-permute-start.29 = (f32[512]{0:T(512)S(1)}, f32[512]{0:T(512)S(1)}, u32[]{:S(2)}, u32[]{:S(2)}) collective-permute-start(f32[512]{0:T(512)S(1)} %fusion.1), channel_id=1, source_target_pairs={{0,1},{1,0},{2,3},{3,2},{4,5},{5,4},{6,7},{7,6},{8,9},{9,8},{10,11... | collective-permute-start | bytes 6152 | tf_op jit(solution)/shard_map/ppermute | solution.py:90
  (11 other events, 113.0 us)

commit v11 on v9

--- a/solution.py
+++ b/solution.py
@@ -4,6 +4,7 @@
 from jax.sharding import PartitionSpec as P
 
 CHUNKS = 2
+GATHER_PARTS = 4
 
 
 def product(left, right):
@@ -34,10 +35,10 @@
     width = state_dim // count
 
     local = section_maps[0]
-    cut = local.shape[0] // 2
-    upper = line_gather(local[:cut], place, count).reshape(count, cut, local.shape[1])
-    lower = line_gather(local[cut:], place, count).reshape(count, cut, local.shape[1])
-    whole_map = jnp.concatenate([upper, lower], axis=1).reshape(count * local.shape[0], local.shape[1])
+    cut = local.shape[0] // GATHER_PARTS
+    parts = [line_gather(local[p * cut:(p + 1) * cut], place, count).reshape(count, cut, local.shape[1])
+             for p in range(GATHER_PARTS)]
+    whole_map = jnp.concatenate(parts, axis=1).reshape(count * local.shape[0], local.shape[1])
     whole_map = lax.optimization_barrier(whole_map)
     rows_id = lax.broadcasted_iota(jnp.int32, (state_dim, width), 0)
     cols_id = lax.broadcasted_iota(jnp.int32, (state_dim, width), 1) + place * width

time: 179 us -> 195 us (1.089)
  starting transfers between devices: 42.8 us -> 56.6 us
  waiting for transfers between devices: 81.8 us -> 87.6 us
  local copies, waits for them, and re-layouts: 8.99 us -> 4.56 us
    ppermute x6 -> x12, waiting for transfers between devices: 14.8 us -> 3.86 us  [line_gather(): lax.ppermute(rightward, 'row', [(z, z + 1) for z in range(t - 1, count -...]
    ppermute x6 -> x12, starting transfers between devices: 13.5 us -> 24.2 us  [line_gather(): lax.ppermute(rightward, 'row', [(z, z + 1) for z in range(t - 1, count -...]
    ppermute x6 -> x12, waiting for transfers between devices: 38.3 us -> 48.4 us  [line_gather(): lax.ppermute(leftward, 'row', [(z, z - 1) for z in range(1, count - t + 1)])]
    ppermute x6 -> x12, starting transfers between devices: 7.71 us -> 15.4 us  [line_gather(): lax.ppermute(leftward, 'row', [(z, z - 1) for z in range(1, count - t + 1)])]
    ppermute x1, starting transfers between devices: 6.19 us -> 0.01 us  [body(): total = total + lax.ppermute(sent, 'row', partner)]
    unnamed x26 -> x36, local copies, waits for them, and re-layouts: 6.11 us -> 0.94 us
    ppermute x3, waiting for transfers between devices: 17 us -> 21.5 us  [body(): lax.ppermute(payload, 'row', [(z, (z + d) % count) for z in range(count)])]
    ppermute x1, waiting for transfers between devices: 1.56 us -> 3.57 us  [body(): total = total + lax.ppermute(sent, 'row', partner)]
  transfers between devices with their start and end apart: 30 -> 42, of which waited for: 12 -> 19; matrix products, arithmetic and copies ran while one was open for 17% -> 13% of each run, Pallas kernels for 0% -> 0%
where the time goes in v11:
time: 195 us; the launch traced here: 194 us
  waiting for transfers between devices  87.6 us (45%)
  starting transfers between devices  56.6 us (29%)
  matrix products  41.5 us (21%)
  local copies, waits for them, and re-layouts  4.56 us (2%)
    ppermute x12, waiting for transfers between devices, line_gather(): lax.ppermute(leftward, 'row', [(z, z - 1) for z in range(1, count - t + 1)])  48.4 us
    dot_general x18, matrix products, product(): jnp.dot(left, right, precision=lax.Precision.HIGH, preferred_element_type...  41.5 us
    ppermute x12, starting transfers between devices, line_gather(): lax.ppermute(rightward, 'row', [(z, z + 1) for z in range(t - 1, count -...  24.2 us
    ppermute x3, waiting for transfers between devices, body(): lax.ppermute(payload, 'row', [(z, (z + d) % count) for z in range(count)])  21.5 us
    ppermute x12, starting transfers between devices, line_gather(): lax.ppermute(leftward, 'row', [(z, z - 1) for z in range(1, count - t + 1)])  15.4 us
    ppermute x14, starting transfers between devices, body(): got = lax.ppermute(fresh, 'tm', [(k, k - 1)])  11.1 us
    ppermute x14, waiting for transfers between devices, body(): got = lax.ppermute(fresh, 'tm', [(k, k - 1)])  10.3 us
    ppermute x3, starting transfers between devices, body(): lax.ppermute(payload, 'row', [(z, (z + d) % count) for z in range(count)])  5.96 us
  transfers between devices with their start and end apart: 42, of which 19 were waited for; matrix products, arithmetic and copies ran while one was open for 13% of the time, Pallas kernels for 0%

profile of v11, /device:TPU:0, one launch (start us, length us, event | category | flops | bytes accessed | tf_op | source)
XLA Modules:
  0.0 193.8 jit_solution(4055738604191300600)
XLA Ops:
  2.6 5.0 %collective-permute-start.6 = (f32[64,1024]{1,0:T(8,128)S(1)}, f32[64,1024]{1,0:T(8,128)S(1)}, u32[]{:S(2)}, u32[]{:S(2)}) collective-permute-start(f32[64,1024]{1,0:T(8,128)S(1)} %get-tuple-element.7), channel_id=1, source_target_pairs={{0,1},{1,2},{2,3},{4,5},{5,6},{6,7},{8,9},{9,10},{10,11},{12,13},{... | collective-permute-start | bytes 786440 | tf_op jit(solution)/shard_map/ppermute | solution.py:20
  7.6 3.5 %collective-permute-start.12 = (f32[64,1024]{1,0:T(8,128)S(1)}, f32[64,1024]{1,0:T(8,128)S(1)}, u32[]{:S(2)}, u32[]{:S(2)}) collective-permute-start(f32[64,1024]{1,0:T(8,128)S(1)} %get-tuple-element.9), channel_id=1, source_target_pairs={{0,1},{1,2},{2,3},{4,5},{5,6},{6,7},{8,9},{9,10},{10,11},{12,13},{... | collective-permute-start | bytes 786440 | tf_op jit(solution)/shard_map/ppermute | solution.py:20
  11.1 3.5 %collective-permute-start.18 = (f32[64,1024]{1,0:T(8,128)S(1)}, f32[64,1024]{1,0:T(8,128)S(1)}, u32[]{:S(2)}, u32[]{:S(2)}) collective-permute-start(f32[64,1024]{1,0:T(8,128)S(1)} %get-tuple-element.8), channel_id=1, source_target_pairs={{0,1},{1,2},{2,3},{4,5},{5,6},{6,7},{8,9},{9,10},{10,11},{12,13},{... | collective-permute-start | bytes 786440 | tf_op jit(solution)/shard_map/ppermute | solution.py:20
  15.3 6.9 %collective-permute-start = (f32[64,1024]{1,0:T(8,128)}, f32[64,1024]{1,0:T(8,128)S(1)}, u32[]{:S(2)}, u32[]{:S(2)}) collective-permute-start(f32[64,1024]{1,0:T(8,128)} %get-tuple-element.6), channel_id=1, source_target_pairs={{0,1},{1,2},{2,3},{4,5},{5,6},{6,7},{8,9},{9,10},{10,11},{12,13},{... | collective-permute-start | bytes 786440 | tf_op jit(solution)/shard_map/ppermute | solution.py:20
  26.9 3.1 %collective-permute-done = f32[64,1024]{1,0:T(8,128)S(1)} collective-permute-done((f32[64,1024]{1,0:T(8,128)}, f32[64,1024]{1,0:T(8,128)S(1)}, u32[]{:S(2)}, u32[]{:S(2)}) %collective-permute-start) | collective-permute-done | bytes 262176 | tf_op jit(solution)/shard_map/ppermute | solution.py:20
  37.5 9.9 %collective-permute-done.15 = f32[64,1024]{1,0:T(8,128)S(1)} collective-permute-done((f32[64,1024]{1,0:T(8,128)S(1)}, f32[64,1024]{1,0:T(8,128)S(1)}, u32[]{:S(2)}, u32[]{:S(2)}) %collective-permute-start.15) | collective-permute-done | bytes 262176 | tf_op jit(solution)/shard_map/ppermute | solution.py:21
  54.9 5.4 %collective-permute-done.4 = f32[64,1024]{1,0:T(8,128)S(1)} collective-permute-done((f32[64,1024]{1,0:T(8,128)S(1)}, f32[64,1024]{1,0:T(8,128)S(1)}, u32[]{:S(2)}, u32[]{:S(2)}) %collective-permute-start.4) | collective-permute-done | bytes 262176 | tf_op jit(solution)/shard_map/ppermute | solution.py:21
  61.0 4.9 %collective-permute-done.10 = f32[64,1024]{1,0:T(8,128)S(1)} collective-permute-done((f32[64,1024]{1,0:T(8,128)S(1)}, f32[64,1024]{1,0:T(8,128)S(1)}, u32[]{:S(2)}, u32[]{:S(2)}) %collective-permute-start.10) | collective-permute-done | bytes 262176 | tf_op jit(solution)/shard_map/ppermute | solution.py:21
  67.3 4.3 %collective-permute-done.16 = f32[64,1024]{1,0:T(8,128)S(1)} collective-permute-done((f32[64,1024]{1,0:T(8,128)S(1)}, f32[64,1024]{1,0:T(8,128)S(1)}, u32[]{:S(2)}, u32[]{:S(2)}) %collective-permute-start.16) | collective-permute-done | bytes 262176 | tf_op jit(solution)/shard_map/ppermute | solution.py:21
  72.9 4.3 %collective-permute-done.22 = f32[64,1024]{1,0:T(8,128)S(1)} collective-permute-done((f32[64,1024]{1,0:T(8,128)S(1)}, f32[64,1024]{1,0:T(8,128)S(1)}, u32[]{:S(2)}, u32[]{:S(2)}) %collective-permute-start.22) | collective-permute-done | bytes 262176 | tf_op jit(solution)/shard_map/ppermute | solution.py:21
  80.3 2.5 %collective-permute-done.5 = f32[64,1024]{1,0:T(8,128)S(1)} collective-permute-done((f32[64,1024]{1,0:T(8,128)S(1)}, f32[64,1024]{1,0:T(8,128)S(1)}, u32[]{:S(2)}, u32[]{:S(2)}) %collective-permute-start.5) | collective-permute-done | bytes 262176 | tf_op jit(solution)/shard_map/ppermute | solution.py:21
  83.0 5.5 %collective-permute-done.11 = f32[64,1024]{1,0:T(8,128)S(1)} collective-permute-done((f32[64,1024]{1,0:T(8,128)S(1)}, f32[64,1024]{1,0:T(8,128)S(1)}, u32[]{:S(2)}, u32[]{:S(2)}) %collective-permute-start.11) | collective-permute-done | bytes 262176 | tf_op jit(solution)/shard_map/ppermute | solution.py:21
  88.6 4.6 %collective-permute-done.17 = f32[64,1024]{1,0:T(8,128)S(1)} collective-permute-done((f32[64,1024]{1,0:T(8,128)S(1)}, f32[64,1024]{1,0:T(8,128)S(1)}, u32[]{:S(2)}, u32[]{:S(2)}) %collective-permute-start.17) | collective-permute-done | bytes 262176 | tf_op jit(solution)/shard_map/ppermute | solution.py:21
  93.3 2.7 %collective-permute-done.23 = f32[64,1024]{1,0:T(8,128)S(1)} collective-permute-done((f32[64,1024]{1,0:T(8,128)S(1)}, f32[64,1024]{1,0:T(8,128)S(1)}, u32[]{:S(2)}, u32[]{:S(2)}) %collective-permute-start.23) | collective-permute-done | bytes 262176 | tf_op jit(solution)/shard_map/ppermute | solution.py:21
  102.7 4.4 %fusion.43 = f32[1024,64]{0,1:T(8,128)S(1)} fusion(f32[1024,1024]{1,0:T(8,128)} %bitcast.93, f32[1024,64]{0,1:T(8,128)S(1)} %get-tuple-element.25), kind=kOutput, calls=%fused_computation.125 | convolution fusion | flops 402653184 | bytes 4718592 | tf_op jit(solution)/shard_map/dot_general | solution.py:11
  139.6 8.9 %collective-permute-done.30 = f32[1024,64]{0,1:T(8,128)S(1)} collective-permute-done((f32[1024,64]{0,1:T(8,128)S(1)}, f32[1024,64]{0,1:T(8,128)S(1)}, u32[]{:S(2)}, u32[]{:S(2)}) %collective-permute-start.30) | collective-permute-done | bytes 262176 | tf_op jit(solution)/shard_map/ppermute | solution.py:56
  148.5 2.0 %convolution_select_fusion.1 = f32[1024,64]{0,1:T(8,128)S(1)} fusion(f32[1024,1024]{1,0:T(8,128)S(1)} %bitcast.105, f32[1024,64]{0,1:T(8,128)S(1)} %fusion.30, f32[1024,64]{0,1:T(8,128)S(1)} %fusion.45, f32[1024,64]{0,1:T(8,128)S(1)} %fusion.32, f32[1024,64]{0,1:T(8,128)S(1)} %fusion.44, f32[1024,64]{0,1:T(8,128)S(1)} %fusion.34, ...), kind=kOutput, calls=%fused_computation.4 | convolution fusion | flops 403243008 | bytes 7077895 | tf_op jit(solution)/shard_map/dot_general | solution.py:11
  151.9 2.0 %convolution_select_fusion = f32[1024,64]{0,1:T(8,128)S(1)} fusion(f32[1024,1024]{1,0:T(8,128)S(1)} %bitcast.106, f32[1024,64]{0,1:T(8,128)S(1)} %fusion.31, f32[1024,64]{0,1:T(8,128)S(1)} %fusion.48, f32[1024,64]{0,1:T(8,128)S(1)} %fusion.33, f32[1024,64]{0,1:T(8,128)S(1)} %fusion.47, f32[1024,64]{0,1:T(8,128)S(1)} %fusion.35, f32[1024,64]{0,1:T(8,128)S(1)} %fusion.46, ...), kind=kOutput, calls=%fused_computation.3 | convolution fusion | flops 403243008 | bytes 7077895 | tf_op jit(solution)/shard_map/dot_general | solution.py:11
  156.5 2.9 %collective-permute-start.39 = (f32[512,128]{0,1:T(8,128)S(1)}, f32[512,128]{0,1:T(8,128)S(1)}, u32[]{:S(2)}, u32[]{:S(2)}) collective-permute-start(f32[512,128]{0,1:T(8,128)S(1)} %pad_maximum_fusion.4), channel_id=1, source_target_pairs={{0,2},{1,3},{2,0},{3,1},{4,6},{5,7},{6,4},{7,5},{8,10},{9,11},{10,... | collective-permute-start | bytes 786440 | tf_op jit(solution)/shard_map/ppermute | solution.py:68
  161.2 3.7 %collective-permute-done.38 = f32[512,128]{0,1:T(8,128)S(1)} collective-permute-done((f32[512,128]{0,1:T(8,128)S(1)}, f32[512,128]{0,1:T(8,128)S(1)}, u32[]{:S(2)}, u32[]{:S(2)}) %collective-permute-start.38) | collective-permute-done | bytes 262176 | tf_op jit(solution)/shard_map/ppermute | solution.py:68
  164.9 17.8 %collective-permute-done.39 = f32[512,128]{0,1:T(8,128)S(1)} collective-permute-done((f32[512,128]{0,1:T(8,128)S(1)}, f32[512,128]{0,1:T(8,128)S(1)}, u32[]{:S(2)}, u32[]{:S(2)}) %collective-permute-start.39) | collective-permute-done | bytes 262176 | tf_op jit(solution)/shard_map/ppermute | solution.py:68
  182.8 4.3 %fusion.1 = f32[256,2048]{1,0:T(8,128)S(1)} fusion(f32[512,2048]{1,0:T(8,128)} %param.5, f32[256,128]{0,1:T(8,128)S(1)} %get-tuple-element.17, f32[256,128]{0,1:T(8,128)S(1)} %get-tuple-element.15, f32[256,128]{0,1:T(8,128)S(1)} %get-tuple-element.14, f32[256,128]{0,1:T(8,128)S(1)} %get-tuple-element.13), kind=kOutput, calls=%fused_computation.8 | convolution fusion | flops 1611005952 | bytes 6815744 | tf_op jit(solution)/shard_map/dot_general | solution.py:11
  187.2 2.2 %fusion = f32[2048]{0:T(1024)S(1)} fusion(f32[256,2048]{1,0:T(8,128)S(1)} %fusion.1, f32[512,2048]{1,0:T(8,128)S(1)} %copy-done.2, f32[256,128]{0,1:T(8,128)S(1)} %get-tuple-element.16, f32[256,128]{0,1:T(8,128)S(1)} %get-tuple-element.12, f32[256,128]{0,1:T(8,128)S(1)} %get-tuple-element.11, f32[256,128]{0,1:T(8,128)S(1)} %get-tuple-element.10), kind=kOutput, calls=%fused_computation.2 | convolution fusion | flops 1612052480 | bytes 6823936 | tf_op jit(solution)/shard_map/dot_general | solution.py:11
  189.6 3.6 %collective-permute-done.41 = f32[512]{0:T(512)S(1)} collective-permute-done((f32[512]{0:T(512)S(1)}, f32[512]{0:T(512)S(1)}, u32[]{:S(2)}, u32[]{:S(2)}) %collective-permute-start.41) | collective-permute-done | bytes 2080 | tf_op jit(solution)/shard_map/ppermute | solution.py:89
  (142 shorter events, 74.2 us)
Async XLA Ops:
  2.6 12.0 %collective-permute-start.6 = (f32[64,1024]{1,0:T(8,128)S(1)}, f32[64,1024]{1,0:T(8,128)S(1)}, u32[]{:S(2)}, u32[]{:S(2)}) collective-permute-start(f32[64,1024]{1,0:T(8,128)S(1)} %get-tuple-element.7), channel_id=1, source_target_pairs={{0,1},{1,2},{2,3},{4,5},{5,6},{6,7},{8,9},{9,10},{10,11},{12,13},{... | collective-permute-start | bytes 786440 | tf_op jit(solution)/shard_map/ppermute | solution.py:20
  7.6 15.9 %collective-permute-start.12 = (f32[64,1024]{1,0:T(8,128)S(1)}, f32[64,1024]{1,0:T(8,128)S(1)}, u32[]{:S(2)}, u32[]{:S(2)}) collective-permute-start(f32[64,1024]{1,0:T(8,128)S(1)} %get-tuple-element.9), channel_id=1, source_target_pairs={{0,1},{1,2},{2,3},{4,5},{5,6},{6,7},{8,9},{9,10},{10,11},{12,13},{... | collective-permute-start | bytes 786440 | tf_op jit(solution)/shard_map/ppermute | solution.py:20
  11.1 14.4 %collective-permute-start.18 = (f32[64,1024]{1,0:T(8,128)S(1)}, f32[64,1024]{1,0:T(8,128)S(1)}, u32[]{:S(2)}, u32[]{:S(2)}) collective-permute-start(f32[64,1024]{1,0:T(8,128)S(1)} %get-tuple-element.8), channel_id=1, source_target_pairs={{0,1},{1,2},{2,3},{4,5},{5,6},{6,7},{8,9},{9,10},{10,11},{12,13},{... | collective-permute-start | bytes 786440 | tf_op jit(solution)/shard_map/ppermute | solution.py:20
  15.3 14.8 %collective-permute-start = (f32[64,1024]{1,0:T(8,128)}, f32[64,1024]{1,0:T(8,128)S(1)}, u32[]{:S(2)}, u32[]{:S(2)}) collective-permute-start(f32[64,1024]{1,0:T(8,128)} %get-tuple-element.6), channel_id=1, source_target_pairs={{0,1},{1,2},{2,3},{4,5},{5,6},{6,7},{8,9},{9,10},{10,11},{12,13},{... | collective-permute-start | bytes 786440 | tf_op jit(solution)/shard_map/ppermute | solution.py:20
  23.5 11.9 %collective-permute-start.9 = (f32[64,1024]{1,0:T(8,128)S(1)}, f32[64,1024]{1,0:T(8,128)S(1)}, u32[]{:S(2)}, u32[]{:S(2)}) collective-permute-start(f32[64,1024]{1,0:T(8,128)S(1)} %get-tuple-element.7), channel_id=1, source_target_pairs={{1,0},{2,1},{3,2},{5,4},{6,5},{7,6},{9,8},{10,9},{11,10},{13,12},{... | collective-permute-start | bytes 786440 | tf_op jit(solution)/shard_map/ppermute | solution.py:21
  30.1 17.3 %collective-permute-start.15 = (f32[64,1024]{1,0:T(8,128)S(1)}, f32[64,1024]{1,0:T(8,128)S(1)}, u32[]{:S(2)}, u32[]{:S(2)}) collective-permute-start(f32[64,1024]{1,0:T(8,128)S(1)} %get-tuple-element.9), channel_id=1, source_target_pairs={{1,0},{2,1},{3,2},{5,4},{6,5},{7,6},{9,8},{10,9},{11,10},{13,12},{... | collective-permute-start | bytes 786440 | tf_op jit(solution)/shard_map/ppermute | solution.py:21
  32.6 17.7 %collective-permute-start.21 = (f32[64,1024]{1,0:T(8,128)S(1)}, f32[64,1024]{1,0:T(8,128)S(1)}, u32[]{:S(2)}, u32[]{:S(2)}) collective-permute-start(f32[64,1024]{1,0:T(8,128)S(1)} %get-tuple-element.8), channel_id=1, source_target_pairs={{1,0},{2,1},{3,2},{5,4},{6,5},{7,6},{9,8},{10,9},{11,10},{13,12},{... | collective-permute-start | bytes 786440 | tf_op jit(solution)/shard_map/ppermute | solution.py:21
  35.4 16.1 %collective-permute-start.19 = (f32[64,1024]{1,0:T(8,128)S(1)}, f32[64,1024]{1,0:T(8,128)S(1)}, u32[]{:S(2)}, u32[]{:S(2)}) collective-permute-start(f32[64,1024]{1,0:T(8,128)S(1)} %collective-permute-done.18), channel_id=1, source_target_pairs={{1,2},{2,3},{5,6},{6,7},{9,10},{10,11},{13,14},{14,15},{17,18},{18... | collective-permute-start | bytes 786440 | tf_op jit(solution)/shard_map/ppermute | solution.py:20
  36.0 16.8 %collective-permute-start.1 = (f32[64,1024]{1,0:T(8,128)S(1)}, f32[64,1024]{1,0:T(8,128)S(1)}, u32[]{:S(2)}, u32[]{:S(2)}) collective-permute-start(f32[64,1024]{1,0:T(8,128)S(1)} %collective-permute-done), channel_id=1, source_target_pairs={{1,2},{2,3},{5,6},{6,7},{9,10},{10,11},{13,14},{14,15},{17,18},{18... | collective-permute-start | bytes 786440 | tf_op jit(solution)/shard_map/ppermute | solution.py:20
  36.7 17.4 %collective-permute-start.14 = (f32[64,1024]{1,0:T(8,128)S(1)}, f32[64,1024]{1,0:T(8,128)S(1)}, u32[]{:S(2)}, u32[]{:S(2)}) collective-permute-start(f32[64,1024]{1,0:T(8,128)S(1)} %collective-permute-done.13), channel_id=1, source_target_pairs={{2,3},{6,7},{10,11},{14,15},{18,19},{22,23},{26,27},{30,31}} | collective-permute-start | bytes 786440 | tf_op jit(solution)/shard_map/ppermute | solution.py:20
  47.4 12.9 %collective-permute-start.4 = (f32[64,1024]{1,0:T(8,128)S(1)}, f32[64,1024]{1,0:T(8,128)S(1)}, u32[]{:S(2)}, u32[]{:S(2)}) collective-permute-start(f32[64,1024]{1,0:T(8,128)S(1)} %collective-permute-done.3), channel_id=1, source_target_pairs={{1,0},{2,1},{5,4},{6,5},{9,8},{10,9},{13,12},{14,13},{17,16},{18,1... | collective-permute-start | bytes 786440 | tf_op jit(solution)/shard_map/ppermute | solution.py:21
  50.2 15.8 %collective-permute-start.10 = (f32[64,1024]{1,0:T(8,128)S(1)}, f32[64,1024]{1,0:T(8,128)S(1)}, u32[]{:S(2)}, u32[]{:S(2)}) collective-permute-start(f32[64,1024]{1,0:T(8,128)S(1)} %collective-permute-done.9), channel_id=1, source_target_pairs={{1,0},{2,1},{5,4},{6,5},{9,8},{10,9},{13,12},{14,13},{17,16},{18,1... | collective-permute-start | bytes 786440 | tf_op jit(solution)/shard_map/ppermute | solution.py:21
  51.5 20.1 %collective-permute-start.16 = (f32[64,1024]{1,0:T(8,128)S(1)}, f32[64,1024]{1,0:T(8,128)S(1)}, u32[]{:S(2)}, u32[]{:S(2)}) collective-permute-start(f32[64,1024]{1,0:T(8,128)S(1)} %collective-permute-done.15), channel_id=1, source_target_pairs={{1,0},{2,1},{5,4},{6,5},{9,8},{10,9},{13,12},{14,13},{17,16},{18,1... | collective-permute-start | bytes 786440 | tf_op jit(solution)/shard_map/ppermute | solution.py:21
  52.8 24.4 %collective-permute-start.22 = (f32[64,1024]{1,0:T(8,128)S(1)}, f32[64,1024]{1,0:T(8,128)S(1)}, u32[]{:S(2)}, u32[]{:S(2)}) collective-permute-start(f32[64,1024]{1,0:T(8,128)S(1)} %collective-permute-done.21), channel_id=1, source_target_pairs={{1,0},{2,1},{5,4},{6,5},{9,8},{10,9},{13,12},{14,13},{17,16},{18,1... | collective-permute-start | bytes 786440 | tf_op jit(solution)/shard_map/ppermute | solution.py:21
  54.1 24.4 %collective-permute-start.20 = (f32[64,1024]{1,0:T(8,128)S(1)}, f32[64,1024]{1,0:T(8,128)S(1)}, u32[]{:S(2)}, u32[]{:S(2)}) collective-permute-start(f32[64,1024]{1,0:T(8,128)S(1)} %collective-permute-done.19), channel_id=1, source_target_pairs={{2,3},{6,7},{10,11},{14,15},{18,19},{22,23},{26,27},{30,31}} | collective-permute-start | bytes 786440 | tf_op jit(solution)/shard_map/ppermute | solution.py:20
  60.4 19.5 %collective-permute-start.2 = (f32[64,1024]{1,0:T(8,128)S(1)}, f32[64,1024]{1,0:T(8,128)S(1)}, u32[]{:S(2)}, u32[]{:S(2)}) collective-permute-start(f32[64,1024]{1,0:T(8,128)S(1)} %collective-permute-done.1), channel_id=1, source_target_pairs={{2,3},{6,7},{10,11},{14,15},{18,19},{22,23},{26,27},{30,31}} | collective-permute-start | bytes 786440 | tf_op jit(solution)/shard_map/ppermute | solution.py:20
  66.0 16.9 %collective-permute-start.5 = (f32[64,1024]{1,0:T(8,128)S(1)}, f32[64,1024]{1,0:T(8,128)S(1)}, u32[]{:S(2)}, u32[]{:S(2)}) collective-permute-start(f32[64,1024]{1,0:T(8,128)S(1)} %collective-permute-done.4), channel_id=1, source_target_pairs={{1,0},{5,4},{9,8},{13,12},{17,16},{21,20},{25,24},{29,28}} | collective-permute-start | bytes 786440 | tf_op jit(solution)/shard_map/ppermute | solution.py:21
  71.6 16.9 %collective-permute-start.11 = (f32[64,1024]{1,0:T(8,128)S(1)}, f32[64,1024]{1,0:T(8,128)S(1)}, u32[]{:S(2)}, u32[]{:S(2)}) collective-permute-start(f32[64,1024]{1,0:T(8,128)S(1)} %collective-permute-done.10), channel_id=1, source_target_pairs={{1,0},{5,4},{9,8},{13,12},{17,16},{21,20},{25,24},{29,28}} | collective-permute-start | bytes 786440 | tf_op jit(solution)/shard_map/ppermute | solution.py:21
  77.2 16.0 %collective-permute-start.17 = (f32[64,1024]{1,0:T(8,128)S(1)}, f32[64,1024]{1,0:T(8,128)S(1)}, u32[]{:S(2)}, u32[]{:S(2)}) collective-permute-start(f32[64,1024]{1,0:T(8,128)S(1)} %collective-permute-done.16), channel_id=1, source_target_pairs={{1,0},{5,4},{9,8},{13,12},{17,16},{21,20},{25,24},{29,28}} | collective-permute-start | bytes 786440 | tf_op jit(solution)/shard_map/ppermute | solution.py:21
  78.5 17.5 %collective-permute-start.23 = (f32[64,1024]{1,0:T(8,128)S(1)}, f32[64,1024]{1,0:T(8,128)S(1)}, u32[]{:S(2)}, u32[]{:S(2)}) collective-permute-start(f32[64,1024]{1,0:T(8,128)S(1)} %collective-permute-done.22), channel_id=1, source_target_pairs={{1,0},{5,4},{9,8},{13,12},{17,16},{21,20},{25,24},{29,28}} | collective-permute-start | bytes 786440 | tf_op jit(solution)/shard_map/ppermute | solution.py:21
  135.0 13.5 %collective-permute-start.30 = (f32[1024,64]{0,1:T(8,128)S(1)}, f32[1024,64]{0,1:T(8,128)S(1)}, u32[]{:S(2)}, u32[]{:S(2)}) collective-permute-start(f32[1024,64]{0,1:T(8,128)S(1)} %fusion.30), channel_id=1, source_target_pairs={{4,0},{5,1},{6,2},{7,3}} | collective-permute-start | bytes 786440 | tf_op jit(solution)/shard_map/ppermute | solution.py:56
  138.3 13.6 %collective-permute-start.37 = (f32[1024,64]{0,1:T(8,128)S(1)}, f32[1024,64]{0,1:T(8,128)S(1)}, u32[]{:S(2)}, u32[]{:S(2)}) collective-permute-start(f32[1024,64]{0,1:T(8,128)S(1)} %fusion.31), channel_id=1, source_target_pairs={{4,0},{5,1},{6,2},{7,3}} | collective-permute-start | bytes 786440 | tf_op jit(solution)/shard_map/ppermute | solution.py:56
  156.5 26.2 %collective-permute-start.39 = (f32[512,128]{0,1:T(8,128)S(1)}, f32[512,128]{0,1:T(8,128)S(1)}, u32[]{:S(2)}, u32[]{:S(2)}) collective-permute-start(f32[512,128]{0,1:T(8,128)S(1)} %pad_maximum_fusion.4), channel_id=1, source_target_pairs={{0,2},{1,3},{2,0},{3,1},{4,6},{5,7},{6,4},{7,5},{8,10},{9,11},{10,... | collective-permute-start | bytes 786440 | tf_op jit(solution)/shard_map/ppermute | solution.py:68
  159.4 23.3 %collective-permute-start.40 = (f32[512,128]{0,1:T(8,128)S(1)}, f32[512,128]{0,1:T(8,128)S(1)}, u32[]{:S(2)}, u32[]{:S(2)}) collective-permute-start(f32[512,128]{0,1:T(8,128)S(1)} %pad_maximum_fusion.5), channel_id=1, source_target_pairs={{0,1},{1,2},{2,3},{3,0},{4,5},{5,6},{6,7},{7,4},{8,9},{9,10},{10,1... | collective-permute-start | bytes 786440 | tf_op jit(solution)/shard_map/ppermute | solution.py:68
  (24 other events, 134.8 us)

commit v12 on v9

--- a/solution.py
+++ b/solution.py
@@ -42,7 +42,7 @@
     rows_id = lax.broadcasted_iota(jnp.int32, (state_dim, width), 0)
     cols_id = lax.broadcasted_iota(jnp.int32, (state_dim, width), 1) + place * width
     identity_cols = (rows_id == cols_id).astype(jnp.float32)
-    incoming = jnp.concatenate([identity_cols, terminal_cost.T], axis=0)
+    incoming = lax.optimization_barrier(jnp.concatenate([identity_cols, terminal_cost.T], axis=0))
 
     step = width // CHUNKS
     incoming = [incoming[:, j * step:(j + 1) * step] for j in range(CHUNKS)]

time: 179 us -> 179 us (level)
  waiting for transfers between devices: 81.8 us -> 77.9 us
    ppermute x6, waiting for transfers between devices: 38.3 us -> 34.4 us  [line_gather(): lax.ppermute(leftward, 'row', [(z, z - 1) for z in range(1, count - t + 1)])]
  transfers between devices with their start and end apart: 30 -> 30, of which waited for: 12 -> 12; matrix products, arithmetic and copies ran while one was open for 17% -> 19% of each run, Pallas kernels for 0% -> 0%
where the time goes in v12:
time: 179 us; the launch traced here: 178 us
  waiting for transfers between devices  77.9 us (44%)
  starting transfers between devices  43.7 us (24%)
  matrix products  41.5 us (23%)
  local copies, waits for them, and re-layouts  10.6 us (6%)
  other arithmetic  2.82 us (2%)
    dot_general x18, matrix products, product(): jnp.dot(left, right, precision=lax.Precision.HIGH, preferred_element_type...  41.5 us
    ppermute x6, waiting for transfers between devices, line_gather(): lax.ppermute(leftward, 'row', [(z, z - 1) for z in range(1, count - t + 1)])  34.4 us
    ppermute x3, waiting for transfers between devices, body(): lax.ppermute(payload, 'row', [(z, (z + d) % count) for z in range(count)])  17 us
    ppermute x6, waiting for transfers between devices, line_gather(): lax.ppermute(rightward, 'row', [(z, z + 1) for z in range(t - 1, count -...  14.8 us
    ppermute x6, starting transfers between devices, line_gather(): lax.ppermute(rightward, 'row', [(z, z + 1) for z in range(t - 1, count -...  14.4 us
    ppermute x14, starting transfers between devices, body(): got = lax.ppermute(fresh, 'tm', [(k, k - 1)])  11.1 us
    ppermute x14, waiting for transfers between devices, body(): got = lax.ppermute(fresh, 'tm', [(k, k - 1)])  10 us
    unnamed x26, local copies, waits for them, and re-layouts  7.84 us
  transfers between devices with their start and end apart: 30, of which 12 were waited for; matrix products, arithmetic and copies ran while one was open for 19% of the time, Pallas kernels for 0%

profile of v12, /device:TPU:0, one launch (start us, length us, event | category | flops | bytes accessed | tf_op | source)
XLA Modules:
  0.0 177.9 jit_solution(14045855209302423167)
XLA Ops:
  2.0 5.1 %collective-permute-start = (f32[128,1024]{1,0:T(8,128)S(1)}, f32[128,1024]{1,0:T(8,128)S(1)}, u32[]{:S(2)}, u32[]{:S(2)}) collective-permute-start(f32[128,1024]{1,0:T(8,128)S(1)} %get-tuple-element.4), channel_id=1, source_target_pairs={{0,1},{1,2},{2,3},{4,5},{5,6},{6,7},{8,9},{9,10},{10,11},{12,13},{... | collective-permute-start | bytes 1572872 | tf_op jit(solution)/shard_map/ppermute | solution.py:19
  7.1 3.5 %collective-permute-start.6 = (f32[128,1024]{1,0:T(8,128)S(1)}, f32[128,1024]{1,0:T(8,128)S(1)}, u32[]{:S(2)}, u32[]{:S(2)}) collective-permute-start(f32[128,1024]{1,0:T(8,128)S(1)} %get-tuple-element.5), channel_id=1, source_target_pairs={{0,1},{1,2},{2,3},{4,5},{5,6},{6,7},{8,9},{9,10},{10,11},{12,13},{... | collective-permute-start | bytes 1572872 | tf_op jit(solution)/shard_map/ppermute | solution.py:19
  13.2 6.2 %collective-permute-done = f32[128,1024]{1,0:T(8,128)S(1)} collective-permute-done((f32[128,1024]{1,0:T(8,128)S(1)}, f32[128,1024]{1,0:T(8,128)S(1)}, u32[]{:S(2)}, u32[]{:S(2)}) %collective-permute-start) | collective-permute-done | bytes 524320 | tf_op jit(solution)/shard_map/ppermute | solution.py:19
  20.8 8.7 %collective-permute-done.6 = f32[128,1024]{1,0:T(8,128)S(1)} collective-permute-done((f32[128,1024]{1,0:T(8,128)S(1)}, f32[128,1024]{1,0:T(8,128)S(1)}, u32[]{:S(2)}, u32[]{:S(2)}) %collective-permute-start.6) | collective-permute-done | bytes 524320 | tf_op jit(solution)/shard_map/ppermute | solution.py:19
  32.2 4.6 %collective-permute-done.3 = f32[128,1024]{1,0:T(8,128)S(1)} collective-permute-done((f32[128,1024]{1,0:T(8,128)S(1)}, f32[128,1024]{1,0:T(8,128)S(1)}, u32[]{:S(2)}, u32[]{:S(2)}) %collective-permute-start.3) | collective-permute-done | bytes 524320 | tf_op jit(solution)/shard_map/ppermute | solution.py:20
  42.2 9.9 %collective-permute-done.10 = f32[128,1024]{1,0:T(8,128)} collective-permute-done((f32[128,1024]{1,0:T(8,128)S(1)}, f32[128,1024]{1,0:T(8,128)}, u32[]{:S(2)}, u32[]{:S(2)}) %collective-permute-start.10) | collective-permute-done | bytes 524320 | tf_op jit(solution)/shard_map/ppermute | solution.py:20
  53.4 9.6 %collective-permute-done.4 = f32[128,1024]{1,0:T(8,128)} collective-permute-done((f32[128,1024]{1,0:T(8,128)S(1)}, f32[128,1024]{1,0:T(8,128)}, u32[]{:S(2)}, u32[]{:S(2)}) %collective-permute-start.4) | collective-permute-done | bytes 524320 | tf_op jit(solution)/shard_map/ppermute | solution.py:20
  74.3 8.3 %collective-permute-done.5 = f32[128,1024]{1,0:T(8,128)S(1)} collective-permute-done((f32[128,1024]{1,0:T(8,128)}, f32[128,1024]{1,0:T(8,128)S(1)}, u32[]{:S(2)}, u32[]{:S(2)}) %collective-permute-start.5) | collective-permute-done | bytes 524320 | tf_op jit(solution)/shard_map/ppermute | solution.py:20
  89.0 4.4 %fusion.44 = f32[1024,64]{0,1:T(8,128)S(1)} fusion(f32[1024,1024]{1,0:T(8,128)} %bitcast.83, f32[1024,64]{0,1:T(8,128)S(1)} %get-tuple-element.22), kind=kOutput, calls=%fused_computation.107 | convolution fusion | flops 402653184 | bytes 4718592 | tf_op jit(solution)/shard_map/dot_general | solution.py:10
  94.1 2.0 %fusion.41 = f32[1024,64]{0,1:T(8,128)S(1)} fusion(f32[1024,1024]{1,0:T(8,128)S(1)} %bitcast.84, f32[1024,64]{0,1:T(8,128)S(1)} %get-tuple-element.21), kind=kOutput, calls=%fused_computation.104 | convolution fusion | flops 402653184 | bytes 4718592 | tf_op jit(solution)/shard_map/dot_general | solution.py:10
  96.8 2.0 %fusion.38 = f32[1024,64]{0,1:T(8,128)S(1)} fusion(f32[1024,1024]{1,0:T(8,128)S(1)} %bitcast.85, f32[1024,64]{0,1:T(8,128)S(1)} %collective-permute-done.20, f32[1024,64]{0,1:T(8,128)S(1)} %get-tuple-element.22, pred[]{:T(512)S(6)} %eq.131), kind=kOutput, calls=%fused_computation.76 | convolution fusion | flops 402718720 | bytes 4980737 | tf_op jit(solution)/shard_map/dot_general | solution.py:10
  99.7 2.0 %fusion.37 = f32[1024,64]{0,1:T(8,128)S(1)} fusion(f32[1024,1024]{1,0:T(8,128)S(1)} %bitcast.86, f32[1024,64]{0,1:T(8,128)S(1)} %collective-permute-done.13, f32[1024,64]{0,1:T(8,128)S(1)} %get-tuple-element.21, pred[]{:T(512)S(6)} %eq.131), kind=kOutput, calls=%fused_computation.75 | convolution fusion | flops 402718720 | bytes 4980737 | tf_op jit(solution)/shard_map/dot_general | solution.py:10
  102.5 2.0 %fusion.45 = f32[1024,64]{0,1:T(8,128)S(1)} fusion(f32[1024,1024]{1,0:T(8,128)S(1)} %bitcast.87, f32[1024,64]{0,1:T(8,128)S(1)} %broadcast_select_fusion.2), kind=kOutput, calls=%fused_computation.108 | convolution fusion | flops 402653184 | bytes 4718592 | tf_op jit(solution)/shard_map/dot_general | solution.py:10
  108.0 2.0 %fusion.36 = f32[1024,64]{0,1:T(8,128)S(1)} fusion(f32[1024,1024]{1,0:T(8,128)S(1)} %bitcast.89, f32[1024,64]{0,1:T(8,128)S(1)} %collective-permute-done.22, f32[1024,64]{0,1:T(8,128)S(1)} %broadcast_select_fusion.2, pred[]{:T(512)S(6)} %eq.129), kind=kOutput, calls=%fused_computation.74 | convolution fusion | flops 402718720 | bytes 4980737 | tf_op jit(solution)/shard_map/dot_general | solution.py:10
  110.8 2.0 %fusion.35 = f32[1024,64]{0,1:T(8,128)S(1)} fusion(f32[1024,1024]{1,0:T(8,128)S(1)} %bitcast.90, f32[1024,64]{0,1:T(8,128)S(1)} %collective-permute-done.15, f32[1024,64]{0,1:T(8,128)S(1)} %broadcast_select_fusion.3, pred[]{:T(512)S(6)} %eq.129), kind=kOutput, calls=%fused_computation.73 | convolution fusion | flops 402718720 | bytes 4980737 | tf_op jit(solution)/shard_map/dot_general | solution.py:10
  125.9 8.5 %collective-permute-done.25 = f32[1024,64]{0,1:T(8,128)S(1)} collective-permute-done((f32[1024,64]{0,1:T(8,128)S(1)}, f32[1024,64]{0,1:T(8,128)S(1)}, u32[]{:S(2)}, u32[]{:S(2)}) %collective-permute-start.25) | collective-permute-done | bytes 262176 | tf_op jit(solution)/shard_map/ppermute | solution.py:55
  134.4 2.0 %convolution_select_fusion = f32[1024,64]{0,1:T(8,128)S(1)} fusion(f32[1024,1024]{1,0:T(8,128)S(1)} %bitcast.95, f32[1024,64]{0,1:T(8,128)S(1)} %fusion.34, f32[1024,64]{0,1:T(8,128)S(1)} %fusion.46, f32[1024,64]{0,1:T(8,128)S(1)} %fusion.36, f32[1024,64]{0,1:T(8,128)S(1)} %fusion.45, f32[1024,64]{0,1:T(8,128)S(1)} %fusion.38, f32[1024,64]{0,1:T(8,128)S(1)} %fusion.44, ...), kind=kOutput, calls=%fused_computation.3 | convolution fusion | flops 403243008 | bytes 7077895 | tf_op jit(solution)/shard_map/dot_general | solution.py:10
  138.0 2.0 %convolution_select_fusion.1 = f32[1024,64]{0,1:T(8,128)S(1)} fusion(f32[1024,1024]{1,0:T(8,128)S(1)} %bitcast.96, f32[1024,64]{0,1:T(8,128)S(1)} %fusion.33, f32[1024,64]{0,1:T(8,128)S(1)} %fusion.43, f32[1024,64]{0,1:T(8,128)S(1)} %fusion.35, f32[1024,64]{0,1:T(8,128)S(1)} %fusion.42, f32[1024,64]{0,1:T(8,128)S(1)} %fusion.37, f32[1024,64]{0,1:T(8,128)S(1)} %fusion.41, ...), kind=kOutput, calls=%fused_computation.4 | convolution fusion | flops 403243008 | bytes 7077895 | tf_op jit(solution)/shard_map/dot_general | solution.py:10
  143.2 2.4 %collective-permute-start.26 = (f32[512,128]{0,1:T(8,128)S(1)}, f32[512,128]{0,1:T(8,128)S(1)}, u32[]{:S(2)}, u32[]{:S(2)}) collective-permute-start(f32[512,128]{0,1:T(8,128)S(1)} %pad_maximum_fusion.3), channel_id=1, source_target_pairs={{0,3},{1,0},{2,1},{3,2},{4,7},{5,4},{6,5},{7,6},{8,11},{9,8},{10,9... | collective-permute-start | bytes 786440 | tf_op jit(solution)/shard_map/ppermute | solution.py:67
  145.6 6.7 %collective-permute-done.28 = f32[512,128]{0,1:T(8,128)S(1)} collective-permute-done((f32[512,128]{0,1:T(8,128)S(1)}, f32[512,128]{0,1:T(8,128)S(1)}, u32[]{:S(2)}, u32[]{:S(2)}) %collective-permute-start.28) | collective-permute-done | bytes 262176 | tf_op jit(solution)/shard_map/ppermute | solution.py:67
  152.3 10.3 %collective-permute-done.27 = f32[512,128]{0,1:T(8,128)S(1)} collective-permute-done((f32[512,128]{0,1:T(8,128)S(1)}, f32[512,128]{0,1:T(8,128)S(1)}, u32[]{:S(2)}, u32[]{:S(2)}) %collective-permute-start.27) | collective-permute-done | bytes 262176 | tf_op jit(solution)/shard_map/ppermute | solution.py:67
  162.8 4.3 %fusion.1 = f32[256,2048]{1,0:T(8,128)S(1)} fusion(f32[512,2048]{1,0:T(8,128)} %param.5, f32[256,128]{0,1:T(8,128)S(1)} %get-tuple-element.13, f32[256,128]{0,1:T(8,128)S(1)} %get-tuple-element.11, f32[256,128]{0,1:T(8,128)S(1)} %get-tuple-element.10, f32[256,128]{0,1:T(8,128)S(1)} %get-tuple-element.9), kind=kOutput, calls=%fused_computation.7 | convolution fusion | flops 1611005952 | bytes 6815744 | tf_op jit(solution)/shard_map/dot_general | solution.py:10
  167.2 2.2 %fusion = f32[2048]{0:T(1024)S(1)} fusion(f32[256,2048]{1,0:T(8,128)S(1)} %fusion.1, f32[512,2048]{1,0:T(8,128)S(1)} %copy-done.2, f32[256,128]{0,1:T(8,128)S(1)} %get-tuple-element.12, f32[256,128]{0,1:T(8,128)S(1)} %get-tuple-element.8, f32[256,128]{0,1:T(8,128)S(1)} %get-tuple-element.7, f32[256,128]{0,1:T(8,128)S(1)} %get-tuple-element.6), kind=kOutput, calls=%fused_computation.2 | convolution fusion | flops 1612052480 | bytes 6823936 | tf_op jit(solution)/shard_map/dot_general | solution.py:10
  169.5 6.2 %collective-permute-start.29 = (f32[512]{0:T(512)S(1)}, f32[512]{0:T(512)S(1)}, u32[]{:S(2)}, u32[]{:S(2)}) collective-permute-start(f32[512]{0:T(512)S(1)} %dynamic_slice.44), channel_id=1, source_target_pairs={{0,1},{1,0},{2,3},{3,2},{4,5},{5,4},{6,7},{7,6},{8,9},{9,8},{10,11... | collective-permute-start | bytes 6152 | tf_op jit(solution)/shard_map/ppermute | solution.py:88
  (105 shorter events, 59.3 us)
Async XLA Ops:
  2.0 17.4 %collective-permute-start = (f32[128,1024]{1,0:T(8,128)S(1)}, f32[128,1024]{1,0:T(8,128)S(1)}, u32[]{:S(2)}, u32[]{:S(2)}) collective-permute-start(f32[128,1024]{1,0:T(8,128)S(1)} %get-tuple-element.4), channel_id=1, source_target_pairs={{0,1},{1,2},{2,3},{4,5},{5,6},{6,7},{8,9},{9,10},{10,11},{12,13},{... | collective-permute-start | bytes 1572872 | tf_op jit(solution)/shard_map/ppermute | solution.py:19
  7.1 22.4 %collective-permute-start.6 = (f32[128,1024]{1,0:T(8,128)S(1)}, f32[128,1024]{1,0:T(8,128)S(1)}, u32[]{:S(2)}, u32[]{:S(2)}) collective-permute-start(f32[128,1024]{1,0:T(8,128)S(1)} %get-tuple-element.5), channel_id=1, source_target_pairs={{0,1},{1,2},{2,3},{4,5},{5,6},{6,7},{8,9},{9,10},{10,11},{12,13},{... | collective-permute-start | bytes 1572872 | tf_op jit(solution)/shard_map/ppermute | solution.py:19
  10.6 20.3 %collective-permute-start.9 = (f32[128,1024]{1,0:T(8,128)S(1)}, f32[128,1024]{1,0:T(8,128)S(1)}, u32[]{:S(2)}, u32[]{:S(2)}) collective-permute-start(f32[128,1024]{1,0:T(8,128)S(1)} %get-tuple-element.5), channel_id=1, source_target_pairs={{1,0},{2,1},{3,2},{5,4},{6,5},{7,6},{9,8},{10,9},{11,10},{13,12},{... | collective-permute-start | bytes 1572872 | tf_op jit(solution)/shard_map/ppermute | solution.py:20
  11.9 24.9 %collective-permute-start.3 = (f32[128,1024]{1,0:T(8,128)S(1)}, f32[128,1024]{1,0:T(8,128)S(1)}, u32[]{:S(2)}, u32[]{:S(2)}) collective-permute-start(f32[128,1024]{1,0:T(8,128)S(1)} %get-tuple-element.4), channel_id=1, source_target_pairs={{1,0},{2,1},{3,2},{5,4},{6,5},{7,6},{9,8},{10,9},{11,10},{13,12},{... | collective-permute-start | bytes 1572872 | tf_op jit(solution)/shard_map/ppermute | solution.py:20
  19.3 18.8 %collective-permute-start.1 = (f32[128,1024]{1,0:T(8,128)S(1)}, f32[128,1024]{1,0:T(8,128)}, u32[]{:S(2)}, u32[]{:S(2)}) collective-permute-start(f32[128,1024]{1,0:T(8,128)S(1)} %collective-permute-done), channel_id=1, source_target_pairs={{1,2},{2,3},{5,6},{6,7},{9,10},{10,11},{13,14},{14,15},{17,18},{18... | collective-permute-start | bytes 1572872 | tf_op jit(solution)/shard_map/ppermute | solution.py:19
  29.4 10.2 %collective-permute-start.7 = (f32[128,1024]{1,0:T(8,128)S(1)}, f32[128,1024]{1,0:T(8,128)}, u32[]{:S(2)}, u32[]{:S(2)}) collective-permute-start(f32[128,1024]{1,0:T(8,128)S(1)} %collective-permute-done.6), channel_id=1, source_target_pairs={{1,2},{2,3},{5,6},{6,7},{9,10},{10,11},{13,14},{14,15},{17,18},{18... | collective-permute-start | bytes 1572872 | tf_op jit(solution)/shard_map/ppermute | solution.py:19
  30.9 21.2 %collective-permute-start.10 = (f32[128,1024]{1,0:T(8,128)S(1)}, f32[128,1024]{1,0:T(8,128)}, u32[]{:S(2)}, u32[]{:S(2)}) collective-permute-start(f32[128,1024]{1,0:T(8,128)S(1)} %collective-permute-done.9), channel_id=1, source_target_pairs={{1,0},{2,1},{5,4},{6,5},{9,8},{10,9},{13,12},{14,13},{17,16},{18,1... | collective-permute-start | bytes 1572872 | tf_op jit(solution)/shard_map/ppermute | solution.py:20
  36.8 26.1 %collective-permute-start.4 = (f32[128,1024]{1,0:T(8,128)S(1)}, f32[128,1024]{1,0:T(8,128)}, u32[]{:S(2)}, u32[]{:S(2)}) collective-permute-start(f32[128,1024]{1,0:T(8,128)S(1)} %collective-permute-done.3), channel_id=1, source_target_pairs={{1,0},{2,1},{5,4},{6,5},{9,8},{10,9},{13,12},{14,13},{17,16},{18,1... | collective-permute-start | bytes 1572872 | tf_op jit(solution)/shard_map/ppermute | solution.py:20
  38.1 26.1 %collective-permute-start.2 = (f32[128,1024]{1,0:T(8,128)}, f32[128,1024]{1,0:T(8,128)}, u32[]{:S(2)}, u32[]{:S(2)}) collective-permute-start(f32[128,1024]{1,0:T(8,128)} %collective-permute-done.1), channel_id=1, source_target_pairs={{2,3},{6,7},{10,11},{14,15},{18,19},{22,23},{26,27},{30,31}} | collective-permute-start | bytes 1572872 | tf_op jit(solution)/shard_map/ppermute | solution.py:19
  39.6 27.9 %collective-permute-start.8 = (f32[128,1024]{1,0:T(8,128)}, f32[128,1024]{1,0:T(8,128)}, u32[]{:S(2)}, u32[]{:S(2)}) collective-permute-start(f32[128,1024]{1,0:T(8,128)} %collective-permute-done.7), channel_id=1, source_target_pairs={{2,3},{6,7},{10,11},{14,15},{18,19},{22,23},{26,27},{30,31}} | collective-permute-start | bytes 1572872 | tf_op jit(solution)/shard_map/ppermute | solution.py:19
  52.1 22.0 %collective-permute-start.11 = (f32[128,1024]{1,0:T(8,128)}, f32[128,1024]{1,0:T(8,128)S(1)}, u32[]{:S(2)}, u32[]{:S(2)}) collective-permute-start(f32[128,1024]{1,0:T(8,128)} %collective-permute-done.10), channel_id=1, source_target_pairs={{1,0},{5,4},{9,8},{13,12},{17,16},{21,20},{25,24},{29,28}} | collective-permute-start | bytes 1572872 | tf_op jit(solution)/shard_map/ppermute | solution.py:20
  62.9 19.6 %collective-permute-start.5 = (f32[128,1024]{1,0:T(8,128)}, f32[128,1024]{1,0:T(8,128)S(1)}, u32[]{:S(2)}, u32[]{:S(2)}) collective-permute-start(f32[128,1024]{1,0:T(8,128)} %collective-permute-done.4), channel_id=1, source_target_pairs={{1,0},{5,4},{9,8},{13,12},{17,16},{21,20},{25,24},{29,28}} | collective-permute-start | bytes 1572872 | tf_op jit(solution)/shard_map/ppermute | solution.py:20
  96.1 3.6 %collective-permute-start.13 = (f32[1024,64]{0,1:T(8,128)S(1)}, f32[1024,64]{0,1:T(8,128)S(1)}, u32[]{:S(2)}, u32[]{:S(2)}) collective-permute-start(f32[1024,64]{0,1:T(8,128)S(1)} %fusion.41), channel_id=1, source_target_pairs={{24,20},{25,21},{26,22},{27,23}} | collective-permute-start | bytes 786440 | tf_op jit(solution)/shard_map/ppermute | solution.py:55
  98.9 3.6 %collective-permute-start.21 = (f32[1024,64]{0,1:T(8,128)S(1)}, f32[1024,64]{0,1:T(8,128)S(1)}, u32[]{:S(2)}, u32[]{:S(2)}) collective-permute-start(f32[1024,64]{0,1:T(8,128)S(1)} %fusion.38), channel_id=1, source_target_pairs={{20,16},{21,17},{22,18},{23,19}} | collective-permute-start | bytes 786440 | tf_op jit(solution)/shard_map/ppermute | solution.py:55
  101.8 3.5 %collective-permute-start.14 = (f32[1024,64]{0,1:T(8,128)S(1)}, f32[1024,64]{0,1:T(8,128)S(1)}, u32[]{:S(2)}, u32[]{:S(2)}) collective-permute-start(f32[1024,64]{0,1:T(8,128)S(1)} %fusion.37), channel_id=1, source_target_pairs={{20,16},{21,17},{22,18},{23,19}} | collective-permute-start | bytes 786440 | tf_op jit(solution)/shard_map/ppermute | solution.py:55
  104.6 3.5 %collective-permute-start.22 = (f32[1024,64]{0,1:T(8,128)S(1)}, f32[1024,64]{0,1:T(8,128)S(1)}, u32[]{:S(2)}, u32[]{:S(2)}) collective-permute-start(f32[1024,64]{0,1:T(8,128)S(1)} %fusion.45), channel_id=1, source_target_pairs={{16,12},{17,13},{18,14},{19,15}} | collective-permute-start | bytes 786440 | tf_op jit(solution)/shard_map/ppermute | solution.py:55
  115.6 3.7 %collective-permute-start.24 = (f32[1024,64]{0,1:T(8,128)S(1)}, f32[1024,64]{0,1:T(8,128)S(1)}, u32[]{:S(2)}, u32[]{:S(2)}) collective-permute-start(f32[1024,64]{0,1:T(8,128)S(1)} %fusion.46), channel_id=1, source_target_pairs={{8,4},{9,5},{10,6},{11,7}} | collective-permute-start | bytes 786440 | tf_op jit(solution)/shard_map/ppermute | solution.py:55
  118.3 4.2 %collective-permute-start.17 = (f32[1024,64]{0,1:T(8,128)S(1)}, f32[1024,64]{0,1:T(8,128)S(1)}, u32[]{:S(2)}, u32[]{:S(2)}) collective-permute-start(f32[1024,64]{0,1:T(8,128)S(1)} %fusion.43), channel_id=1, source_target_pairs={{8,4},{9,5},{10,6},{11,7}} | collective-permute-start | bytes 786440 | tf_op jit(solution)/shard_map/ppermute | solution.py:55
  121.3 13.2 %collective-permute-start.25 = (f32[1024,64]{0,1:T(8,128)S(1)}, f32[1024,64]{0,1:T(8,128)S(1)}, u32[]{:S(2)}, u32[]{:S(2)}) collective-permute-start(f32[1024,64]{0,1:T(8,128)S(1)} %fusion.34), channel_id=1, source_target_pairs={{4,0},{5,1},{6,2},{7,3}} | collective-permute-start | bytes 786440 | tf_op jit(solution)/shard_map/ppermute | solution.py:55
  124.6 13.4 %collective-permute-start.18 = (f32[1024,64]{0,1:T(8,128)S(1)}, f32[1024,64]{0,1:T(8,128)S(1)}, u32[]{:S(2)}, u32[]{:S(2)}) collective-permute-start(f32[1024,64]{0,1:T(8,128)S(1)} %fusion.33), channel_id=1, source_target_pairs={{4,0},{5,1},{6,2},{7,3}} | collective-permute-start | bytes 786440 | tf_op jit(solution)/shard_map/ppermute | solution.py:55
  141.2 11.1 %collective-permute-start.28 = (f32[512,128]{0,1:T(8,128)S(1)}, f32[512,128]{0,1:T(8,128)S(1)}, u32[]{:S(2)}, u32[]{:S(2)}) collective-permute-start(f32[512,128]{0,1:T(8,128)S(1)} %pad_maximum_fusion.5), channel_id=1, source_target_pairs={{0,1},{1,2},{2,3},{3,0},{4,5},{5,6},{6,7},{7,4},{8,9},{9,10},{10,1... | collective-permute-start | bytes 786440 | tf_op jit(solution)/shard_map/ppermute | solution.py:67
  141.3 21.3 %collective-permute-start.27 = (f32[512,128]{0,1:T(8,128)S(1)}, f32[512,128]{0,1:T(8,128)S(1)}, u32[]{:S(2)}, u32[]{:S(2)}) collective-permute-start(f32[512,128]{0,1:T(8,128)S(1)} %pad_maximum_fusion.4), channel_id=1, source_target_pairs={{0,2},{1,3},{2,0},{3,1},{4,6},{5,7},{6,4},{7,5},{8,10},{9,11},{10,... | collective-permute-start | bytes 786440 | tf_op jit(solution)/shard_map/ppermute | solution.py:67
  143.2 19.4 %collective-permute-start.26 = (f32[512,128]{0,1:T(8,128)S(1)}, f32[512,128]{0,1:T(8,128)S(1)}, u32[]{:S(2)}, u32[]{:S(2)}) collective-permute-start(f32[512,128]{0,1:T(8,128)S(1)} %pad_maximum_fusion.3), channel_id=1, source_target_pairs={{0,3},{1,0},{2,1},{3,2},{4,7},{5,4},{6,5},{7,6},{8,11},{9,8},{10,9... | collective-permute-start | bytes 786440 | tf_op jit(solution)/shard_map/ppermute | solution.py:67
  169.5 7.8 %collective-permute-start.29 = (f32[512]{0:T(512)S(1)}, f32[512]{0:T(512)S(1)}, u32[]{:S(2)}, u32[]{:S(2)}) collective-permute-start(f32[512]{0:T(512)S(1)} %dynamic_slice.44), channel_id=1, source_target_pairs={{0,1},{1,0},{2,3},{3,2},{4,5},{5,4},{6,7},{7,6},{8,9},{9,8},{10,11... | collective-permute-start | bytes 6152 | tf_op jit(solution)/shard_map/ppermute | solution.py:88
  (12 other events, 130.2 us)

commit v13 on v9

--- a/solution.py
+++ b/solution.py
@@ -77,8 +77,9 @@
             ordered.append(picked)
         return jnp.concatenate(ordered, axis=1)
 
-    rows_traj = product(in_order(main_pieces), terminal_states)
-    pair_traj = product(in_order(pair_pieces), terminal_states)
+    both_traj = product(jnp.concatenate([in_order(main_pieces), in_order(pair_pieces)], axis=0), terminal_states)
+    rows_traj = both_traj[:rows]
+    pair_traj = both_traj[rows:]
     partial = jnp.sum(rows_traj * pair_traj, axis=0)
     cols = terminal_states.shape[1] // count
     total = lax.dynamic_slice_in_dim(partial, place * cols, cols, 0)

time: 179 us -> 180 us (level)
    dot_general x18 -> x17, matrix products: 41.5 us -> 40.3 us  [product(): jnp.dot(left, right, precision=lax.Precision.HIGH, preferred_element_type...]
    unnamed x26 -> x22, local copies, waits for them, and re-layouts: 6.11 us -> 6.1 us
where the time goes in v13:
time: 180 us; the launch traced here: 179 us
  waiting for transfers between devices  82.1 us (46%)
  starting transfers between devices  42.5 us (24%)
  matrix products  40.3 us (22%)
  local copies, waits for them, and re-layouts  8.98 us (5%)
  other arithmetic  3.54 us (2%)
    dot_general x17, matrix products, product(): jnp.dot(left, right, precision=lax.Precision.HIGH, preferred_element_type...  40.3 us
    ppermute x6, waiting for transfers between devices, line_gather(): lax.ppermute(leftward, 'row', [(z, z - 1) for z in range(1, count - t + 1)])  38.3 us
    ppermute x3, waiting for transfers between devices, body(): lax.ppermute(payload, 'row', [(z, (z + d) % count) for z in range(count)])  17.3 us
    ppermute x6, waiting for transfers between devices, line_gather(): lax.ppermute(rightward, 'row', [(z, z + 1) for z in range(t - 1, count -...  14.8 us
    ppermute x6, starting transfers between devices, line_gather(): lax.ppermute(rightward, 'row', [(z, z + 1) for z in range(t - 1, count -...  13.6 us
    ppermute x14, starting transfers between devices, body(): got = lax.ppermute(fresh, 'tm', [(k, k - 1)])  11.1 us
    ppermute x14, waiting for transfers between devices, body(): got = lax.ppermute(fresh, 'tm', [(k, k - 1)])  10.1 us
    ppermute x6, starting transfers between devices, line_gather(): lax.ppermute(leftward, 'row', [(z, z - 1) for z in range(1, count - t + 1)])  7.71 us
  transfers between devices with their start and end apart: 30, of which 12 were waited for; matrix products, arithmetic and copies ran while one was open for 17% of the time, Pallas kernels for 0%

profile of v13, /device:TPU:0, one launch (start us, length us, event | category | flops | bytes accessed | tf_op | source)
XLA Modules:
  0.0 178.7 jit_solution(10811789038616479353)
XLA Ops:
  2.0 5.0 %collective-permute-start = (f32[128,1024]{1,0:T(8,128)S(1)}, f32[128,1024]{1,0:T(8,128)S(1)}, u32[]{:S(2)}, u32[]{:S(2)}) collective-permute-start(f32[128,1024]{1,0:T(8,128)S(1)} %get-tuple-element.6), channel_id=1, source_target_pairs={{0,1},{1,2},{2,3},{4,5},{5,6},{6,7},{8,9},{9,10},{10,11},{12,13},{... | collective-permute-start | bytes 1572872 | tf_op jit(solution)/shard_map/ppermute | solution.py:19
  7.0 3.5 %collective-permute-start.6 = (f32[128,1024]{1,0:T(8,128)S(1)}, f32[128,1024]{1,0:T(8,128)S(1)}, u32[]{:S(2)}, u32[]{:S(2)}) collective-permute-start(f32[128,1024]{1,0:T(8,128)S(1)} %get-tuple-element.7), channel_id=1, source_target_pairs={{0,1},{1,2},{2,3},{4,5},{5,6},{6,7},{8,9},{9,10},{10,11},{12,13},{... | collective-permute-start | bytes 1572872 | tf_op jit(solution)/shard_map/ppermute | solution.py:19
  13.1 6.2 %collective-permute-done = f32[128,1024]{1,0:T(8,128)S(1)} collective-permute-done((f32[128,1024]{1,0:T(8,128)S(1)}, f32[128,1024]{1,0:T(8,128)S(1)}, u32[]{:S(2)}, u32[]{:S(2)}) %collective-permute-start) | collective-permute-done | bytes 524320 | tf_op jit(solution)/shard_map/ppermute | solution.py:19
  20.7 8.7 %collective-permute-done.6 = f32[128,1024]{1,0:T(8,128)S(1)} collective-permute-done((f32[128,1024]{1,0:T(8,128)S(1)}, f32[128,1024]{1,0:T(8,128)S(1)}, u32[]{:S(2)}, u32[]{:S(2)}) %collective-permute-start.6) | collective-permute-done | bytes 524320 | tf_op jit(solution)/shard_map/ppermute | solution.py:19
  32.2 4.6 %collective-permute-done.3 = f32[128,1024]{1,0:T(8,128)S(1)} collective-permute-done((f32[128,1024]{1,0:T(8,128)S(1)}, f32[128,1024]{1,0:T(8,128)S(1)}, u32[]{:S(2)}, u32[]{:S(2)}) %collective-permute-start.3) | collective-permute-done | bytes 524320 | tf_op jit(solution)/shard_map/ppermute | solution.py:20
  40.3 11.8 %collective-permute-done.10 = f32[128,1024]{1,0:T(8,128)} collective-permute-done((f32[128,1024]{1,0:T(8,128)S(1)}, f32[128,1024]{1,0:T(8,128)}, u32[]{:S(2)}, u32[]{:S(2)}) %collective-permute-start.10) | collective-permute-done | bytes 524320 | tf_op jit(solution)/shard_map/ppermute | solution.py:20
  53.4 9.9 %collective-permute-done.4 = f32[128,1024]{1,0:T(8,128)} collective-permute-done((f32[128,1024]{1,0:T(8,128)S(1)}, f32[128,1024]{1,0:T(8,128)}, u32[]{:S(2)}, u32[]{:S(2)}) %collective-permute-start.4) | collective-permute-done | bytes 524320 | tf_op jit(solution)/shard_map/ppermute | solution.py:20
  70.4 4.1 %collective-permute-done.11 = f32[128,1024]{1,0:T(8,128)S(1)} collective-permute-done((f32[128,1024]{1,0:T(8,128)}, f32[128,1024]{1,0:T(8,128)S(1)}, u32[]{:S(2)}, u32[]{:S(2)}) %collective-permute-start.11) | collective-permute-done | bytes 524320 | tf_op jit(solution)/shard_map/ppermute | solution.py:20
  74.7 7.9 %collective-permute-done.5 = f32[128,1024]{1,0:T(8,128)S(1)} collective-permute-done((f32[128,1024]{1,0:T(8,128)}, f32[128,1024]{1,0:T(8,128)S(1)}, u32[]{:S(2)}, u32[]{:S(2)}) %collective-permute-start.5) | collective-permute-done | bytes 524320 | tf_op jit(solution)/shard_map/ppermute | solution.py:20
  85.8 2.0 %fusion.37 = f32[1024,64]{0,1:T(8,128)S(1)} fusion(f32[1024,1024]{1,0:T(8,128)S(1)} %bitcast.82, f32[512,128]{0,1:T(8,128)S(1)} %bitcast.100, f32[512,128]{0,1:T(8,128)S(1)} %fusion.20), kind=kOutput, calls=%fused_computation.78 | convolution fusion | flops 402718720 | bytes 4980736 | tf_op jit(solution)/shard_map/dot_general | solution.py:10
  89.4 4.4 %fusion.46 = f32[1024,64]{0,1:T(8,128)S(1)} fusion(f32[1024,1024]{1,0:T(8,128)} %bitcast.83, f32[1024,64]{0,1:T(8,128)S(1)} %get-tuple-element.24), kind=kOutput, calls=%fused_computation.111 | convolution fusion | flops 402653184 | bytes 4718592 | tf_op jit(solution)/shard_map/dot_general | solution.py:10
  94.5 2.0 %fusion.43 = f32[1024,64]{0,1:T(8,128)S(1)} fusion(f32[1024,1024]{1,0:T(8,128)S(1)} %bitcast.84, f32[1024,64]{0,1:T(8,128)S(1)} %get-tuple-element.23), kind=kOutput, calls=%fused_computation.108 | convolution fusion | flops 402653184 | bytes 4718592 | tf_op jit(solution)/shard_map/dot_general | solution.py:10
  97.2 2.0 %fusion.36 = f32[1024,64]{0,1:T(8,128)S(1)} fusion(f32[1024,1024]{1,0:T(8,128)S(1)} %bitcast.85, f32[1024,64]{0,1:T(8,128)S(1)} %collective-permute-done.20, f32[1024,64]{0,1:T(8,128)S(1)} %get-tuple-element.24, pred[]{:T(512)S(6)} %eq.131), kind=kOutput, calls=%fused_computation.77 | convolution fusion | flops 402718720 | bytes 4980737 | tf_op jit(solution)/shard_map/dot_general | solution.py:10
  105.7 2.0 %fusion.44 = f32[1024,64]{0,1:T(8,128)S(1)} fusion(f32[1024,1024]{1,0:T(8,128)S(1)} %bitcast.88, f32[1024,64]{0,1:T(8,128)S(1)} %broadcast_select_fusion.5), kind=kOutput, calls=%fused_computation.109 | convolution fusion | flops 402653184 | bytes 4718592 | tf_op jit(solution)/shard_map/dot_general | solution.py:10
  108.4 2.0 %fusion.34 = f32[1024,64]{0,1:T(8,128)S(1)} fusion(f32[1024,1024]{1,0:T(8,128)S(1)} %bitcast.89, f32[1024,64]{0,1:T(8,128)S(1)} %collective-permute-done.22, f32[1024,64]{0,1:T(8,128)S(1)} %broadcast_select_fusion.4, pred[]{:T(512)S(6)} %eq.129), kind=kOutput, calls=%fused_computation.75 | convolution fusion | flops 402718720 | bytes 4980737 | tf_op jit(solution)/shard_map/dot_general | solution.py:10
  111.1 2.0 %fusion.33 = f32[1024,64]{0,1:T(8,128)S(1)} fusion(f32[1024,1024]{1,0:T(8,128)S(1)} %bitcast.90, f32[1024,64]{0,1:T(8,128)S(1)} %collective-permute-done.15, f32[1024,64]{0,1:T(8,128)S(1)} %broadcast_select_fusion.5, pred[]{:T(512)S(6)} %eq.129), kind=kOutput, calls=%fused_computation.74 | convolution fusion | flops 402718720 | bytes 4980737 | tf_op jit(solution)/shard_map/dot_general | solution.py:10
  126.3 8.5 %collective-permute-done.25 = f32[1024,64]{0,1:T(8,128)S(1)} collective-permute-done((f32[1024,64]{0,1:T(8,128)S(1)}, f32[1024,64]{0,1:T(8,128)S(1)}, u32[]{:S(2)}, u32[]{:S(2)}) %collective-permute-start.25) | collective-permute-done | bytes 262176 | tf_op jit(solution)/shard_map/ppermute | solution.py:55
  134.8 2.0 %convolution_select_fusion = f32[1024,64]{0,1:T(8,128)S(1)} fusion(f32[1024,1024]{1,0:T(8,128)S(1)} %bitcast.95, f32[1024,64]{0,1:T(8,128)S(1)} %fusion.32, f32[1024,64]{0,1:T(8,128)S(1)} %fusion.48, f32[1024,64]{0,1:T(8,128)S(1)} %fusion.34, f32[1024,64]{0,1:T(8,128)S(1)} %fusion.47, f32[1024,64]{0,1:T(8,128)S(1)} %fusion.36, f32[1024,64]{0,1:T(8,128)S(1)} %fusion.46, ...), kind=kOutput, calls=%fused_computation.4 | convolution fusion | flops 403243008 | bytes 7077895 | tf_op jit(solution)/shard_map/dot_general | solution.py:10
  138.3 2.0 %convolution_select_fusion.1 = f32[1024,64]{0,1:T(8,128)S(1)} fusion(f32[1024,1024]{1,0:T(8,128)S(1)} %bitcast.96, f32[1024,64]{0,1:T(8,128)S(1)} %fusion.31, f32[1024,64]{0,1:T(8,128)S(1)} %fusion.45, f32[1024,64]{0,1:T(8,128)S(1)} %fusion.33, f32[1024,64]{0,1:T(8,128)S(1)} %fusion.44, f32[1024,64]{0,1:T(8,128)S(1)} %fusion.35, f32[1024,64]{0,1:T(8,128)S(1)} %fusion.43, ...), kind=kOutput, calls=%fused_computation.5 | convolution fusion | flops 403243008 | bytes 7077895 | tf_op jit(solution)/shard_map/dot_general | solution.py:10
  142.4 3.3 %collective-permute-start.26 = (f32[512,128]{0,1:T(8,128)S(1)}, f32[512,128]{0,1:T(8,128)S(1)}, u32[]{:S(2)}, u32[]{:S(2)}) collective-permute-start(f32[512,128]{0,1:T(8,128)S(1)} %pad_maximum_fusion.3), channel_id=1, source_target_pairs={{0,3},{1,0},{2,1},{3,2},{4,7},{5,4},{6,5},{7,6},{8,11},{9,8},{10,9... | collective-permute-start | bytes 786440 | tf_op jit(solution)/shard_map/ppermute | solution.py:67
  145.7 7.0 %collective-permute-done.28 = f32[512,128]{0,1:T(8,128)S(1)} collective-permute-done((f32[512,128]{0,1:T(8,128)S(1)}, f32[512,128]{0,1:T(8,128)S(1)}, u32[]{:S(2)}, u32[]{:S(2)}) %collective-permute-start.28) | collective-permute-done | bytes 262176 | tf_op jit(solution)/shard_map/ppermute | solution.py:67
  152.7 10.3 %collective-permute-done.27 = f32[512,128]{0,1:T(8,128)S(1)} collective-permute-done((f32[512,128]{0,1:T(8,128)S(1)}, f32[512,128]{0,1:T(8,128)S(1)}, u32[]{:S(2)}, u32[]{:S(2)}) %collective-permute-start.27) | collective-permute-done | bytes 262176 | tf_op jit(solution)/shard_map/ppermute | solution.py:67
  163.2 5.4 %fusion.1 = f32[512,2048]{1,0:T(8,128)S(1)} fusion(f32[512,2048]{1,0:T(8,128)} %param.5, f32[256,128]{0,1:T(8,128)S(1)} %get-tuple-element.15, f32[256,128]{0,1:T(8,128)S(1)} %get-tuple-element.13, f32[256,128]{0,1:T(8,128)S(1)} %get-tuple-element.12, f32[256,128]{0,1:T(8,128)S(1)} %get-tuple-element.11, f32[256,128]{0,1:T(8,128)S(1)} %get-tuple-element.14, ...), kind=kOutput, calls=%fused_computation.6 | convolution fusion | flops 3223060480 | bytes 9437184 | tf_op jit(solution)/shard_map/dot_general | solution.py:10
  170.3 6.2 %collective-permute-start.29 = (f32[512]{0:T(512)S(1)}, f32[512]{0:T(512)S(1)}, u32[]{:S(2)}, u32[]{:S(2)}) collective-permute-start(f32[512]{0:T(512)S(1)} %dynamic_slice.44), channel_id=1, source_target_pairs={{0,1},{1,0},{2,3},{3,2},{4,5},{5,4},{6,7},{7,6},{8,9},{9,8},{10,11... | collective-permute-start | bytes 6152 | tf_op jit(solution)/shard_map/ppermute | solution.py:89
  (100 shorter events, 54.4 us)
Async XLA Ops:
  2.0 17.3 %collective-permute-start = (f32[128,1024]{1,0:T(8,128)S(1)}, f32[128,1024]{1,0:T(8,128)S(1)}, u32[]{:S(2)}, u32[]{:S(2)}) collective-permute-start(f32[128,1024]{1,0:T(8,128)S(1)} %get-tuple-element.6), channel_id=1, source_target_pairs={{0,1},{1,2},{2,3},{4,5},{5,6},{6,7},{8,9},{9,10},{10,11},{12,13},{... | collective-permute-start | bytes 1572872 | tf_op jit(solution)/shard_map/ppermute | solution.py:19
  7.0 22.4 %collective-permute-start.6 = (f32[128,1024]{1,0:T(8,128)S(1)}, f32[128,1024]{1,0:T(8,128)S(1)}, u32[]{:S(2)}, u32[]{:S(2)}) collective-permute-start(f32[128,1024]{1,0:T(8,128)S(1)} %get-tuple-element.7), channel_id=1, source_target_pairs={{0,1},{1,2},{2,3},{4,5},{5,6},{6,7},{8,9},{9,10},{10,11},{12,13},{... | collective-permute-start | bytes 1572872 | tf_op jit(solution)/shard_map/ppermute | solution.py:19
  10.5 20.4 %collective-permute-start.9 = (f32[128,1024]{1,0:T(8,128)S(1)}, f32[128,1024]{1,0:T(8,128)S(1)}, u32[]{:S(2)}, u32[]{:S(2)}) collective-permute-start(f32[128,1024]{1,0:T(8,128)S(1)} %get-tuple-element.7), channel_id=1, source_target_pairs={{1,0},{2,1},{3,2},{5,4},{6,5},{7,6},{9,8},{10,9},{11,10},{13,12},{... | collective-permute-start | bytes 1572872 | tf_op jit(solution)/shard_map/ppermute | solution.py:20
  11.8 24.9 %collective-permute-start.3 = (f32[128,1024]{1,0:T(8,128)S(1)}, f32[128,1024]{1,0:T(8,128)S(1)}, u32[]{:S(2)}, u32[]{:S(2)}) collective-permute-start(f32[128,1024]{1,0:T(8,128)S(1)} %get-tuple-element.6), channel_id=1, source_target_pairs={{1,0},{2,1},{3,2},{5,4},{6,5},{7,6},{9,8},{10,9},{11,10},{13,12},{... | collective-permute-start | bytes 1572872 | tf_op jit(solution)/shard_map/ppermute | solution.py:20
  19.3 18.8 %collective-permute-start.1 = (f32[128,1024]{1,0:T(8,128)S(1)}, f32[128,1024]{1,0:T(8,128)}, u32[]{:S(2)}, u32[]{:S(2)}) collective-permute-start(f32[128,1024]{1,0:T(8,128)S(1)} %collective-permute-done), channel_id=1, source_target_pairs={{1,2},{2,3},{5,6},{6,7},{9,10},{10,11},{13,14},{14,15},{17,18},{18... | collective-permute-start | bytes 1572872 | tf_op jit(solution)/shard_map/ppermute | solution.py:19
  29.4 10.1 %collective-permute-start.7 = (f32[128,1024]{1,0:T(8,128)S(1)}, f32[128,1024]{1,0:T(8,128)}, u32[]{:S(2)}, u32[]{:S(2)}) collective-permute-start(f32[128,1024]{1,0:T(8,128)S(1)} %collective-permute-done.6), channel_id=1, source_target_pairs={{1,2},{2,3},{5,6},{6,7},{9,10},{10,11},{13,14},{14,15},{17,18},{18... | collective-permute-start | bytes 1572872 | tf_op jit(solution)/shard_map/ppermute | solution.py:19
  30.9 21.2 %collective-permute-start.10 = (f32[128,1024]{1,0:T(8,128)S(1)}, f32[128,1024]{1,0:T(8,128)}, u32[]{:S(2)}, u32[]{:S(2)}) collective-permute-start(f32[128,1024]{1,0:T(8,128)S(1)} %collective-permute-done.9), channel_id=1, source_target_pairs={{1,0},{2,1},{5,4},{6,5},{9,8},{10,9},{13,12},{14,13},{17,16},{18,1... | collective-permute-start | bytes 1572872 | tf_op jit(solution)/shard_map/ppermute | solution.py:20
  36.8 26.6 %collective-permute-start.4 = (f32[128,1024]{1,0:T(8,128)S(1)}, f32[128,1024]{1,0:T(8,128)}, u32[]{:S(2)}, u32[]{:S(2)}) collective-permute-start(f32[128,1024]{1,0:T(8,128)S(1)} %collective-permute-done.3), channel_id=1, source_target_pairs={{1,0},{2,1},{5,4},{6,5},{9,8},{10,9},{13,12},{14,13},{17,16},{18,1... | collective-permute-start | bytes 1572872 | tf_op jit(solution)/shard_map/ppermute | solution.py:20
  38.1 26.6 %collective-permute-start.2 = (f32[128,1024]{1,0:T(8,128)}, f32[128,1024]{1,0:T(8,128)}, u32[]{:S(2)}, u32[]{:S(2)}) collective-permute-start(f32[128,1024]{1,0:T(8,128)} %collective-permute-done.1), channel_id=1, source_target_pairs={{2,3},{6,7},{10,11},{14,15},{18,19},{22,23},{26,27},{30,31}} | collective-permute-start | bytes 1572872 | tf_op jit(solution)/shard_map/ppermute | solution.py:19
  39.5 27.3 %collective-permute-start.8 = (f32[128,1024]{1,0:T(8,128)}, f32[128,1024]{1,0:T(8,128)S(1)}, u32[]{:S(2)}, u32[]{:S(2)}) collective-permute-start(f32[128,1024]{1,0:T(8,128)} %collective-permute-done.7), channel_id=1, source_target_pairs={{2,3},{6,7},{10,11},{14,15},{18,19},{22,23},{26,27},{30,31}} | collective-permute-start | bytes 1572872 | tf_op jit(solution)/shard_map/ppermute | solution.py:19
  52.1 22.4 %collective-permute-start.11 = (f32[128,1024]{1,0:T(8,128)}, f32[128,1024]{1,0:T(8,128)S(1)}, u32[]{:S(2)}, u32[]{:S(2)}) collective-permute-start(f32[128,1024]{1,0:T(8,128)} %collective-permute-done.10), channel_id=1, source_target_pairs={{1,0},{5,4},{9,8},{13,12},{17,16},{21,20},{25,24},{29,28}} | collective-permute-start | bytes 1572872 | tf_op jit(solution)/shard_map/ppermute | solution.py:20
  63.3 19.2 %collective-permute-start.5 = (f32[128,1024]{1,0:T(8,128)}, f32[128,1024]{1,0:T(8,128)S(1)}, u32[]{:S(2)}, u32[]{:S(2)}) collective-permute-start(f32[128,1024]{1,0:T(8,128)} %collective-permute-done.4), channel_id=1, source_target_pairs={{1,0},{5,4},{9,8},{13,12},{17,16},{21,20},{25,24},{29,28}} | collective-permute-start | bytes 1572872 | tf_op jit(solution)/shard_map/ppermute | solution.py:20
  96.5 3.6 %collective-permute-start.13 = (f32[1024,64]{0,1:T(8,128)S(1)}, f32[1024,64]{0,1:T(8,128)S(1)}, u32[]{:S(2)}, u32[]{:S(2)}) collective-permute-start(f32[1024,64]{0,1:T(8,128)S(1)} %fusion.43), channel_id=1, source_target_pairs={{24,20},{25,21},{26,22},{27,23}} | collective-permute-start | bytes 786440 | tf_op jit(solution)/shard_map/ppermute | solution.py:55
  99.2 3.6 %collective-permute-start.21 = (f32[1024,64]{0,1:T(8,128)S(1)}, f32[1024,64]{0,1:T(8,128)S(1)}, u32[]{:S(2)}, u32[]{:S(2)}) collective-permute-start(f32[1024,64]{0,1:T(8,128)S(1)} %fusion.36), channel_id=1, source_target_pairs={{20,16},{21,17},{22,18},{23,19}} | collective-permute-start | bytes 786440 | tf_op jit(solution)/shard_map/ppermute | solution.py:55
  104.9 3.5 %collective-permute-start.22 = (f32[1024,64]{0,1:T(8,128)S(1)}, f32[1024,64]{0,1:T(8,128)S(1)}, u32[]{:S(2)}, u32[]{:S(2)}) collective-permute-start(f32[1024,64]{0,1:T(8,128)S(1)} %fusion.47), channel_id=1, source_target_pairs={{16,12},{17,13},{18,14},{19,15}} | collective-permute-start | bytes 786440 | tf_op jit(solution)/shard_map/ppermute | solution.py:55
  113.1 3.5 %collective-permute-start.16 = (f32[1024,64]{0,1:T(8,128)S(1)}, f32[1024,64]{0,1:T(8,128)S(1)}, u32[]{:S(2)}, u32[]{:S(2)}) collective-permute-start(f32[1024,64]{0,1:T(8,128)S(1)} %fusion.33), channel_id=1, source_target_pairs={{12,8},{13,9},{14,10},{15,11}} | collective-permute-start | bytes 786440 | tf_op jit(solution)/shard_map/ppermute | solution.py:55
  115.9 3.7 %collective-permute-start.24 = (f32[1024,64]{0,1:T(8,128)S(1)}, f32[1024,64]{0,1:T(8,128)S(1)}, u32[]{:S(2)}, u32[]{:S(2)}) collective-permute-start(f32[1024,64]{0,1:T(8,128)S(1)} %fusion.48), channel_id=1, source_target_pairs={{8,4},{9,5},{10,6},{11,7}} | collective-permute-start | bytes 786440 | tf_op jit(solution)/shard_map/ppermute | solution.py:55
  118.7 4.2 %collective-permute-start.17 = (f32[1024,64]{0,1:T(8,128)S(1)}, f32[1024,64]{0,1:T(8,128)S(1)}, u32[]{:S(2)}, u32[]{:S(2)}) collective-permute-start(f32[1024,64]{0,1:T(8,128)S(1)} %fusion.45), channel_id=1, source_target_pairs={{8,4},{9,5},{10,6},{11,7}} | collective-permute-start | bytes 786440 | tf_op jit(solution)/shard_map/ppermute | solution.py:55
  121.6 13.2 %collective-permute-start.25 = (f32[1024,64]{0,1:T(8,128)S(1)}, f32[1024,64]{0,1:T(8,128)S(1)}, u32[]{:S(2)}, u32[]{:S(2)}) collective-permute-start(f32[1024,64]{0,1:T(8,128)S(1)} %fusion.32), channel_id=1, source_target_pairs={{4,0},{5,1},{6,2},{7,3}} | collective-permute-start | bytes 786440 | tf_op jit(solution)/shard_map/ppermute | solution.py:55
  125.0 13.4 %collective-permute-start.18 = (f32[1024,64]{0,1:T(8,128)S(1)}, f32[1024,64]{0,1:T(8,128)S(1)}, u32[]{:S(2)}, u32[]{:S(2)}) collective-permute-start(f32[1024,64]{0,1:T(8,128)S(1)} %fusion.31), channel_id=1, source_target_pairs={{4,0},{5,1},{6,2},{7,3}} | collective-permute-start | bytes 786440 | tf_op jit(solution)/shard_map/ppermute | solution.py:55
  141.6 11.1 %collective-permute-start.28 = (f32[512,128]{0,1:T(8,128)S(1)}, f32[512,128]{0,1:T(8,128)S(1)}, u32[]{:S(2)}, u32[]{:S(2)}) collective-permute-start(f32[512,128]{0,1:T(8,128)S(1)} %pad_maximum_fusion.5), channel_id=1, source_target_pairs={{0,1},{1,2},{2,3},{3,0},{4,5},{5,6},{6,7},{7,4},{8,9},{9,10},{10,1... | collective-permute-start | bytes 786440 | tf_op jit(solution)/shard_map/ppermute | solution.py:67
  141.7 21.3 %collective-permute-start.27 = (f32[512,128]{0,1:T(8,128)S(1)}, f32[512,128]{0,1:T(8,128)S(1)}, u32[]{:S(2)}, u32[]{:S(2)}) collective-permute-start(f32[512,128]{0,1:T(8,128)S(1)} %pad_maximum_fusion.4), channel_id=1, source_target_pairs={{0,2},{1,3},{2,0},{3,1},{4,6},{5,7},{6,4},{7,5},{8,10},{9,11},{10,... | collective-permute-start | bytes 786440 | tf_op jit(solution)/shard_map/ppermute | solution.py:67
  142.4 20.6 %collective-permute-start.26 = (f32[512,128]{0,1:T(8,128)S(1)}, f32[512,128]{0,1:T(8,128)S(1)}, u32[]{:S(2)}, u32[]{:S(2)}) collective-permute-start(f32[512,128]{0,1:T(8,128)S(1)} %pad_maximum_fusion.3), channel_id=1, source_target_pairs={{0,3},{1,0},{2,1},{3,2},{4,7},{5,4},{6,5},{7,6},{8,11},{9,8},{10,9... | collective-permute-start | bytes 786440 | tf_op jit(solution)/shard_map/ppermute | solution.py:67
  170.3 7.7 %collective-permute-start.29 = (f32[512]{0:T(512)S(1)}, f32[512]{0:T(512)S(1)}, u32[]{:S(2)}, u32[]{:S(2)}) collective-permute-start(f32[512]{0:T(512)S(1)} %dynamic_slice.44), channel_id=1, source_target_pairs={{0,1},{1,0},{2,3},{3,2},{4,5},{5,4},{6,7},{7,6},{8,9},{9,8},{10,11... | collective-permute-start | bytes 6152 | tf_op jit(solution)/shard_map/ppermute | solution.py:89
  (10 other events, 94.0 us)

commit v14 on v9

--- a/solution.py
+++ b/solution.py
@@ -49,7 +49,11 @@
     own = [None] * CHUNKS
     for k in range(groups - 1, -1, -1):
         for j in range(CHUNKS):
-            fresh = product(whole_map, incoming[j])
+            if k == groups - 1:
+                picked = lax.dynamic_slice_in_dim(whole_map, place * width + j * step, step, 1)
+                fresh = picked + product(whole_map[:, state_dim:], incoming[j][state_dim:])
+            else:
+                fresh = product(whole_map, incoming[j])
             own[j] = fresh if own[j] is None else jnp.where(group == k, fresh, own[j])
             if k > 0:
                 got = lax.ppermute(fresh, "tm", [(k, k - 1)])

time: 179 us -> 181 us (1.011)
  matrix products: 41.5 us -> 32.2 us
  local copies, waits for them, and re-layouts: 8.99 us -> 15.1 us
  waiting for transfers between devices: 81.8 us -> 84.4 us
  other arithmetic: 1.85 us -> 3.8 us
    dot_general x18, matrix products: 41.5 us -> 32.2 us  [product(): jnp.dot(left, right, precision=lax.Precision.HIGH, preferred_element_type...]
    reshape x0 -> x1, local copies, waits for them, and re-layouts: none -> 5.5 us  [body(): jnp.concatenate([upper, lower], axis=1)]
    ppermute x14, waiting for transfers between devices: 10 us -> 14.3 us  [body(): got = lax.ppermute(fresh, 'tm', [(k, k - 1)])]
    concatenate x1, other arithmetic: 0.58 us -> 2.52 us  [body(): jnp.concatenate([upper, lower], axis=1)]
    unnamed x26 -> x24, local copies, waits for them, and re-layouts: 6.11 us -> 6.8 us
  transfers between devices with their start and end apart: 30 -> 30, of which waited for: 12 -> 12; matrix products, arithmetic and copies ran while one was open for 17% -> 14% of each run, Pallas kernels for 0% -> 0%
where the time goes in v14:
time: 181 us; the launch traced here: 180 us
  waiting for transfers between devices  84.4 us (47%)
  starting transfers between devices  42.9 us (24%)
  matrix products  32.2 us (18%)
  local copies, waits for them, and re-layouts  15.1 us (8%)
  other arithmetic  3.8 us (2%)
    ppermute x6, waiting for transfers between devices, line_gather(): lax.ppermute(leftward, 'row', [(z, z - 1) for z in range(1, count - t + 1)])  36.6 us
    dot_general x18, matrix products, product(): jnp.dot(left, right, precision=lax.Precision.HIGH, preferred_element_type...  32.2 us
    ppermute x3, waiting for transfers between devices, body(): lax.ppermute(payload, 'row', [(z, (z + d) % count) for z in range(count)])  17.2 us
    ppermute x6, waiting for transfers between devices, line_gather(): lax.ppermute(rightward, 'row', [(z, z + 1) for z in range(t - 1, count -...  14.8 us
    ppermute x6, starting transfers between devices, line_gather(): lax.ppermute(rightward, 'row', [(z, z + 1) for z in range(t - 1, count -...  14.4 us
    ppermute x14, waiting for transfers between devices, body(): got = lax.ppermute(fresh, 'tm', [(k, k - 1)])  14.3 us
    ppermute x14, starting transfers between devices, body(): got = lax.ppermute(fresh, 'tm', [(k, k - 1)])  10.9 us
    ppermute x6, starting transfers between devices, line_gather(): lax.ppermute(leftward, 'row', [(z, z - 1) for z in range(1, count - t + 1)])  7.71 us
  transfers between devices with their start and end apart: 30, of which 12 were waited for; matrix products, arithmetic and copies ran while one was open for 14% of the time, Pallas kernels for 0%

profile of v14, /device:TPU:0, one launch (start us, length us, event | category | flops | bytes accessed | tf_op | source)
XLA Modules:
  0.0 179.9 jit_solution(4546266275567642701)
XLA Ops:
  2.0 5.1 %collective-permute-start = (f32[128,1024]{1,0:T(8,128)S(1)}, f32[128,1024]{1,0:T(8,128)S(1)}, u32[]{:S(2)}, u32[]{:S(2)}) collective-permute-start(f32[128,1024]{1,0:T(8,128)S(1)} %get-tuple-element.4), channel_id=1, source_target_pairs={{0,1},{1,2},{2,3},{4,5},{5,6},{6,7},{8,9},{9,10},{10,11},{12,13},{... | collective-permute-start | bytes 1572872 | tf_op jit(solution)/shard_map/ppermute | solution.py:19
  7.1 3.5 %collective-permute-start.6 = (f32[128,1024]{1,0:T(8,128)S(1)}, f32[128,1024]{1,0:T(8,128)S(1)}, u32[]{:S(2)}, u32[]{:S(2)}) collective-permute-start(f32[128,1024]{1,0:T(8,128)S(1)} %get-tuple-element.5), channel_id=1, source_target_pairs={{0,1},{1,2},{2,3},{4,5},{5,6},{6,7},{8,9},{9,10},{10,11},{12,13},{... | collective-permute-start | bytes 1572872 | tf_op jit(solution)/shard_map/ppermute | solution.py:19
  13.2 6.2 %collective-permute-done = f32[128,1024]{1,0:T(8,128)S(1)} collective-permute-done((f32[128,1024]{1,0:T(8,128)S(1)}, f32[128,1024]{1,0:T(8,128)S(1)}, u32[]{:S(2)}, u32[]{:S(2)}) %collective-permute-start) | collective-permute-done | bytes 524320 | tf_op jit(solution)/shard_map/ppermute | solution.py:19
  20.8 8.6 %collective-permute-done.6 = f32[128,1024]{1,0:T(8,128)S(1)} collective-permute-done((f32[128,1024]{1,0:T(8,128)S(1)}, f32[128,1024]{1,0:T(8,128)S(1)}, u32[]{:S(2)}, u32[]{:S(2)}) %collective-permute-start.6) | collective-permute-done | bytes 524320 | tf_op jit(solution)/shard_map/ppermute | solution.py:19
  32.2 4.6 %collective-permute-done.3 = f32[128,1024]{1,0:T(8,128)S(1)} collective-permute-done((f32[128,1024]{1,0:T(8,128)S(1)}, f32[128,1024]{1,0:T(8,128)S(1)}, u32[]{:S(2)}, u32[]{:S(2)}) %collective-permute-start.3) | collective-permute-done | bytes 524320 | tf_op jit(solution)/shard_map/ppermute | solution.py:20
  38.1 1.5 collective-permute-start.2
  41.0 11.0 %collective-permute-done.10 = f32[128,1024]{1,0:T(8,128)} collective-permute-done((f32[128,1024]{1,0:T(8,128)S(1)}, f32[128,1024]{1,0:T(8,128)}, u32[]{:S(2)}, u32[]{:S(2)}) %collective-permute-start.10) | collective-permute-done | bytes 524320 | tf_op jit(solution)/shard_map/ppermute | solution.py:20
  53.4 9.9 %collective-permute-done.4 = f32[128,1024]{1,0:T(8,128)} collective-permute-done((f32[128,1024]{1,0:T(8,128)S(1)}, f32[128,1024]{1,0:T(8,128)}, u32[]{:S(2)}, u32[]{:S(2)}) %collective-permute-start.4) | collective-permute-done | bytes 524320 | tf_op jit(solution)/shard_map/ppermute | solution.py:20
  71.4 3.0 %collective-permute-done.11 = f32[128,1024]{1,0:T(8,128)S(1)} collective-permute-done((f32[128,1024]{1,0:T(8,128)}, f32[128,1024]{1,0:T(8,128)S(1)}, u32[]{:S(2)}, u32[]{:S(2)}) %collective-permute-start.11) | collective-permute-done | bytes 524320 | tf_op jit(solution)/shard_map/ppermute | solution.py:20
  74.6 7.9 %collective-permute-done.5 = f32[128,1024]{1,0:T(8,128)S(1)} collective-permute-done((f32[128,1024]{1,0:T(8,128)}, f32[128,1024]{1,0:T(8,128)S(1)}, u32[]{:S(2)}, u32[]{:S(2)}) %collective-permute-start.5) | collective-permute-done | bytes 524320 | tf_op jit(solution)/shard_map/ppermute | solution.py:20
  82.8 2.5 %pad_maximum_fusion = f32[4,256,1024]{2,1,0:T(8,128)} fusion(f32[4,128,1024]{2,1,0:T(8,128)S(1)} %bitcast.81, f32[4,128,1024]{2,1,0:T(8,128)S(1)} %bitcast.82), kind=kLoop, calls=%fused_computation | loop fusion | flops 1048576 | bytes 8388608 | tf_op jit(solution)/shard_map/concatenate | solution.py:40
  85.3 5.5 %copy.6 = f32[1024,1024]{0,1:T(8,128)} copy(f32[1024,1024]{1,0:T(8,128)} %bitcast.79) | data formatting | bytes 8388608 | tf_op jit(solution)/shard_map/reshape | solution.py:40
  90.8 2.3 %fusion.5 = f32[1024,64]{0,1:T(8,128)S(1)} fusion(f32[1024,1024]{0,1:T(8,128)} %copy.6, s32[]{:T(128)S(6)} %select_n.381, f32[512,128]{0,1:T(8,128)S(1)} %bitcast.83), kind=kOutput, calls=%fused_computation.7 | convolution fusion | flops 201392128 | bytes 2752516 | tf_op jit(solution)/shard_map/dot_general | solution.py:10
  93.8 2.3 %fusion.8 = f32[1024,64]{0,1:T(8,128)S(1)} fusion(f32[1024,1024]{0,1:T(8,128)} %copy.6, s32[]{:T(128)S(6)} %select_n.396, f32[512,128]{0,1:T(8,128)S(1)} %bitcast.84), kind=kOutput, calls=%fused_computation.8 | convolution fusion | flops 201392128 | bytes 2752516 | tf_op jit(solution)/shard_map/dot_general | solution.py:10
  97.1 3.6 %fusion.55 = f32[1024,64]{0,1:T(8,128)S(1)} fusion(f32[1024,1024]{0,1:T(8,128)} %copy.6, f32[1024,64]{0,1:T(8,128)S(1)} %get-tuple-element.22), kind=kOutput, calls=%fused_computation.114 | convolution fusion | flops 402653184 | bytes 4718592 | tf_op jit(solution)/shard_map/dot_general | solution.py:10
  125.5 12.8 %collective-permute-done.25 = f32[1024,64]{0,1:T(8,128)S(1)} collective-permute-done((f32[1024,64]{0,1:T(8,128)S(1)}, f32[1024,64]{0,1:T(8,128)S(1)}, u32[]{:S(2)}, u32[]{:S(2)}) %collective-permute-start.25) | collective-permute-done | bytes 262176 | tf_op jit(solution)/shard_map/ppermute | solution.py:59
  143.7 1.8 %collective-permute-start.27 = (f32[512,128]{0,1:T(8,128)S(1)}, f32[512,128]{0,1:T(8,128)S(1)}, u32[]{:S(2)}, u32[]{:S(2)}) collective-permute-start(f32[512,128]{0,1:T(8,128)S(1)} %pad_maximum_fusion.4), channel_id=1, source_target_pairs={{0,2},{1,3},{2,0},{3,1},{4,6},{5,7},{6,4},{7,5},{8,10},{9,11},{10,... | collective-permute-start | bytes 786440 | tf_op jit(solution)/shard_map/ppermute | solution.py:71
  145.6 2.3 %collective-permute-start.26 = (f32[512,128]{0,1:T(8,128)S(1)}, f32[512,128]{0,1:T(8,128)S(1)}, u32[]{:S(2)}, u32[]{:S(2)}) collective-permute-start(f32[512,128]{0,1:T(8,128)S(1)} %pad_maximum_fusion.3), channel_id=1, source_target_pairs={{0,3},{1,0},{2,1},{3,2},{4,7},{5,4},{6,5},{7,6},{8,11},{9,8},{10,9... | collective-permute-start | bytes 786440 | tf_op jit(solution)/shard_map/ppermute | solution.py:71
  147.9 6.8 %collective-permute-done.28 = f32[512,128]{0,1:T(8,128)S(1)} collective-permute-done((f32[512,128]{0,1:T(8,128)S(1)}, f32[512,128]{0,1:T(8,128)S(1)}, u32[]{:S(2)}, u32[]{:S(2)}) %collective-permute-start.28) | collective-permute-done | bytes 262176 | tf_op jit(solution)/shard_map/ppermute | solution.py:71
  154.8 10.4 %collective-permute-done.27 = f32[512,128]{0,1:T(8,128)S(1)} collective-permute-done((f32[512,128]{0,1:T(8,128)S(1)}, f32[512,128]{0,1:T(8,128)S(1)}, u32[]{:S(2)}, u32[]{:S(2)}) %collective-permute-start.27) | collective-permute-done | bytes 262176 | tf_op jit(solution)/shard_map/ppermute | solution.py:71
  165.3 4.3 %fusion.11 = f32[256,2048]{1,0:T(8,128)S(1)} fusion(f32[512,2048]{1,0:T(8,128)} %param.5, f32[256,128]{0,1:T(8,128)S(1)} %get-tuple-element.13, f32[256,128]{0,1:T(8,128)S(1)} %get-tuple-element.11, f32[256,128]{0,1:T(8,128)S(1)} %get-tuple-element.10, f32[256,128]{0,1:T(8,128)S(1)} %get-tuple-element.9), kind=kOutput, calls=%fused_computation.14 | convolution fusion | flops 1611005952 | bytes 6815744 | tf_op jit(solution)/shard_map/dot_general | solution.py:10
  169.7 2.2 %fusion.4 = f32[2048]{0:T(1024)S(1)} fusion(f32[256,2048]{1,0:T(8,128)S(1)} %fusion.11, f32[512,2048]{1,0:T(8,128)S(1)} %copy-done.1, f32[256,128]{0,1:T(8,128)S(1)} %get-tuple-element.12, f32[256,128]{0,1:T(8,128)S(1)} %get-tuple-element.8, f32[256,128]{0,1:T(8,128)S(1)} %get-tuple-element.7, f32[256,128]{0,1:T(8,128)S(1)} %get-tuple-element.6), kind=kOutput, calls=%fused_computation.6 | convolution fusion | flops 1612052480 | bytes 6823936 | tf_op jit(solution)/shard_map/dot_general | solution.py:10
  172.1 5.6 %collective-permute-start.29 = (f32[512]{0:T(512)S(1)}, f32[512]{0:T(512)S(1)}, u32[]{:S(2)}, u32[]{:S(2)}) collective-permute-start(f32[512]{0:T(512)S(1)} %dynamic_slice.52), channel_id=1, source_target_pairs={{0,1},{1,0},{2,3},{3,2},{4,5},{5,4},{6,7},{7,6},{8,9},{9,8},{10,11... | collective-permute-start | bytes 6152 | tf_op jit(solution)/shard_map/ppermute | solution.py:92
  177.7 1.6 collective-permute-done.29
  (103 shorter events, 52.8 us)
Async XLA Ops:
  2.0 17.4 %collective-permute-start = (f32[128,1024]{1,0:T(8,128)S(1)}, f32[128,1024]{1,0:T(8,128)S(1)}, u32[]{:S(2)}, u32[]{:S(2)}) collective-permute-start(f32[128,1024]{1,0:T(8,128)S(1)} %get-tuple-element.4), channel_id=1, source_target_pairs={{0,1},{1,2},{2,3},{4,5},{5,6},{6,7},{8,9},{9,10},{10,11},{12,13},{... | collective-permute-start | bytes 1572872 | tf_op jit(solution)/shard_map/ppermute | solution.py:19
  7.1 22.4 %collective-permute-start.6 = (f32[128,1024]{1,0:T(8,128)S(1)}, f32[128,1024]{1,0:T(8,128)S(1)}, u32[]{:S(2)}, u32[]{:S(2)}) collective-permute-start(f32[128,1024]{1,0:T(8,128)S(1)} %get-tuple-element.5), channel_id=1, source_target_pairs={{0,1},{1,2},{2,3},{4,5},{5,6},{6,7},{8,9},{9,10},{10,11},{12,13},{... | collective-permute-start | bytes 1572872 | tf_op jit(solution)/shard_map/ppermute | solution.py:19
  10.6 20.3 %collective-permute-start.9 = (f32[128,1024]{1,0:T(8,128)S(1)}, f32[128,1024]{1,0:T(8,128)S(1)}, u32[]{:S(2)}, u32[]{:S(2)}) collective-permute-start(f32[128,1024]{1,0:T(8,128)S(1)} %get-tuple-element.5), channel_id=1, source_target_pairs={{1,0},{2,1},{3,2},{5,4},{6,5},{7,6},{9,8},{10,9},{11,10},{13,12},{... | collective-permute-start | bytes 1572872 | tf_op jit(solution)/shard_map/ppermute | solution.py:20
  11.9 24.9 %collective-permute-start.3 = (f32[128,1024]{1,0:T(8,128)S(1)}, f32[128,1024]{1,0:T(8,128)S(1)}, u32[]{:S(2)}, u32[]{:S(2)}) collective-permute-start(f32[128,1024]{1,0:T(8,128)S(1)} %get-tuple-element.4), channel_id=1, source_target_pairs={{1,0},{2,1},{3,2},{5,4},{6,5},{7,6},{9,8},{10,9},{11,10},{13,12},{... | collective-permute-start | bytes 1572872 | tf_op jit(solution)/shard_map/ppermute | solution.py:20
  19.3 18.8 %collective-permute-start.1 = (f32[128,1024]{1,0:T(8,128)S(1)}, f32[128,1024]{1,0:T(8,128)}, u32[]{:S(2)}, u32[]{:S(2)}) collective-permute-start(f32[128,1024]{1,0:T(8,128)S(1)} %collective-permute-done), channel_id=1, source_target_pairs={{1,2},{2,3},{5,6},{6,7},{9,10},{10,11},{13,14},{14,15},{17,18},{18... | collective-permute-start | bytes 1572872 | tf_op jit(solution)/shard_map/ppermute | solution.py:19
  29.4 10.1 %collective-permute-start.7 = (f32[128,1024]{1,0:T(8,128)S(1)}, f32[128,1024]{1,0:T(8,128)}, u32[]{:S(2)}, u32[]{:S(2)}) collective-permute-start(f32[128,1024]{1,0:T(8,128)S(1)} %collective-permute-done.6), channel_id=1, source_target_pairs={{1,2},{2,3},{5,6},{6,7},{9,10},{10,11},{13,14},{14,15},{17,18},{18... | collective-permute-start | bytes 1572872 | tf_op jit(solution)/shard_map/ppermute | solution.py:19
  30.9 21.2 %collective-permute-start.10 = (f32[128,1024]{1,0:T(8,128)S(1)}, f32[128,1024]{1,0:T(8,128)}, u32[]{:S(2)}, u32[]{:S(2)}) collective-permute-start(f32[128,1024]{1,0:T(8,128)S(1)} %collective-permute-done.9), channel_id=1, source_target_pairs={{1,0},{2,1},{5,4},{6,5},{9,8},{10,9},{13,12},{14,13},{17,16},{18,1... | collective-permute-start | bytes 1572872 | tf_op jit(solution)/shard_map/ppermute | solution.py:20
  36.8 26.5 %collective-permute-start.4 = (f32[128,1024]{1,0:T(8,128)S(1)}, f32[128,1024]{1,0:T(8,128)}, u32[]{:S(2)}, u32[]{:S(2)}) collective-permute-start(f32[128,1024]{1,0:T(8,128)S(1)} %collective-permute-done.3), channel_id=1, source_target_pairs={{1,0},{2,1},{5,4},{6,5},{9,8},{10,9},{13,12},{14,13},{17,16},{18,1... | collective-permute-start | bytes 1572872 | tf_op jit(solution)/shard_map/ppermute | solution.py:20
  38.1 26.5 %collective-permute-start.2 = (f32[128,1024]{1,0:T(8,128)}, f32[128,1024]{1,0:T(8,128)}, u32[]{:S(2)}, u32[]{:S(2)}) collective-permute-start(f32[128,1024]{1,0:T(8,128)} %collective-permute-done.1), channel_id=1, source_target_pairs={{2,3},{6,7},{10,11},{14,15},{18,19},{22,23},{26,27},{30,31}} | collective-permute-start | bytes 1572872 | tf_op jit(solution)/shard_map/ppermute | solution.py:19
  39.6 27.3 %collective-permute-start.8 = (f32[128,1024]{1,0:T(8,128)}, f32[128,1024]{1,0:T(8,128)}, u32[]{:S(2)}, u32[]{:S(2)}) collective-permute-start(f32[128,1024]{1,0:T(8,128)} %collective-permute-done.7), channel_id=1, source_target_pairs={{2,3},{6,7},{10,11},{14,15},{18,19},{22,23},{26,27},{30,31}} | collective-permute-start | bytes 1572872 | tf_op jit(solution)/shard_map/ppermute | solution.py:19
  52.1 22.4 %collective-permute-start.11 = (f32[128,1024]{1,0:T(8,128)}, f32[128,1024]{1,0:T(8,128)S(1)}, u32[]{:S(2)}, u32[]{:S(2)}) collective-permute-start(f32[128,1024]{1,0:T(8,128)} %collective-permute-done.10), channel_id=1, source_target_pairs={{1,0},{5,4},{9,8},{13,12},{17,16},{21,20},{25,24},{29,28}} | collective-permute-start | bytes 1572872 | tf_op jit(solution)/shard_map/ppermute | solution.py:20
  63.3 19.2 %collective-permute-start.5 = (f32[128,1024]{1,0:T(8,128)}, f32[128,1024]{1,0:T(8,128)S(1)}, u32[]{:S(2)}, u32[]{:S(2)}) collective-permute-start(f32[128,1024]{1,0:T(8,128)} %collective-permute-done.4), channel_id=1, source_target_pairs={{1,0},{5,4},{9,8},{13,12},{17,16},{21,20},{25,24},{29,28}} | collective-permute-start | bytes 1572872 | tf_op jit(solution)/shard_map/ppermute | solution.py:20
  93.1 3.9 %collective-permute-start.12 = (f32[1024,64]{0,1:T(8,128)S(1)}, f32[1024,64]{0,1:T(8,128)S(1)}, u32[]{:S(2)}, u32[]{:S(2)}) collective-permute-start(f32[1024,64]{0,1:T(8,128)S(1)} %fusion.5), channel_id=1, source_target_pairs={{28,24},{29,25},{30,26},{31,27}} | collective-permute-start | bytes 786440 | tf_op jit(solution)/shard_map/ppermute | solution.py:59
  106.9 2.8 %collective-permute-start.14 = (f32[1024,64]{0,1:T(8,128)S(1)}, f32[1024,64]{0,1:T(8,128)S(1)}, u32[]{:S(2)}, u32[]{:S(2)}) collective-permute-start(f32[1024,64]{0,1:T(8,128)S(1)} %fusion.48), channel_id=1, source_target_pairs={{20,16},{21,17},{22,18},{23,19}} | collective-permute-start | bytes 786440 | tf_op jit(solution)/shard_map/ppermute | solution.py:59
  108.9 2.9 %collective-permute-start.22 = (f32[1024,64]{0,1:T(8,128)S(1)}, f32[1024,64]{0,1:T(8,128)S(1)}, u32[]{:S(2)}, u32[]{:S(2)}) collective-permute-start(f32[1024,64]{0,1:T(8,128)S(1)} %fusion.56), channel_id=1, source_target_pairs={{16,12},{17,13},{18,14},{19,15}} | collective-permute-start | bytes 786440 | tf_op jit(solution)/shard_map/ppermute | solution.py:59
  111.0 2.9 %collective-permute-start.15 = (f32[1024,64]{0,1:T(8,128)S(1)}, f32[1024,64]{0,1:T(8,128)S(1)}, u32[]{:S(2)}, u32[]{:S(2)}) collective-permute-start(f32[1024,64]{0,1:T(8,128)S(1)} %fusion.53), channel_id=1, source_target_pairs={{16,12},{17,13},{18,14},{19,15}} | collective-permute-start | bytes 786440 | tf_op jit(solution)/shard_map/ppermute | solution.py:59
  117.4 2.8 %collective-permute-start.24 = (f32[1024,64]{0,1:T(8,128)S(1)}, f32[1024,64]{0,1:T(8,128)S(1)}, u32[]{:S(2)}, u32[]{:S(2)}) collective-permute-start(f32[1024,64]{0,1:T(8,128)S(1)} %fusion.57), channel_id=1, source_target_pairs={{8,4},{9,5},{10,6},{11,7}} | collective-permute-start | bytes 786440 | tf_op jit(solution)/shard_map/ppermute | solution.py:59
  119.5 3.3 %collective-permute-start.17 = (f32[1024,64]{0,1:T(8,128)S(1)}, f32[1024,64]{0,1:T(8,128)S(1)}, u32[]{:S(2)}, u32[]{:S(2)}) collective-permute-start(f32[1024,64]{0,1:T(8,128)S(1)} %fusion.54), channel_id=1, source_target_pairs={{8,4},{9,5},{10,6},{11,7}} | collective-permute-start | bytes 786440 | tf_op jit(solution)/shard_map/ppermute | solution.py:59
  121.5 16.7 %collective-permute-start.25 = (f32[1024,64]{0,1:T(8,128)S(1)}, f32[1024,64]{0,1:T(8,128)S(1)}, u32[]{:S(2)}, u32[]{:S(2)}) collective-permute-start(f32[1024,64]{0,1:T(8,128)S(1)} %fusion.45), channel_id=1, source_target_pairs={{4,0},{5,1},{6,2},{7,3}} | collective-permute-start | bytes 786440 | tf_op jit(solution)/shard_map/ppermute | solution.py:59
  124.2 16.9 %collective-permute-start.18 = (f32[1024,64]{0,1:T(8,128)S(1)}, f32[1024,64]{0,1:T(8,128)S(1)}, u32[]{:S(2)}, u32[]{:S(2)}) collective-permute-start(f32[1024,64]{0,1:T(8,128)S(1)} %fusion.44), channel_id=1, source_target_pairs={{4,0},{5,1},{6,2},{7,3}} | collective-permute-start | bytes 786440 | tf_op jit(solution)/shard_map/ppermute | solution.py:59
  143.6 11.2 %collective-permute-start.28 = (f32[512,128]{0,1:T(8,128)S(1)}, f32[512,128]{0,1:T(8,128)S(1)}, u32[]{:S(2)}, u32[]{:S(2)}) collective-permute-start(f32[512,128]{0,1:T(8,128)S(1)} %pad_maximum_fusion.5), channel_id=1, source_target_pairs={{0,1},{1,2},{2,3},{3,0},{4,5},{5,6},{6,7},{7,4},{8,9},{9,10},{10,1... | collective-permute-start | bytes 786440 | tf_op jit(solution)/shard_map/ppermute | solution.py:71
  143.7 21.4 %collective-permute-start.27 = (f32[512,128]{0,1:T(8,128)S(1)}, f32[512,128]{0,1:T(8,128)S(1)}, u32[]{:S(2)}, u32[]{:S(2)}) collective-permute-start(f32[512,128]{0,1:T(8,128)S(1)} %pad_maximum_fusion.4), channel_id=1, source_target_pairs={{0,2},{1,3},{2,0},{3,1},{4,6},{5,7},{6,4},{7,5},{8,10},{9,11},{10,... | collective-permute-start | bytes 786440 | tf_op jit(solution)/shard_map/ppermute | solution.py:71
  145.6 19.5 %collective-permute-start.26 = (f32[512,128]{0,1:T(8,128)S(1)}, f32[512,128]{0,1:T(8,128)S(1)}, u32[]{:S(2)}, u32[]{:S(2)}) collective-permute-start(f32[512,128]{0,1:T(8,128)S(1)} %pad_maximum_fusion.3), channel_id=1, source_target_pairs={{0,3},{1,0},{2,1},{3,2},{4,7},{5,4},{6,5},{7,6},{8,11},{9,8},{10,9... | collective-permute-start | bytes 786440 | tf_op jit(solution)/shard_map/ppermute | solution.py:71
  172.1 7.2 %collective-permute-start.29 = (f32[512]{0:T(512)S(1)}, f32[512]{0:T(512)S(1)}, u32[]{:S(2)}, u32[]{:S(2)}) collective-permute-start(f32[512]{0:T(512)S(1)} %dynamic_slice.52), channel_id=1, source_target_pairs={{0,1},{1,0},{2,3},{3,2},{4,5},{5,4},{6,7},{7,6},{8,9},{9,8},{10,11... | collective-permute-start | bytes 6152 | tf_op jit(solution)/shard_map/ppermute | solution.py:92
  (11 other events, 98.5 us)

commit v15 on v9

--- a/solution.py
+++ b/solution.py
@@ -52,8 +52,7 @@
             fresh = product(whole_map, incoming[j])
             own[j] = fresh if own[j] is None else jnp.where(group == k, fresh, own[j])
             if k > 0:
-                got = lax.ppermute(fresh, "tm", [(k, k - 1)])
-                incoming[j] = jnp.where(group == k - 1, got, incoming[j])
+                incoming[j] = lax.ppermute(fresh, "tm", [(k, k - 1)])
 
     own_cols = jnp.concatenate(own, axis=1)
     rows = own_cols.shape[0] // count

time: 179 us -> 175 us (0.978)
  matrix products: 41.5 us -> 39.2 us
  waiting for transfers between devices: 81.8 us -> 80 us
    dot_general x18, matrix products: 41.5 us -> 39.2 us  [product(): jnp.dot(left, right, precision=lax.Precision.HIGH, preferred_element_type...]
    unnamed x26 -> x22, local copies, waits for them, and re-layouts: 6.11 us -> 6.11 us
  transfers between devices with their start and end apart: 30 -> 30, of which waited for: 12 -> 12; matrix products, arithmetic and copies ran while one was open for 17% -> 20% of each run, Pallas kernels for 0% -> 0%
where the time goes in v15:
time: 175 us; the launch traced here: 174 us
  waiting for transfers between devices  80 us (46%)
  starting transfers between devices  42.7 us (24%)
  matrix products  39.2 us (22%)
  local copies, waits for them, and re-layouts  8.98 us (5%)
    dot_general x18, matrix products, product(): jnp.dot(left, right, precision=lax.Precision.HIGH, preferred_element_type...  39.2 us
    ppermute x6, waiting for transfers between devices, line_gather(): lax.ppermute(leftward, 'row', [(z, z - 1) for z in range(1, count - t + 1)])  38.3 us
    ppermute x3, waiting for transfers between devices, body(): lax.ppermute(payload, 'row', [(z, (z + d) % count) for z in range(count)])  17 us
    ppermute x6, waiting for transfers between devices, line_gather(): lax.ppermute(rightward, 'row', [(z, z + 1) for z in range(t - 1, count -...  14.8 us
    ppermute x6, starting transfers between devices, line_gather(): lax.ppermute(rightward, 'row', [(z, z + 1) for z in range(t - 1, count -...  13.6 us
    ppermute x14, starting transfers between devices, body(): incoming[j] = lax.ppermute(fresh, 'tm', [(k, k - 1)])  11.1 us
    ppermute x14, waiting for transfers between devices, body(): incoming[j] = lax.ppermute(fresh, 'tm', [(k, k - 1)])  8.31 us
    ppermute x6, starting transfers between devices, line_gather(): lax.ppermute(leftward, 'row', [(z, z - 1) for z in range(1, count - t + 1)])  7.71 us
  transfers between devices with their start and end apart: 30, of which 12 were waited for; matrix products, arithmetic and copies ran while one was open for 20% of the time, Pallas kernels for 0%

profile of v15, /device:TPU:0, one launch (start us, length us, event | category | flops | bytes accessed | tf_op | source)
XLA Modules:
  0.0 173.8 jit_solution(10040913251478436244)
XLA Ops:
  2.0 5.0 %collective-permute-start = (f32[128,1024]{1,0:T(8,128)S(1)}, f32[128,1024]{1,0:T(8,128)S(1)}, u32[]{:S(2)}, u32[]{:S(2)}) collective-permute-start(f32[128,1024]{1,0:T(8,128)S(1)} %get-tuple-element.4), channel_id=1, source_target_pairs={{0,1},{1,2},{2,3},{4,5},{5,6},{6,7},{8,9},{9,10},{10,11},{12,13},{... | collective-permute-start | bytes 1572872 | tf_op jit(solution)/shard_map/ppermute | solution.py:19
  7.0 3.5 %collective-permute-start.6 = (f32[128,1024]{1,0:T(8,128)S(1)}, f32[128,1024]{1,0:T(8,128)S(1)}, u32[]{:S(2)}, u32[]{:S(2)}) collective-permute-start(f32[128,1024]{1,0:T(8,128)S(1)} %get-tuple-element.5), channel_id=1, source_target_pairs={{0,1},{1,2},{2,3},{4,5},{5,6},{6,7},{8,9},{9,10},{10,11},{12,13},{... | collective-permute-start | bytes 1572872 | tf_op jit(solution)/shard_map/ppermute | solution.py:19
  13.1 6.2 %collective-permute-done = f32[128,1024]{1,0:T(8,128)S(1)} collective-permute-done((f32[128,1024]{1,0:T(8,128)S(1)}, f32[128,1024]{1,0:T(8,128)S(1)}, u32[]{:S(2)}, u32[]{:S(2)}) %collective-permute-start) | collective-permute-done | bytes 524320 | tf_op jit(solution)/shard_map/ppermute | solution.py:19
  20.8 8.6 %collective-permute-done.6 = f32[128,1024]{1,0:T(8,128)S(1)} collective-permute-done((f32[128,1024]{1,0:T(8,128)S(1)}, f32[128,1024]{1,0:T(8,128)S(1)}, u32[]{:S(2)}, u32[]{:S(2)}) %collective-permute-start.6) | collective-permute-done | bytes 524320 | tf_op jit(solution)/shard_map/ppermute | solution.py:19
  32.2 4.6 %collective-permute-done.3 = f32[128,1024]{1,0:T(8,128)S(1)} collective-permute-done((f32[128,1024]{1,0:T(8,128)S(1)}, f32[128,1024]{1,0:T(8,128)S(1)}, u32[]{:S(2)}, u32[]{:S(2)}) %collective-permute-start.3) | collective-permute-done | bytes 524320 | tf_op jit(solution)/shard_map/ppermute | solution.py:20
  40.3 11.8 %collective-permute-done.10 = f32[128,1024]{1,0:T(8,128)} collective-permute-done((f32[128,1024]{1,0:T(8,128)S(1)}, f32[128,1024]{1,0:T(8,128)}, u32[]{:S(2)}, u32[]{:S(2)}) %collective-permute-start.10) | collective-permute-done | bytes 524320 | tf_op jit(solution)/shard_map/ppermute | solution.py:20
  53.4 9.9 %collective-permute-done.4 = f32[128,1024]{1,0:T(8,128)} collective-permute-done((f32[128,1024]{1,0:T(8,128)S(1)}, f32[128,1024]{1,0:T(8,128)}, u32[]{:S(2)}, u32[]{:S(2)}) %collective-permute-start.4) | collective-permute-done | bytes 524320 | tf_op jit(solution)/shard_map/ppermute | solution.py:20
  70.4 4.1 %collective-permute-done.11 = f32[128,1024]{1,0:T(8,128)S(1)} collective-permute-done((f32[128,1024]{1,0:T(8,128)}, f32[128,1024]{1,0:T(8,128)S(1)}, u32[]{:S(2)}, u32[]{:S(2)}) %collective-permute-start.11) | collective-permute-done | bytes 524320 | tf_op jit(solution)/shard_map/ppermute | solution.py:20
  74.6 7.9 %collective-permute-done.5 = f32[128,1024]{1,0:T(8,128)S(1)} collective-permute-done((f32[128,1024]{1,0:T(8,128)}, f32[128,1024]{1,0:T(8,128)S(1)}, u32[]{:S(2)}, u32[]{:S(2)}) %collective-permute-start.5) | collective-permute-done | bytes 524320 | tf_op jit(solution)/shard_map/ppermute | solution.py:20
  86.4 2.0 %fusion.17 = f32[1024,64]{0,1:T(8,128)S(1)} fusion(f32[1024,1024]{1,0:T(8,128)S(1)} %bitcast.90, f32[512,128]{0,1:T(8,128)S(1)} %fusion.21, f32[512,128]{0,1:T(8,128)S(1)} %bitcast.109), kind=kOutput, calls=%fused_computation.26 | convolution fusion | flops 402718720 | bytes 4980736 | tf_op jit(solution)/shard_map/dot_general | solution.py:10
  94.6 2.0 %fusion.41 = f32[1024,64]{0,1:T(8,128)S(1)} fusion(f32[1024,1024]{1,0:T(8,128)S(1)} %bitcast.93, f32[1024,64]{0,1:T(8,128)S(1)} %collective-permute-done.20), kind=kOutput, calls=%fused_computation.93 | convolution fusion | flops 402653184 | bytes 4718592 | tf_op jit(solution)/shard_map/dot_general | solution.py:10
  100.2 2.0 %fusion.42 = f32[1024,64]{0,1:T(8,128)S(1)} fusion(f32[1024,1024]{1,0:T(8,128)S(1)} %bitcast.95, f32[1024,64]{0,1:T(8,128)S(1)} %collective-permute-done.21), kind=kOutput, calls=%fused_computation.94 | convolution fusion | flops 402653184 | bytes 4718592 | tf_op jit(solution)/shard_map/dot_general | solution.py:10
  105.7 2.0 %fusion.43 = f32[1024,64]{0,1:T(8,128)S(1)} fusion(f32[1024,1024]{1,0:T(8,128)S(1)} %bitcast.97, f32[1024,64]{0,1:T(8,128)S(1)} %collective-permute-done.22), kind=kOutput, calls=%fused_computation.95 | convolution fusion | flops 402653184 | bytes 4718592 | tf_op jit(solution)/shard_map/dot_general | solution.py:10
  111.1 2.0 %fusion.44 = f32[1024,64]{0,1:T(8,128)S(1)} fusion(f32[1024,1024]{1,0:T(8,128)S(1)} %bitcast.99, f32[1024,64]{0,1:T(8,128)S(1)} %collective-permute-done.23), kind=kOutput, calls=%fused_computation.96 | convolution fusion | flops 402653184 | bytes 4718592 | tf_op jit(solution)/shard_map/dot_general | solution.py:10
  120.1 2.0 %fusion.39 = f32[1024,64]{0,1:T(8,128)S(1)} fusion(f32[1024,1024]{1,0:T(8,128)S(1)} %bitcast.102, f32[1024,64]{0,1:T(8,128)S(1)} %collective-permute-done.17), kind=kOutput, calls=%fused_computation.91 | convolution fusion | flops 402653184 | bytes 4718592 | tf_op jit(solution)/shard_map/dot_general | solution.py:10
  123.5 6.8 %collective-permute-done.25 = f32[1024,64]{0,1:T(8,128)S(1)} collective-permute-done((f32[1024,64]{0,1:T(8,128)S(1)}, f32[1024,64]{0,1:T(8,128)S(1)}, u32[]{:S(2)}, u32[]{:S(2)}) %collective-permute-start.25) | collective-permute-done | bytes 262176 | tf_op jit(solution)/shard_map/ppermute | solution.py:55
  130.3 2.1 %convolution_select_fusion = f32[1024,64]{0,1:T(8,128)S(1)} fusion(f32[1024,1024]{1,0:T(8,128)S(1)} %bitcast.103, f32[1024,64]{0,1:T(8,128)S(1)} %collective-permute-done.25, f32[1024,64]{0,1:T(8,128)S(1)} %fusion.45, f32[1024,64]{0,1:T(8,128)S(1)} %fusion.44, f32[1024,64]{0,1:T(8,128)S(1)} %fusion.43, f32[1024,64]{0,1:T(8,128)S(1)} %fusion.42, ...), kind=kOutput, calls=%fused_computation.3 | convolution fusion | flops 403111936 | bytes 6553607 | tf_op jit(solution)/shard_map/dot_general | solution.py:10
  133.8 2.1 %convolution_select_fusion.1 = f32[1024,64]{0,1:T(8,128)S(1)} fusion(f32[1024,1024]{1,0:T(8,128)S(1)} %bitcast.104, f32[1024,64]{0,1:T(8,128)S(1)} %collective-permute-done.18, f32[1024,64]{0,1:T(8,128)S(1)} %fusion.39, f32[1024,64]{0,1:T(8,128)S(1)} %fusion.38, f32[1024,64]{0,1:T(8,128)S(1)} %fusion.37, f32[1024,64]{0,1:T(8,128)S(1)} %fusion.36, ...), kind=kOutput, calls=%fused_computation.4 | convolution fusion | flops 403111936 | bytes 6553607 | tf_op jit(solution)/shard_map/dot_general | solution.py:10
  137.9 3.5 %collective-permute-start.26 = (f32[512,128]{0,1:T(8,128)S(1)}, f32[512,128]{0,1:T(8,128)S(1)}, u32[]{:S(2)}, u32[]{:S(2)}) collective-permute-start(f32[512,128]{0,1:T(8,128)S(1)} %pad_maximum_fusion.4), channel_id=1, source_target_pairs={{0,3},{1,0},{2,1},{3,2},{4,7},{5,4},{6,5},{7,6},{8,11},{9,8},{10,9... | collective-permute-start | bytes 786440 | tf_op jit(solution)/shard_map/ppermute | solution.py:66
  141.4 6.7 %collective-permute-done.28 = f32[512,128]{0,1:T(8,128)S(1)} collective-permute-done((f32[512,128]{0,1:T(8,128)S(1)}, f32[512,128]{0,1:T(8,128)S(1)}, u32[]{:S(2)}, u32[]{:S(2)}) %collective-permute-start.28) | collective-permute-done | bytes 262176 | tf_op jit(solution)/shard_map/ppermute | solution.py:66
  148.1 10.3 %collective-permute-done.27 = f32[512,128]{0,1:T(8,128)S(1)} collective-permute-done((f32[512,128]{0,1:T(8,128)S(1)}, f32[512,128]{0,1:T(8,128)S(1)}, u32[]{:S(2)}, u32[]{:S(2)}) %collective-permute-start.27) | collective-permute-done | bytes 262176 | tf_op jit(solution)/shard_map/ppermute | solution.py:66
  158.6 4.4 %fusion.1 = f32[256,2048]{1,0:T(8,128)S(1)} fusion(f32[512,2048]{1,0:T(8,128)} %param.5, f32[256,128]{0,1:T(8,128)S(1)} %get-tuple-element.13, f32[256,128]{0,1:T(8,128)S(1)} %get-tuple-element.11, f32[256,128]{0,1:T(8,128)S(1)} %get-tuple-element.10, f32[256,128]{0,1:T(8,128)S(1)} %get-tuple-element.9), kind=kOutput, calls=%fused_computation.8 | convolution fusion | flops 1611005952 | bytes 6815744 | tf_op jit(solution)/shard_map/dot_general | solution.py:10
  163.1 2.2 %fusion = f32[2048]{0:T(1024)S(1)} fusion(f32[256,2048]{1,0:T(8,128)S(1)} %fusion.1, f32[512,2048]{1,0:T(8,128)S(1)} %copy-done, f32[256,128]{0,1:T(8,128)S(1)} %get-tuple-element.12, f32[256,128]{0,1:T(8,128)S(1)} %get-tuple-element.8, f32[256,128]{0,1:T(8,128)S(1)} %get-tuple-element.7, f32[256,128]{0,1:T(8,128)S(1)} %get-tuple-element.6), kind=kOutput, calls=%fused_computation.2 | convolution fusion | flops 1612052480 | bytes 6823936 | tf_op jit(solution)/shard_map/dot_general | solution.py:10
  165.4 6.2 %collective-permute-start.29 = (f32[512]{0:T(512)S(1)}, f32[512]{0:T(512)S(1)}, u32[]{:S(2)}, u32[]{:S(2)}) collective-permute-start(f32[512]{0:T(512)S(1)} %dynamic_slice.44), channel_id=1, source_target_pairs={{0,1},{1,0},{2,3},{3,2},{4,5},{5,4},{6,7},{7,6},{8,9},{9,8},{10,11... | collective-permute-start | bytes 6152 | tf_op jit(solution)/shard_map/ppermute | solution.py:87
  (95 shorter events, 54.5 us)
Async XLA Ops:
  2.0 17.3 %collective-permute-start = (f32[128,1024]{1,0:T(8,128)S(1)}, f32[128,1024]{1,0:T(8,128)S(1)}, u32[]{:S(2)}, u32[]{:S(2)}) collective-permute-start(f32[128,1024]{1,0:T(8,128)S(1)} %get-tuple-element.4), channel_id=1, source_target_pairs={{0,1},{1,2},{2,3},{4,5},{5,6},{6,7},{8,9},{9,10},{10,11},{12,13},{... | collective-permute-start | bytes 1572872 | tf_op jit(solution)/shard_map/ppermute | solution.py:19
  7.0 22.4 %collective-permute-start.6 = (f32[128,1024]{1,0:T(8,128)S(1)}, f32[128,1024]{1,0:T(8,128)S(1)}, u32[]{:S(2)}, u32[]{:S(2)}) collective-permute-start(f32[128,1024]{1,0:T(8,128)S(1)} %get-tuple-element.5), channel_id=1, source_target_pairs={{0,1},{1,2},{2,3},{4,5},{5,6},{6,7},{8,9},{9,10},{10,11},{12,13},{... | collective-permute-start | bytes 1572872 | tf_op jit(solution)/shard_map/ppermute | solution.py:19
  10.5 20.3 %collective-permute-start.9 = (f32[128,1024]{1,0:T(8,128)S(1)}, f32[128,1024]{1,0:T(8,128)S(1)}, u32[]{:S(2)}, u32[]{:S(2)}) collective-permute-start(f32[128,1024]{1,0:T(8,128)S(1)} %get-tuple-element.5), channel_id=1, source_target_pairs={{1,0},{2,1},{3,2},{5,4},{6,5},{7,6},{9,8},{10,9},{11,10},{13,12},{... | collective-permute-start | bytes 1572872 | tf_op jit(solution)/shard_map/ppermute | solution.py:20
  11.8 24.9 %collective-permute-start.3 = (f32[128,1024]{1,0:T(8,128)S(1)}, f32[128,1024]{1,0:T(8,128)S(1)}, u32[]{:S(2)}, u32[]{:S(2)}) collective-permute-start(f32[128,1024]{1,0:T(8,128)S(1)} %get-tuple-element.4), channel_id=1, source_target_pairs={{1,0},{2,1},{3,2},{5,4},{6,5},{7,6},{9,8},{10,9},{11,10},{13,12},{... | collective-permute-start | bytes 1572872 | tf_op jit(solution)/shard_map/ppermute | solution.py:20
  19.3 18.8 %collective-permute-start.1 = (f32[128,1024]{1,0:T(8,128)S(1)}, f32[128,1024]{1,0:T(8,128)}, u32[]{:S(2)}, u32[]{:S(2)}) collective-permute-start(f32[128,1024]{1,0:T(8,128)S(1)} %collective-permute-done), channel_id=1, source_target_pairs={{1,2},{2,3},{5,6},{6,7},{9,10},{10,11},{13,14},{14,15},{17,18},{18... | collective-permute-start | bytes 1572872 | tf_op jit(solution)/shard_map/ppermute | solution.py:19
  29.4 10.1 %collective-permute-start.7 = (f32[128,1024]{1,0:T(8,128)S(1)}, f32[128,1024]{1,0:T(8,128)}, u32[]{:S(2)}, u32[]{:S(2)}) collective-permute-start(f32[128,1024]{1,0:T(8,128)S(1)} %collective-permute-done.6), channel_id=1, source_target_pairs={{1,2},{2,3},{5,6},{6,7},{9,10},{10,11},{13,14},{14,15},{17,18},{18... | collective-permute-start | bytes 1572872 | tf_op jit(solution)/shard_map/ppermute | solution.py:19
  30.9 21.2 %collective-permute-start.10 = (f32[128,1024]{1,0:T(8,128)S(1)}, f32[128,1024]{1,0:T(8,128)}, u32[]{:S(2)}, u32[]{:S(2)}) collective-permute-start(f32[128,1024]{1,0:T(8,128)S(1)} %collective-permute-done.9), channel_id=1, source_target_pairs={{1,0},{2,1},{5,4},{6,5},{9,8},{10,9},{13,12},{14,13},{17,16},{18,1... | collective-permute-start | bytes 1572872 | tf_op jit(solution)/shard_map/ppermute | solution.py:20
  36.8 26.5 %collective-permute-start.4 = (f32[128,1024]{1,0:T(8,128)S(1)}, f32[128,1024]{1,0:T(8,128)}, u32[]{:S(2)}, u32[]{:S(2)}) collective-permute-start(f32[128,1024]{1,0:T(8,128)S(1)} %collective-permute-done.3), channel_id=1, source_target_pairs={{1,0},{2,1},{5,4},{6,5},{9,8},{10,9},{13,12},{14,13},{17,16},{18,1... | collective-permute-start | bytes 1572872 | tf_op jit(solution)/shard_map/ppermute | solution.py:20
  38.1 26.5 %collective-permute-start.2 = (f32[128,1024]{1,0:T(8,128)}, f32[128,1024]{1,0:T(8,128)}, u32[]{:S(2)}, u32[]{:S(2)}) collective-permute-start(f32[128,1024]{1,0:T(8,128)} %collective-permute-done.1), channel_id=1, source_target_pairs={{2,3},{6,7},{10,11},{14,15},{18,19},{22,23},{26,27},{30,31}} | collective-permute-start | bytes 1572872 | tf_op jit(solution)/shard_map/ppermute | solution.py:19
  39.5 27.3 %collective-permute-start.8 = (f32[128,1024]{1,0:T(8,128)}, f32[128,1024]{1,0:T(8,128)S(1)}, u32[]{:S(2)}, u32[]{:S(2)}) collective-permute-start(f32[128,1024]{1,0:T(8,128)} %collective-permute-done.7), channel_id=1, source_target_pairs={{2,3},{6,7},{10,11},{14,15},{18,19},{22,23},{26,27},{30,31}} | collective-permute-start | bytes 1572872 | tf_op jit(solution)/shard_map/ppermute | solution.py:19
  52.1 22.4 %collective-permute-start.11 = (f32[128,1024]{1,0:T(8,128)}, f32[128,1024]{1,0:T(8,128)S(1)}, u32[]{:S(2)}, u32[]{:S(2)}) collective-permute-start(f32[128,1024]{1,0:T(8,128)} %collective-permute-done.10), channel_id=1, source_target_pairs={{1,0},{5,4},{9,8},{13,12},{17,16},{21,20},{25,24},{29,28}} | collective-permute-start | bytes 1572872 | tf_op jit(solution)/shard_map/ppermute | solution.py:20
  63.3 19.2 %collective-permute-start.5 = (f32[128,1024]{1,0:T(8,128)}, f32[128,1024]{1,0:T(8,128)S(1)}, u32[]{:S(2)}, u32[]{:S(2)}) collective-permute-start(f32[128,1024]{1,0:T(8,128)} %collective-permute-done.4), channel_id=1, source_target_pairs={{1,0},{5,4},{9,8},{13,12},{17,16},{21,20},{25,24},{29,28}} | collective-permute-start | bytes 1572872 | tf_op jit(solution)/shard_map/ppermute | solution.py:20
  93.9 3.6 %collective-permute-start.13 = (f32[1024,64]{0,1:T(8,128)S(1)}, f32[1024,64]{0,1:T(8,128)S(1)}, u32[]{:S(2)}, u32[]{:S(2)}) collective-permute-start(f32[1024,64]{0,1:T(8,128)S(1)} %fusion.34), channel_id=1, source_target_pairs={{24,20},{25,21},{26,22},{27,23}} | collective-permute-start | bytes 786440 | tf_op jit(solution)/shard_map/ppermute | solution.py:55
  96.6 3.6 %collective-permute-start.21 = (f32[1024,64]{0,1:T(8,128)S(1)}, f32[1024,64]{0,1:T(8,128)S(1)}, u32[]{:S(2)}, u32[]{:S(2)}) collective-permute-start(f32[1024,64]{0,1:T(8,128)S(1)} %fusion.41), channel_id=1, source_target_pairs={{20,16},{21,17},{22,18},{23,19}} | collective-permute-start | bytes 786440 | tf_op jit(solution)/shard_map/ppermute | solution.py:55
  99.5 3.4 %collective-permute-start.14 = (f32[1024,64]{0,1:T(8,128)S(1)}, f32[1024,64]{0,1:T(8,128)S(1)}, u32[]{:S(2)}, u32[]{:S(2)}) collective-permute-start(f32[1024,64]{0,1:T(8,128)S(1)} %fusion.35), channel_id=1, source_target_pairs={{20,16},{21,17},{22,18},{23,19}} | collective-permute-start | bytes 786440 | tf_op jit(solution)/shard_map/ppermute | solution.py:55
  105.0 3.4 %collective-permute-start.15 = (f32[1024,64]{0,1:T(8,128)S(1)}, f32[1024,64]{0,1:T(8,128)S(1)}, u32[]{:S(2)}, u32[]{:S(2)}) collective-permute-start(f32[1024,64]{0,1:T(8,128)S(1)} %fusion.36), channel_id=1, source_target_pairs={{16,12},{17,13},{18,14},{19,15}} | collective-permute-start | bytes 786440 | tf_op jit(solution)/shard_map/ppermute | solution.py:55
  113.2 3.6 %collective-permute-start.24 = (f32[1024,64]{0,1:T(8,128)S(1)}, f32[1024,64]{0,1:T(8,128)S(1)}, u32[]{:S(2)}, u32[]{:S(2)}) collective-permute-start(f32[1024,64]{0,1:T(8,128)S(1)} %fusion.44), channel_id=1, source_target_pairs={{8,4},{9,5},{10,6},{11,7}} | collective-permute-start | bytes 786440 | tf_op jit(solution)/shard_map/ppermute | solution.py:55
  115.9 4.2 %collective-permute-start.17 = (f32[1024,64]{0,1:T(8,128)S(1)}, f32[1024,64]{0,1:T(8,128)S(1)}, u32[]{:S(2)}, u32[]{:S(2)}) collective-permute-start(f32[1024,64]{0,1:T(8,128)S(1)} %fusion.38), channel_id=1, source_target_pairs={{8,4},{9,5},{10,6},{11,7}} | collective-permute-start | bytes 786440 | tf_op jit(solution)/shard_map/ppermute | solution.py:55
  118.8 11.4 %collective-permute-start.25 = (f32[1024,64]{0,1:T(8,128)S(1)}, f32[1024,64]{0,1:T(8,128)S(1)}, u32[]{:S(2)}, u32[]{:S(2)}) collective-permute-start(f32[1024,64]{0,1:T(8,128)S(1)} %fusion.45), channel_id=1, source_target_pairs={{4,0},{5,1},{6,2},{7,3}} | collective-permute-start | bytes 786440 | tf_op jit(solution)/shard_map/ppermute | solution.py:55
  122.2 11.6 %collective-permute-start.18 = (f32[1024,64]{0,1:T(8,128)S(1)}, f32[1024,64]{0,1:T(8,128)S(1)}, u32[]{:S(2)}, u32[]{:S(2)}) collective-permute-start(f32[1024,64]{0,1:T(8,128)S(1)} %fusion.39), channel_id=1, source_target_pairs={{4,0},{5,1},{6,2},{7,3}} | collective-permute-start | bytes 786440 | tf_op jit(solution)/shard_map/ppermute | solution.py:55
  137.0 11.1 %collective-permute-start.28 = (f32[512,128]{0,1:T(8,128)S(1)}, f32[512,128]{0,1:T(8,128)S(1)}, u32[]{:S(2)}, u32[]{:S(2)}) collective-permute-start(f32[512,128]{0,1:T(8,128)S(1)} %pad_maximum_fusion.6), channel_id=1, source_target_pairs={{0,1},{1,2},{2,3},{3,0},{4,5},{5,6},{6,7},{7,4},{8,9},{9,10},{10,1... | collective-permute-start | bytes 786440 | tf_op jit(solution)/shard_map/ppermute | solution.py:66
  137.2 21.3 %collective-permute-start.27 = (f32[512,128]{0,1:T(8,128)S(1)}, f32[512,128]{0,1:T(8,128)S(1)}, u32[]{:S(2)}, u32[]{:S(2)}) collective-permute-start(f32[512,128]{0,1:T(8,128)S(1)} %pad_maximum_fusion.5), channel_id=1, source_target_pairs={{0,2},{1,3},{2,0},{3,1},{4,6},{5,7},{6,4},{7,5},{8,10},{9,11},{10,... | collective-permute-start | bytes 786440 | tf_op jit(solution)/shard_map/ppermute | solution.py:66
  137.9 20.6 %collective-permute-start.26 = (f32[512,128]{0,1:T(8,128)S(1)}, f32[512,128]{0,1:T(8,128)S(1)}, u32[]{:S(2)}, u32[]{:S(2)}) collective-permute-start(f32[512,128]{0,1:T(8,128)S(1)} %pad_maximum_fusion.4), channel_id=1, source_target_pairs={{0,3},{1,0},{2,1},{3,2},{4,7},{5,4},{6,5},{7,6},{8,11},{9,8},{10,9... | collective-permute-start | bytes 786440 | tf_op jit(solution)/shard_map/ppermute | solution.py:66
  165.4 7.7 %collective-permute-start.29 = (f32[512]{0:T(512)S(1)}, f32[512]{0:T(512)S(1)}, u32[]{:S(2)}, u32[]{:S(2)}) collective-permute-start(f32[512]{0:T(512)S(1)} %dynamic_slice.44), channel_id=1, source_target_pairs={{0,1},{1,0},{2,3},{3,2},{4,5},{5,4},{6,7},{7,6},{8,9},{9,8},{10,11... | collective-permute-start | bytes 6152 | tf_op jit(solution)/shard_map/ppermute | solution.py:87
  (10 other events, 104.1 us)

commit v16 on v15

--- a/solution.py
+++ b/solution.py
@@ -68,13 +68,8 @@
         pair_pieces.append(got[rows:])
 
     def in_order(pieces):
-        ordered = []
-        for q in range(count):
-            picked = pieces[0]
-            for d in range(1, count):
-                picked = jnp.where((place - d) % count == q, pieces[d], picked)
-            ordered.append(picked)
-        return jnp.concatenate(ordered, axis=1)
+        by_offset = jnp.concatenate(pieces[::-1] + pieces[:0:-1], axis=1)
+        return lax.dynamic_slice_in_dim(by_offset, (count - 1 - place) * width, count * width, 1)
 
     rows_traj = product(in_order(main_pieces), terminal_states)
     pair_traj = product(in_order(pair_pieces), terminal_states)

time: 175 us -> 172 us (0.983)
  starting transfers between devices: 42.7 us -> 34.9 us
  waiting for transfers between devices: 80 us -> 87.4 us
  matrix products: 39.2 us -> 37.1 us
    ppermute x1, starting transfers between devices: 6.17 us -> 0.07 us  [body(): total = total + lax.ppermute(sent, 'row', partner)]
    ppermute x3, waiting for transfers between devices: 17 us -> 22.5 us  [body(): lax.ppermute(payload, 'row', [(z, (z + d) % count) for z in range(count)])]
    dot_general x18, matrix products: 39.2 us -> 37.1 us  [product(): jnp.dot(left, right, precision=lax.Precision.HIGH, preferred_element_type...]
    ppermute x1, waiting for transfers between devices: 1.56 us -> 3.52 us  [body(): total = total + lax.ppermute(sent, 'row', partner)]
    ppermute x3, starting transfers between devices: 4.26 us -> 2.48 us  [body(): lax.ppermute(payload, 'row', [(z, (z + d) % count) for z in range(count)])]
    unnamed x22 -> x31, local copies, waits for them, and re-layouts: 6.11 us -> 6.22 us
where the time goes in v16:
time: 172 us; the launch traced here: 171 us
  waiting for transfers between devices  87.4 us (51%)
  matrix products  37.1 us (22%)
  starting transfers between devices  34.9 us (20%)
  local copies, waits for them, and re-layouts  9.13 us (5%)
    ppermute x6, waiting for transfers between devices, line_gather(): lax.ppermute(leftward, 'row', [(z, z - 1) for z in range(1, count - t + 1)])  38.3 us
    dot_general x18, matrix products, product(): jnp.dot(left, right, precision=lax.Precision.HIGH, preferred_element_type...  37.1 us
    ppermute x3, waiting for transfers between devices, body(): lax.ppermute(payload, 'row', [(z, (z + d) % count) for z in range(count)])  22.5 us
    ppermute x6, waiting for transfers between devices, line_gather(): lax.ppermute(rightward, 'row', [(z, z + 1) for z in range(t - 1, count -...  14.8 us
    ppermute x6, starting transfers between devices, line_gather(): lax.ppermute(rightward, 'row', [(z, z + 1) for z in range(t - 1, count -...  13.6 us
    ppermute x14, starting transfers between devices, body(): incoming[j] = lax.ppermute(fresh, 'tm', [(k, k - 1)])  11.1 us
    ppermute x14, waiting for transfers between devices, body(): incoming[j] = lax.ppermute(fresh, 'tm', [(k, k - 1)])  8.31 us
    ppermute x6, starting transfers between devices, line_gather(): lax.ppermute(leftward, 'row', [(z, z - 1) for z in range(1, count - t + 1)])  7.71 us
  transfers between devices with their start and end apart: 30, of which 12 were waited for; matrix products, arithmetic and copies ran while one was open for 20% of the time, Pallas kernels for 0%

profile of v16, /device:TPU:0, one launch (start us, length us, event | category | flops | bytes accessed | tf_op | source)
XLA Modules:
  0.0 171.2 jit_solution(141441109392704386)
XLA Ops:
  2.0 5.0 %collective-permute-start = (f32[128,1024]{1,0:T(8,128)S(1)}, f32[128,1024]{1,0:T(8,128)S(1)}, u32[]{:S(2)}, u32[]{:S(2)}) collective-permute-start(f32[128,1024]{1,0:T(8,128)S(1)} %get-tuple-element.4), channel_id=1, source_target_pairs={{0,1},{1,2},{2,3},{4,5},{5,6},{6,7},{8,9},{9,10},{10,11},{12,13},{... | collective-permute-start | bytes 1572872 | tf_op jit(solution)/shard_map/ppermute | solution.py:19
  7.0 3.5 %collective-permute-start.6 = (f32[128,1024]{1,0:T(8,128)S(1)}, f32[128,1024]{1,0:T(8,128)S(1)}, u32[]{:S(2)}, u32[]{:S(2)}) collective-permute-start(f32[128,1024]{1,0:T(8,128)S(1)} %get-tuple-element.5), channel_id=1, source_target_pairs={{0,1},{1,2},{2,3},{4,5},{5,6},{6,7},{8,9},{9,10},{10,11},{12,13},{... | collective-permute-start | bytes 1572872 | tf_op jit(solution)/shard_map/ppermute | solution.py:19
  13.1 6.2 %collective-permute-done = f32[128,1024]{1,0:T(8,128)S(1)} collective-permute-done((f32[128,1024]{1,0:T(8,128)S(1)}, f32[128,1024]{1,0:T(8,128)S(1)}, u32[]{:S(2)}, u32[]{:S(2)}) %collective-permute-start) | collective-permute-done | bytes 524320 | tf_op jit(solution)/shard_map/ppermute | solution.py:19
  20.8 8.6 %collective-permute-done.6 = f32[128,1024]{1,0:T(8,128)S(1)} collective-permute-done((f32[128,1024]{1,0:T(8,128)S(1)}, f32[128,1024]{1,0:T(8,128)S(1)}, u32[]{:S(2)}, u32[]{:S(2)}) %collective-permute-start.6) | collective-permute-done | bytes 524320 | tf_op jit(solution)/shard_map/ppermute | solution.py:19
  32.2 4.6 %collective-permute-done.3 = f32[128,1024]{1,0:T(8,128)S(1)} collective-permute-done((f32[128,1024]{1,0:T(8,128)S(1)}, f32[128,1024]{1,0:T(8,128)S(1)}, u32[]{:S(2)}, u32[]{:S(2)}) %collective-permute-start.3) | collective-permute-done | bytes 524320 | tf_op jit(solution)/shard_map/ppermute | solution.py:20
  40.3 11.8 %collective-permute-done.10 = f32[128,1024]{1,0:T(8,128)} collective-permute-done((f32[128,1024]{1,0:T(8,128)S(1)}, f32[128,1024]{1,0:T(8,128)}, u32[]{:S(2)}, u32[]{:S(2)}) %collective-permute-start.10) | collective-permute-done | bytes 524320 | tf_op jit(solution)/shard_map/ppermute | solution.py:20
  53.4 9.9 %collective-permute-done.4 = f32[128,1024]{1,0:T(8,128)} collective-permute-done((f32[128,1024]{1,0:T(8,128)S(1)}, f32[128,1024]{1,0:T(8,128)}, u32[]{:S(2)}, u32[]{:S(2)}) %collective-permute-start.4) | collective-permute-done | bytes 524320 | tf_op jit(solution)/shard_map/ppermute | solution.py:20
  70.4 4.1 %collective-permute-done.11 = f32[128,1024]{1,0:T(8,128)S(1)} collective-permute-done((f32[128,1024]{1,0:T(8,128)}, f32[128,1024]{1,0:T(8,128)S(1)}, u32[]{:S(2)}, u32[]{:S(2)}) %collective-permute-start.11) | collective-permute-done | bytes 524320 | tf_op jit(solution)/shard_map/ppermute | solution.py:20
  74.6 7.9 %collective-permute-done.5 = f32[128,1024]{1,0:T(8,128)S(1)} collective-permute-done((f32[128,1024]{1,0:T(8,128)}, f32[128,1024]{1,0:T(8,128)S(1)}, u32[]{:S(2)}, u32[]{:S(2)}) %collective-permute-start.5) | collective-permute-done | bytes 524320 | tf_op jit(solution)/shard_map/ppermute | solution.py:20
  86.4 2.0 %fusion.5 = f32[1024,64]{0,1:T(8,128)S(1)} fusion(f32[1024,1024]{1,0:T(8,128)S(1)} %bitcast.65, f32[512,128]{0,1:T(8,128)S(1)} %fusion.9, f32[512,128]{0,1:T(8,128)S(1)} %bitcast.84), kind=kOutput, calls=%fused_computation.14 | convolution fusion | flops 402718720 | bytes 4980736 | tf_op jit(solution)/shard_map/dot_general | solution.py:10
  94.6 2.0 %fusion.21 = f32[1024,64]{0,1:T(8,128)S(1)} fusion(f32[1024,1024]{1,0:T(8,128)S(1)} %bitcast.68, f32[1024,64]{0,1:T(8,128)S(1)} %collective-permute-done.20), kind=kOutput, calls=%fused_computation.79 | convolution fusion | flops 402653184 | bytes 4718592 | tf_op jit(solution)/shard_map/dot_general | solution.py:10
  100.2 2.0 %fusion.22 = f32[1024,64]{0,1:T(8,128)S(1)} fusion(f32[1024,1024]{1,0:T(8,128)S(1)} %bitcast.70, f32[1024,64]{0,1:T(8,128)S(1)} %collective-permute-done.21), kind=kOutput, calls=%fused_computation.80 | convolution fusion | flops 402653184 | bytes 4718592 | tf_op jit(solution)/shard_map/dot_general | solution.py:10
  105.7 2.0 %fusion.23 = f32[1024,64]{0,1:T(8,128)S(1)} fusion(f32[1024,1024]{1,0:T(8,128)S(1)} %bitcast.72, f32[1024,64]{0,1:T(8,128)S(1)} %collective-permute-done.22), kind=kOutput, calls=%fused_computation.81 | convolution fusion | flops 402653184 | bytes 4718592 | tf_op jit(solution)/shard_map/dot_general | solution.py:10
  108.4 2.0 %fusion.17 = f32[1024,64]{0,1:T(8,128)S(1)} fusion(f32[1024,1024]{1,0:T(8,128)S(1)} %bitcast.73, f32[1024,64]{0,1:T(8,128)S(1)} %collective-permute-done.15), kind=kOutput, calls=%fused_computation.75 | convolution fusion | flops 402653184 | bytes 4718592 | tf_op jit(solution)/shard_map/dot_general | solution.py:10
  111.1 2.0 %fusion.24 = f32[1024,64]{0,1:T(8,128)S(1)} fusion(f32[1024,1024]{1,0:T(8,128)S(1)} %bitcast.74, f32[1024,64]{0,1:T(8,128)S(1)} %collective-permute-done.23), kind=kOutput, calls=%fused_computation.82 | convolution fusion | flops 402653184 | bytes 4718592 | tf_op jit(solution)/shard_map/dot_general | solution.py:10
  120.1 2.0 %fusion.19 = f32[1024,64]{0,1:T(8,128)S(1)} fusion(f32[1024,1024]{1,0:T(8,128)S(1)} %bitcast.77, f32[1024,64]{0,1:T(8,128)S(1)} %collective-permute-done.17), kind=kOutput, calls=%fused_computation.77 | convolution fusion | flops 402653184 | bytes 4718592 | tf_op jit(solution)/shard_map/dot_general | solution.py:10
  123.5 6.8 %collective-permute-done.25 = f32[1024,64]{0,1:T(8,128)S(1)} collective-permute-done((f32[1024,64]{0,1:T(8,128)S(1)}, f32[1024,64]{0,1:T(8,128)S(1)}, u32[]{:S(2)}, u32[]{:S(2)}) %collective-permute-start.25) | collective-permute-done | bytes 262176 | tf_op jit(solution)/shard_map/ppermute | solution.py:55
  130.3 2.1 %convolution_select_fusion = f32[1024,64]{0,1:T(8,128)S(1)} fusion(f32[1024,1024]{1,0:T(8,128)S(1)} %bitcast.78, f32[1024,64]{0,1:T(8,128)S(1)} %collective-permute-done.25, f32[1024,64]{0,1:T(8,128)S(1)} %fusion.25, f32[1024,64]{0,1:T(8,128)S(1)} %fusion.24, f32[1024,64]{0,1:T(8,128)S(1)} %fusion.23, f32[1024,64]{0,1:T(8,128)S(1)} %fusion.22, ...), kind=kOutput, calls=%fused_computation.3 | convolution fusion | flops 403111936 | bytes 6553607 | tf_op jit(solution)/shard_map/dot_general | solution.py:10
  133.8 2.1 %convolution_select_fusion.1 = f32[1024,64]{0,1:T(8,128)S(1)} fusion(f32[1024,1024]{1,0:T(8,128)S(1)} %bitcast.79, f32[1024,64]{0,1:T(8,128)S(1)} %collective-permute-done.18, f32[1024,64]{0,1:T(8,128)S(1)} %fusion.19, f32[1024,64]{0,1:T(8,128)S(1)} %fusion.18, f32[1024,64]{0,1:T(8,128)S(1)} %fusion.17, f32[1024,64]{0,1:T(8,128)S(1)} %fusion.16, ...), kind=kOutput, calls=%fused_computation.4 | convolution fusion | flops 403111936 | bytes 6553607 | tf_op jit(solution)/shard_map/dot_general | solution.py:10
  139.6 6.5 %collective-permute-done.26 = f32[512,128]{0,1:T(8,128)S(1)} collective-permute-done((f32[512,128]{0,1:T(8,128)S(1)}, f32[512,128]{0,1:T(8,128)S(1)}, u32[]{:S(2)}, u32[]{:S(2)}) %collective-permute-start.26) | collective-permute-done | bytes 262176 | tf_op jit(solution)/shard_map/ppermute | solution.py:66
  146.2 15.9 %collective-permute-done.27 = f32[512,128]{0,1:T(8,128)S(1)} collective-permute-done((f32[512,128]{0,1:T(8,128)S(1)}, f32[512,128]{0,1:T(8,128)S(1)}, u32[]{:S(2)}, u32[]{:S(2)}) %collective-permute-start.27) | collective-permute-done | bytes 262176 | tf_op jit(solution)/shard_map/ppermute | solution.py:66
  162.3 2.2 %fusion.2 = f32[256,2048]{1,0:T(8,128)S(1)} fusion(f32[512,2048]{1,0:T(8,128)S(1)} %copy-done, f32[256,896]{0,1:T(8,128)S(1)} %slice_dynamic-update-slice_fusion.7, s32[]{:T(128)S(6)} %select_n.136), kind=kOutput, calls=%fused_computation.9 | convolution fusion | flops 1610612736 | bytes 6815748 | tf_op jit(solution)/shard_map/dot_general | solution.py:10
  164.6 2.3 %fusion = f32[2048]{0:T(1024)S(1)} fusion(f32[256,2048]{1,0:T(8,128)S(1)} %fusion.2, f32[512,2048]{1,0:T(8,128)S(1)} %copy-done, f32[256,896]{0,1:T(8,128)S(1)} %get-tuple-element.13, s32[]{:T(128)S(6)} %select_n.136), kind=kOutput, calls=%fused_computation.2 | convolution fusion | flops 1611659264 | bytes 6823940 | tf_op jit(solution)/shard_map/dot_general | solution.py:10
  167.0 3.5 %collective-permute-done.29 = f32[512]{0:T(512)S(1)} collective-permute-done((f32[512]{0:T(512)S(1)}, f32[512]{0:T(512)S(1)}, u32[]{:S(2)}, u32[]{:S(2)}) %collective-permute-start.29) | collective-permute-done | bytes 2080 | tf_op jit(solution)/shard_map/ppermute | solution.py:82
  (103 shorter events, 52.7 us)
Async XLA Ops:
  2.0 17.3 %collective-permute-start = (f32[128,1024]{1,0:T(8,128)S(1)}, f32[128,1024]{1,0:T(8,128)S(1)}, u32[]{:S(2)}, u32[]{:S(2)}) collective-permute-start(f32[128,1024]{1,0:T(8,128)S(1)} %get-tuple-element.4), channel_id=1, source_target_pairs={{0,1},{1,2},{2,3},{4,5},{5,6},{6,7},{8,9},{9,10},{10,11},{12,13},{... | collective-permute-start | bytes 1572872 | tf_op jit(solution)/shard_map/ppermute | solution.py:19
  7.0 22.4 %collective-permute-start.6 = (f32[128,1024]{1,0:T(8,128)S(1)}, f32[128,1024]{1,0:T(8,128)S(1)}, u32[]{:S(2)}, u32[]{:S(2)}) collective-permute-start(f32[128,1024]{1,0:T(8,128)S(1)} %get-tuple-element.5), channel_id=1, source_target_pairs={{0,1},{1,2},{2,3},{4,5},{5,6},{6,7},{8,9},{9,10},{10,11},{12,13},{... | collective-permute-start | bytes 1572872 | tf_op jit(solution)/shard_map/ppermute | solution.py:19
  10.5 20.3 %collective-permute-start.9 = (f32[128,1024]{1,0:T(8,128)S(1)}, f32[128,1024]{1,0:T(8,128)S(1)}, u32[]{:S(2)}, u32[]{:S(2)}) collective-permute-start(f32[128,1024]{1,0:T(8,128)S(1)} %get-tuple-element.5), channel_id=1, source_target_pairs={{1,0},{2,1},{3,2},{5,4},{6,5},{7,6},{9,8},{10,9},{11,10},{13,12},{... | collective-permute-start | bytes 1572872 | tf_op jit(solution)/shard_map/ppermute | solution.py:20
  11.8 24.9 %collective-permute-start.3 = (f32[128,1024]{1,0:T(8,128)S(1)}, f32[128,1024]{1,0:T(8,128)S(1)}, u32[]{:S(2)}, u32[]{:S(2)}) collective-permute-start(f32[128,1024]{1,0:T(8,128)S(1)} %get-tuple-element.4), channel_id=1, source_target_pairs={{1,0},{2,1},{3,2},{5,4},{6,5},{7,6},{9,8},{10,9},{11,10},{13,12},{... | collective-permute-start | bytes 1572872 | tf_op jit(solution)/shard_map/ppermute | solution.py:20
  19.3 18.8 %collective-permute-start.1 = (f32[128,1024]{1,0:T(8,128)S(1)}, f32[128,1024]{1,0:T(8,128)}, u32[]{:S(2)}, u32[]{:S(2)}) collective-permute-start(f32[128,1024]{1,0:T(8,128)S(1)} %collective-permute-done), channel_id=1, source_target_pairs={{1,2},{2,3},{5,6},{6,7},{9,10},{10,11},{13,14},{14,15},{17,18},{18... | collective-permute-start | bytes 1572872 | tf_op jit(solution)/shard_map/ppermute | solution.py:19
  29.4 10.1 %collective-permute-start.7 = (f32[128,1024]{1,0:T(8,128)S(1)}, f32[128,1024]{1,0:T(8,128)}, u32[]{:S(2)}, u32[]{:S(2)}) collective-permute-start(f32[128,1024]{1,0:T(8,128)S(1)} %collective-permute-done.6), channel_id=1, source_target_pairs={{1,2},{2,3},{5,6},{6,7},{9,10},{10,11},{13,14},{14,15},{17,18},{18... | collective-permute-start | bytes 1572872 | tf_op jit(solution)/shard_map/ppermute | solution.py:19
  30.9 21.2 %collective-permute-start.10 = (f32[128,1024]{1,0:T(8,128)S(1)}, f32[128,1024]{1,0:T(8,128)}, u32[]{:S(2)}, u32[]{:S(2)}) collective-permute-start(f32[128,1024]{1,0:T(8,128)S(1)} %collective-permute-done.9), channel_id=1, source_target_pairs={{1,0},{2,1},{5,4},{6,5},{9,8},{10,9},{13,12},{14,13},{17,16},{18,1... | collective-permute-start | bytes 1572872 | tf_op jit(solution)/shard_map/ppermute | solution.py:20
  36.8 26.5 %collective-permute-start.4 = (f32[128,1024]{1,0:T(8,128)S(1)}, f32[128,1024]{1,0:T(8,128)}, u32[]{:S(2)}, u32[]{:S(2)}) collective-permute-start(f32[128,1024]{1,0:T(8,128)S(1)} %collective-permute-done.3), channel_id=1, source_target_pairs={{1,0},{2,1},{5,4},{6,5},{9,8},{10,9},{13,12},{14,13},{17,16},{18,1... | collective-permute-start | bytes 1572872 | tf_op jit(solution)/shard_map/ppermute | solution.py:20
  38.1 26.5 %collective-permute-start.2 = (f32[128,1024]{1,0:T(8,128)}, f32[128,1024]{1,0:T(8,128)}, u32[]{:S(2)}, u32[]{:S(2)}) collective-permute-start(f32[128,1024]{1,0:T(8,128)} %collective-permute-done.1), channel_id=1, source_target_pairs={{2,3},{6,7},{10,11},{14,15},{18,19},{22,23},{26,27},{30,31}} | collective-permute-start | bytes 1572872 | tf_op jit(solution)/shard_map/ppermute | solution.py:19
  39.5 27.3 %collective-permute-start.8 = (f32[128,1024]{1,0:T(8,128)}, f32[128,1024]{1,0:T(8,128)S(1)}, u32[]{:S(2)}, u32[]{:S(2)}) collective-permute-start(f32[128,1024]{1,0:T(8,128)} %collective-permute-done.7), channel_id=1, source_target_pairs={{2,3},{6,7},{10,11},{14,15},{18,19},{22,23},{26,27},{30,31}} | collective-permute-start | bytes 1572872 | tf_op jit(solution)/shard_map/ppermute | solution.py:19
  52.1 22.4 %collective-permute-start.11 = (f32[128,1024]{1,0:T(8,128)}, f32[128,1024]{1,0:T(8,128)S(1)}, u32[]{:S(2)}, u32[]{:S(2)}) collective-permute-start(f32[128,1024]{1,0:T(8,128)} %collective-permute-done.10), channel_id=1, source_target_pairs={{1,0},{5,4},{9,8},{13,12},{17,16},{21,20},{25,24},{29,28}} | collective-permute-start | bytes 1572872 | tf_op jit(solution)/shard_map/ppermute | solution.py:20
  63.3 19.2 %collective-permute-start.5 = (f32[128,1024]{1,0:T(8,128)}, f32[128,1024]{1,0:T(8,128)S(1)}, u32[]{:S(2)}, u32[]{:S(2)}) collective-permute-start(f32[128,1024]{1,0:T(8,128)} %collective-permute-done.4), channel_id=1, source_target_pairs={{1,0},{5,4},{9,8},{13,12},{17,16},{21,20},{25,24},{29,28}} | collective-permute-start | bytes 1572872 | tf_op jit(solution)/shard_map/ppermute | solution.py:20
  93.9 3.6 %collective-permute-start.13 = (f32[1024,64]{0,1:T(8,128)S(1)}, f32[1024,64]{0,1:T(8,128)S(1)}, u32[]{:S(2)}, u32[]{:S(2)}) collective-permute-start(f32[1024,64]{0,1:T(8,128)S(1)} %fusion.14), channel_id=1, source_target_pairs={{24,20},{25,21},{26,22},{27,23}} | collective-permute-start | bytes 786440 | tf_op jit(solution)/shard_map/ppermute | solution.py:55
  96.6 3.6 %collective-permute-start.21 = (f32[1024,64]{0,1:T(8,128)S(1)}, f32[1024,64]{0,1:T(8,128)S(1)}, u32[]{:S(2)}, u32[]{:S(2)}) collective-permute-start(f32[1024,64]{0,1:T(8,128)S(1)} %fusion.21), channel_id=1, source_target_pairs={{20,16},{21,17},{22,18},{23,19}} | collective-permute-start | bytes 786440 | tf_op jit(solution)/shard_map/ppermute | solution.py:55
  99.5 3.4 %collective-permute-start.14 = (f32[1024,64]{0,1:T(8,128)S(1)}, f32[1024,64]{0,1:T(8,128)S(1)}, u32[]{:S(2)}, u32[]{:S(2)}) collective-permute-start(f32[1024,64]{0,1:T(8,128)S(1)} %fusion.15), channel_id=1, source_target_pairs={{20,16},{21,17},{22,18},{23,19}} | collective-permute-start | bytes 786440 | tf_op jit(solution)/shard_map/ppermute | solution.py:55
  105.0 3.4 %collective-permute-start.15 = (f32[1024,64]{0,1:T(8,128)S(1)}, f32[1024,64]{0,1:T(8,128)S(1)}, u32[]{:S(2)}, u32[]{:S(2)}) collective-permute-start(f32[1024,64]{0,1:T(8,128)S(1)} %fusion.16), channel_id=1, source_target_pairs={{16,12},{17,13},{18,14},{19,15}} | collective-permute-start | bytes 786440 | tf_op jit(solution)/shard_map/ppermute | solution.py:55
  113.2 3.6 %collective-permute-start.24 = (f32[1024,64]{0,1:T(8,128)S(1)}, f32[1024,64]{0,1:T(8,128)S(1)}, u32[]{:S(2)}, u32[]{:S(2)}) collective-permute-start(f32[1024,64]{0,1:T(8,128)S(1)} %fusion.24), channel_id=1, source_target_pairs={{8,4},{9,5},{10,6},{11,7}} | collective-permute-start | bytes 786440 | tf_op jit(solution)/shard_map/ppermute | solution.py:55
  115.9 4.2 %collective-permute-start.17 = (f32[1024,64]{0,1:T(8,128)S(1)}, f32[1024,64]{0,1:T(8,128)S(1)}, u32[]{:S(2)}, u32[]{:S(2)}) collective-permute-start(f32[1024,64]{0,1:T(8,128)S(1)} %fusion.18), channel_id=1, source_target_pairs={{8,4},{9,5},{10,6},{11,7}} | collective-permute-start | bytes 786440 | tf_op jit(solution)/shard_map/ppermute | solution.py:55
  118.8 11.4 %collective-permute-start.25 = (f32[1024,64]{0,1:T(8,128)S(1)}, f32[1024,64]{0,1:T(8,128)S(1)}, u32[]{:S(2)}, u32[]{:S(2)}) collective-permute-start(f32[1024,64]{0,1:T(8,128)S(1)} %fusion.25), channel_id=1, source_target_pairs={{4,0},{5,1},{6,2},{7,3}} | collective-permute-start | bytes 786440 | tf_op jit(solution)/shard_map/ppermute | solution.py:55
  122.2 11.6 %collective-permute-start.18 = (f32[1024,64]{0,1:T(8,128)S(1)}, f32[1024,64]{0,1:T(8,128)S(1)}, u32[]{:S(2)}, u32[]{:S(2)}) collective-permute-start(f32[1024,64]{0,1:T(8,128)S(1)} %fusion.19), channel_id=1, source_target_pairs={{4,0},{5,1},{6,2},{7,3}} | collective-permute-start | bytes 786440 | tf_op jit(solution)/shard_map/ppermute | solution.py:55
  137.0 9.1 %collective-permute-start.26 = (f32[512,128]{0,1:T(8,128)S(1)}, f32[512,128]{0,1:T(8,128)S(1)}, u32[]{:S(2)}, u32[]{:S(2)}) collective-permute-start(f32[512,128]{0,1:T(8,128)S(1)} %pad_maximum_fusion.4), channel_id=1, source_target_pairs={{0,3},{1,0},{2,1},{3,2},{4,7},{5,4},{6,5},{7,6},{8,11},{9,8},{10,9... | collective-permute-start | bytes 786440 | tf_op jit(solution)/shard_map/ppermute | solution.py:66
  137.2 24.9 %collective-permute-start.27 = (f32[512,128]{0,1:T(8,128)S(1)}, f32[512,128]{0,1:T(8,128)S(1)}, u32[]{:S(2)}, u32[]{:S(2)}) collective-permute-start(f32[512,128]{0,1:T(8,128)S(1)} %pad_maximum_fusion.5), channel_id=1, source_target_pairs={{0,2},{1,3},{2,0},{3,1},{4,6},{5,7},{6,4},{7,5},{8,10},{9,11},{10,... | collective-permute-start | bytes 786440 | tf_op jit(solution)/shard_map/ppermute | solution.py:66
  138.4 23.7 %collective-permute-start.28 = (f32[512,128]{0,1:T(8,128)S(1)}, f32[512,128]{0,1:T(8,128)S(1)}, u32[]{:S(2)}, u32[]{:S(2)}) collective-permute-start(f32[512,128]{0,1:T(8,128)S(1)} %pad_maximum_fusion.6), channel_id=1, source_target_pairs={{0,1},{1,2},{2,3},{3,0},{4,5},{5,6},{6,7},{7,4},{8,9},{9,10},{10,1... | collective-permute-start | bytes 786440 | tf_op jit(solution)/shard_map/ppermute | solution.py:66
  166.9 3.6 %collective-permute-start.29 = (f32[512]{0:T(512)S(1)}, f32[512]{0:T(512)S(1)}, u32[]{:S(2)}, u32[]{:S(2)}) collective-permute-start(f32[512]{0:T(512)S(1)} %dynamic_slice.52), channel_id=1, source_target_pairs={{0,1},{1,0},{2,3},{3,2},{4,5},{5,4},{6,7},{7,6},{8,9},{9,8},{10,11... | collective-permute-start | bytes 6152 | tf_op jit(solution)/shard_map/ppermute | solution.py:82
  (10 other events, 121.5 us)

commit v17 on v16

--- a/solution.py
+++ b/solution.py
@@ -58,21 +58,19 @@
     rows = own_cols.shape[0] // count
     half = count // 2
     blocks = own_cols.reshape(count, rows, width)
-    main_pieces = [blocks[place]]
-    pair_pieces = [blocks[(place + half) % count]]
+    pieces = [jnp.concatenate([blocks[place], blocks[(place + half) % count]], axis=0)]
     for d in range(1, count):
         target = (place + d) % count
         payload = jnp.concatenate([blocks[target], blocks[(target + half) % count]], axis=0)
-        got = lax.ppermute(payload, "row", [(z, (z + d) % count) for z in range(count)])
-        main_pieces.append(got[:rows])
-        pair_pieces.append(got[rows:])
+        pieces.append(lax.ppermute(payload, "row", [(z, (z + d) % count) for z in range(count)]))
 
     def in_order(pieces):
         by_offset = jnp.concatenate(pieces[::-1] + pieces[:0:-1], axis=1)
         return lax.dynamic_slice_in_dim(by_offset, (count - 1 - place) * width, count * width, 1)
 
-    rows_traj = product(in_order(main_pieces), terminal_states)
-    pair_traj = product(in_order(pair_pieces), terminal_states)
+    both_traj = product(in_order(pieces), terminal_states)
+    rows_traj = both_traj[:rows]
+    pair_traj = both_traj[rows:]
     partial = jnp.sum(rows_traj * pair_traj, axis=0)
     cols = terminal_states.shape[1] // count
     total = lax.dynamic_slice_in_dim(partial, place * cols, cols, 0)

time: 172 us -> 175 us (1.017)
    dot_general x18 -> x17, matrix products: 37.1 us -> 38.1 us  [product(): jnp.dot(left, right, precision=lax.Precision.HIGH, preferred_element_type...]
    unnamed x31 -> x24, local copies, waits for them, and re-layouts: 6.22 us -> 6.21 us
where the time goes in v17:
time: 175 us; the launch traced here: 174 us
  waiting for transfers between devices  87.6 us (50%)
  matrix products  38.1 us (22%)
  starting transfers between devices  34.7 us (20%)
  local copies, waits for them, and re-layouts  9.01 us (5%)
  other arithmetic  3.08 us (2%)
    ppermute x6, waiting for transfers between devices, line_gather(): lax.ppermute(leftward, 'row', [(z, z - 1) for z in range(1, count - t + 1)])  38.3 us
    dot_general x17, matrix products, product(): jnp.dot(left, right, precision=lax.Precision.HIGH, preferred_element_type...  38.1 us
    ppermute x3, waiting for transfers between devices, body(): lax.ppermute(payload, 'row', [(z, (z + d) % count) for z in range(count)])  22.7 us
    ppermute x6, waiting for transfers between devices, line_gather(): lax.ppermute(rightward, 'row', [(z, z + 1) for z in range(t - 1, count -...  14.8 us
    ppermute x6, starting transfers between devices, line_gather(): lax.ppermute(rightward, 'row', [(z, z + 1) for z in range(t - 1, count -...  13.7 us
    ppermute x14, starting transfers between devices, body(): incoming[j] = lax.ppermute(fresh, 'tm', [(k, k - 1)])  11.1 us
    ppermute x14, waiting for transfers between devices, body(): incoming[j] = lax.ppermute(fresh, 'tm', [(k, k - 1)])  8.31 us
    ppermute x6, starting transfers between devices, line_gather(): lax.ppermute(leftward, 'row', [(z, z - 1) for z in range(1, count - t + 1)])  7.71 us
  transfers between devices with their start and end apart: 30, of which 12 were waited for; matrix products, arithmetic and copies ran while one was open for 20% of the time, Pallas kernels for 0%

profile of v17, /device:TPU:0, one launch (start us, length us, event | category | flops | bytes accessed | tf_op | source)
XLA Modules:
  0.0 173.8 jit_solution(447772090595641488)
XLA Ops:
  2.0 5.1 %collective-permute-start = (f32[128,1024]{1,0:T(8,128)S(1)}, f32[128,1024]{1,0:T(8,128)S(1)}, u32[]{:S(2)}, u32[]{:S(2)}) collective-permute-start(f32[128,1024]{1,0:T(8,128)S(1)} %get-tuple-element.6), channel_id=1, source_target_pairs={{0,1},{1,2},{2,3},{4,5},{5,6},{6,7},{8,9},{9,10},{10,11},{12,13},{... | collective-permute-start | bytes 1572872 | tf_op jit(solution)/shard_map/ppermute | solution.py:19
  7.1 3.5 %collective-permute-start.6 = (f32[128,1024]{1,0:T(8,128)S(1)}, f32[128,1024]{1,0:T(8,128)S(1)}, u32[]{:S(2)}, u32[]{:S(2)}) collective-permute-start(f32[128,1024]{1,0:T(8,128)S(1)} %get-tuple-element.7), channel_id=1, source_target_pairs={{0,1},{1,2},{2,3},{4,5},{5,6},{6,7},{8,9},{9,10},{10,11},{12,13},{... | collective-permute-start | bytes 1572872 | tf_op jit(solution)/shard_map/ppermute | solution.py:19
  13.2 6.2 %collective-permute-done = f32[128,1024]{1,0:T(8,128)S(1)} collective-permute-done((f32[128,1024]{1,0:T(8,128)S(1)}, f32[128,1024]{1,0:T(8,128)S(1)}, u32[]{:S(2)}, u32[]{:S(2)}) %collective-permute-start) | collective-permute-done | bytes 524320 | tf_op jit(solution)/shard_map/ppermute | solution.py:19
  20.8 8.7 %collective-permute-done.6 = f32[128,1024]{1,0:T(8,128)S(1)} collective-permute-done((f32[128,1024]{1,0:T(8,128)S(1)}, f32[128,1024]{1,0:T(8,128)S(1)}, u32[]{:S(2)}, u32[]{:S(2)}) %collective-permute-start.6) | collective-permute-done | bytes 524320 | tf_op jit(solution)/shard_map/ppermute | solution.py:19
  32.2 4.6 %collective-permute-done.3 = f32[128,1024]{1,0:T(8,128)S(1)} collective-permute-done((f32[128,1024]{1,0:T(8,128)S(1)}, f32[128,1024]{1,0:T(8,128)S(1)}, u32[]{:S(2)}, u32[]{:S(2)}) %collective-permute-start.3) | collective-permute-done | bytes 524320 | tf_op jit(solution)/shard_map/ppermute | solution.py:20
  40.4 11.7 %collective-permute-done.10 = f32[128,1024]{1,0:T(8,128)} collective-permute-done((f32[128,1024]{1,0:T(8,128)S(1)}, f32[128,1024]{1,0:T(8,128)}, u32[]{:S(2)}, u32[]{:S(2)}) %collective-permute-start.10) | collective-permute-done | bytes 524320 | tf_op jit(solution)/shard_map/ppermute | solution.py:20
  53.4 9.9 %collective-permute-done.4 = f32[128,1024]{1,0:T(8,128)} collective-permute-done((f32[128,1024]{1,0:T(8,128)S(1)}, f32[128,1024]{1,0:T(8,128)}, u32[]{:S(2)}, u32[]{:S(2)}) %collective-permute-start.4) | collective-permute-done | bytes 524320 | tf_op jit(solution)/shard_map/ppermute | solution.py:20
  70.4 4.1 %collective-permute-done.11 = f32[128,1024]{1,0:T(8,128)S(1)} collective-permute-done((f32[128,1024]{1,0:T(8,128)}, f32[128,1024]{1,0:T(8,128)S(1)}, u32[]{:S(2)}, u32[]{:S(2)}) %collective-permute-start.11) | collective-permute-done | bytes 524320 | tf_op jit(solution)/shard_map/ppermute | solution.py:20
  74.7 7.9 %collective-permute-done.5 = f32[128,1024]{1,0:T(8,128)S(1)} collective-permute-done((f32[128,1024]{1,0:T(8,128)}, f32[128,1024]{1,0:T(8,128)S(1)}, u32[]{:S(2)}, u32[]{:S(2)}) %collective-permute-start.5) | collective-permute-done | bytes 524320 | tf_op jit(solution)/shard_map/ppermute | solution.py:20
  91.9 2.0 %fusion.12 = f32[1024,64]{0,1:T(8,128)S(1)} fusion(f32[1024,1024]{1,0:T(8,128)S(1)} %bitcast.66, f32[1024,64]{0,1:T(8,128)S(1)} %collective-permute-done.12), kind=kOutput, calls=%fused_computation.65 | convolution fusion | flops 402653184 | bytes 4718592 | tf_op jit(solution)/shard_map/dot_general | solution.py:10
  94.6 2.0 %fusion.19 = f32[1024,64]{0,1:T(8,128)S(1)} fusion(f32[1024,1024]{1,0:T(8,128)S(1)} %bitcast.67, f32[1024,64]{0,1:T(8,128)S(1)} %collective-permute-done.20), kind=kOutput, calls=%fused_computation.72 | convolution fusion | flops 402653184 | bytes 4718592 | tf_op jit(solution)/shard_map/dot_general | solution.py:10
  97.5 2.0 %fusion.13 = f32[1024,64]{0,1:T(8,128)S(1)} fusion(f32[1024,1024]{1,0:T(8,128)S(1)} %bitcast.68, f32[1024,64]{0,1:T(8,128)S(1)} %collective-permute-done.13), kind=kOutput, calls=%fused_computation.66 | convolution fusion | flops 402653184 | bytes 4718592 | tf_op jit(solution)/shard_map/dot_general | solution.py:10
  100.3 2.0 %fusion.20 = f32[1024,64]{0,1:T(8,128)S(1)} fusion(f32[1024,1024]{1,0:T(8,128)S(1)} %bitcast.69, f32[1024,64]{0,1:T(8,128)S(1)} %collective-permute-done.21), kind=kOutput, calls=%fused_computation.73 | convolution fusion | flops 402653184 | bytes 4718592 | tf_op jit(solution)/shard_map/dot_general | solution.py:10
  105.7 2.0 %fusion.21 = f32[1024,64]{0,1:T(8,128)S(1)} fusion(f32[1024,1024]{1,0:T(8,128)S(1)} %bitcast.71, f32[1024,64]{0,1:T(8,128)S(1)} %collective-permute-done.22), kind=kOutput, calls=%fused_computation.74 | convolution fusion | flops 402653184 | bytes 4718592 | tf_op jit(solution)/shard_map/dot_general | solution.py:10
  108.5 2.0 %fusion.15 = f32[1024,64]{0,1:T(8,128)S(1)} fusion(f32[1024,1024]{1,0:T(8,128)S(1)} %bitcast.72, f32[1024,64]{0,1:T(8,128)S(1)} %collective-permute-done.15), kind=kOutput, calls=%fused_computation.68 | convolution fusion | flops 402653184 | bytes 4718592 | tf_op jit(solution)/shard_map/dot_general | solution.py:10
  111.2 2.0 %fusion.22 = f32[1024,64]{0,1:T(8,128)S(1)} fusion(f32[1024,1024]{1,0:T(8,128)S(1)} %bitcast.73, f32[1024,64]{0,1:T(8,128)S(1)} %collective-permute-done.23), kind=kOutput, calls=%fused_computation.75 | convolution fusion | flops 402653184 | bytes 4718592 | tf_op jit(solution)/shard_map/dot_general | solution.py:10
  116.9 2.0 %fusion.23 = f32[1024,64]{0,1:T(8,128)S(1)} fusion(f32[1024,1024]{1,0:T(8,128)S(1)} %bitcast.75, f32[1024,64]{0,1:T(8,128)S(1)} %collective-permute-done.24), kind=kOutput, calls=%fused_computation.76 | convolution fusion | flops 402653184 | bytes 4718592 | tf_op jit(solution)/shard_map/dot_general | solution.py:10
  123.5 6.8 %collective-permute-done.25 = f32[1024,64]{0,1:T(8,128)S(1)} collective-permute-done((f32[1024,64]{0,1:T(8,128)S(1)}, f32[1024,64]{0,1:T(8,128)S(1)}, u32[]{:S(2)}, u32[]{:S(2)}) %collective-permute-start.25) | collective-permute-done | bytes 262176 | tf_op jit(solution)/shard_map/ppermute | solution.py:55
  130.3 2.1 %convolution_select_fusion = f32[1024,64]{0,1:T(8,128)S(1)} fusion(f32[1024,1024]{1,0:T(8,128)S(1)} %bitcast.77, f32[1024,64]{0,1:T(8,128)S(1)} %collective-permute-done.25, f32[1024,64]{0,1:T(8,128)S(1)} %fusion.23, f32[1024,64]{0,1:T(8,128)S(1)} %fusion.22, f32[1024,64]{0,1:T(8,128)S(1)} %fusion.21, f32[1024,64]{0,1:T(8,128)S(1)} %fusion.20, ...), kind=kOutput, calls=%fused_computation.4 | convolution fusion | flops 403111936 | bytes 6553607 | tf_op jit(solution)/shard_map/dot_general | solution.py:10
  133.9 2.1 %convolution_select_fusion.1 = f32[1024,64]{0,1:T(8,128)S(1)} fusion(f32[1024,1024]{1,0:T(8,128)S(1)} %bitcast.78, f32[1024,64]{0,1:T(8,128)S(1)} %collective-permute-done.18, f32[1024,64]{0,1:T(8,128)S(1)} %fusion.17, f32[1024,64]{0,1:T(8,128)S(1)} %fusion.16, f32[1024,64]{0,1:T(8,128)S(1)} %fusion.15, f32[1024,64]{0,1:T(8,128)S(1)} %fusion.14, ...), kind=kOutput, calls=%fused_computation.5 | convolution fusion | flops 403111936 | bytes 6553607 | tf_op jit(solution)/shard_map/dot_general | solution.py:10
  139.4 6.8 %collective-permute-done.26 = f32[512,128]{0,1:T(8,128)S(1)} collective-permute-done((f32[512,128]{0,1:T(8,128)S(1)}, f32[512,128]{0,1:T(8,128)S(1)}, u32[]{:S(2)}, u32[]{:S(2)}) %collective-permute-start.26) | collective-permute-done | bytes 262176 | tf_op jit(solution)/shard_map/ppermute | solution.py:65
  146.2 15.9 %collective-permute-done.27 = f32[512,128]{0,1:T(8,128)S(1)} collective-permute-done((f32[512,128]{0,1:T(8,128)S(1)}, f32[512,128]{0,1:T(8,128)S(1)}, u32[]{:S(2)}, u32[]{:S(2)}) %collective-permute-start.27) | collective-permute-done | bytes 262176 | tf_op jit(solution)/shard_map/ppermute | solution.py:65
  162.3 5.5 %fusion.1 = f32[512,2048]{1,0:T(8,128)S(1)} fusion(f32[512,2048]{1,0:T(8,128)} %param.5, f32[512,896]{0,1:T(8,128)S(1)} %constant_dynamic-update-slice_fusion.14, s32[]{:T(128)S(6)} %select_n.135), kind=kOutput, calls=%fused_computation.6 | convolution fusion | flops 3221225472 | bytes 9437188 | tf_op jit(solution)/shard_map/dot_general | solution.py:10
  169.6 3.5 %collective-permute-done.29 = f32[512]{0:T(512)S(1)} collective-permute-done((f32[512]{0:T(512)S(1)}, f32[512]{0:T(512)S(1)}, u32[]{:S(2)}, u32[]{:S(2)}) %collective-permute-start.29) | collective-permute-done | bytes 2080 | tf_op jit(solution)/shard_map/ppermute | solution.py:80
  (96 shorter events, 51.9 us)
Async XLA Ops:
  2.0 17.4 %collective-permute-start = (f32[128,1024]{1,0:T(8,128)S(1)}, f32[128,1024]{1,0:T(8,128)S(1)}, u32[]{:S(2)}, u32[]{:S(2)}) collective-permute-start(f32[128,1024]{1,0:T(8,128)S(1)} %get-tuple-element.6), channel_id=1, source_target_pairs={{0,1},{1,2},{2,3},{4,5},{5,6},{6,7},{8,9},{9,10},{10,11},{12,13},{... | collective-permute-start | bytes 1572872 | tf_op jit(solution)/shard_map/ppermute | solution.py:19
  7.1 22.4 %collective-permute-start.6 = (f32[128,1024]{1,0:T(8,128)S(1)}, f32[128,1024]{1,0:T(8,128)S(1)}, u32[]{:S(2)}, u32[]{:S(2)}) collective-permute-start(f32[128,1024]{1,0:T(8,128)S(1)} %get-tuple-element.7), channel_id=1, source_target_pairs={{0,1},{1,2},{2,3},{4,5},{5,6},{6,7},{8,9},{9,10},{10,11},{12,13},{... | collective-permute-start | bytes 1572872 | tf_op jit(solution)/shard_map/ppermute | solution.py:19
  10.6 20.3 %collective-permute-start.9 = (f32[128,1024]{1,0:T(8,128)S(1)}, f32[128,1024]{1,0:T(8,128)S(1)}, u32[]{:S(2)}, u32[]{:S(2)}) collective-permute-start(f32[128,1024]{1,0:T(8,128)S(1)} %get-tuple-element.7), channel_id=1, source_target_pairs={{1,0},{2,1},{3,2},{5,4},{6,5},{7,6},{9,8},{10,9},{11,10},{13,12},{... | collective-permute-start | bytes 1572872 | tf_op jit(solution)/shard_map/ppermute | solution.py:20
  11.9 24.9 %collective-permute-start.3 = (f32[128,1024]{1,0:T(8,128)S(1)}, f32[128,1024]{1,0:T(8,128)S(1)}, u32[]{:S(2)}, u32[]{:S(2)}) collective-permute-start(f32[128,1024]{1,0:T(8,128)S(1)} %get-tuple-element.6), channel_id=1, source_target_pairs={{1,0},{2,1},{3,2},{5,4},{6,5},{7,6},{9,8},{10,9},{11,10},{13,12},{... | collective-permute-start | bytes 1572872 | tf_op jit(solution)/shard_map/ppermute | solution.py:20
  19.3 18.8 %collective-permute-start.1 = (f32[128,1024]{1,0:T(8,128)S(1)}, f32[128,1024]{1,0:T(8,128)}, u32[]{:S(2)}, u32[]{:S(2)}) collective-permute-start(f32[128,1024]{1,0:T(8,128)S(1)} %collective-permute-done), channel_id=1, source_target_pairs={{1,2},{2,3},{5,6},{6,7},{9,10},{10,11},{13,14},{14,15},{17,18},{18... | collective-permute-start | bytes 1572872 | tf_op jit(solution)/shard_map/ppermute | solution.py:19
  29.4 10.1 %collective-permute-start.7 = (f32[128,1024]{1,0:T(8,128)S(1)}, f32[128,1024]{1,0:T(8,128)}, u32[]{:S(2)}, u32[]{:S(2)}) collective-permute-start(f32[128,1024]{1,0:T(8,128)S(1)} %collective-permute-done.6), channel_id=1, source_target_pairs={{1,2},{2,3},{5,6},{6,7},{9,10},{10,11},{13,14},{14,15},{17,18},{18... | collective-permute-start | bytes 1572872 | tf_op jit(solution)/shard_map/ppermute | solution.py:19
  30.9 21.2 %collective-permute-start.10 = (f32[128,1024]{1,0:T(8,128)S(1)}, f32[128,1024]{1,0:T(8,128)}, u32[]{:S(2)}, u32[]{:S(2)}) collective-permute-start(f32[128,1024]{1,0:T(8,128)S(1)} %collective-permute-done.9), channel_id=1, source_target_pairs={{1,0},{2,1},{5,4},{6,5},{9,8},{10,9},{13,12},{14,13},{17,16},{18,1... | collective-permute-start | bytes 1572872 | tf_op jit(solution)/shard_map/ppermute | solution.py:20
  36.8 26.5 %collective-permute-start.4 = (f32[128,1024]{1,0:T(8,128)S(1)}, f32[128,1024]{1,0:T(8,128)}, u32[]{:S(2)}, u32[]{:S(2)}) collective-permute-start(f32[128,1024]{1,0:T(8,128)S(1)} %collective-permute-done.3), channel_id=1, source_target_pairs={{1,0},{2,1},{5,4},{6,5},{9,8},{10,9},{13,12},{14,13},{17,16},{18,1... | collective-permute-start | bytes 1572872 | tf_op jit(solution)/shard_map/ppermute | solution.py:20
  38.1 26.5 %collective-permute-start.2 = (f32[128,1024]{1,0:T(8,128)}, f32[128,1024]{1,0:T(8,128)}, u32[]{:S(2)}, u32[]{:S(2)}) collective-permute-start(f32[128,1024]{1,0:T(8,128)} %collective-permute-done.1), channel_id=1, source_target_pairs={{2,3},{6,7},{10,11},{14,15},{18,19},{22,23},{26,27},{30,31}} | collective-permute-start | bytes 1572872 | tf_op jit(solution)/shard_map/ppermute | solution.py:19
  39.6 27.3 %collective-permute-start.8 = (f32[128,1024]{1,0:T(8,128)}, f32[128,1024]{1,0:T(8,128)S(1)}, u32[]{:S(2)}, u32[]{:S(2)}) collective-permute-start(f32[128,1024]{1,0:T(8,128)} %collective-permute-done.7), channel_id=1, source_target_pairs={{2,3},{6,7},{10,11},{14,15},{18,19},{22,23},{26,27},{30,31}} | collective-permute-start | bytes 1572872 | tf_op jit(solution)/shard_map/ppermute | solution.py:19
  52.1 22.4 %collective-permute-start.11 = (f32[128,1024]{1,0:T(8,128)}, f32[128,1024]{1,0:T(8,128)S(1)}, u32[]{:S(2)}, u32[]{:S(2)}) collective-permute-start(f32[128,1024]{1,0:T(8,128)} %collective-permute-done.10), channel_id=1, source_target_pairs={{1,0},{5,4},{9,8},{13,12},{17,16},{21,20},{25,24},{29,28}} | collective-permute-start | bytes 1572872 | tf_op jit(solution)/shard_map/ppermute | solution.py:20
  63.4 19.2 %collective-permute-start.5 = (f32[128,1024]{1,0:T(8,128)}, f32[128,1024]{1,0:T(8,128)S(1)}, u32[]{:S(2)}, u32[]{:S(2)}) collective-permute-start(f32[128,1024]{1,0:T(8,128)} %collective-permute-done.4), channel_id=1, source_target_pairs={{1,0},{5,4},{9,8},{13,12},{17,16},{21,20},{25,24},{29,28}} | collective-permute-start | bytes 1572872 | tf_op jit(solution)/shard_map/ppermute | solution.py:20
  93.9 3.6 %collective-permute-start.13 = (f32[1024,64]{0,1:T(8,128)S(1)}, f32[1024,64]{0,1:T(8,128)S(1)}, u32[]{:S(2)}, u32[]{:S(2)}) collective-permute-start(f32[1024,64]{0,1:T(8,128)S(1)} %fusion.12), channel_id=1, source_target_pairs={{24,20},{25,21},{26,22},{27,23}} | collective-permute-start | bytes 786440 | tf_op jit(solution)/shard_map/ppermute | solution.py:55
  96.7 3.6 %collective-permute-start.21 = (f32[1024,64]{0,1:T(8,128)S(1)}, f32[1024,64]{0,1:T(8,128)S(1)}, u32[]{:S(2)}, u32[]{:S(2)}) collective-permute-start(f32[1024,64]{0,1:T(8,128)S(1)} %fusion.19), channel_id=1, source_target_pairs={{20,16},{21,17},{22,18},{23,19}} | collective-permute-start | bytes 786440 | tf_op jit(solution)/shard_map/ppermute | solution.py:55
  99.6 3.4 %collective-permute-start.14 = (f32[1024,64]{0,1:T(8,128)S(1)}, f32[1024,64]{0,1:T(8,128)S(1)}, u32[]{:S(2)}, u32[]{:S(2)}) collective-permute-start(f32[1024,64]{0,1:T(8,128)S(1)} %fusion.13), channel_id=1, source_target_pairs={{20,16},{21,17},{22,18},{23,19}} | collective-permute-start | bytes 786440 | tf_op jit(solution)/shard_map/ppermute | solution.py:55
  105.0 3.4 %collective-permute-start.15 = (f32[1024,64]{0,1:T(8,128)S(1)}, f32[1024,64]{0,1:T(8,128)S(1)}, u32[]{:S(2)}, u32[]{:S(2)}) collective-permute-start(f32[1024,64]{0,1:T(8,128)S(1)} %fusion.14), channel_id=1, source_target_pairs={{16,12},{17,13},{18,14},{19,15}} | collective-permute-start | bytes 786440 | tf_op jit(solution)/shard_map/ppermute | solution.py:55
  113.2 3.6 %collective-permute-start.24 = (f32[1024,64]{0,1:T(8,128)S(1)}, f32[1024,64]{0,1:T(8,128)S(1)}, u32[]{:S(2)}, u32[]{:S(2)}) collective-permute-start(f32[1024,64]{0,1:T(8,128)S(1)} %fusion.22), channel_id=1, source_target_pairs={{8,4},{9,5},{10,6},{11,7}} | collective-permute-start | bytes 786440 | tf_op jit(solution)/shard_map/ppermute | solution.py:55
  115.9 4.2 %collective-permute-start.17 = (f32[1024,64]{0,1:T(8,128)S(1)}, f32[1024,64]{0,1:T(8,128)S(1)}, u32[]{:S(2)}, u32[]{:S(2)}) collective-permute-start(f32[1024,64]{0,1:T(8,128)S(1)} %fusion.16), channel_id=1, source_target_pairs={{8,4},{9,5},{10,6},{11,7}} | collective-permute-start | bytes 786440 | tf_op jit(solution)/shard_map/ppermute | solution.py:55
  118.9 11.4 %collective-permute-start.25 = (f32[1024,64]{0,1:T(8,128)S(1)}, f32[1024,64]{0,1:T(8,128)S(1)}, u32[]{:S(2)}, u32[]{:S(2)}) collective-permute-start(f32[1024,64]{0,1:T(8,128)S(1)} %fusion.23), channel_id=1, source_target_pairs={{4,0},{5,1},{6,2},{7,3}} | collective-permute-start | bytes 786440 | tf_op jit(solution)/shard_map/ppermute | solution.py:55
  122.2 11.6 %collective-permute-start.18 = (f32[1024,64]{0,1:T(8,128)S(1)}, f32[1024,64]{0,1:T(8,128)S(1)}, u32[]{:S(2)}, u32[]{:S(2)}) collective-permute-start(f32[1024,64]{0,1:T(8,128)S(1)} %fusion.17), channel_id=1, source_target_pairs={{4,0},{5,1},{6,2},{7,3}} | collective-permute-start | bytes 786440 | tf_op jit(solution)/shard_map/ppermute | solution.py:55
  137.1 9.1 %collective-permute-start.26 = (f32[512,128]{0,1:T(8,128)S(1)}, f32[512,128]{0,1:T(8,128)S(1)}, u32[]{:S(2)}, u32[]{:S(2)}) collective-permute-start(f32[512,128]{0,1:T(8,128)S(1)} %pad_maximum_fusion.4), channel_id=1, source_target_pairs={{0,3},{1,0},{2,1},{3,2},{4,7},{5,4},{6,5},{7,6},{8,11},{9,8},{10,9... | collective-permute-start | bytes 786440 | tf_op jit(solution)/shard_map/ppermute | solution.py:65
  137.2 24.9 %collective-permute-start.27 = (f32[512,128]{0,1:T(8,128)S(1)}, f32[512,128]{0,1:T(8,128)S(1)}, u32[]{:S(2)}, u32[]{:S(2)}) collective-permute-start(f32[512,128]{0,1:T(8,128)S(1)} %pad_maximum_fusion.5), channel_id=1, source_target_pairs={{0,2},{1,3},{2,0},{3,1},{4,6},{5,7},{6,4},{7,5},{8,10},{9,11},{10,... | collective-permute-start | bytes 786440 | tf_op jit(solution)/shard_map/ppermute | solution.py:65
  138.4 23.7 %collective-permute-start.28 = (f32[512,128]{0,1:T(8,128)S(1)}, f32[512,128]{0,1:T(8,128)S(1)}, u32[]{:S(2)}, u32[]{:S(2)}) collective-permute-start(f32[512,128]{0,1:T(8,128)S(1)} %pad_maximum_fusion.6), channel_id=1, source_target_pairs={{0,1},{1,2},{2,3},{3,0},{4,5},{5,6},{6,7},{7,4},{8,9},{9,10},{10,1... | collective-permute-start | bytes 786440 | tf_op jit(solution)/shard_map/ppermute | solution.py:65
  169.5 3.6 %collective-permute-start.29 = (f32[512]{0:T(512)S(1)}, f32[512]{0:T(512)S(1)}, u32[]{:S(2)}, u32[]{:S(2)}) collective-permute-start(f32[512]{0:T(512)S(1)} %dynamic_slice.48), channel_id=1, source_target_pairs={{0,1},{1,0},{2,3},{3,2},{4,5},{5,4},{6,7},{7,6},{8,9},{9,8},{10,11... | collective-permute-start | bytes 6152 | tf_op jit(solution)/shard_map/ppermute | solution.py:80
  (8 other events, 87.5 us)

commit v18 on v16

--- a/solution.py
+++ b/solution.py
@@ -49,7 +49,11 @@
     own = [None] * CHUNKS
     for k in range(groups - 1, -1, -1):
         for j in range(CHUNKS):
-            fresh = product(whole_map, incoming[j])
+            if k == groups - 1:
+                picked = lax.dynamic_slice_in_dim(whole_map, place * width + j * step, step, 1)
+                fresh = picked + product(whole_map[:, state_dim:], incoming[j][state_dim:])
+            else:
+                fresh = product(whole_map, incoming[j])
             own[j] = fresh if own[j] is None else jnp.where(group == k, fresh, own[j])
             if k > 0:
                 incoming[j] = lax.ppermute(fresh, "tm", [(k, k - 1)])

time: 172 us -> 174 us (1.012)
  matrix products: 37.1 us -> 27.8 us
  local copies, waits for them, and re-layouts: 9.13 us -> 15.2 us
  other arithmetic: 1.41 us -> 3.25 us
  waiting for transfers between devices: 87.4 us -> 89.2 us
    dot_general x18, matrix products: 37.1 us -> 27.8 us  [product(): jnp.dot(left, right, precision=lax.Precision.HIGH, preferred_element_type...]
    reshape x0 -> x1, local copies, waits for them, and re-layouts: none -> 5.5 us  [body(): jnp.concatenate([upper, lower], axis=1)]
    ppermute x14, waiting for transfers between devices: 8.31 us -> 12.7 us  [body(): incoming[j] = lax.ppermute(fresh, 'tm', [(k, k - 1)])]
    concatenate x1, other arithmetic: 0.58 us -> 2.5 us  [body(): jnp.concatenate([upper, lower], axis=1)]
    unnamed x31 -> x33, local copies, waits for them, and re-layouts: 6.22 us -> 6.91 us
  transfers between devices with their start and end apart: 30 -> 30, of which waited for: 12 -> 12; matrix products, arithmetic and copies ran while one was open for 20% -> 15% of each run, Pallas kernels for 0% -> 0%
where the time goes in v18:
time: 174 us; the launch traced here: 173 us
  waiting for transfers between devices  89.2 us (51%)
  starting transfers between devices  36.1 us (21%)
  matrix products  27.8 us (16%)
  local copies, waits for them, and re-layouts  15.2 us (9%)
  other arithmetic  3.25 us (2%)
    ppermute x6, waiting for transfers between devices, line_gather(): lax.ppermute(leftward, 'row', [(z, z - 1) for z in range(1, count - t + 1)])  36.6 us
    dot_general x18, matrix products, product(): jnp.dot(left, right, precision=lax.Precision.HIGH, preferred_element_type...  27.8 us
    ppermute x3, waiting for transfers between devices, body(): lax.ppermute(payload, 'row', [(z, (z + d) % count) for z in range(count)])  22 us
    ppermute x6, waiting for transfers between devices, line_gather(): lax.ppermute(rightward, 'row', [(z, z + 1) for z in range(t - 1, count -...  14.8 us
    ppermute x6, starting transfers between devices, line_gather(): lax.ppermute(rightward, 'row', [(z, z + 1) for z in range(t - 1, count -...  14.4 us
    ppermute x14, waiting for transfers between devices, body(): incoming[j] = lax.ppermute(fresh, 'tm', [(k, k - 1)])  12.7 us
    ppermute x14, starting transfers between devices, body(): incoming[j] = lax.ppermute(fresh, 'tm', [(k, k - 1)])  10.9 us
    ppermute x6, starting transfers between devices, line_gather(): lax.ppermute(leftward, 'row', [(z, z - 1) for z in range(1, count - t + 1)])  7.71 us
  transfers between devices with their start and end apart: 30, of which 12 were waited for; matrix products, arithmetic and copies ran while one was open for 15% of the time, Pallas kernels for 0%

profile of v18, /device:TPU:0, one launch (start us, length us, event | category | flops | bytes accessed | tf_op | source)
XLA Modules:
  0.0 172.9 jit_solution(5705433533447360208)
XLA Ops:
  2.0 5.1 %collective-permute-start = (f32[128,1024]{1,0:T(8,128)S(1)}, f32[128,1024]{1,0:T(8,128)S(1)}, u32[]{:S(2)}, u32[]{:S(2)}) collective-permute-start(f32[128,1024]{1,0:T(8,128)S(1)} %get-tuple-element.4), channel_id=1, source_target_pairs={{0,1},{1,2},{2,3},{4,5},{5,6},{6,7},{8,9},{9,10},{10,11},{12,13},{... | collective-permute-start | bytes 1572872 | tf_op jit(solution)/shard_map/ppermute | solution.py:19
  7.1 3.5 %collective-permute-start.6 = (f32[128,1024]{1,0:T(8,128)S(1)}, f32[128,1024]{1,0:T(8,128)S(1)}, u32[]{:S(2)}, u32[]{:S(2)}) collective-permute-start(f32[128,1024]{1,0:T(8,128)S(1)} %get-tuple-element.5), channel_id=1, source_target_pairs={{0,1},{1,2},{2,3},{4,5},{5,6},{6,7},{8,9},{9,10},{10,11},{12,13},{... | collective-permute-start | bytes 1572872 | tf_op jit(solution)/shard_map/ppermute | solution.py:19
  13.2 6.2 %collective-permute-done = f32[128,1024]{1,0:T(8,128)S(1)} collective-permute-done((f32[128,1024]{1,0:T(8,128)S(1)}, f32[128,1024]{1,0:T(8,128)S(1)}, u32[]{:S(2)}, u32[]{:S(2)}) %collective-permute-start) | collective-permute-done | bytes 524320 | tf_op jit(solution)/shard_map/ppermute | solution.py:19
  19.3 1.5 collective-permute-start.1
  20.8 8.6 %collective-permute-done.6 = f32[128,1024]{1,0:T(8,128)S(1)} collective-permute-done((f32[128,1024]{1,0:T(8,128)S(1)}, f32[128,1024]{1,0:T(8,128)S(1)}, u32[]{:S(2)}, u32[]{:S(2)}) %collective-permute-start.6) | collective-permute-done | bytes 524320 | tf_op jit(solution)/shard_map/ppermute | solution.py:19
  29.4 1.4 collective-permute-start.7
  32.2 4.6 %collective-permute-done.3 = f32[128,1024]{1,0:T(8,128)S(1)} collective-permute-done((f32[128,1024]{1,0:T(8,128)S(1)}, f32[128,1024]{1,0:T(8,128)S(1)}, u32[]{:S(2)}, u32[]{:S(2)}) %collective-permute-start.3) | collective-permute-done | bytes 524320 | tf_op jit(solution)/shard_map/ppermute | solution.py:20
  38.1 1.5 collective-permute-start.2
  39.6 1.5 collective-permute-start.8
  41.0 11.1 %collective-permute-done.10 = f32[128,1024]{1,0:T(8,128)} collective-permute-done((f32[128,1024]{1,0:T(8,128)S(1)}, f32[128,1024]{1,0:T(8,128)}, u32[]{:S(2)}, u32[]{:S(2)}) %collective-permute-start.10) | collective-permute-done | bytes 524320 | tf_op jit(solution)/shard_map/ppermute | solution.py:20
  53.4 9.9 %collective-permute-done.4 = f32[128,1024]{1,0:T(8,128)} collective-permute-done((f32[128,1024]{1,0:T(8,128)S(1)}, f32[128,1024]{1,0:T(8,128)}, u32[]{:S(2)}, u32[]{:S(2)}) %collective-permute-start.4) | collective-permute-done | bytes 524320 | tf_op jit(solution)/shard_map/ppermute | solution.py:20
  71.4 3.0 %collective-permute-done.11 = f32[128,1024]{1,0:T(8,128)S(1)} collective-permute-done((f32[128,1024]{1,0:T(8,128)}, f32[128,1024]{1,0:T(8,128)S(1)}, u32[]{:S(2)}, u32[]{:S(2)}) %collective-permute-start.11) | collective-permute-done | bytes 524320 | tf_op jit(solution)/shard_map/ppermute | solution.py:20
  74.7 7.9 %collective-permute-done.5 = f32[128,1024]{1,0:T(8,128)S(1)} collective-permute-done((f32[128,1024]{1,0:T(8,128)}, f32[128,1024]{1,0:T(8,128)S(1)}, u32[]{:S(2)}, u32[]{:S(2)}) %collective-permute-start.5) | collective-permute-done | bytes 524320 | tf_op jit(solution)/shard_map/ppermute | solution.py:20
  82.8 2.5 %pad_maximum_fusion = f32[4,256,1024]{2,1,0:T(8,128)} fusion(f32[4,128,1024]{2,1,0:T(8,128)S(1)} %bitcast.64, f32[4,128,1024]{2,1,0:T(8,128)S(1)} %bitcast.65), kind=kLoop, calls=%fused_computation | loop fusion | flops 1048576 | bytes 8388608 | tf_op jit(solution)/shard_map/concatenate | solution.py:40
  85.3 5.5 %copy.6 = f32[1024,1024]{0,1:T(8,128)} copy(f32[1024,1024]{1,0:T(8,128)} %bitcast.62) | data formatting | bytes 8388608 | tf_op jit(solution)/shard_map/reshape | solution.py:40
  90.8 2.4 %fusion.8 = f32[1024,64]{0,1:T(8,128)S(1)} fusion(f32[1024,1024]{0,1:T(8,128)} %copy.6, s32[]{:T(128)S(6)} %select_n.157, f32[512,128]{0,1:T(8,128)S(1)} %bitcast.66), kind=kOutput, calls=%fused_computation.8 | convolution fusion | flops 201392128 | bytes 2752516 | tf_op jit(solution)/shard_map/dot_general | solution.py:10
  93.9 2.3 %fusion.5 = f32[1024,64]{0,1:T(8,128)S(1)} fusion(f32[1024,1024]{0,1:T(8,128)} %copy.6, s32[]{:T(128)S(6)} %select_n.143, f32[512,128]{0,1:T(8,128)S(1)} %bitcast.67), kind=kOutput, calls=%fused_computation.7 | convolution fusion | flops 201392128 | bytes 2752516 | tf_op jit(solution)/shard_map/dot_general | solution.py:10
  122.7 11.2 %collective-permute-done.25 = f32[1024,64]{0,1:T(8,128)S(1)} collective-permute-done((f32[1024,64]{0,1:T(8,128)S(1)}, f32[1024,64]{0,1:T(8,128)S(1)}, u32[]{:S(2)}, u32[]{:S(2)}) %collective-permute-start.25) | collective-permute-done | bytes 262176 | tf_op jit(solution)/shard_map/ppermute | solution.py:59
  135.2 1.5 collective-permute-done.18
  141.8 6.7 %collective-permute-done.26 = f32[512,128]{0,1:T(8,128)S(1)} collective-permute-done((f32[512,128]{0,1:T(8,128)S(1)}, f32[512,128]{0,1:T(8,128)S(1)}, u32[]{:S(2)}, u32[]{:S(2)}) %collective-permute-start.26) | collective-permute-done | bytes 262176 | tf_op jit(solution)/shard_map/ppermute | solution.py:70
  148.4 15.4 %collective-permute-done.27 = f32[512,128]{0,1:T(8,128)S(1)} collective-permute-done((f32[512,128]{0,1:T(8,128)S(1)}, f32[512,128]{0,1:T(8,128)S(1)}, u32[]{:S(2)}, u32[]{:S(2)}) %collective-permute-start.27) | collective-permute-done | bytes 262176 | tf_op jit(solution)/shard_map/ppermute | solution.py:70
  164.0 2.2 %fusion.12 = f32[256,2048]{1,0:T(8,128)S(1)} fusion(f32[512,2048]{1,0:T(8,128)S(1)} %copy-done.1, f32[256,896]{0,1:T(8,128)S(1)} %slice_dynamic-update-slice_fusion.7, s32[]{:T(128)S(6)} %select_n.142), kind=kOutput, calls=%fused_computation.13 | convolution fusion | flops 1610612736 | bytes 6815748 | tf_op jit(solution)/shard_map/dot_general | solution.py:10
  166.3 2.3 %fusion.4 = f32[2048]{0:T(1024)S(1)} fusion(f32[256,2048]{1,0:T(8,128)S(1)} %fusion.12, f32[512,2048]{1,0:T(8,128)S(1)} %copy-done.1, f32[256,896]{0,1:T(8,128)S(1)} %get-tuple-element.13, s32[]{:T(128)S(6)} %select_n.142), kind=kOutput, calls=%fused_computation.6 | convolution fusion | flops 1611659264 | bytes 6823940 | tf_op jit(solution)/shard_map/dot_general | solution.py:10
  169.3 3.0 %collective-permute-done.29 = f32[512]{0:T(512)S(1)} collective-permute-done((f32[512]{0:T(512)S(1)}, f32[512]{0:T(512)S(1)}, u32[]{:S(2)}, u32[]{:S(2)}) %collective-permute-start.29) | collective-permute-done | bytes 2080 | tf_op jit(solution)/shard_map/ppermute | solution.py:86
  (104 shorter events, 50.7 us)
Async XLA Ops:
  2.0 17.4 %collective-permute-start = (f32[128,1024]{1,0:T(8,128)S(1)}, f32[128,1024]{1,0:T(8,128)S(1)}, u32[]{:S(2)}, u32[]{:S(2)}) collective-permute-start(f32[128,1024]{1,0:T(8,128)S(1)} %get-tuple-element.4), channel_id=1, source_target_pairs={{0,1},{1,2},{2,3},{4,5},{5,6},{6,7},{8,9},{9,10},{10,11},{12,13},{... | collective-permute-start | bytes 1572872 | tf_op jit(solution)/shard_map/ppermute | solution.py:19
  7.1 22.4 %collective-permute-start.6 = (f32[128,1024]{1,0:T(8,128)S(1)}, f32[128,1024]{1,0:T(8,128)S(1)}, u32[]{:S(2)}, u32[]{:S(2)}) collective-permute-start(f32[128,1024]{1,0:T(8,128)S(1)} %get-tuple-element.5), channel_id=1, source_target_pairs={{0,1},{1,2},{2,3},{4,5},{5,6},{6,7},{8,9},{9,10},{10,11},{12,13},{... | collective-permute-start | bytes 1572872 | tf_op jit(solution)/shard_map/ppermute | solution.py:19
  10.6 20.3 %collective-permute-start.9 = (f32[128,1024]{1,0:T(8,128)S(1)}, f32[128,1024]{1,0:T(8,128)S(1)}, u32[]{:S(2)}, u32[]{:S(2)}) collective-permute-start(f32[128,1024]{1,0:T(8,128)S(1)} %get-tuple-element.5), channel_id=1, source_target_pairs={{1,0},{2,1},{3,2},{5,4},{6,5},{7,6},{9,8},{10,9},{11,10},{13,12},{... | collective-permute-start | bytes 1572872 | tf_op jit(solution)/shard_map/ppermute | solution.py:20
  11.9 24.9 %collective-permute-start.3 = (f32[128,1024]{1,0:T(8,128)S(1)}, f32[128,1024]{1,0:T(8,128)S(1)}, u32[]{:S(2)}, u32[]{:S(2)}) collective-permute-start(f32[128,1024]{1,0:T(8,128)S(1)} %get-tuple-element.4), channel_id=1, source_target_pairs={{1,0},{2,1},{3,2},{5,4},{6,5},{7,6},{9,8},{10,9},{11,10},{13,12},{... | collective-permute-start | bytes 1572872 | tf_op jit(solution)/shard_map/ppermute | solution.py:20
  19.3 18.8 %collective-permute-start.1 = (f32[128,1024]{1,0:T(8,128)S(1)}, f32[128,1024]{1,0:T(8,128)}, u32[]{:S(2)}, u32[]{:S(2)}) collective-permute-start(f32[128,1024]{1,0:T(8,128)S(1)} %collective-permute-done), channel_id=1, source_target_pairs={{1,2},{2,3},{5,6},{6,7},{9,10},{10,11},{13,14},{14,15},{17,18},{18... | collective-permute-start | bytes 1572872 | tf_op jit(solution)/shard_map/ppermute | solution.py:19
  29.4 10.1 %collective-permute-start.7 = (f32[128,1024]{1,0:T(8,128)S(1)}, f32[128,1024]{1,0:T(8,128)}, u32[]{:S(2)}, u32[]{:S(2)}) collective-permute-start(f32[128,1024]{1,0:T(8,128)S(1)} %collective-permute-done.6), channel_id=1, source_target_pairs={{1,2},{2,3},{5,6},{6,7},{9,10},{10,11},{13,14},{14,15},{17,18},{18... | collective-permute-start | bytes 1572872 | tf_op jit(solution)/shard_map/ppermute | solution.py:19
  30.9 21.2 %collective-permute-start.10 = (f32[128,1024]{1,0:T(8,128)S(1)}, f32[128,1024]{1,0:T(8,128)}, u32[]{:S(2)}, u32[]{:S(2)}) collective-permute-start(f32[128,1024]{1,0:T(8,128)S(1)} %collective-permute-done.9), channel_id=1, source_target_pairs={{1,0},{2,1},{5,4},{6,5},{9,8},{10,9},{13,12},{14,13},{17,16},{18,1... | collective-permute-start | bytes 1572872 | tf_op jit(solution)/shard_map/ppermute | solution.py:20
  36.8 26.5 %collective-permute-start.4 = (f32[128,1024]{1,0:T(8,128)S(1)}, f32[128,1024]{1,0:T(8,128)}, u32[]{:S(2)}, u32[]{:S(2)}) collective-permute-start(f32[128,1024]{1,0:T(8,128)S(1)} %collective-permute-done.3), channel_id=1, source_target_pairs={{1,0},{2,1},{5,4},{6,5},{9,8},{10,9},{13,12},{14,13},{17,16},{18,1... | collective-permute-start | bytes 1572872 | tf_op jit(solution)/shard_map/ppermute | solution.py:20
  38.1 26.5 %collective-permute-start.2 = (f32[128,1024]{1,0:T(8,128)}, f32[128,1024]{1,0:T(8,128)}, u32[]{:S(2)}, u32[]{:S(2)}) collective-permute-start(f32[128,1024]{1,0:T(8,128)} %collective-permute-done.1), channel_id=1, source_target_pairs={{2,3},{6,7},{10,11},{14,15},{18,19},{22,23},{26,27},{30,31}} | collective-permute-start | bytes 1572872 | tf_op jit(solution)/shard_map/ppermute | solution.py:19
  39.6 27.3 %collective-permute-start.8 = (f32[128,1024]{1,0:T(8,128)}, f32[128,1024]{1,0:T(8,128)}, u32[]{:S(2)}, u32[]{:S(2)}) collective-permute-start(f32[128,1024]{1,0:T(8,128)} %collective-permute-done.7), channel_id=1, source_target_pairs={{2,3},{6,7},{10,11},{14,15},{18,19},{22,23},{26,27},{30,31}} | collective-permute-start | bytes 1572872 | tf_op jit(solution)/shard_map/ppermute | solution.py:19
  52.1 22.4 %collective-permute-start.11 = (f32[128,1024]{1,0:T(8,128)}, f32[128,1024]{1,0:T(8,128)S(1)}, u32[]{:S(2)}, u32[]{:S(2)}) collective-permute-start(f32[128,1024]{1,0:T(8,128)} %collective-permute-done.10), channel_id=1, source_target_pairs={{1,0},{5,4},{9,8},{13,12},{17,16},{21,20},{25,24},{29,28}} | collective-permute-start | bytes 1572872 | tf_op jit(solution)/shard_map/ppermute | solution.py:20
  63.3 19.2 %collective-permute-start.5 = (f32[128,1024]{1,0:T(8,128)}, f32[128,1024]{1,0:T(8,128)S(1)}, u32[]{:S(2)}, u32[]{:S(2)}) collective-permute-start(f32[128,1024]{1,0:T(8,128)} %collective-permute-done.4), channel_id=1, source_target_pairs={{1,0},{5,4},{9,8},{13,12},{17,16},{21,20},{25,24},{29,28}} | collective-permute-start | bytes 1572872 | tf_op jit(solution)/shard_map/ppermute | solution.py:20
  93.2 3.7 %collective-permute-start.19 = (f32[1024,64]{0,1:T(8,128)S(1)}, f32[1024,64]{0,1:T(8,128)S(1)}, u32[]{:S(2)}, u32[]{:S(2)}) collective-permute-start(f32[1024,64]{0,1:T(8,128)S(1)} %fusion.8), channel_id=1, source_target_pairs={{28,24},{29,25},{30,26},{31,27}} | collective-permute-start | bytes 786440 | tf_op jit(solution)/shard_map/ppermute | solution.py:59
  96.2 2.7 %collective-permute-start.12 = (f32[1024,64]{0,1:T(8,128)S(1)}, f32[1024,64]{0,1:T(8,128)S(1)}, u32[]{:S(2)}, u32[]{:S(2)}) collective-permute-start(f32[1024,64]{0,1:T(8,128)S(1)} %fusion.5), channel_id=1, source_target_pairs={{28,24},{29,25},{30,26},{31,27}} | collective-permute-start | bytes 786440 | tf_op jit(solution)/shard_map/ppermute | solution.py:59
  106.4 2.9 %collective-permute-start.22 = (f32[1024,64]{0,1:T(8,128)S(1)}, f32[1024,64]{0,1:T(8,128)S(1)}, u32[]{:S(2)}, u32[]{:S(2)}) collective-permute-start(f32[1024,64]{0,1:T(8,128)S(1)} %fusion.26), channel_id=1, source_target_pairs={{16,12},{17,13},{18,14},{19,15}} | collective-permute-start | bytes 786440 | tf_op jit(solution)/shard_map/ppermute | solution.py:59
  108.4 2.9 %collective-permute-start.15 = (f32[1024,64]{0,1:T(8,128)S(1)}, f32[1024,64]{0,1:T(8,128)S(1)}, u32[]{:S(2)}, u32[]{:S(2)}) collective-permute-start(f32[1024,64]{0,1:T(8,128)S(1)} %fusion.20), channel_id=1, source_target_pairs={{16,12},{17,13},{18,14},{19,15}} | collective-permute-start | bytes 786440 | tf_op jit(solution)/shard_map/ppermute | solution.py:59
  110.6 2.7 %collective-permute-start.23 = (f32[1024,64]{0,1:T(8,128)S(1)}, f32[1024,64]{0,1:T(8,128)S(1)}, u32[]{:S(2)}, u32[]{:S(2)}) collective-permute-start(f32[1024,64]{0,1:T(8,128)S(1)} %fusion.27), channel_id=1, source_target_pairs={{12,8},{13,9},{14,10},{15,11}} | collective-permute-start | bytes 786440 | tf_op jit(solution)/shard_map/ppermute | solution.py:59
  116.7 3.3 %collective-permute-start.17 = (f32[1024,64]{0,1:T(8,128)S(1)}, f32[1024,64]{0,1:T(8,128)S(1)}, u32[]{:S(2)}, u32[]{:S(2)}) collective-permute-start(f32[1024,64]{0,1:T(8,128)S(1)} %fusion.22), channel_id=1, source_target_pairs={{8,4},{9,5},{10,6},{11,7}} | collective-permute-start | bytes 786440 | tf_op jit(solution)/shard_map/ppermute | solution.py:59
  118.7 15.2 %collective-permute-start.25 = (f32[1024,64]{0,1:T(8,128)S(1)}, f32[1024,64]{0,1:T(8,128)S(1)}, u32[]{:S(2)}, u32[]{:S(2)}) collective-permute-start(f32[1024,64]{0,1:T(8,128)S(1)} %fusion.29), channel_id=1, source_target_pairs={{4,0},{5,1},{6,2},{7,3}} | collective-permute-start | bytes 786440 | tf_op jit(solution)/shard_map/ppermute | solution.py:59
  121.4 15.3 %collective-permute-start.18 = (f32[1024,64]{0,1:T(8,128)S(1)}, f32[1024,64]{0,1:T(8,128)S(1)}, u32[]{:S(2)}, u32[]{:S(2)}) collective-permute-start(f32[1024,64]{0,1:T(8,128)S(1)} %fusion.23), channel_id=1, source_target_pairs={{4,0},{5,1},{6,2},{7,3}} | collective-permute-start | bytes 786440 | tf_op jit(solution)/shard_map/ppermute | solution.py:59
  139.2 9.2 %collective-permute-start.26 = (f32[512,128]{0,1:T(8,128)S(1)}, f32[512,128]{0,1:T(8,128)S(1)}, u32[]{:S(2)}, u32[]{:S(2)}) collective-permute-start(f32[512,128]{0,1:T(8,128)S(1)} %pad_maximum_fusion.2), channel_id=1, source_target_pairs={{0,3},{1,0},{2,1},{3,2},{4,7},{5,4},{6,5},{7,6},{8,11},{9,8},{10,9... | collective-permute-start | bytes 786440 | tf_op jit(solution)/shard_map/ppermute | solution.py:70
  140.6 23.2 %collective-permute-start.27 = (f32[512,128]{0,1:T(8,128)S(1)}, f32[512,128]{0,1:T(8,128)S(1)}, u32[]{:S(2)}, u32[]{:S(2)}) collective-permute-start(f32[512,128]{0,1:T(8,128)S(1)} %pad_maximum_fusion.3), channel_id=1, source_target_pairs={{0,2},{1,3},{2,0},{3,1},{4,6},{5,7},{6,4},{7,5},{8,10},{9,11},{10,... | collective-permute-start | bytes 786440 | tf_op jit(solution)/shard_map/ppermute | solution.py:70
  140.7 23.1 %collective-permute-start.28 = (f32[512,128]{0,1:T(8,128)S(1)}, f32[512,128]{0,1:T(8,128)S(1)}, u32[]{:S(2)}, u32[]{:S(2)}) collective-permute-start(f32[512,128]{0,1:T(8,128)S(1)} %pad_maximum_fusion.4), channel_id=1, source_target_pairs={{0,1},{1,2},{2,3},{3,0},{4,5},{5,6},{6,7},{7,4},{8,9},{9,10},{10,1... | collective-permute-start | bytes 786440 | tf_op jit(solution)/shard_map/ppermute | solution.py:70
  168.6 3.6 %collective-permute-start.29 = (f32[512]{0:T(512)S(1)}, f32[512]{0:T(512)S(1)}, u32[]{:S(2)}, u32[]{:S(2)}) collective-permute-start(f32[512]{0:T(512)S(1)} %dynamic_slice.60), channel_id=1, source_target_pairs={{0,1},{1,0},{2,3},{3,2},{4,5},{5,4},{6,7},{7,6},{8,9},{9,8},{10,11... | collective-permute-start | bytes 6152 | tf_op jit(solution)/shard_map/ppermute | solution.py:86
  (11 other events, 126.5 us)
